TPU v7x, 256 devices: a whole 4x4x8 slice. The times are simulated.
256 devices in a mesh: ctx: 64 (over y, z, core), ch: 4 (over x).
Axes of the slice: x: 4, y: 4, z: 8, core: 2. Of those that a mesh axis runs over, the one named last changes fastest.
Arguments:
- stream: bfloat16 [8192, 4096], P('ctx', 'ch'), may hold values from -6 to 6
- norm_gain: float32 [4096], P('ch'), may hold values from 0.25 to 1.75
- short_filters: float32 [3, 3, 4096], P(None, None, 'ch'), may hold values from -3.5 to 3.5
- mode_rates: float32 [16, 4096], P(None, 'ch'), as said below
- residues: float32 [16, 4096], P(None, 'ch'), as said below
- grad_out: bfloat16 [8192, 4096], P('ctx', 'ch'), may hold values from -6 to 6
Outputs:
- output: bfloat16 [8192, 4096], P('ctx', 'ch')
- grad_stream: bfloat16 [8192, 4096], P('ctx', 'ch')
- grad_residues: float32 [16, 4096], P(None, 'ch')
- grad_short: float32 [3, 3, 4096], P(None, None, 'ch')
Inputs may be any that keep to these rules, and one draw needn't show every extreme that they name: `mode_rates`: each rate lies between 0.05 / 8192 and 0.03. `residues`: each weight is at most 4 * sqrt(0.06 / 16) in magnitude.
All inputs are finite; a program needn't handle non-finite values.
Results may differ from a plain program's by a relative error of at most 0.0054.
Values may be sent and summed in bfloat16 or wider, within the bound.
No kernel may reach another device: no remote copies, remote signals or barrier semaphores. Data moves between devices by JAX's collectives and lax.ppermute only.
A program may use at most 192 MiB of HBM per device.

v0:
```python
import jax
import jax.numpy as jnp
from jax import lax
from jax.sharding import PartitionSpec as P

M = 16
KS = 3
P_SIZE = 32


HIGHEST = lax.Precision.HIGHEST
HIGHER = lax.Precision.HIGH
EPSILON = 1e-05


def passed_along(value, axis, steps):
    count = lax.axis_size(axis)
    first, last = (max(0, -steps), min(count, count - steps))
    return lax.ppermute(value, axis, [(source, source + steps) for source in range(first, last)])


def entering(part, axis, combine, identity, reverse):
    count = lax.axis_size(axis)
    place = lax.axis_index(axis)
    ahead = count - 1 - place if reverse else place
    gathered = jax.tree.map(lambda a: lax.all_gather(a, axis), part)
    state = jax.tree.map(lambda a, e: jnp.zeros_like(a) + jnp.asarray(e, a.dtype), part, identity)

    def one(step, state):
        source = count - 1 - step if reverse else step
        return combine(
            state, jax.tree.map(lambda a: lax.dynamic_index_in_dim(a, source, 0, False), gathered)
        )

    return lax.fori_loop(0, ahead, one, state)


def lag_table(length):
    steps = jnp.arange(length)
    return (steps[:, None, None] - steps[None, :, None] == steps[None, None, :]).astype(jnp.float32)


def filter_tables(decay_rates, residues):
    steps = jnp.arange(P_SIZE).astype(jnp.float32)
    decay_table = jnp.exp(-decay_rates[:, None, :] * steps[None, :, None])
    shifted = jnp.exp(-decay_rates[:, None, :] * (steps[None, :, None] + 1.0))
    response = jnp.sum(residues[:, None, :] * decay_table, axis=0)
    toeplitz = jnp.einsum("nc,ijn->ijc", response, lag_table(P_SIZE), precision=HIGHEST)
    step_decay = jnp.exp(-decay_rates * P_SIZE)
    return (decay_table, shifted, toeplitz, step_decay)


def chain(earlier, later):
    return (earlier[0] * later[0], earlier[1] * later[0] + later[1])


def per_device(stream, norm_gain, short_filters, mode_rates, residues, grad_out):
    row_count, chan_count = stream.shape
    block_count = row_count // P_SIZE
    total_chans = chan_count * lax.axis_size("ch")
    total_rows = row_count * lax.axis_size("ctx")
    stream_wide = stream.astype(jnp.float32)
    squares = lax.psum(jnp.sum(stream_wide * stream_wide, axis=1), "ch")
    row_scale = lax.rsqrt(squares / total_chans + EPSILON)
    normed = (stream_wide * row_scale[:, None] * norm_gain[None, :]).astype(jnp.bfloat16)
    rim_rows = passed_along(normed[row_count - (KS - 1) :], "ctx", 1)
    padded_half = jnp.concatenate([rim_rows, lax.optimization_barrier(normed)], 0)
    padded = padded_half.astype(jnp.float32)
    branches = [
        sum(
            (
                short_filters[branch, offset][None, :]
                * padded[KS - 1 - offset : KS - 1 - offset + row_count]
                for offset in range(KS)
            )
        )
        for branch in range(3)
    ]
    query_part, key_part, value_part = branches
    product = lax.optimization_barrier((key_part * value_part).astype(jnp.bfloat16)).astype(
        jnp.float32
    )
    decay_table, shifted, toeplitz, step_decay = filter_tables(mode_rates, residues)
    blocks = product.reshape(block_count, P_SIZE, chan_count)
    block_ends = jnp.einsum("mjc,bjc->bmc", decay_table[:, ::-1, :], blocks, precision=HIGHER)
    block_steps = jnp.arange(block_count).astype(jnp.float32)
    own_state = jnp.sum(
        jnp.exp(-mode_rates[None] * (P_SIZE * (block_count - 1 - block_steps))[:, None, None])
        * block_ends,
        axis=0,
    )
    cotangent = grad_out.astype(jnp.float32)
    grad_conv = cotangent * query_part
    grad_blocks = grad_conv.reshape(block_count, P_SIZE, chan_count)
    block_heads = jnp.einsum("mic,bic->bmc", decay_table, grad_blocks, precision=HIGHEST)
    own_back = jnp.sum(
        jnp.exp(-mode_rates[None] * (P_SIZE * block_steps)[:, None, None]) * block_heads, axis=0
    )
    zero_state = jnp.zeros((M, chan_count), jnp.float32)
    whole_decay = jnp.exp(-mode_rates * row_count)
    _, incoming = entering(
        (whole_decay, own_state), "ctx", chain, (jnp.ones_like(whole_decay), zero_state), False
    )
    carried_table = shifted * residues[:, None, :]

    def forward_step(carry_state, inputs):
        one_block, block_end = inputs
        local_part = jnp.einsum("ijc,jc->ic", toeplitz, one_block, precision=HIGHER)
        carried = jnp.einsum("mc,mic->ic", carry_state, carried_table, precision=HIGHEST)
        return (step_decay * carry_state + block_end, (local_part + carried, carry_state))

    _, (long_conv, starts) = lax.scan(forward_step, incoming, (blocks, block_ends))
    long_conv = long_conv.reshape(row_count, chan_count)
    output = (query_part * long_conv).astype(jnp.bfloat16)
    grad_query = (cotangent * long_conv).astype(jnp.bfloat16)
    whole_back = jnp.exp(-mode_rates * row_count)
    _, later_state = entering(
        (whole_back, own_back), "ctx", chain, (jnp.ones_like(whole_back), zero_state), True
    )
    back_table = carried_table[:, ::-1, :]

    def backward_step(carry_state, inputs):
        one_block, block_head = inputs
        local_part = jnp.einsum("ijc,ic->jc", toeplitz, one_block, precision=HIGHEST)
        carried = jnp.einsum("mc,mjc->jc", carry_state, back_table, precision=HIGHEST)
        return (step_decay * carry_state + block_head, local_part + carried)

    _, grad_product = lax.scan(backward_step, later_state, (grad_blocks, block_heads), reverse=True)
    grad_product = grad_product.reshape(row_count, chan_count)
    grad_key = (grad_product * value_part).astype(jnp.bfloat16)
    grad_value = (grad_product * key_part).astype(jnp.bfloat16)
    weighted = jnp.einsum("mic,bic->bmc", shifted, grad_blocks, precision=HIGHEST)
    cross_part = jnp.sum(weighted * starts, axis=0)
    pairs = jnp.einsum("bic,bjc->ijc", grad_blocks, blocks, precision=HIGHEST)
    by_lag = jnp.einsum("ijc,ijn->nc", pairs, lag_table(P_SIZE), precision=HIGHEST)
    local_terms = jnp.einsum("nc,mnc->mc", by_lag, decay_table, precision=HIGHEST)
    stacked_half = lax.optimization_barrier(jnp.stack([grad_query, grad_key, grad_value], 0))
    next_rows = passed_along(stacked_half[:, : KS - 1], "ctx", -1)
    stacked = stacked_half.astype(jnp.float32)
    after = jnp.concatenate([stacked, next_rows.astype(jnp.float32)], 1)
    grad_normed = sum(
        (
            short_filters[branch, offset][None, :] * after[branch, offset : offset + row_count]
            for branch in range(3)
            for offset in range(KS)
        )
    )
    short_terms = jnp.stack(
        [
            jnp.einsum(
                "btc,tc->bc",
                stacked_half,
                padded_half[KS - 1 - offset : KS - 1 - offset + row_count],
                preferred_element_type=jnp.float32,
            )
            for offset in range(KS)
        ],
        1,
    )
    residue_sum, short_sum = lax.psum((cross_part + local_terms, short_terms), "ctx")
    norm_factor = 1.0 / jnp.sqrt(jnp.float32(total_rows))
    grad_residues = residue_sum * norm_factor
    grad_short = short_sum * norm_factor
    row_dot = lax.psum(jnp.sum(norm_gain[None, :] * grad_normed * stream_wide, axis=1), "ch")
    grad_stream = (
        row_scale[:, None] * norm_gain[None, :] * grad_normed
        - stream_wide * (row_scale**3 * row_dot / total_chans)[:, None]
    ).astype(jnp.bfloat16)
    return (output, grad_stream, grad_residues, grad_short)


def solution(mesh):
    return jax.shard_map(
        per_device,
        mesh=mesh,
        in_specs=(
            P("ctx", "ch"),
            P("ch"),
            P(None, None, "ch"),
            P(None, "ch"),
            P(None, "ch"),
            P("ctx", "ch"),
        ),
        out_specs=(P("ctx", "ch"), P("ctx", "ch"), P(None, "ch"), P(None, None, "ch")),
        check_vma=False,
    )
```

profile of v0, /device:TPU:32, one launch (start us, length us, event | category | flops | bytes accessed | tf_op | source)
XLA Modules:
  0.0 788.1 jit_solution(16224774663394047859)
XLA Ops:
  9.9 10.5 %psum.28 = f32[128]{0:T(128)S(1)} all-reduce(f32[128]{0:T(128)S(1)} %fusion.7), channel_id=1, replica_groups=mesh['ctx'=64,'ch'=4] {'ch'}, use_global_device_ids=true, to_apply=%region_1.0 | all-reduce | flops 128 | bytes 1024 | tf_op jit(solution)/shard_map/psum | solution.py:63
  25.0 4.5 broadcast_multiply_fusion
  29.5 3.3 rev.6
  32.8 6.2 copy.74
  40.1 7.5 copy.69
  51.9 8.6 %convolution_bitcast_fusion.2 = f32[4,16,1024]{1,0,2:T(4,128)S(1)} fusion(bf16[4,32,1024]{1,0,2:T(4,128)(2,1)S(1)} %copy.68, f32[16,32,1024]{1,0,2:T(8,128)} %copy.69), kind=kOutput, calls=%fused_computation.33 | convolution fusion | flops 12582912 | bytes 2621440 | tf_op jit(solution)/shard_map/mjc,bjc->bmc/dot_general | solution.py:85
  60.5 21.3 %multiply_reduce_fusion.4 = (f32[16,1024]{0,1:T(8,128)}, f32[16,1024]{0,1:T(8,128)}, f32[4,16,1024]{1,0,2:T(4,128)}) fusion(f32[4]{0:T(128)S(1)} %get-tuple-element.590, f32[16,1024]{0,1:T(8,128)S(1)} %copy-done.7, f32[4,16,1024]{1,0,2:T(4,128)S(1)} %convolution_bitcast_fusion.2, f32[4]{0:T(128)S(1)} %get-tuple-element.589, f32[4,32,1024]{1,0,2:T(4,128)S(1)} %copy.73, ...), kind=kOutput, calls=%fused_computation.27 | convolution fusion | flops 25526272 | bytes 3342368 | tf_op jit(solution)/shard_map/mic,bic->bmc/dot_general | solution.py:95
  85.7 4.6 rev.7
  90.3 7.5 copy.78
  97.8 4.3 fusion.45
  109.0 10.7 %convolution_bitcast_fusion = f32[32,32,1024]{0,1,2:T(8,128)} fusion(bf16[4,32,1024]{1,0,2:T(4,128)(2,1)S(1)} %copy.68, f32[4,32,1024]{1,0,2:T(4,128)} %copy-done), kind=kOutput, calls=%fused_computation.16 | convolution fusion | flops 50331648 | bytes 4980736 | tf_op jit(solution)/shard_map/bic,bjc->ijc/dot_general | solution.py:134
  119.8 12.1 %copy.82 = f32[32,32,1024]{2,1,0:T(8,128)} copy(f32[32,32,1024]{0,1,2:T(8,128)} %convolution_bitcast_fusion) | data formatting | bytes 8388608 | tf_op jit(solution)/shard_map/bic,bjc->ijc/transpose | solution.py:134
  133.1 15.0 %fusion.44 = f32[32,1024,1]{0,1,2:T(8,128)S(1)} fusion(f32[32,32,1024]{2,1,0:T(8,128)} %copy.82, s32[32,32]{1,0:T(8,128)S(1)} %iota_subtract_fusion), kind=kOutput, calls=%fused_computation.96 | convolution fusion | flops 402685952 | bytes 4329472 | tf_op jit(solution)/shard_map/ijc,ijn->nc/dot_general | solution.py:135
  148.1 16.4 %fusion.60 = f32[1024,1,16]{2,1,0:T(1,128)} fusion(f32[16,32,1024]{1,0,2:T(8,128)} %copy.74, f32[32,1024,1]{0,2,1:T(1,128)S(1)} %bitcast.249), kind=kOutput, calls=%fused_computation.131 | convolution fusion | flops 6291456 | bytes 2293760 | tf_op jit(solution)/shard_map/nc,mnc->mc/dot_general | solution.py:136
  164.5 6.9 all-gather.11.cloned.1.call-done
  171.4 56.8 %while.58 = (s32[]{:T(128)}, f32[16,1024]{1,0:T(8,128)S(1)}, s32[]{:T(128)}, f32[64,16,1024]{2,1,0:T(8,128)}, f32[64,16,1024]{2,1,0:T(8,128)}, /*index=5*/s32[]{:T(128)}, s32[]{:T(128)}, s32[]{:T(128)}, s32[]{:T(128)}) while((s32[]{:T(128)}, f32[16,1024]{1,0:T(8,128)S(1)}, s32[]{:T(128)}, f32[64,16,1024]{2,1,0:T(8,128)}, ...), condition=%wide.region_10.11_spmd, body=%wide.region_9.10_spmd.sunk | while | flops 32774 | bytes 262287 | solution.py:35
  228.3 19.5 %while.59 = (s32[]{:T(128)}, f32[16,1024]{1,0:T(8,128)S(1)}, f32[4,32,1024]{2,1,0:T(8,128)S(1)}, f32[16,1024]{1,0:T(8,128)S(1)}, f32[4,16,1024]{2,1,0:T(8,128)},...) while((s32[]{:T(128)}, f32[16,1024]{1,0:T(8,128)S(1)}, ...), condition=%wide.region_12.13_spmd, body=%wide.region_11.12_spmd.sunk | while | flops 3145731 | bytes 7667837 | solution.py:128
  252.5 21.3 %while.60 = (s32[]{:T(128)}, f32[16,1024]{1,0:T(8,128)S(1)}, f32[4,32,1024]{2,1,0:T(8,128)S(1)}, f32[4,16,1024]{2,1,0:T(8,128)S(1)}, f32[16,1024]{1,0:T(8,128)S(...) while((s32[]{:T(128)}, f32[16,1024]{1,0:T(8,128)S(1)}, ...), condition=%wide.region_7.8_spmd.clone, body=%wide.region_6.7_spmd.clone.sunk | while | flops 4194306 | bytes 6095137 | solution.py:112
  253.5 2.9 multiply_reduce_fusion.13
  258.8 2.9 multiply_reduce_fusion.13
  276.6 300.9 %psum.31 = f32[3,3,1024]{2,0,1:T(4,128)S(1)} all-reduce(f32[3,3,1024]{2,0,1:T(4,128)S(1)} %pad_maximum_fusion.3), channel_id=1, replica_groups=mesh['ctx'=64,'ch'=4] {'ctx'}, use_global_device_ids=true, to_apply=%region_17.18 | all-reduce | flops 9216 | bytes 73728 | tf_op jit(solution)/shard_map/psum | solution.py:160
  581.1 18.7 %fusion.2 = f32[16,1024]{0,1:T(8,128)S(1)} fusion(f32[4,16,1024]{1,0,2:T(4,128)} %copy.79, f32[4,32,1024]{1,0,2:T(4,128)S(1)} %copy-done.1, f32[16,32,1024]{1,0,2:T(8,128)} %copy.78), kind=kOutput, calls=%fused_computation.26 | convolution fusion | flops 25280512 | bytes 2949120 | tf_op jit(solution)/shard_map/mic,bic->bmc/dot_general | solution.py:132
  602.6 10.6 %psum.29 = f32[128]{0:T(128)S(1)} all-reduce(f32[128]{0:T(128)S(1)} %get-tuple-element.556), channel_id=1, replica_groups=mesh['ctx'=64,'ch'=4] {'ch'}, use_global_device_ids=true, to_apply=%region_14.15 | all-reduce | flops 128 | bytes 1024 | tf_op jit(solution)/shard_map/psum | solution.py:164
  614.1 165.4 %all-reduce.2.cloned.1.call-done = f32[16,1024]{0,1:T(8,128)} async-done(((f32[16,1024]{0,1:T(8,128)}), f32[16,1024]{0,1:T(8,128)}) %all-reduce.2.cloned.1.call-update) | async-done | bytes 65552 | tf_op jit(solution)/shard_map/psum | solution.py:160
  (261 shorter events, 132.3 us)
Async XLA Ops:
  7.2 157.3 %all-gather.7.cloned.1.call-start = ((), (), s32[]{:S(2)}) async-start(), calls=%async_computation.1 | async-start | bytes 4259840 | tf_op jit(solution)/shard_map/all_gather | solution.py:26
  8.7 162.6 %all-gather.11.cloned.1.call-start = ((), (), s32[]{:S(2)}) async-start(), calls=%async_computation.3 | async-start | bytes 4259840 | tf_op jit(solution)/shard_map/all_gather | solution.py:26
  22.0 25.6 %collective-permute-start = (bf16[2,1024]{1,0:T(2,128)(2,1)S(1)}, bf16[2,1024]{1,0:T(2,128)(2,1)S(1)}, u32[]{:S(2)}, u32[]{:S(2)}) collective-permute-start(bf16[2,1024]{1,0:T(2,128)(2,1)S(1)} %slice.115), channel_id=1, source_target_pairs={{0,4},{4,8},{8,12},{12,16},{16,20},{20,24},{24,28},{28,32},{32,36}... | collective-permute-start | bytes 12296 | tf_op jit(solution)/shard_map/ppermute | solution.py:19
  24.9 22.8 %copy-start.20 = (f32[1,1,1024]{2,1,0:T(1,128)}, f32[1,1,1024]{2,1,0:T(1,128)S(1)}, u32[]{:S(2)}) copy-start(f32[1,1,1024]{2,1,0:T(1,128)S(1)} %get-tuple-element.579) | copy-start | bytes 12292
  24.9 22.8 %copy-start.22 = (f32[1,1,1024]{2,1,0:T(1,128)}, f32[1,1,1024]{2,1,0:T(1,128)S(1)}, u32[]{:S(2)}) copy-start(f32[1,1,1024]{2,1,0:T(1,128)S(1)} %get-tuple-element.580) | copy-start | bytes 12292
  24.9 22.8 %copy-start.24 = (f32[1,1,1024]{2,1,0:T(1,128)}, f32[1,1,1024]{2,1,0:T(1,128)S(1)}, u32[]{:S(2)}) copy-start(f32[1,1,1024]{2,1,0:T(1,128)S(1)} %get-tuple-element.581) | copy-start | bytes 12292
  24.9 22.8 %copy-start.26 = (f32[1,1,1024]{2,1,0:T(1,128)}, f32[1,1,1024]{2,1,0:T(1,128)S(1)}, u32[]{:S(2)}) copy-start(f32[1,1,1024]{2,1,0:T(1,128)S(1)} %get-tuple-element.582) | copy-start | bytes 12292
  24.9 22.8 %copy-start.28 = (f32[1,1,1024]{2,1,0:T(1,128)}, f32[1,1,1024]{2,1,0:T(1,128)S(1)}, u32[]{:S(2)}) copy-start(f32[1,1,1024]{2,1,0:T(1,128)S(1)} %get-tuple-element.583) | copy-start | bytes 12292
  24.9 22.8 %copy-start.30 = (f32[1,1,1024]{2,1,0:T(1,128)}, f32[1,1,1024]{2,1,0:T(1,128)S(1)}, u32[]{:S(2)}) copy-start(f32[1,1,1024]{2,1,0:T(1,128)S(1)} %get-tuple-element.584) | copy-start | bytes 12292
  24.9 22.8 %copy-start.32 = (f32[1,1,1024]{2,1,0:T(1,128)}, f32[1,1,1024]{2,1,0:T(1,128)S(1)}, u32[]{:S(2)}) copy-start(f32[1,1,1024]{2,1,0:T(1,128)S(1)} %get-tuple-element.585) | copy-start | bytes 12292
  25.0 22.8 %copy-start.34 = (f32[1,1,1024]{2,1,0:T(1,128)}, f32[1,1,1024]{2,1,0:T(1,128)S(1)}, u32[]{:S(2)}) copy-start(f32[1,1,1024]{2,1,0:T(1,128)S(1)} %get-tuple-element.586) | copy-start | bytes 12292
  25.0 22.8 %copy-start.36 = (f32[1,1,1024]{2,1,0:T(1,128)}, f32[1,1,1024]{2,1,0:T(1,128)S(1)}, u32[]{:S(2)}) copy-start(f32[1,1,1024]{2,1,0:T(1,128)S(1)} %get-tuple-element.587) | copy-start | bytes 12292
  60.5 21.4 %copy-start.2 = (f32[4,16,1024]{1,0,2:T(4,128)}, f32[4,16,1024]{1,0,2:T(4,128)S(1)}, u32[]{:S(2)}) copy-start(f32[4,16,1024]{1,0,2:T(4,128)S(1)} %convolution_bitcast_fusion.2) | copy-start | bytes 786436
  83.7 166.8 %all-gather.9.cloned.1.call-start = ((), (), s32[]{:S(2)}) async-start(), calls=%async_computation.2 | async-start | bytes 4259840 | tf_op jit(solution)/shard_map/all_gather | solution.py:26
  85.6 693.8 %all-reduce.2.cloned.1.call-start = ((), (), s32[]{:S(2)}) async-start(), calls=%async_computation | async-start | bytes 1048576 | tf_op jit(solution)/shard_map/psum | solution.py:160
  119.8 12.1 %copy-start.39 = (bf16[2,1024]{1,0:T(2,128)(2,1)S(1)}, bf16[2,1024]{1,0:T(2,128)(2,1)}, u32[]{:S(2)}) copy-start(bf16[2,1024]{1,0:T(2,128)(2,1)} %copy-done.38) | copy-start | bytes 12292
  228.3 24.2 %copy-start.17 = (f32[4,16,1024]{2,1,0:T(8,128)S(1)}, f32[4,16,1024]{2,1,0:T(8,128)}, u32[]{:S(2)}) copy-start(f32[4,16,1024]{2,1,0:T(8,128)} %custom-call) | copy-start | bytes 786436
  228.3 24.2 %copy-start.43 = (f32[32]{0:T(128)S(1)}, f32[32]{0:T(128)}, u32[]{:S(2)}) copy-start(f32[32]{0:T(128)} %copy-done.42) | copy-start | bytes 388
  252.4 21.3 %copy-start.5 = (f32[128,1024]{1,0:T(8,128)S(1)}, f32[128,1024]{1,0:T(8,128)}, u32[]{:S(2)}) copy-start(f32[128,1024]{1,0:T(8,128)} %get-tuple-element.564) | copy-start | bytes 1572868
  252.5 21.3 %copy-start.16 = (bf16[128,1024]{1,0:T(8,128)(2,1)S(1)}, bf16[128,1024]{1,0:T(8,128)(2,1)}, u32[]{:S(2)}) copy-start(bf16[128,1024]{1,0:T(8,128)(2,1)} %param.19) | copy-start | bytes 786436
  276.1 305.0 %copy-start.1 = (f32[4,32,1024]{1,0,2:T(4,128)S(1)}, f32[4,32,1024]{1,0,2:T(4,128)}, u32[]{:S(2)}) copy-start(f32[4,32,1024]{1,0,2:T(4,128)} %copy-done) | copy-start | bytes 1572868
  579.2 22.7 %collective-permute-start.1 = (bf16[3,2,1024]{2,1,0:T(2,128)(2,1)S(1)}, bf16[3,2,1024]{2,1,0:T(2,128)(2,1)S(1)}, u32[]{:S(2)}, u32[]{:S(2)}) collective-permute-start(bf16[3,2,1024]{2,1,0:T(2,128)(2,1)S(1)} %slice.120), channel_id=1, source_target_pairs={{4,0},{8,4},{12,8},{16,12},{20,16},{24,20},{28,24},{32,28},{36,32}... | collective-permute-start | bytes 36872 | tf_op jit(solution)/shard_map/ppermute | solution.py:19
  601.8 11.4 %copy-start.45 = (f32[128]{0:T(128)S(1)}, f32[128]{0:T(128)}, u32[]{:S(2)}) copy-start(f32[128]{0:T(128)} %copy-done.44) | copy-start | bytes 1540
  601.8 11.4 %copy-start.41 = (f32[128]{0:T(128)S(1)}, f32[128]{0:T(128)}, u32[]{:S(2)}) copy-start(f32[128]{0:T(128)} %copy-done.40) | copy-start | bytes 1540
  (31 other events, 84.3 us)
Sparse Core Ops, SparseCore 0:
  11.3 80.8 all-gather.6
  95.0 76.3 all-gather.10
  174.2 76.3 all-gather.8
  601.9 177.4 all-reduce.1
where the time goes:
time: 802 us; the launch traced here: 788 us
  blocking collectives  322 us (40%)
  waiting for transfers between devices  175 us (22%)
  other arithmetic  108 us (13%)
  matrix products  95.1 us (12%)
  local copies, waits for them, and re-layouts  67.2 us (8%)
  between operations  14.8 us (2%)
    psum x1, blocking collectives, per_device(): lax.psum((cross_part + local_terms, short_terms), 'ctx')  301 us
    psum x1, waiting for transfers between devices, per_device(): lax.psum((cross_part + local_terms, short_terms), 'ctx')  165 us
    add x63, other arithmetic, chain(): return (earlier[0] * later[0], earlier[1] * later[0] + later[1])  57.1 us
    dot_general x1, matrix products, per_device(): jnp.einsum('mic,bic->bmc', decay_table, grad_blocks, precision=HIGHEST)  21.3 us
    dot_general x1, matrix products, per_device(): jnp.einsum('mic,bic->bmc', shifted, grad_blocks, precision=HIGHEST)  18.7 us
    dot_general x1, matrix products, per_device(): jnp.einsum('nc,mnc->mc', by_lag, decay_table, precision=HIGHEST)  16.4 us
  transfers between devices with their start and end apart: 6, of which 3 were waited for; matrix products, arithmetic and copies ran while one was open for 30% of the time, Pallas kernels for 0%

commit v1 on v0

v1 whole, which is shorter than its diff:
```python
import jax
import jax.numpy as jnp
from jax import lax
from jax.sharding import PartitionSpec as P

M = 16
KS = 3
P_SIZE = 32


HIGHEST = lax.Precision.HIGHEST
EPSILON = 1e-05


def passed_along(value, axis, steps):
    count = lax.axis_size(axis)
    first, last = (max(0, -steps), min(count, count - steps))
    return lax.ppermute(value, axis, [(source, source + steps) for source in range(first, last)])


def entering(own, rates, rows, axis, reverse):
    count = lax.axis_size(axis)
    sign = -1 if reverse else 1
    state = passed_along(own, axis, sign)
    shift = 1
    while shift < count:
        decay = jnp.exp(-rates * jnp.float32(rows * shift))
        state = state + decay * passed_along(state, axis, sign * shift)
        shift *= 2
    return state


def summed(value, axis):
    count = lax.axis_size(axis)
    if count & (count - 1):
        return lax.psum(value, axis)
    shift = 1
    while shift < count:
        value = value + lax.ppermute(value, axis, [(i, i ^ shift) for i in range(count)])
        shift *= 2
    return value


def lag_table(length):
    steps = jnp.arange(length)
    return (steps[:, None, None] - steps[None, :, None] == steps[None, None, :]).astype(jnp.float32)


def per_device(stream, norm_gain, short_filters, mode_rates, residues, grad_out):
    row_count, chan_count = stream.shape
    block_count = row_count // P_SIZE
    total_chans = chan_count * lax.axis_size("ch")
    total_rows = row_count * lax.axis_size("ctx")
    stream_wide = stream.astype(jnp.float32)
    squares = lax.psum(jnp.sum(stream_wide * stream_wide, axis=1), "ch")
    row_scale = lax.rsqrt(squares / total_chans + EPSILON)
    normed = (stream_wide * row_scale[:, None] * norm_gain[None, :]).astype(jnp.bfloat16)
    rim_rows = passed_along(normed[row_count - (KS - 1) :], "ctx", 1)
    padded_half = jnp.concatenate([rim_rows, lax.optimization_barrier(normed)], 0)
    padded = padded_half.astype(jnp.float32)
    branches = [
        sum(
            (
                short_filters[branch, offset][None, :]
                * padded[KS - 1 - offset : KS - 1 - offset + row_count]
                for offset in range(KS)
            )
        )
        for branch in range(3)
    ]
    query_part, key_part, value_part = branches
    product = lax.optimization_barrier((key_part * value_part).astype(jnp.bfloat16)).astype(
        jnp.float32
    )
    cotangent = grad_out.astype(jnp.float32)
    grad_conv = cotangent * query_part

    steps = jnp.arange(P_SIZE).astype(jnp.float32)
    decay_table = jnp.exp(-mode_rates[:, None, :] * steps[None, :, None])
    shifted = jnp.exp(-mode_rates[:, None, :] * (steps[None, :, None] + 1.0))
    response = jnp.sum(residues[:, None, :] * decay_table, axis=0)
    lags = steps[:, None] - steps[None, :]
    lag_index = jnp.clip(lags, 0, P_SIZE - 1).astype(jnp.int32)
    toeplitz = jnp.where((lags >= 0)[:, :, None], response[lag_index], 0.0)
    carried_table = shifted * residues[:, None, :]

    blocks = product.reshape(block_count, P_SIZE, chan_count)
    grad_blocks = grad_conv.reshape(block_count, P_SIZE, chan_count)
    block_ends = jnp.sum(decay_table[None, :, ::-1, :] * blocks[:, None], axis=2)
    block_heads = jnp.sum(decay_table[None] * grad_blocks[:, None], axis=2)
    block_steps = jnp.arange(block_count).astype(jnp.float32)
    own_state = jnp.sum(
        jnp.exp(-mode_rates[None] * (P_SIZE * (block_count - 1 - block_steps))[:, None, None])
        * block_ends,
        axis=0,
    )
    own_back = jnp.sum(
        jnp.exp(-mode_rates[None] * (P_SIZE * block_steps)[:, None, None]) * block_heads, axis=0
    )
    incoming = entering(own_state, mode_rates, row_count, "ctx", False)
    later_state = entering(own_back, mode_rates, row_count, "ctx", True)

    gap = block_steps[:, None] - block_steps[None, :] - 1.0
    earlier = (gap >= 0).astype(jnp.float32)
    pair_decay = jnp.exp(
        -mode_rates[None, None] * (P_SIZE * jnp.maximum(gap, 0.0))[:, :, None, None]
    ) * earlier[:, :, None, None]
    starts = jnp.sum(pair_decay * block_ends[None], axis=1) + jnp.exp(
        -mode_rates[None] * (P_SIZE * block_steps)[:, None, None]
    ) * incoming[None]
    later_gap = block_steps[None, :] - block_steps[:, None] - 1.0
    later_mask = (later_gap >= 0).astype(jnp.float32)
    later_decay = jnp.exp(
        -mode_rates[None, None] * (P_SIZE * jnp.maximum(later_gap, 0.0))[:, :, None, None]
    ) * later_mask[:, :, None, None]
    ends_back = jnp.sum(later_decay * block_heads[None], axis=1) + jnp.exp(
        -mode_rates[None] * (P_SIZE * (block_count - 1 - block_steps))[:, None, None]
    ) * later_state[None]

    local_part = jnp.sum(toeplitz[None] * blocks[:, None], axis=2)
    carried = jnp.sum(starts[:, :, None, :] * carried_table[None], axis=1)
    long_conv = (local_part + carried).reshape(row_count, chan_count)
    output = (query_part * long_conv).astype(jnp.bfloat16)
    grad_query = (cotangent * long_conv).astype(jnp.bfloat16)

    back_local = jnp.sum(toeplitz[None] * grad_blocks[:, :, None], axis=1)
    back_carried = jnp.sum(ends_back[:, :, None, :] * carried_table[None, :, ::-1, :], axis=1)
    grad_product = (back_local + back_carried).reshape(row_count, chan_count)
    grad_key = (grad_product * value_part).astype(jnp.bfloat16)
    grad_value = (grad_product * key_part).astype(jnp.bfloat16)

    weighted = jnp.sum(shifted[None] * grad_blocks[:, None], axis=2)
    cross_part = jnp.sum(weighted * starts, axis=0)
    pairs = jnp.einsum("bic,bjc->ijc", grad_blocks, blocks, precision=HIGHEST)
    by_lag = jnp.einsum("ijc,ijn->nc", pairs, lag_table(P_SIZE), precision=HIGHEST)
    local_terms = jnp.sum(by_lag[None] * decay_table, axis=1)

    stacked_half = lax.optimization_barrier(jnp.stack([grad_query, grad_key, grad_value], 0))
    next_rows = passed_along(stacked_half[:, : KS - 1], "ctx", -1)
    stacked = stacked_half.astype(jnp.float32)
    after = jnp.concatenate([stacked, next_rows.astype(jnp.float32)], 1)
    grad_normed = sum(
        (
            short_filters[branch, offset][None, :] * after[branch, offset : offset + row_count]
            for branch in range(3)
            for offset in range(KS)
        )
    )
    short_terms = jnp.stack(
        [
            jnp.einsum(
                "btc,tc->bc",
                stacked_half,
                padded_half[KS - 1 - offset : KS - 1 - offset + row_count],
                preferred_element_type=jnp.float32,
            )
            for offset in range(KS)
        ],
        1,
    )
    partial_sums = jnp.concatenate(
        [cross_part + local_terms, short_terms.reshape(3 * KS, chan_count)], 0
    )
    whole_sums = summed(partial_sums, "ctx")
    norm_factor = 1.0 / jnp.sqrt(jnp.float32(total_rows))
    grad_residues = whole_sums[:M] * norm_factor
    grad_short = whole_sums[M:].reshape(3, KS, chan_count) * norm_factor
    row_dot = lax.psum(jnp.sum(norm_gain[None, :] * grad_normed * stream_wide, axis=1), "ch")
    grad_stream = (
        row_scale[:, None] * norm_gain[None, :] * grad_normed
        - stream_wide * (row_scale**3 * row_dot / total_chans)[:, None]
    ).astype(jnp.bfloat16)
    return (output, grad_stream, grad_residues, grad_short)


def solution(mesh):
    return jax.shard_map(
        per_device,
        mesh=mesh,
        in_specs=(
            P("ctx", "ch"),
            P("ch"),
            P(None, None, "ch"),
            P(None, "ch"),
            P(None, "ch"),
            P("ctx", "ch"),
        ),
        out_specs=(P("ctx", "ch"), P("ctx", "ch"), P(None, "ch"), P(None, None, "ch")),
        check_vma=False,
    )
```

time: 802 us -> 219 us (0.27); the launches traced: 788 us -> 216 us
  blocking collectives: 322 us -> 18.2 us
  waiting for transfers between devices: 175 us -> 51.7 us
  matrix products: 95.1 us -> 14.7 us
  other arithmetic: 108 us -> 38.9 us
  starting transfers between devices: 4.02 us -> 57.6 us
  local copies, waits for them, and re-layouts: 67.2 us -> 33.4 us
  between operations: 14.8 us -> 1.69 us
    psum x1 -> x0, blocking collectives: 301 us -> none  [per_device(): lax.psum((cross_part + local_terms, short_terms), 'ctx')]
    psum x1 -> x0, waiting for transfers between devices: 165 us -> none  [per_device(): lax.psum((cross_part + local_terms, short_terms), 'ctx')]
    dot_general x5 -> x0, matrix products: 69.4 us -> none  [the longest x1 21.3 us: per_device(): jnp.einsum('mic,bic->bmc', decay_table, grad_blocks, precision=HIGHEST)]
    add x72 -> x20, other arithmetic: 64.1 us -> 2.77 us  [the longest x11 2.55 us: entering(): state = state + decay * passed_along(state, axis, sign * shift)]
    ppermute x2 -> x16, starting transfers between devices: 3.86 us -> 52 us  [passed_along(): lax.ppermute(value, axis, [(source, source + steps) for source in range(f...]
    ppermute x2 -> x16, waiting for transfers between devices: 0.01 us -> 31.9 us  [passed_along(): lax.ppermute(value, axis, [(source, source + steps) for source in range(f...]
    dot_general x16 -> x0, other arithmetic: 25.7 us -> none  [the longest x4 11.7 us: forward_step(): local_part = jnp.einsum('ijc,jc->ic', toeplitz, one_block, precision=HIGHER)]
    ppermute x0 -> x6, waiting for transfers between devices: none -> 19.9 us  [summed(): lax.ppermute(value, axis, [(i, i ^ shift) for i in range(count)])]
  transfers between devices with their start and end apart: 6 -> 22, of which waited for: 3 -> 15; matrix products, arithmetic and copies ran while one was open for 30% -> 12% of each run, Pallas kernels for 0% -> 0%
where the time goes in v1:
time: 219 us; the launch traced here: 216 us
  starting transfers between devices  57.6 us (26%)
  waiting for transfers between devices  51.7 us (24%)
  other arithmetic  38.9 us (18%)
  local copies, waits for them, and re-layouts  33.4 us (15%)
  blocking collectives  18.2 us (8%)
  matrix products  14.7 us (7%)
    ppermute x16, starting transfers between devices, passed_along(): lax.ppermute(value, axis, [(source, source + steps) for source in range(f...  52 us
    ppermute x16, waiting for transfers between devices, passed_along(): lax.ppermute(value, axis, [(source, source + steps) for source in range(f...  31.9 us
    ppermute x6, waiting for transfers between devices, summed(): lax.ppermute(value, axis, [(i, i ^ shift) for i in range(count)])  19.9 us
    transpose x1, local copies, waits for them, and re-layouts, per_device(): pairs = jnp.einsum('bic,bjc->ijc', grad_blocks, blocks, precision=HIGHEST)  12.1 us
    dot_general x1, matrix products, per_device(): pairs = jnp.einsum('bic,bjc->ijc', grad_blocks, blocks, precision=HIGHEST)  10.6 us
    psum x1, blocking collectives, per_device(): squares = lax.psum(jnp.sum(stream_wide * stream_wide, axis=1), 'ch')  10.5 us
    psum x1, blocking collectives, per_device(): lax.psum(jnp.sum(norm_gain[None, :] * grad_normed * stream_wide, axis=1),...  7.74 us
    reduce_sum x1, other arithmetic, per_device(): weighted = jnp.sum(shifted[None] * grad_blocks[:, None], axis=2)  6.11 us
  transfers between devices with their start and end apart: 22, of which 15 were waited for; matrix products, arithmetic and copies ran while one was open for 12% of the time, Pallas kernels for 0%

profile of v1, /device:TPU:32, one launch (start us, length us, event | category | flops | bytes accessed | tf_op | source)
XLA Modules:
  0.0 216.3 jit_solution(11313999302209718637)
XLA Ops:
  1.7 10.5 %psum.14 = f32[128]{0:T(128)S(1)} all-reduce(f32[128]{0:T(128)S(1)} %fusion.4), channel_id=1, replica_groups=mesh['ctx'=64,'ch'=4] {'ch'}, use_global_device_ids=true, to_apply=%region_1.0 | all-reduce | flops 128 | bytes 1024 | tf_op jit(solution)/shard_map/psum | solution.py:55
  25.0 10.6 %convolution_bitcast_fusion = f32[32,32,1024]{0,1,2:T(8,128)} fusion(bf16[4,32,1024]{1,0,2:T(4,128)(2,1)} %copy.10, f32[4,32,1024]{1,0,2:T(4,128)S(1)} %copy.11), kind=kOutput, calls=%fused_computation.3 | convolution fusion | flops 50331648 | bytes 4980736 | tf_op jit(solution)/shard_map/bic,bjc->ijc/dot_general | solution.py:134
  35.6 12.1 %copy.12 = f32[32,32,1024]{2,1,0:T(8,128)} copy(f32[32,32,1024]{0,1,2:T(8,128)} %convolution_bitcast_fusion) | data formatting | bytes 8388608 | tf_op jit(solution)/shard_map/bic,bjc->ijc/transpose | solution.py:134
  47.7 4.1 %convolution_bitcast_fusion.1 = f32[32,1024]{1,0:T(8,128)S(1)} fusion(f32[32,32,1024]{2,1,0:T(8,128)} %copy.12, s32[32,32]{1,0:T(8,128)S(1)} %iota_subtract_fusion), kind=kOutput, calls=%fused_computation.30 | convolution fusion | flops 402685952 | bytes 4329472 | tf_op jit(solution)/shard_map/ijc,ijn->nc/dot_general | solution.py:135
  54.8 5.7 %rev.6 = f32[16,32,1024]{2,1,0:T(8,128)} reverse(f32[16,32,1024]{2,1,0:T(8,128)} %get-tuple-element.36), dimensions={1} | reverse | bytes 4194304 | tf_op jit(solution)/shard_map/rev | solution.py:89
  60.5 6.1 %multiply_reduce_fusion.2 = (f32[4,16,1024]{2,1,0:T(8,128)}, f32[4,16,1024]{2,1,0:T(8,128)S(1)}) fusion(f32[16,32,1024]{2,1,0:T(8,128)} %get-tuple-element.37, f32[4,32,1024]{2,1,0:T(8,128)S(1)} %bitcast.135, f32[16,32,1024]{2,1,0:T(8,128)} %get-tuple-element.36), kind=kLoop, calls=%fused_computation.4 | loop fusion | flops 8257536 | bytes 5242880 | tf_op jit(solution)/shard_map/reduce_sum | solution.py:132
  73.0 3.9 %collective-permute-start.9 = (f32[16,1024]{1,0:T(8,128)S(1)}, f32[16,1024]{1,0:T(8,128)S(1)}, u32[]{:S(2)}, u32[]{:S(2)}) collective-permute-start(f32[16,1024]{1,0:T(8,128)S(1)} %collective-permute-done.8), channel_id=1, source_target_pairs={{4,0},{8,4},{12,8},{16,12},{20,16},{24,20},{28,24},{32,28},{36,32}... | collective-permute-start | bytes 196616 | tf_op jit(solution)/shard_map/ppermute | solution.py:18
  81.3 3.6 %collective-permute-done.10 = f32[16,1024]{1,0:T(8,128)} collective-permute-done((f32[16,1024]{1,0:T(8,128)S(1)}, f32[16,1024]{1,0:T(8,128)}, u32[]{:S(2)}, u32[]{:S(2)}) %collective-permute-start.10) | collective-permute-done | bytes 65568 | tf_op jit(solution)/shard_map/ppermute | solution.py:18
  87.8 9.0 %collective-permute-done.11 = f32[16,1024]{1,0:T(8,128)S(1)} collective-permute-done((f32[16,1024]{1,0:T(8,128)S(1)}, f32[16,1024]{1,0:T(8,128)S(1)}, u32[]{:S(2)}, u32[]{:S(2)}) %collective-permute-start.11) | collective-permute-done | bytes 65568 | tf_op jit(solution)/shard_map/ppermute | solution.py:18
  98.0 4.6 %collective-permute-start.1 = (f32[16,1024]{1,0:T(8,128)}, f32[16,1024]{1,0:T(8,128)S(1)}, u32[]{:S(2)}, u32[]{:S(2)}) collective-permute-start(f32[16,1024]{1,0:T(8,128)} %get-tuple-element.14), channel_id=1, source_target_pairs={{0,4},{4,8},{8,12},{12,16},{16,20},{20,24},{24,28},{28,32},{32,36}... | collective-permute-start | bytes 196616 | tf_op jit(solution)/shard_map/ppermute | solution.py:18
  102.6 4.2 %collective-permute-done.12 = f32[16,1024]{1,0:T(8,128)S(1)} collective-permute-done((f32[16,1024]{1,0:T(8,128)S(1)}, f32[16,1024]{1,0:T(8,128)S(1)}, u32[]{:S(2)}, u32[]{:S(2)}) %collective-permute-start.12) | collective-permute-done | bytes 65568 | tf_op jit(solution)/shard_map/ppermute | solution.py:18
  108.2 3.4 %collective-permute-start.2 = (f32[16,1024]{1,0:T(8,128)S(1)}, f32[16,1024]{1,0:T(8,128)S(1)}, u32[]{:S(2)}, u32[]{:S(2)}) collective-permute-start(f32[16,1024]{1,0:T(8,128)S(1)} %collective-permute-done.1), channel_id=1, source_target_pairs={{0,4},{4,8},{8,12},{12,16},{16,20},{20,24},{24,28},{28,32},{32,36}... | collective-permute-start | bytes 196616 | tf_op jit(solution)/shard_map/ppermute | solution.py:18
  115.7 6.3 %collective-permute-done.14 = f32[16,1024]{1,0:T(8,128)S(1)} collective-permute-done((f32[16,1024]{1,0:T(8,128)S(1)}, f32[16,1024]{1,0:T(8,128)S(1)}, u32[]{:S(2)}, u32[]{:S(2)}) %collective-permute-start.14) | collective-permute-done | bytes 65568 | tf_op jit(solution)/shard_map/ppermute | solution.py:18
  122.7 4.5 %collective-permute-start.3 = (f32[16,1024]{1,0:T(8,128)S(1)}, f32[16,1024]{1,0:T(8,128)}, u32[]{:S(2)}, u32[]{:S(2)}) collective-permute-start(f32[16,1024]{1,0:T(8,128)S(1)} %get-tuple-element.40), channel_id=1, source_target_pairs={{0,8},{4,12},{8,16},{12,20},{16,24},{20,28},{24,32},{28,36},{32,40... | collective-permute-start | bytes 196616 | tf_op jit(solution)/shard_map/ppermute | solution.py:18
  128.1 5.4 %gather_fusion = f32[1024,1024]{1,0:T(8,128)} fusion(f32[32,1024]{1,0:T(8,128)S(1)} %get-tuple-element.12, s32[1024]{0:T(1024)S(1)} %broadcast_clamp_fusion), kind=kCustom, calls=%fused_computation | custom fusion | bytes 8392704 | tf_op jit(solution)/shard_map/gather | solution.py:84
  134.3 5.5 %collective-permute-start.4 = (f32[16,1024]{1,0:T(8,128)S(1)}, f32[16,1024]{1,0:T(8,128)S(1)}, u32[]{:S(2)}, u32[]{:S(2)}) collective-permute-start(f32[16,1024]{1,0:T(8,128)S(1)} %multiply_add_fusion.15), channel_id=1, source_target_pairs={{0,16},{4,20},{8,24},{12,28},{16,32},{20,36},{24,40},{28,44},{32,4... | collective-permute-start | bytes 196616 | tf_op jit(solution)/shard_map/ppermute | solution.py:18
  142.4 6.5 %collective-permute-start.5 = (f32[16,1024]{1,0:T(8,128)S(1)}, f32[16,1024]{1,0:T(8,128)S(1)}, u32[]{:S(2)}, u32[]{:S(2)}) collective-permute-start(f32[16,1024]{1,0:T(8,128)S(1)} %multiply_add_fusion.14), channel_id=1, source_target_pairs={{0,32},{4,36},{8,40},{12,44},{16,48},{20,52},{24,56},{28,60},{32,6... | collective-permute-start | bytes 196616 | tf_op jit(solution)/shard_map/ppermute | solution.py:18
  148.9 4.6 %multiply_reduce_fusion = (f32[4,32,1024]{2,1,0:T(8,128)}, f32[4,32,1024]{2,1,0:T(8,128)}) fusion(f32[4,32,1024]{2,1,0:T(8,128)S(1)} %bitcast.136, f32[32,32,1024]{2,1,0:T(8,128)S(1)} %broadcast_select_fusion, f32[4,32,1024]{2,1,0:T(8,128)S(1)} %bitcast_convert_fusion.1), kind=kLoop, calls=%fused_computation.1 | loop fusion | flops 16515072 | bytes 6291456 | tf_op jit(solution)/shard_map/reduce_sum | solution.py:126
  153.6 5.8 %collective-permute-start.6 = (f32[16,1024]{1,0:T(8,128)S(1)}, f32[16,1024]{1,0:T(8,128)S(1)}, u32[]{:S(2)}, u32[]{:S(2)}) collective-permute-start(f32[16,1024]{1,0:T(8,128)S(1)} %multiply_add_fusion.13), channel_id=1, source_target_pairs={{0,64},{4,68},{8,72},{12,76},{16,80},{20,84},{24,88},{28,92},{32,9... | collective-permute-start | bytes 196616 | tf_op jit(solution)/shard_map/ppermute | solution.py:18
  161.3 4.3 %collective-permute-start.7 = (f32[16,1024]{1,0:T(8,128)S(1)}, f32[16,1024]{1,0:T(8,128)S(1)}, u32[]{:S(2)}, u32[]{:S(2)}) collective-permute-start(f32[16,1024]{1,0:T(8,128)S(1)} %multiply_add_fusion.12), channel_id=1, source_target_pairs={{0,128},{4,132},{8,136},{12,140},{16,144},{20,148},{24,152},{28,15... | collective-permute-start | bytes 196616 | tf_op jit(solution)/shard_map/ppermute | solution.py:18
  179.0 4.6 %collective-permute-done.17 = f32[25,1024]{1,0:T(8,128)S(1)} collective-permute-done((f32[25,1024]{1,0:T(8,128)S(1)}, f32[25,1024]{1,0:T(8,128)S(1)}, u32[]{:S(2)}, u32[]{:S(2)}) %collective-permute-start.17) | collective-permute-done | bytes 102432 | tf_op jit(solution)/shard_map/ppermute | solution.py:39
  193.8 7.7 %psum.15 = f32[128]{0:T(128)S(1)} all-reduce(f32[128]{0:T(128)S(1)} %get-tuple-element.19), channel_id=1, replica_groups=mesh['ctx'=64,'ch'=4] {'ch'}, use_global_device_ids=true, to_apply=%region_14.15 | all-reduce | flops 128 | bytes 1024 | tf_op jit(solution)/shard_map/psum | solution.py:168
  201.7 6.2 %collective-permute-done.20 = f32[25,1024]{1,0:T(8,128)S(1)} collective-permute-done((f32[25,1024]{1,0:T(8,128)S(1)}, f32[25,1024]{1,0:T(8,128)S(1)}, u32[]{:S(2)}, u32[]{:S(2)}) %collective-permute-start.20) | collective-permute-done | bytes 102432 | tf_op jit(solution)/shard_map/ppermute | solution.py:39
  209.7 5.2 %collective-permute-done.21 = f32[25,1024]{1,0:T(8,128)S(1)} collective-permute-done((f32[25,1024]{1,0:T(8,128)S(1)}, f32[25,1024]{1,0:T(8,128)S(1)}, u32[]{:S(2)}, u32[]{:S(2)}) %collective-permute-start.21) | collective-permute-done | bytes 102432 | tf_op jit(solution)/shard_map/ppermute | solution.py:39
  (204 shorter events, 70.3 us)
Async XLA Ops:
  13.3 4.9 %collective-permute-start = (bf16[2,1024]{1,0:T(2,128)(2,1)S(1)}, bf16[2,1024]{1,0:T(2,128)(2,1)S(1)}, u32[]{:S(2)}, u32[]{:S(2)}) collective-permute-start(bf16[2,1024]{1,0:T(2,128)(2,1)S(1)} %slice.125), channel_id=1, source_target_pairs={{0,4},{4,8},{8,12},{12,16},{16,20},{20,24},{24,28},{28,32},{32,36}... | collective-permute-start | bytes 12296 | tf_op jit(solution)/shard_map/ppermute | solution.py:18
  15.3 52.4 %copy-start.46 = (f32[4]{0:T(128)}, f32[4]{0:T(128)S(1)}, u32[]{:S(2)}) copy-start(f32[4]{0:T(128)S(1)} %broadcast_multiply_fusion.1) | copy-start | bytes 52
  16.3 51.4 %copy-start.48 = (f32[4]{0:T(128)}, f32[4]{0:T(128)S(1)}, u32[]{:S(2)}) copy-start(f32[4]{0:T(128)S(1)} %subtract_multiply_fusion) | copy-start | bytes 52
  68.5 4.5 %collective-permute-start.8 = (f32[16,1024]{1,0:T(8,128)S(1)}, f32[16,1024]{1,0:T(8,128)S(1)}, u32[]{:S(2)}, u32[]{:S(2)}) collective-permute-start(f32[16,1024]{1,0:T(8,128)S(1)} %get-tuple-element.13), channel_id=1, source_target_pairs={{4,0},{8,4},{12,8},{16,12},{20,16},{24,20},{28,24},{32,28},{36,32}... | collective-permute-start | bytes 196616 | tf_op jit(solution)/shard_map/ppermute | solution.py:18
  73.0 5.6 %collective-permute-start.9 = (f32[16,1024]{1,0:T(8,128)S(1)}, f32[16,1024]{1,0:T(8,128)S(1)}, u32[]{:S(2)}, u32[]{:S(2)}) collective-permute-start(f32[16,1024]{1,0:T(8,128)S(1)} %collective-permute-done.8), channel_id=1, source_target_pairs={{4,0},{8,4},{12,8},{16,12},{20,16},{24,20},{28,24},{32,28},{36,32}... | collective-permute-start | bytes 196616 | tf_op jit(solution)/shard_map/ppermute | solution.py:18
  78.6 6.3 %collective-permute-start.10 = (f32[16,1024]{1,0:T(8,128)S(1)}, f32[16,1024]{1,0:T(8,128)}, u32[]{:S(2)}, u32[]{:S(2)}) collective-permute-start(f32[16,1024]{1,0:T(8,128)S(1)} %multiply_add_fusion.10), channel_id=1, source_target_pairs={{8,0},{12,4},{16,8},{20,12},{24,16},{28,20},{32,24},{36,28},{40,32... | collective-permute-start | bytes 196616 | tf_op jit(solution)/shard_map/ppermute | solution.py:18
  85.8 10.9 %collective-permute-start.11 = (f32[16,1024]{1,0:T(8,128)S(1)}, f32[16,1024]{1,0:T(8,128)S(1)}, u32[]{:S(2)}, u32[]{:S(2)}) collective-permute-start(f32[16,1024]{1,0:T(8,128)S(1)} %multiply_add_fusion.9), channel_id=1, source_target_pairs={{16,0},{20,4},{24,8},{28,12},{32,16},{36,20},{40,24},{44,28},{48,3... | collective-permute-start | bytes 196616 | tf_op jit(solution)/shard_map/ppermute | solution.py:18
  96.7 10.1 %collective-permute-start.12 = (f32[16,1024]{1,0:T(8,128)S(1)}, f32[16,1024]{1,0:T(8,128)S(1)}, u32[]{:S(2)}, u32[]{:S(2)}) collective-permute-start(f32[16,1024]{1,0:T(8,128)S(1)} %multiply_add_fusion.8), channel_id=1, source_target_pairs={{32,0},{36,4},{40,8},{44,12},{48,16},{52,20},{56,24},{60,28},{64,3... | collective-permute-start | bytes 196616 | tf_op jit(solution)/shard_map/ppermute | solution.py:18
  98.0 10.2 %collective-permute-start.1 = (f32[16,1024]{1,0:T(8,128)}, f32[16,1024]{1,0:T(8,128)S(1)}, u32[]{:S(2)}, u32[]{:S(2)}) collective-permute-start(f32[16,1024]{1,0:T(8,128)} %get-tuple-element.14), channel_id=1, source_target_pairs={{0,4},{4,8},{8,12},{12,16},{16,20},{20,24},{24,28},{28,32},{32,36}... | collective-permute-start | bytes 196616 | tf_op jit(solution)/shard_map/ppermute | solution.py:18
  106.8 6.9 %collective-permute-start.13 = (f32[16,1024]{1,0:T(8,128)S(1)}, f32[16,1024]{1,0:T(8,128)S(1)}, u32[]{:S(2)}, u32[]{:S(2)}) collective-permute-start(f32[16,1024]{1,0:T(8,128)S(1)} %multiply_add_fusion.7), channel_id=1, source_target_pairs={{64,0},{68,4},{72,8},{76,12},{80,16},{84,20},{88,24},{92,28},{96,3... | collective-permute-start | bytes 196616 | tf_op jit(solution)/shard_map/ppermute | solution.py:18
  108.2 7.5 %collective-permute-start.2 = (f32[16,1024]{1,0:T(8,128)S(1)}, f32[16,1024]{1,0:T(8,128)S(1)}, u32[]{:S(2)}, u32[]{:S(2)}) collective-permute-start(f32[16,1024]{1,0:T(8,128)S(1)} %collective-permute-done.1), channel_id=1, source_target_pairs={{0,4},{4,8},{8,12},{12,16},{16,20},{20,24},{24,28},{28,32},{32,36}... | collective-permute-start | bytes 196616 | tf_op jit(solution)/shard_map/ppermute | solution.py:18
  113.8 8.3 %collective-permute-start.14 = (f32[16,1024]{1,0:T(8,128)S(1)}, f32[16,1024]{1,0:T(8,128)S(1)}, u32[]{:S(2)}, u32[]{:S(2)}) collective-permute-start(f32[16,1024]{1,0:T(8,128)S(1)} %multiply_add_fusion.6), channel_id=1, source_target_pairs={{128,0},{132,4},{136,8},{140,12},{144,16},{148,20},{152,24},{156,2... | collective-permute-start | bytes 196616 | tf_op jit(solution)/shard_map/ppermute | solution.py:18
  122.7 10.7 %collective-permute-start.3 = (f32[16,1024]{1,0:T(8,128)S(1)}, f32[16,1024]{1,0:T(8,128)}, u32[]{:S(2)}, u32[]{:S(2)}) collective-permute-start(f32[16,1024]{1,0:T(8,128)S(1)} %get-tuple-element.40), channel_id=1, source_target_pairs={{0,8},{4,12},{8,16},{12,20},{16,24},{20,28},{24,32},{28,36},{32,40... | collective-permute-start | bytes 196616 | tf_op jit(solution)/shard_map/ppermute | solution.py:18
  134.3 8.0 %collective-permute-start.4 = (f32[16,1024]{1,0:T(8,128)S(1)}, f32[16,1024]{1,0:T(8,128)S(1)}, u32[]{:S(2)}, u32[]{:S(2)}) collective-permute-start(f32[16,1024]{1,0:T(8,128)S(1)} %multiply_add_fusion.15), channel_id=1, source_target_pairs={{0,16},{4,20},{8,24},{12,28},{16,32},{20,36},{24,40},{28,44},{32,4... | collective-permute-start | bytes 196616 | tf_op jit(solution)/shard_map/ppermute | solution.py:18
  142.4 11.2 %collective-permute-start.5 = (f32[16,1024]{1,0:T(8,128)S(1)}, f32[16,1024]{1,0:T(8,128)S(1)}, u32[]{:S(2)}, u32[]{:S(2)}) collective-permute-start(f32[16,1024]{1,0:T(8,128)S(1)} %multiply_add_fusion.14), channel_id=1, source_target_pairs={{0,32},{4,36},{8,40},{12,44},{16,48},{20,52},{24,56},{28,60},{32,6... | collective-permute-start | bytes 196616 | tf_op jit(solution)/shard_map/ppermute | solution.py:18
  153.6 7.6 %collective-permute-start.6 = (f32[16,1024]{1,0:T(8,128)S(1)}, f32[16,1024]{1,0:T(8,128)S(1)}, u32[]{:S(2)}, u32[]{:S(2)}) collective-permute-start(f32[16,1024]{1,0:T(8,128)S(1)} %multiply_add_fusion.13), channel_id=1, source_target_pairs={{0,64},{4,68},{8,72},{12,76},{16,80},{20,84},{24,88},{28,92},{32,9... | collective-permute-start | bytes 196616 | tf_op jit(solution)/shard_map/ppermute | solution.py:18
  161.3 9.2 %collective-permute-start.7 = (f32[16,1024]{1,0:T(8,128)S(1)}, f32[16,1024]{1,0:T(8,128)S(1)}, u32[]{:S(2)}, u32[]{:S(2)}) collective-permute-start(f32[16,1024]{1,0:T(8,128)S(1)} %multiply_add_fusion.12), channel_id=1, source_target_pairs={{0,128},{4,132},{8,136},{12,140},{16,144},{20,148},{24,152},{28,15... | collective-permute-start | bytes 196616 | tf_op jit(solution)/shard_map/ppermute | solution.py:18
  176.6 1.4 collective-permute-start.16
  178.0 5.6 %collective-permute-start.17 = (f32[25,1024]{1,0:T(8,128)S(1)}, f32[25,1024]{1,0:T(8,128)S(1)}, u32[]{:S(2)}, u32[]{:S(2)}) collective-permute-start(f32[25,1024]{1,0:T(8,128)S(1)} %fusion.55), channel_id=1, source_target_pairs={{0,8},{4,12},{8,0},{12,4},{16,24},{20,28},{24,16},{28,20},{32,40},... | collective-permute-start | bytes 307208 | tf_op jit(solution)/shard_map/ppermute | solution.py:39
  183.7 6.0 %collective-permute-start.18 = (f32[25,1024]{1,0:T(8,128)S(1)}, f32[25,1024]{1,0:T(8,128)S(1)}, u32[]{:S(2)}, u32[]{:S(2)}) collective-permute-start(f32[25,1024]{1,0:T(8,128)S(1)} %add.217), channel_id=1, source_target_pairs={{0,16},{4,20},{8,24},{12,28},{16,0},{20,4},{24,8},{28,12},{32,48},... | collective-permute-start | bytes 307208 | tf_op jit(solution)/shard_map/ppermute | solution.py:39
  183.8 3.3 %collective-permute-start.15 = (bf16[3,2,1024]{2,1,0:T(2,128)(2,1)S(1)}, bf16[3,2,1024]{2,1,0:T(2,128)(2,1)S(1)}, u32[]{:S(2)}, u32[]{:S(2)}) collective-permute-start(bf16[3,2,1024]{2,1,0:T(2,128)(2,1)S(1)} %slice.130), channel_id=1, source_target_pairs={{4,0},{8,4},{12,8},{16,12},{20,16},{24,20},{28,24},{32,28},{36,32}... | collective-permute-start | bytes 36872 | tf_op jit(solution)/shard_map/ppermute | solution.py:18
  189.7 11.9 %collective-permute-start.19 = (f32[25,1024]{1,0:T(8,128)S(1)}, f32[25,1024]{1,0:T(8,128)S(1)}, u32[]{:S(2)}, u32[]{:S(2)}) collective-permute-start(f32[25,1024]{1,0:T(8,128)S(1)} %add.218), channel_id=1, source_target_pairs={{0,32},{4,36},{8,40},{12,44},{16,48},{20,52},{24,56},{28,60},{32,0... | collective-permute-start | bytes 307208 | tf_op jit(solution)/shard_map/ppermute | solution.py:39
  201.5 6.3 %collective-permute-start.20 = (f32[25,1024]{1,0:T(8,128)S(1)}, f32[25,1024]{1,0:T(8,128)S(1)}, u32[]{:S(2)}, u32[]{:S(2)}) collective-permute-start(f32[25,1024]{1,0:T(8,128)S(1)} %add.219), channel_id=1, source_target_pairs={{0,64},{4,68},{8,72},{12,76},{16,80},{20,84},{24,88},{28,92},{32,9... | collective-permute-start | bytes 307208 | tf_op jit(solution)/shard_map/ppermute | solution.py:39
  207.9 7.1 %collective-permute-start.21 = (f32[25,1024]{1,0:T(8,128)S(1)}, f32[25,1024]{1,0:T(8,128)S(1)}, u32[]{:S(2)}, u32[]{:S(2)}) collective-permute-start(f32[25,1024]{1,0:T(8,128)S(1)} %add.220), channel_id=1, source_target_pairs={{0,128},{4,132},{8,136},{12,140},{16,144},{20,148},{24,152},{28,15... | collective-permute-start | bytes 307208 | tf_op jit(solution)/shard_map/ppermute | solution.py:39
  (50 other events, 455.1 us)

commit v2 on v1

--- a/solution.py
+++ b/solution.py
@@ -18,26 +18,82 @@
     return lax.ppermute(value, axis, [(source, source + steps) for source in range(first, last)])
 
 
-def entering(own, rates, rows, axis, reverse):
-    count = lax.axis_size(axis)
-    sign = -1 if reverse else 1
-    state = passed_along(own, axis, sign)
-    shift = 1
-    while shift < count:
-        decay = jnp.exp(-rates * jnp.float32(rows * shift))
-        state = state + decay * passed_along(state, axis, sign * shift)
-        shift *= 2
-    return state
+def radices(count):
+    levels = []
+    while count > 1:
+        radix = 4 if count % 4 == 0 else 2
+        levels.append(radix)
+        count //= radix
+    return levels
+
+
+def members(value, axis, stride, radix):
+    count = lax.axis_size(axis)
+    digit = (lax.axis_index(axis) // stride) % radix
+    received = [value]
+    for step in range(1, radix):
+        pairs = []
+        for source in range(count):
+            source_digit = (source // stride) % radix
+            target = source + (((source_digit - step) % radix) - source_digit) * stride
+            pairs.append((source, target))
+        received.append(lax.ppermute(value, axis, pairs))
+    ordered = [
+        lax.select_n(((position - digit) % radix).astype(jnp.int32), *received)
+        for position in range(radix)
+    ]
+    return ordered, digit
+
+
+def power_of_two(count):
+    return count & (count - 1) == 0
+
+
+def entering(own_state, own_back, rates, rows, axis):
+    count = lax.axis_size(axis)
+    place = lax.axis_index(axis)
+    incoming = jnp.zeros_like(own_state)
+    later = jnp.zeros_like(own_back)
+    totals = jnp.stack([own_state, own_back], 0)
+    stride = 1
+    for radix in radices(count):
+        group, digit = members(totals, axis, stride, radix)
+        position = (place % stride).astype(jnp.float32)
+        for other in range(radix):
+            before = (digit > other).astype(jnp.float32)
+            after = (digit < other).astype(jnp.float32)
+            ahead = jnp.maximum(digit - 1 - other, 0).astype(jnp.float32) * stride + position
+            behind = jnp.maximum(other - 1 - digit, 0).astype(jnp.float32) * stride + (
+                stride - 1 - position
+            )
+            incoming = incoming + before * jnp.exp(-rates * (rows * ahead)) * group[other][0]
+            later = later + after * jnp.exp(-rates * (rows * behind)) * group[other][1]
+        forward_total = group[0][0]
+        backward_total = group[0][1]
+        for other in range(1, radix):
+            forward_total = (
+                jnp.exp(-rates * jnp.float32(rows * stride)) * forward_total + group[other][0]
+            )
+            backward_total = backward_total + jnp.exp(
+                -rates * jnp.float32(rows * stride * other)
+            ) * group[other][1]
+        totals = jnp.stack([forward_total, backward_total], 0)
+        stride *= radix
+    return incoming, later
 
 
 def summed(value, axis):
     count = lax.axis_size(axis)
-    if count & (count - 1):
+    if not power_of_two(count):
         return lax.psum(value, axis)
-    shift = 1
-    while shift < count:
-        value = value + lax.ppermute(value, axis, [(i, i ^ shift) for i in range(count)])
-        shift *= 2
+    stride = 1
+    for radix in radices(count):
+        group, _ = members(value, axis, stride, radix)
+        if radix == 4:
+            value = (group[0] + group[1]) + (group[2] + group[3])
+        else:
+            value = group[0] + group[1]
+        stride *= radix
     return value
 
 
@@ -52,7 +108,7 @@
     total_chans = chan_count * lax.axis_size("ch")
     total_rows = row_count * lax.axis_size("ctx")
     stream_wide = stream.astype(jnp.float32)
-    squares = lax.psum(jnp.sum(stream_wide * stream_wide, axis=1), "ch")
+    squares = summed(jnp.sum(stream_wide * stream_wide, axis=1), "ch")
     row_scale = lax.rsqrt(squares / total_chans + EPSILON)
     normed = (stream_wide * row_scale[:, None] * norm_gain[None, :]).astype(jnp.bfloat16)
     rim_rows = passed_along(normed[row_count - (KS - 1) :], "ctx", 1)
@@ -97,8 +153,7 @@
     own_back = jnp.sum(
         jnp.exp(-mode_rates[None] * (P_SIZE * block_steps)[:, None, None]) * block_heads, axis=0
     )
-    incoming = entering(own_state, mode_rates, row_count, "ctx", False)
-    later_state = entering(own_back, mode_rates, row_count, "ctx", True)
+    incoming, later_state = entering(own_state, own_back, mode_rates, row_count, "ctx")
 
     gap = block_steps[:, None] - block_steps[None, :] - 1.0
     earlier = (gap >= 0).astype(jnp.float32)
@@ -165,7 +220,7 @@
     norm_factor = 1.0 / jnp.sqrt(jnp.float32(total_rows))
     grad_residues = whole_sums[:M] * norm_factor
     grad_short = whole_sums[M:].reshape(3, KS, chan_count) * norm_factor
-    row_dot = lax.psum(jnp.sum(norm_gain[None, :] * grad_normed * stream_wide, axis=1), "ch")
+    row_dot = summed(jnp.sum(norm_gain[None, :] * grad_normed * stream_wide, axis=1), "ch")
     grad_stream = (
         row_scale[:, None] * norm_gain[None, :] * grad_normed
         - stream_wide * (row_scale**3 * row_dot / total_chans)[:, None]

time: 219 us -> 171 us (0.78)
  the two profiles are of different devices: /device:TPU:32 before, /device:TPU:1 now
where the time goes in v2:
time: 171 us; the launch traced here: 168 us
  starting transfers between devices  48.1 us (28%)
  other arithmetic  40.8 us (24%)
  local copies, waits for them, and re-layouts  33.5 us (20%)
  waiting for transfers between devices  28.5 us (17%)
  matrix products  14.7 us (9%)
  between operations  2.15 us (1%)
    ppermute x24, starting transfers between devices, members(): received.append(lax.ppermute(value, axis, pairs))  39.8 us
    ppermute x24, waiting for transfers between devices, members(): received.append(lax.ppermute(value, axis, pairs))  28.2 us
    transpose x1, local copies, waits for them, and re-layouts, per_device(): pairs = jnp.einsum('bic,bjc->ijc', grad_blocks, blocks, precision=HIGHEST)  12.1 us
    dot_general x1, matrix products, per_device(): pairs = jnp.einsum('bic,bjc->ijc', grad_blocks, blocks, precision=HIGHEST)  10.6 us
    ppermute x2, starting transfers between devices, passed_along(): lax.ppermute(value, axis, [(source, source + steps) for source in range(f...  8.26 us
    reduce_sum x1, other arithmetic, per_device(): weighted = jnp.sum(shifted[None] * grad_blocks[:, None], axis=2)  6.11 us
    rev x1, local copies, waits for them, and re-layouts, per_device(): decay_table[None, :, ::-1, :] * blocks[:, None]  5.7 us
    gather x1, local copies, waits for them, and re-layouts, per_device(): toeplitz = jnp.where((lags >= 0)[:, :, None], response[lag_index], 0.0)  5.39 us
  transfers between devices with their start and end apart: 26, of which 12 were waited for; matrix products, arithmetic and copies ran while one was open for 16% of the time, Pallas kernels for 0%

profile of v2, /device:TPU:1, one launch (start us, length us, event | category | flops | bytes accessed | tf_op | source)
XLA Modules:
  0.0 167.7 jit_solution(3679977401064564647)
XLA Ops:
  1.8 3.7 %collective-permute-start.1 = (f32[128]{0:T(128)S(1)}, f32[128]{0:T(128)S(1)}, u32[]{:S(2)}, u32[]{:S(2)}) collective-permute-start(f32[128]{0:T(128)S(1)} %fusion.4), channel_id=1, source_target_pairs={{0,2},{1,3},{2,0},{3,1},{4,6},{5,7},{6,4},{7,5},{8,10},{9,11},{10,... | collective-permute-start | bytes 1544 | tf_op jit(solution)/shard_map/ppermute | solution.py:40
  15.5 5.1 %collective-permute-start.3 = (bf16[2,1024]{1,0:T(2,128)(2,1)S(1)}, bf16[2,1024]{1,0:T(2,128)(2,1)S(1)}, u32[]{:S(2)}, u32[]{:S(2)}) collective-permute-start(bf16[2,1024]{1,0:T(2,128)(2,1)S(1)} %slice.237), channel_id=1, source_target_pairs={{0,4},{4,8},{8,12},{12,16},{16,20},{20,24},{24,28},{28,32},{32,36}... | collective-permute-start | bytes 12296 | tf_op jit(solution)/shard_map/ppermute | solution.py:18
  25.1 10.6 %convolution_bitcast_fusion = f32[32,32,1024]{0,1,2:T(8,128)} fusion(bf16[4,32,1024]{1,0,2:T(4,128)(2,1)} %copy.10, f32[4,32,1024]{1,0,2:T(4,128)S(1)} %copy.11), kind=kOutput, calls=%fused_computation.3 | convolution fusion | flops 50331648 | bytes 4980736 | tf_op jit(solution)/shard_map/bic,bjc->ijc/dot_general | solution.py:189
  35.7 12.1 %copy.12 = f32[32,32,1024]{2,1,0:T(8,128)} copy(f32[32,32,1024]{0,1,2:T(8,128)} %convolution_bitcast_fusion) | data formatting | bytes 8388608 | tf_op jit(solution)/shard_map/bic,bjc->ijc/transpose | solution.py:189
  47.8 4.1 %convolution_bitcast_fusion.1 = f32[32,1024]{1,0:T(8,128)S(1)} fusion(f32[32,32,1024]{2,1,0:T(8,128)} %copy.12, s32[32,32]{1,0:T(8,128)S(1)} %iota_subtract_fusion), kind=kOutput, calls=%fused_computation.30 | convolution fusion | flops 402685952 | bytes 4329472 | tf_op jit(solution)/shard_map/ijc,ijn->nc/dot_general | solution.py:190
  51.9 3.7 %multiply_reduce_fusion.7 = (f32[16,1024]{1,0:T(8,128)}, f32[32,1024]{1,0:T(8,128)S(1)}, f32[16,32,1024]{2,1,0:T(8,128)S(1)}, f32[16,32,1024]{2,1,0:T(8,128)}, f32[16,32,1024]{2,1,0:T(8,128)}) fusion(f32[32,1024]{1,0:T(8,128)S(1)} %convolution_bitcast_fusion.1, f32[32]{0:T(128)S(1)} %copy-done.53, f32[16,1024]{1,0:T(8,128)S(1)} %copy-done.15, ...), kind=kLoop, calls=%fused_computation.17 | loop fusion | flops 3620864 | bytes 6750464 | tf_op jit(solution)/shard_map/reduce_sum | solution.py:191
  55.6 5.7 %rev.6 = f32[16,32,1024]{2,1,0:T(8,128)} reverse(f32[16,32,1024]{2,1,0:T(8,128)} %get-tuple-element.49), dimensions={1} | reverse | bytes 4194304 | tf_op jit(solution)/shard_map/rev | solution.py:145
  61.3 6.1 %multiply_reduce_fusion.2 = (f32[4,16,1024]{2,1,0:T(8,128)}, f32[4,16,1024]{2,1,0:T(8,128)S(1)}) fusion(f32[16,32,1024]{2,1,0:T(8,128)} %get-tuple-element.50, f32[4,32,1024]{2,1,0:T(8,128)S(1)} %bitcast.301, f32[16,32,1024]{2,1,0:T(8,128)} %get-tuple-element.49), kind=kLoop, calls=%fused_computation.4 | loop fusion | flops 8257536 | bytes 5242880 | tf_op jit(solution)/shard_map/reduce_sum | solution.py:187
  73.7 5.4 %gather_fusion = f32[1024,1024]{1,0:T(8,128)} fusion(f32[32,1024]{1,0:T(8,128)S(1)} %get-tuple-element.12, s32[1024]{0:T(1024)S(1)} %broadcast_clamp_fusion), kind=kCustom, calls=%fused_computation | custom fusion | bytes 8392704 | tf_op jit(solution)/shard_map/gather | solution.py:140
  81.7 4.6 %multiply_reduce_fusion = (f32[4,32,1024]{2,1,0:T(8,128)}, f32[4,32,1024]{2,1,0:T(8,128)}) fusion(f32[4,32,1024]{2,1,0:T(8,128)S(1)} %bitcast.302, f32[32,32,1024]{2,1,0:T(8,128)S(1)} %broadcast_select_fusion, f32[4,32,1024]{2,1,0:T(8,128)S(1)} %bitcast_convert_fusion.1), kind=kLoop, calls=%fused_computation.1 | loop fusion | flops 16515072 | bytes 6291456 | tf_op jit(solution)/shard_map/reduce_sum | solution.py:181
  89.3 7.8 %collective-permute-start.8 = (f32[2,16,1024]{2,1,0:T(8,128)}, f32[2,16,1024]{2,1,0:T(8,128)}, u32[]{:S(2)}, u32[]{:S(2)}) collective-permute-start(f32[2,16,1024]{2,1,0:T(8,128)} %pad_maximum_fusion.4), channel_id=1, source_target_pairs={{0,32},{4,36},{8,40},{12,44},{16,48},{20,52},{24,56},{28,60},{32,0... | collective-permute-start | bytes 393224 | tf_op jit(solution)/shard_map/ppermute | solution.py:40
  97.2 3.6 %collective-permute-start.7 = (f32[2,16,1024]{2,1,0:T(8,128)}, f32[2,16,1024]{2,1,0:T(8,128)}, u32[]{:S(2)}, u32[]{:S(2)}) collective-permute-start(f32[2,16,1024]{2,1,0:T(8,128)} %pad_maximum_fusion.4), channel_id=1, source_target_pairs={{0,48},{4,52},{8,56},{12,60},{16,0},{20,4},{24,8},{28,12},{32,16},... | collective-permute-start | bytes 393224 | tf_op jit(solution)/shard_map/ppermute | solution.py:40
  101.8 3.3 %rev.7 = f32[16,32,1024]{2,1,0:T(8,128)} reverse(f32[16,32,1024]{2,1,0:T(8,128)S(1)} %get-tuple-element.48), dimensions={1} | reverse | bytes 4194304 | tf_op jit(solution)/shard_map/rev | solution.py:182
  105.8 4.0 %collective-permute-done.7 = f32[2,16,1024]{2,1,0:T(8,128)} collective-permute-done((f32[2,16,1024]{2,1,0:T(8,128)}, f32[2,16,1024]{2,1,0:T(8,128)}, u32[]{:S(2)}, u32[]{:S(2)}) %collective-permute-start.7) | collective-permute-done | bytes 131104 | tf_op jit(solution)/shard_map/ppermute | solution.py:40
  112.1 3.0 %collective-permute-start.11 = (f32[2,16,1024]{2,1,0:T(8,128)S(1)}, f32[2,16,1024]{2,1,0:T(8,128)S(1)}, u32[]{:S(2)}, u32[]{:S(2)}) collective-permute-start(f32[2,16,1024]{2,1,0:T(8,128)S(1)} %pad_maximum_fusion.5), channel_id=1, source_target_pairs={{0,128},{4,132},{8,136},{12,140},{16,144},{20,148},{24,152},{28,15... | collective-permute-start | bytes 393224 | tf_op jit(solution)/shard_map/ppermute | solution.py:40
  118.7 2.9 %collective-permute-done.12 = f32[2,16,1024]{2,1,0:T(8,128)S(1)} collective-permute-done((f32[2,16,1024]{2,1,0:T(8,128)S(1)}, f32[2,16,1024]{2,1,0:T(8,128)S(1)}, u32[]{:S(2)}, u32[]{:S(2)}) %collective-permute-start.12) | collective-permute-done | bytes 131104 | tf_op jit(solution)/shard_map/ppermute | solution.py:40
  126.6 3.1 %collective-permute-start.13 = (bf16[3,2,1024]{2,1,0:T(2,128)(2,1)S(1)}, bf16[3,2,1024]{2,1,0:T(2,128)(2,1)S(1)}, u32[]{:S(2)}, u32[]{:S(2)}) collective-permute-start(bf16[3,2,1024]{2,1,0:T(2,128)(2,1)S(1)} %slice.266), channel_id=1, source_target_pairs={{4,0},{8,4},{12,8},{16,12},{20,16},{24,20},{28,24},{32,28},{36,32}... | collective-permute-start | bytes 36872 | tf_op jit(solution)/shard_map/ppermute | solution.py:18
  133.2 2.8 %collective-permute-done.18 = f32[25,1024]{1,0:T(8,128)S(1)} collective-permute-done((f32[25,1024]{1,0:T(8,128)S(1)}, f32[25,1024]{1,0:T(8,128)S(1)}, u32[]{:S(2)}, u32[]{:S(2)}) %collective-permute-start.18) | collective-permute-done | bytes 102432 | tf_op jit(solution)/shard_map/ppermute | solution.py:40
  135.9 2.8 %collective-permute-done.17 = f32[25,1024]{1,0:T(8,128)S(1)} collective-permute-done((f32[25,1024]{1,0:T(8,128)S(1)}, f32[25,1024]{1,0:T(8,128)S(1)}, u32[]{:S(2)}, u32[]{:S(2)}) %collective-permute-start.17) | collective-permute-done | bytes 102432 | tf_op jit(solution)/shard_map/ppermute | solution.py:40
  138.8 2.9 %collective-permute-start.21 = (f32[25,1024]{1,0:T(8,128)S(1)}, f32[25,1024]{1,0:T(8,128)S(1)}, u32[]{:S(2)}, u32[]{:S(2)}) collective-permute-start(f32[25,1024]{1,0:T(8,128)S(1)} %add_add_fusion.2), channel_id=1, source_target_pairs={{0,32},{4,36},{8,40},{12,44},{16,48},{20,52},{24,56},{28,60},{32,0... | collective-permute-start | bytes 307208 | tf_op jit(solution)/shard_map/ppermute | solution.py:40
  141.7 2.9 %collective-permute-start.22 = (f32[25,1024]{1,0:T(8,128)S(1)}, f32[25,1024]{1,0:T(8,128)S(1)}, u32[]{:S(2)}, u32[]{:S(2)}) collective-permute-start(f32[25,1024]{1,0:T(8,128)S(1)} %add_add_fusion.2), channel_id=1, source_target_pairs={{0,16},{4,20},{8,24},{12,28},{16,32},{20,36},{24,40},{28,44},{32,4... | collective-permute-start | bytes 307208 | tf_op jit(solution)/shard_map/ppermute | solution.py:40
  147.3 5.4 %collective-permute-done.22 = f32[25,1024]{1,0:T(8,128)S(1)} collective-permute-done((f32[25,1024]{1,0:T(8,128)S(1)}, f32[25,1024]{1,0:T(8,128)S(1)}, u32[]{:S(2)}, u32[]{:S(2)}) %collective-permute-start.22) | collective-permute-done | bytes 102432 | tf_op jit(solution)/shard_map/ppermute | solution.py:40
  152.6 3.8 %collective-permute-done.20 = f32[25,1024]{1,0:T(8,128)S(1)} collective-permute-done((f32[25,1024]{1,0:T(8,128)S(1)}, f32[25,1024]{1,0:T(8,128)S(1)}, u32[]{:S(2)}, u32[]{:S(2)}) %collective-permute-start.20) | collective-permute-done | bytes 102432 | tf_op jit(solution)/shard_map/ppermute | solution.py:40
  162.7 3.3 %collective-permute-done.25 = f32[25,1024]{1,0:T(8,128)S(1)} collective-permute-done((f32[25,1024]{1,0:T(8,128)S(1)}, f32[25,1024]{1,0:T(8,128)S(1)}, u32[]{:S(2)}, u32[]{:S(2)}) %collective-permute-start.25) | collective-permute-done | bytes 102432 | tf_op jit(solution)/shard_map/ppermute | solution.py:40
  (235 shorter events, 52.8 us)
Async XLA Ops:
  1.8 12.6 %collective-permute-start.1 = (f32[128]{0:T(128)S(1)}, f32[128]{0:T(128)S(1)}, u32[]{:S(2)}, u32[]{:S(2)}) collective-permute-start(f32[128]{0:T(128)S(1)} %fusion.4), channel_id=1, source_target_pairs={{0,2},{1,3},{2,0},{3,1},{4,6},{5,7},{6,4},{7,5},{8,10},{9,11},{10,... | collective-permute-start | bytes 1544 | tf_op jit(solution)/shard_map/ppermute | solution.py:40
  5.4 9.0 %collective-permute-start.2 = (f32[128]{0:T(128)S(1)}, f32[128]{0:T(128)S(1)}, u32[]{:S(2)}, u32[]{:S(2)}) collective-permute-start(f32[128]{0:T(128)S(1)} %fusion.4), channel_id=1, source_target_pairs={{0,1},{1,2},{2,3},{3,0},{4,5},{5,6},{6,7},{7,4},{8,9},{9,10},{10,1... | collective-permute-start | bytes 1544 | tf_op jit(solution)/shard_map/ppermute | solution.py:40
  5.7 8.6 %collective-permute-start = (f32[128]{0:T(128)S(1)}, f32[128]{0:T(128)S(1)}, u32[]{:S(2)}, u32[]{:S(2)}) collective-permute-start(f32[128]{0:T(128)S(1)} %fusion.4), channel_id=1, source_target_pairs={{0,3},{1,0},{2,1},{3,2},{4,7},{5,4},{6,5},{7,6},{8,11},{9,8},{10,9... | collective-permute-start | bytes 1544 | tf_op jit(solution)/shard_map/ppermute | solution.py:40
  15.5 5.7 %collective-permute-start.3 = (bf16[2,1024]{1,0:T(2,128)(2,1)S(1)}, bf16[2,1024]{1,0:T(2,128)(2,1)S(1)}, u32[]{:S(2)}, u32[]{:S(2)}) collective-permute-start(bf16[2,1024]{1,0:T(2,128)(2,1)S(1)} %slice.237), channel_id=1, source_target_pairs={{0,4},{4,8},{8,12},{12,16},{16,20},{20,24},{24,28},{28,32},{32,36}... | collective-permute-start | bytes 12296 | tf_op jit(solution)/shard_map/ppermute | solution.py:18
  70.6 15.8 %collective-permute-start.5 = (f32[2,16,1024]{2,1,0:T(8,128)}, f32[2,16,1024]{2,1,0:T(8,128)}, u32[]{:S(2)}, u32[]{:S(2)}) collective-permute-start(f32[2,16,1024]{2,1,0:T(8,128)} %pad_maximum_fusion.3), channel_id=1, source_target_pairs={{0,8},{4,12},{8,0},{12,4},{16,24},{20,28},{24,16},{28,20},{32,40},... | collective-permute-start | bytes 393224 | tf_op jit(solution)/shard_map/ppermute | solution.py:40
  72.2 14.1 %collective-permute-start.6 = (f32[2,16,1024]{2,1,0:T(8,128)}, f32[2,16,1024]{2,1,0:T(8,128)}, u32[]{:S(2)}, u32[]{:S(2)}) collective-permute-start(f32[2,16,1024]{2,1,0:T(8,128)} %pad_maximum_fusion.3), channel_id=1, source_target_pairs={{0,4},{4,8},{8,12},{12,0},{16,20},{20,24},{24,28},{28,16},{32,36},... | collective-permute-start | bytes 393224 | tf_op jit(solution)/shard_map/ppermute | solution.py:40
  73.2 13.1 %collective-permute-start.4 = (f32[2,16,1024]{2,1,0:T(8,128)}, f32[2,16,1024]{2,1,0:T(8,128)}, u32[]{:S(2)}, u32[]{:S(2)}) collective-permute-start(f32[2,16,1024]{2,1,0:T(8,128)} %pad_maximum_fusion.3), channel_id=1, source_target_pairs={{0,12},{4,0},{8,4},{12,8},{16,28},{20,16},{24,20},{28,24},{32,44},... | collective-permute-start | bytes 393224 | tf_op jit(solution)/shard_map/ppermute | solution.py:40
  89.3 15.8 %collective-permute-start.8 = (f32[2,16,1024]{2,1,0:T(8,128)}, f32[2,16,1024]{2,1,0:T(8,128)}, u32[]{:S(2)}, u32[]{:S(2)}) collective-permute-start(f32[2,16,1024]{2,1,0:T(8,128)} %pad_maximum_fusion.4), channel_id=1, source_target_pairs={{0,32},{4,36},{8,40},{12,44},{16,48},{20,52},{24,56},{28,60},{32,0... | collective-permute-start | bytes 393224 | tf_op jit(solution)/shard_map/ppermute | solution.py:40
  97.1 8.7 %collective-permute-start.9 = (f32[2,16,1024]{2,1,0:T(8,128)}, f32[2,16,1024]{2,1,0:T(8,128)}, u32[]{:S(2)}, u32[]{:S(2)}) collective-permute-start(f32[2,16,1024]{2,1,0:T(8,128)} %pad_maximum_fusion.4), channel_id=1, source_target_pairs={{0,16},{4,20},{8,24},{12,28},{16,32},{20,36},{24,40},{28,44},{32,4... | collective-permute-start | bytes 393224 | tf_op jit(solution)/shard_map/ppermute | solution.py:40
  97.2 12.6 %collective-permute-start.7 = (f32[2,16,1024]{2,1,0:T(8,128)}, f32[2,16,1024]{2,1,0:T(8,128)}, u32[]{:S(2)}, u32[]{:S(2)}) collective-permute-start(f32[2,16,1024]{2,1,0:T(8,128)} %pad_maximum_fusion.4), channel_id=1, source_target_pairs={{0,48},{4,52},{8,56},{12,60},{16,0},{20,4},{24,8},{28,12},{32,16},... | collective-permute-start | bytes 393224 | tf_op jit(solution)/shard_map/ppermute | solution.py:40
  112.1 6.6 %collective-permute-start.11 = (f32[2,16,1024]{2,1,0:T(8,128)S(1)}, f32[2,16,1024]{2,1,0:T(8,128)S(1)}, u32[]{:S(2)}, u32[]{:S(2)}) collective-permute-start(f32[2,16,1024]{2,1,0:T(8,128)S(1)} %pad_maximum_fusion.5), channel_id=1, source_target_pairs={{0,128},{4,132},{8,136},{12,140},{16,144},{20,148},{24,152},{28,15... | collective-permute-start | bytes 393224 | tf_op jit(solution)/shard_map/ppermute | solution.py:40
  115.1 6.5 %collective-permute-start.12 = (f32[2,16,1024]{2,1,0:T(8,128)S(1)}, f32[2,16,1024]{2,1,0:T(8,128)S(1)}, u32[]{:S(2)}, u32[]{:S(2)}) collective-permute-start(f32[2,16,1024]{2,1,0:T(8,128)S(1)} %pad_maximum_fusion.5), channel_id=1, source_target_pairs={{0,64},{4,68},{8,72},{12,76},{16,80},{20,84},{24,88},{28,92},{32,9... | collective-permute-start | bytes 393224 | tf_op jit(solution)/shard_map/ppermute | solution.py:40
  115.5 6.0 %collective-permute-start.10 = (f32[2,16,1024]{2,1,0:T(8,128)S(1)}, f32[2,16,1024]{2,1,0:T(8,128)S(1)}, u32[]{:S(2)}, u32[]{:S(2)}) collective-permute-start(f32[2,16,1024]{2,1,0:T(8,128)S(1)} %pad_maximum_fusion.5), channel_id=1, source_target_pairs={{0,192},{4,196},{8,200},{12,204},{16,208},{20,212},{24,216},{28,22... | collective-permute-start | bytes 393224 | tf_op jit(solution)/shard_map/ppermute | solution.py:40
  130.6 5.3 %collective-permute-start.18 = (f32[25,1024]{1,0:T(8,128)S(1)}, f32[25,1024]{1,0:T(8,128)S(1)}, u32[]{:S(2)}, u32[]{:S(2)}) collective-permute-start(f32[25,1024]{1,0:T(8,128)S(1)} %pad_maximum_fusion.6), channel_id=1, source_target_pairs={{0,8},{4,12},{8,0},{12,4},{16,24},{20,28},{24,16},{28,20},{32,40},... | collective-permute-start | bytes 307208 | tf_op jit(solution)/shard_map/ppermute | solution.py:40
  131.7 7.0 %collective-permute-start.17 = (f32[25,1024]{1,0:T(8,128)S(1)}, f32[25,1024]{1,0:T(8,128)S(1)}, u32[]{:S(2)}, u32[]{:S(2)}) collective-permute-start(f32[25,1024]{1,0:T(8,128)S(1)} %pad_maximum_fusion.6), channel_id=1, source_target_pairs={{0,12},{4,0},{8,4},{12,8},{16,28},{20,16},{24,20},{28,24},{32,44},... | collective-permute-start | bytes 307208 | tf_op jit(solution)/shard_map/ppermute | solution.py:40
  132.5 12.1 %collective-permute-start.15 = (f32[128]{0:T(128)S(1)}, f32[128]{0:T(128)S(1)}, u32[]{:S(2)}, u32[]{:S(2)}) collective-permute-start(f32[128]{0:T(128)S(1)} %get-tuple-element.19), channel_id=1, source_target_pairs={{0,2},{1,3},{2,0},{3,1},{4,6},{5,7},{6,4},{7,5},{8,10},{9,11},{10,... | collective-permute-start | bytes 1544 | tf_op jit(solution)/shard_map/ppermute | solution.py:40
  132.6 12.7 %collective-permute-start.16 = (f32[128]{0:T(128)S(1)}, f32[128]{0:T(128)S(1)}, u32[]{:S(2)}, u32[]{:S(2)}) collective-permute-start(f32[128]{0:T(128)S(1)} %get-tuple-element.19), channel_id=1, source_target_pairs={{0,1},{1,2},{2,3},{3,0},{4,5},{5,6},{6,7},{7,4},{8,9},{9,10},{10,1... | collective-permute-start | bytes 1544 | tf_op jit(solution)/shard_map/ppermute | solution.py:40
  135.9 9.4 %collective-permute-start.14 = (f32[128]{0:T(128)S(1)}, f32[128]{0:T(128)S(1)}, u32[]{:S(2)}, u32[]{:S(2)}) collective-permute-start(f32[128]{0:T(128)S(1)} %get-tuple-element.19), channel_id=1, source_target_pairs={{0,3},{1,0},{2,1},{3,2},{4,7},{5,4},{6,5},{7,6},{8,11},{9,8},{10,9... | collective-permute-start | bytes 1544 | tf_op jit(solution)/shard_map/ppermute | solution.py:40
  138.8 8.5 %collective-permute-start.21 = (f32[25,1024]{1,0:T(8,128)S(1)}, f32[25,1024]{1,0:T(8,128)S(1)}, u32[]{:S(2)}, u32[]{:S(2)}) collective-permute-start(f32[25,1024]{1,0:T(8,128)S(1)} %add_add_fusion.2), channel_id=1, source_target_pairs={{0,32},{4,36},{8,40},{12,44},{16,48},{20,52},{24,56},{28,60},{32,0... | collective-permute-start | bytes 307208 | tf_op jit(solution)/shard_map/ppermute | solution.py:40
  141.7 10.9 %collective-permute-start.22 = (f32[25,1024]{1,0:T(8,128)S(1)}, f32[25,1024]{1,0:T(8,128)S(1)}, u32[]{:S(2)}, u32[]{:S(2)}) collective-permute-start(f32[25,1024]{1,0:T(8,128)S(1)} %add_add_fusion.2), channel_id=1, source_target_pairs={{0,16},{4,20},{8,24},{12,28},{16,32},{20,36},{24,40},{28,44},{32,4... | collective-permute-start | bytes 307208 | tf_op jit(solution)/shard_map/ppermute | solution.py:40
  144.7 11.8 %collective-permute-start.20 = (f32[25,1024]{1,0:T(8,128)S(1)}, f32[25,1024]{1,0:T(8,128)S(1)}, u32[]{:S(2)}, u32[]{:S(2)}) collective-permute-start(f32[25,1024]{1,0:T(8,128)S(1)} %add_add_fusion.2), channel_id=1, source_target_pairs={{0,48},{4,52},{8,56},{12,60},{16,0},{20,4},{24,8},{28,12},{32,16},... | collective-permute-start | bytes 307208 | tf_op jit(solution)/shard_map/ppermute | solution.py:40
  156.5 6.2 %collective-permute-start.24 = (f32[25,1024]{1,0:T(8,128)S(1)}, f32[25,1024]{1,0:T(8,128)S(1)}, u32[]{:S(2)}, u32[]{:S(2)}) collective-permute-start(f32[25,1024]{1,0:T(8,128)S(1)} %add_add_fusion.1), channel_id=1, source_target_pairs={{0,128},{4,132},{8,136},{12,140},{16,144},{20,148},{24,152},{28,15... | collective-permute-start | bytes 307208 | tf_op jit(solution)/shard_map/ppermute | solution.py:40
  158.7 7.3 %collective-permute-start.25 = (f32[25,1024]{1,0:T(8,128)S(1)}, f32[25,1024]{1,0:T(8,128)S(1)}, u32[]{:S(2)}, u32[]{:S(2)}) collective-permute-start(f32[25,1024]{1,0:T(8,128)S(1)} %add_add_fusion.1), channel_id=1, source_target_pairs={{0,64},{4,68},{8,72},{12,76},{16,80},{20,84},{24,88},{28,92},{32,9... | collective-permute-start | bytes 307208 | tf_op jit(solution)/shard_map/ppermute | solution.py:40
  160.2 5.9 %collective-permute-start.23 = (f32[25,1024]{1,0:T(8,128)S(1)}, f32[25,1024]{1,0:T(8,128)S(1)}, u32[]{:S(2)}, u32[]{:S(2)}) collective-permute-start(f32[25,1024]{1,0:T(8,128)S(1)} %add_add_fusion.1), channel_id=1, source_target_pairs={{0,192},{4,196},{8,200},{12,204},{16,208},{20,212},{24,216},{28,22... | collective-permute-start | bytes 307208 | tf_op jit(solution)/shard_map/ppermute | solution.py:40
  (67 other events, 409.6 us)

commit v3 on v2

--- a/solution.py
+++ b/solution.py
@@ -8,7 +8,6 @@
 P_SIZE = 32
 
 
-HIGHEST = lax.Precision.HIGHEST
 EPSILON = 1e-05
 
 
@@ -95,11 +94,6 @@
             value = group[0] + group[1]
         stride *= radix
     return value
-
-
-def lag_table(length):
-    steps = jnp.arange(length)
-    return (steps[:, None, None] - steps[None, :, None] == steps[None, None, :]).astype(jnp.float32)
 
 
 def per_device(stream, norm_gain, short_filters, mode_rates, residues, grad_out):
@@ -133,16 +127,17 @@
 
     steps = jnp.arange(P_SIZE).astype(jnp.float32)
     decay_table = jnp.exp(-mode_rates[:, None, :] * steps[None, :, None])
+    decay_reversed = jnp.exp(-mode_rates[:, None, :] * (P_SIZE - 1.0 - steps)[None, :, None])
     shifted = jnp.exp(-mode_rates[:, None, :] * (steps[None, :, None] + 1.0))
     response = jnp.sum(residues[:, None, :] * decay_table, axis=0)
-    lags = steps[:, None] - steps[None, :]
-    lag_index = jnp.clip(lags, 0, P_SIZE - 1).astype(jnp.int32)
-    toeplitz = jnp.where((lags >= 0)[:, :, None], response[lag_index], 0.0)
     carried_table = shifted * residues[:, None, :]
+    carried_reversed = (
+        jnp.exp(-mode_rates[:, None, :] * (P_SIZE - steps)[None, :, None]) * residues[:, None, :]
+    )
 
     blocks = product.reshape(block_count, P_SIZE, chan_count)
     grad_blocks = grad_conv.reshape(block_count, P_SIZE, chan_count)
-    block_ends = jnp.sum(decay_table[None, :, ::-1, :] * blocks[:, None], axis=2)
+    block_ends = jnp.sum(decay_reversed[None] * blocks[:, None], axis=2)
     block_heads = jnp.sum(decay_table[None] * grad_blocks[:, None], axis=2)
     block_steps = jnp.arange(block_count).astype(jnp.float32)
     own_state = jnp.sum(
@@ -172,22 +167,37 @@
         -mode_rates[None] * (P_SIZE * (block_count - 1 - block_steps))[:, None, None]
     ) * later_state[None]
 
-    local_part = jnp.sum(toeplitz[None] * blocks[:, None], axis=2)
+    lead = jnp.zeros((block_count, P_SIZE - 1, chan_count), jnp.float32)
+    blocks_padded = jnp.concatenate([lead, blocks], 1)
+    grads_padded = jnp.concatenate([grad_blocks, lead], 1)
+    local_part = sum(
+        response[lag][None, None, :] * blocks_padded[:, P_SIZE - 1 - lag : 2 * P_SIZE - 1 - lag]
+        for lag in range(P_SIZE)
+    )
     carried = jnp.sum(starts[:, :, None, :] * carried_table[None], axis=1)
     long_conv = (local_part + carried).reshape(row_count, chan_count)
     output = (query_part * long_conv).astype(jnp.bfloat16)
     grad_query = (cotangent * long_conv).astype(jnp.bfloat16)
 
-    back_local = jnp.sum(toeplitz[None] * grad_blocks[:, :, None], axis=1)
-    back_carried = jnp.sum(ends_back[:, :, None, :] * carried_table[None, :, ::-1, :], axis=1)
+    back_local = sum(
+        response[lag][None, None, :] * grads_padded[:, lag : lag + P_SIZE] for lag in range(P_SIZE)
+    )
+    back_carried = jnp.sum(ends_back[:, :, None, :] * carried_reversed[None], axis=1)
     grad_product = (back_local + back_carried).reshape(row_count, chan_count)
     grad_key = (grad_product * value_part).astype(jnp.bfloat16)
     grad_value = (grad_product * key_part).astype(jnp.bfloat16)
 
     weighted = jnp.sum(shifted[None] * grad_blocks[:, None], axis=2)
     cross_part = jnp.sum(weighted * starts, axis=0)
-    pairs = jnp.einsum("bic,bjc->ijc", grad_blocks, blocks, precision=HIGHEST)
-    by_lag = jnp.einsum("ijc,ijn->nc", pairs, lag_table(P_SIZE), precision=HIGHEST)
+    by_lag = jnp.stack(
+        [
+            jnp.sum(
+                blocks_padded[:, P_SIZE - 1 - lag : 2 * P_SIZE - 1 - lag] * grad_blocks, axis=(0, 1)
+            )
+            for lag in range(P_SIZE)
+        ],
+        0,
+    )
     local_terms = jnp.sum(by_lag[None] * decay_table, axis=1)
 
     stacked_half = lax.optimization_barrier(jnp.stack([grad_query, grad_key, grad_value], 0))

time: 171 us -> 119 us (0.70)
  the two profiles are of different devices: /device:TPU:1 before, /device:TPU:32 now
where the time goes in v3:
time: 119 us; the launch traced here: 118 us
  starting transfers between devices  47.9 us (40%)
  waiting for transfers between devices  36.6 us (31%)
  other arithmetic  28.5 us (24%)
  local copies, waits for them, and re-layouts  3.43 us (3%)
  between operations  1.42 us (1%)
    ppermute x24, starting transfers between devices, members(): received.append(lax.ppermute(value, axis, pairs))  44 us
    ppermute x24, waiting for transfers between devices, members(): received.append(lax.ppermute(value, axis, pairs))  33.8 us
    reduce_sum x1, other arithmetic, per_device(): weighted = jnp.sum(shifted[None] * grad_blocks[:, None], axis=2)  5.28 us
    ppermute x2, starting transfers between devices, passed_along(): lax.ppermute(value, axis, [(source, source + steps) for source in range(f...  3.9 us
    ppermute x2, waiting for transfers between devices, passed_along(): lax.ppermute(value, axis, [(source, source + steps) for source in range(f...  2.76 us
    reduce_sum x3, other arithmetic, per_device(): jnp.sum(blocks_padded[:, P_SIZE - 1 - lag:2 * P_SIZE - 1 - lag] * grad_bl...  2.53 us
  transfers between devices with their start and end apart: 26, of which 14 were waited for; matrix products, arithmetic and copies ran while one was open for 8% of the time, Pallas kernels for 0%

profile of v3, /device:TPU:32, one launch (start us, length us, event | category | flops | bytes accessed | tf_op | source)
XLA Modules:
  0.0 117.8 jit_solution(10259832267040334023)
XLA Ops:
  1.7 3.1 %collective-permute-start.1 = (f32[128]{0:T(128)S(1)}, f32[128]{0:T(128)S(1)}, u32[]{:S(2)}, u32[]{:S(2)}) collective-permute-start(f32[128]{0:T(128)S(1)} %fusion.4), channel_id=1, source_target_pairs={{0,2},{1,3},{2,0},{3,1},{4,6},{5,7},{6,4},{7,5},{8,10},{9,11},{10,... | collective-permute-start | bytes 1544 | tf_op jit(solution)/shard_map/ppermute | solution.py:39
  5.4 2.6 %collective-permute-start = (f32[128]{0:T(128)S(1)}, f32[128]{0:T(128)S(1)}, u32[]{:S(2)}, u32[]{:S(2)}) collective-permute-start(f32[128]{0:T(128)S(1)} %fusion.4), channel_id=1, source_target_pairs={{0,3},{1,0},{2,1},{3,2},{4,7},{5,4},{6,5},{7,6},{8,11},{9,8},{10,9... | collective-permute-start | bytes 1544 | tf_op jit(solution)/shard_map/ppermute | solution.py:39
  15.1 1.9 %collective-permute-start.3 = (bf16[2,1024]{1,0:T(2,128)(2,1)S(1)}, bf16[2,1024]{1,0:T(2,128)(2,1)S(1)}, u32[]{:S(2)}, u32[]{:S(2)}) collective-permute-start(bf16[2,1024]{1,0:T(2,128)(2,1)S(1)} %slice.674), channel_id=1, source_target_pairs={{0,4},{4,8},{8,12},{12,16},{16,20},{20,24},{24,28},{28,32},{32,36}... | collective-permute-start | bytes 12296 | tf_op jit(solution)/shard_map/ppermute | solution.py:17
  17.2 2.8 %collective-permute-done.3 = bf16[2,1024]{1,0:T(2,128)(2,1)S(1)} collective-permute-done((bf16[2,1024]{1,0:T(2,128)(2,1)S(1)}, bf16[2,1024]{1,0:T(2,128)(2,1)S(1)}, u32[]{:S(2)}, u32[]{:S(2)}) %collective-permute-start.3) | collective-permute-done | bytes 4128 | tf_op jit(solution)/shard_map/ppermute | solution.py:17
  24.6 2.2 %multiply_reduce_fusion.5 = (f32[16,1024]{1,0:T(8,128)S(1)}, f32[32,1024]{1,0:T(8,128)S(1)}, f32[16,32,1024]{2,1,0:T(8,128)S(1)}, f32[16,32,1024]{2,1,0:T(8,128)...) fusion(f32[32,1024]{1,0:T(8,128)S(1)} %stack.195, ...), kind=kLoop, calls=%fused_computation.75 | loop fusion | flops 5193728 | bytes 10945024 | tf_op jit(solution)/shard_map/reduce_sum | solution.py:201
  26.8 5.3 %multiply_reduce_fusion = (f32[4,16,1024]{2,1,0:T(8,128)S(1)}, f32[4,16,1024]{2,1,0:T(8,128)S(1)}, f32[4,16,1024]{2,1,0:T(8,128)S(1)}) fusion(f32[16,32,1024]{2,1,0:T(8,128)S(1)} %get-tuple-element.110, f32[4,32,1024]{2,1,0:T(8,128)S(1)} %bitcast.385, f32[16,32,1024]{2,1,0:T(8,128)S(1)} %get-tuple-element.109, f32[4,32,1024]{2,1,0:T(8,128)S(1)} %bitcast_convert_fusion.1, ...), kind=kLoop, calls=%fused_computation | loop fusion | flops 12386304 | bytes 8126464 | tf_op jit(solution)/shard_map/reduce_sum | solution.py:190
  32.5 1.7 %collective-permute-start.4 = (f32[2,16,1024]{2,1,0:T(8,128)S(1)}, f32[2,16,1024]{2,1,0:T(8,128)S(1)}, u32[]{:S(2)}, u32[]{:S(2)}) collective-permute-start(f32[2,16,1024]{2,1,0:T(8,128)S(1)} %pad_maximum_fusion.3), channel_id=1, source_target_pairs={{0,12},{4,0},{8,4},{12,8},{16,28},{20,16},{24,20},{28,24},{32,44},... | collective-permute-start | bytes 393224 | tf_op jit(solution)/shard_map/ppermute | solution.py:39
  34.5 4.3 %collective-permute-done.5 = f32[2,16,1024]{2,1,0:T(8,128)S(1)} collective-permute-done((f32[2,16,1024]{2,1,0:T(8,128)S(1)}, f32[2,16,1024]{2,1,0:T(8,128)S(1)}, u32[]{:S(2)}, u32[]{:S(2)}) %collective-permute-start.5) | collective-permute-done | bytes 131104 | tf_op jit(solution)/shard_map/ppermute | solution.py:39
  39.4 7.5 %collective-permute-start.8 = (f32[2,16,1024]{2,1,0:T(8,128)S(1)}, f32[2,16,1024]{2,1,0:T(8,128)S(1)}, u32[]{:S(2)}, u32[]{:S(2)}) collective-permute-start(f32[2,16,1024]{2,1,0:T(8,128)S(1)} %pad_maximum_fusion.4), channel_id=1, source_target_pairs={{0,32},{4,36},{8,40},{12,44},{16,48},{20,52},{24,56},{28,60},{32,0... | collective-permute-start | bytes 393224 | tf_op jit(solution)/shard_map/ppermute | solution.py:39
  47.4 3.7 %collective-permute-start.7 = (f32[2,16,1024]{2,1,0:T(8,128)S(1)}, f32[2,16,1024]{2,1,0:T(8,128)S(1)}, u32[]{:S(2)}, u32[]{:S(2)}) collective-permute-start(f32[2,16,1024]{2,1,0:T(8,128)S(1)} %pad_maximum_fusion.4), channel_id=1, source_target_pairs={{0,48},{4,52},{8,56},{12,60},{16,0},{20,4},{24,8},{28,12},{32,16},... | collective-permute-start | bytes 393224 | tf_op jit(solution)/shard_map/ppermute | solution.py:39
  51.1 8.5 %collective-permute-done.9 = f32[2,16,1024]{2,1,0:T(8,128)S(1)} collective-permute-done((f32[2,16,1024]{2,1,0:T(8,128)S(1)}, f32[2,16,1024]{2,1,0:T(8,128)S(1)}, u32[]{:S(2)}, u32[]{:S(2)}) %collective-permute-start.9) | collective-permute-done | bytes 131104 | tf_op jit(solution)/shard_map/ppermute | solution.py:39
  59.8 3.5 %collective-permute-start.11 = (f32[2,16,1024]{2,1,0:T(8,128)S(1)}, f32[2,16,1024]{2,1,0:T(8,128)S(1)}, u32[]{:S(2)}, u32[]{:S(2)}) collective-permute-start(f32[2,16,1024]{2,1,0:T(8,128)S(1)} %pad_maximum_fusion.5), channel_id=1, source_target_pairs={{0,128},{4,132},{8,136},{12,140},{16,144},{20,148},{24,152},{28,15... | collective-permute-start | bytes 393224 | tf_op jit(solution)/shard_map/ppermute | solution.py:39
  64.2 2.3 %collective-permute-start.10 = (f32[2,16,1024]{2,1,0:T(8,128)S(1)}, f32[2,16,1024]{2,1,0:T(8,128)S(1)}, u32[]{:S(2)}, u32[]{:S(2)}) collective-permute-start(f32[2,16,1024]{2,1,0:T(8,128)S(1)} %pad_maximum_fusion.5), channel_id=1, source_target_pairs={{0,192},{4,196},{8,200},{12,204},{16,208},{20,212},{24,216},{28,22... | collective-permute-start | bytes 393224 | tf_op jit(solution)/shard_map/ppermute | solution.py:39
  67.3 2.3 %collective-permute-done.12 = f32[2,16,1024]{2,1,0:T(8,128)S(1)} collective-permute-done((f32[2,16,1024]{2,1,0:T(8,128)S(1)}, f32[2,16,1024]{2,1,0:T(8,128)S(1)}, u32[]{:S(2)}, u32[]{:S(2)}) %collective-permute-start.12) | collective-permute-done | bytes 131104 | tf_op jit(solution)/shard_map/ppermute | solution.py:39
  73.6 1.9 %fusion.87 = f32[4,32,1024]{2,1,0:T(8,128)S(1)} fusion(f32[4,32,1024]{2,1,0:T(8,128)S(1)} %multiply_reduce_fusion.1, f32[4,32,1024]{2,1,0:T(8,128)S(1)} %bitcast.386, f32[1024]{0:T(1024)S(1)} %bitcast.402, f32[1024]{0:T(1024)S(1)} %bitcast.404, f32[1024]{0:T(1024)S(1)} %bitcast.406, f32[1024]{0:T(1024)S(1)} %bitcast.408, f32[1024]{0:T(1024)S(1)} %bitcast.410, ...), kind=kLoop, calls=%fused_computation.183 | loop fusion | flops 8388608 | bytes 1703936 | tf_op jit(solution)/shard_map/add | solution.py:186
  76.6 2.0 %collective-permute-start.13 = (bf16[3,2,1024]{2,1,0:T(2,128)(2,1)S(1)}, bf16[3,2,1024]{2,1,0:T(2,128)(2,1)S(1)}, u32[]{:S(2)}, u32[]{:S(2)}) collective-permute-start(bf16[3,2,1024]{2,1,0:T(2,128)(2,1)S(1)} %slice.735), channel_id=1, source_target_pairs={{4,0},{8,4},{12,8},{16,12},{20,16},{24,20},{28,24},{32,28},{36,32}... | collective-permute-start | bytes 36872 | tf_op jit(solution)/shard_map/ppermute | solution.py:17
  83.8 1.9 %collective-permute-done.18 = f32[25,1024]{1,0:T(8,128)S(1)} collective-permute-done((f32[25,1024]{1,0:T(8,128)S(1)}, f32[25,1024]{1,0:T(8,128)S(1)}, u32[]{:S(2)}, u32[]{:S(2)}) %collective-permute-start.18) | collective-permute-done | bytes 102432 | tf_op jit(solution)/shard_map/ppermute | solution.py:39
  87.7 3.8 %collective-permute-start.21 = (f32[25,1024]{1,0:T(8,128)S(1)}, f32[25,1024]{1,0:T(8,128)S(1)}, u32[]{:S(2)}, u32[]{:S(2)}) collective-permute-start(f32[25,1024]{1,0:T(8,128)S(1)} %add_add_fusion.3), channel_id=1, source_target_pairs={{0,32},{4,36},{8,40},{12,44},{16,48},{20,52},{24,56},{28,60},{32,0... | collective-permute-start | bytes 307208 | tf_op jit(solution)/shard_map/ppermute | solution.py:39
  93.2 2.4 %collective-permute-start.20 = (f32[25,1024]{1,0:T(8,128)S(1)}, f32[25,1024]{1,0:T(8,128)S(1)}, u32[]{:S(2)}, u32[]{:S(2)}) collective-permute-start(f32[25,1024]{1,0:T(8,128)S(1)} %add_add_fusion.3), channel_id=1, source_target_pairs={{0,48},{4,52},{8,56},{12,60},{16,0},{20,4},{24,8},{28,12},{32,16},... | collective-permute-start | bytes 307208 | tf_op jit(solution)/shard_map/ppermute | solution.py:39
  95.6 3.3 %collective-permute-done.21 = f32[25,1024]{1,0:T(8,128)S(1)} collective-permute-done((f32[25,1024]{1,0:T(8,128)S(1)}, f32[25,1024]{1,0:T(8,128)S(1)}, u32[]{:S(2)}, u32[]{:S(2)}) %collective-permute-start.21) | collective-permute-done | bytes 102432 | tf_op jit(solution)/shard_map/ppermute | solution.py:39
  98.9 7.5 %collective-permute-done.22 = f32[25,1024]{1,0:T(8,128)S(1)} collective-permute-done((f32[25,1024]{1,0:T(8,128)S(1)}, f32[25,1024]{1,0:T(8,128)S(1)}, u32[]{:S(2)}, u32[]{:S(2)}) %collective-permute-start.22) | collective-permute-done | bytes 102432 | tf_op jit(solution)/shard_map/ppermute | solution.py:39
  106.5 2.1 %collective-permute-start.24 = (f32[25,1024]{1,0:T(8,128)S(1)}, f32[25,1024]{1,0:T(8,128)S(1)}, u32[]{:S(2)}, u32[]{:S(2)}) collective-permute-start(f32[25,1024]{1,0:T(8,128)S(1)} %add_add_fusion.2), channel_id=1, source_target_pairs={{0,128},{4,132},{8,136},{12,140},{16,144},{20,148},{24,152},{28,15... | collective-permute-start | bytes 307208 | tf_op jit(solution)/shard_map/ppermute | solution.py:39
  112.7 1.7 %collective-permute-done.24 = f32[25,1024]{1,0:T(8,128)S(1)} collective-permute-done((f32[25,1024]{1,0:T(8,128)S(1)}, f32[25,1024]{1,0:T(8,128)S(1)}, u32[]{:S(2)}, u32[]{:S(2)}) %collective-permute-start.24) | collective-permute-done | bytes 102432 | tf_op jit(solution)/shard_map/ppermute | solution.py:39
  114.5 1.9 %collective-permute-done.25 = f32[25,1024]{1,0:T(8,128)S(1)} collective-permute-done((f32[25,1024]{1,0:T(8,128)S(1)}, f32[25,1024]{1,0:T(8,128)S(1)}, u32[]{:S(2)}, u32[]{:S(2)}) %collective-permute-start.25) | collective-permute-done | bytes 102432 | tf_op jit(solution)/shard_map/ppermute | solution.py:39
  (123 shorter events, 36.3 us)
Async XLA Ops:
  1.7 12.2 %collective-permute-start.1 = (f32[128]{0:T(128)S(1)}, f32[128]{0:T(128)S(1)}, u32[]{:S(2)}, u32[]{:S(2)}) collective-permute-start(f32[128]{0:T(128)S(1)} %fusion.4), channel_id=1, source_target_pairs={{0,2},{1,3},{2,0},{3,1},{4,6},{5,7},{6,4},{7,5},{8,10},{9,11},{10,... | collective-permute-start | bytes 1544 | tf_op jit(solution)/shard_map/ppermute | solution.py:39
  4.8 9.1 %collective-permute-start.2 = (f32[128]{0:T(128)S(1)}, f32[128]{0:T(128)S(1)}, u32[]{:S(2)}, u32[]{:S(2)}) collective-permute-start(f32[128]{0:T(128)S(1)} %fusion.4), channel_id=1, source_target_pairs={{0,1},{1,2},{2,3},{3,0},{4,5},{5,6},{6,7},{7,4},{8,9},{9,10},{10,1... | collective-permute-start | bytes 1544 | tf_op jit(solution)/shard_map/ppermute | solution.py:39
  5.4 8.5 %collective-permute-start = (f32[128]{0:T(128)S(1)}, f32[128]{0:T(128)S(1)}, u32[]{:S(2)}, u32[]{:S(2)}) collective-permute-start(f32[128]{0:T(128)S(1)} %fusion.4), channel_id=1, source_target_pairs={{0,3},{1,0},{2,1},{3,2},{4,7},{5,4},{6,5},{7,6},{8,11},{9,8},{10,9... | collective-permute-start | bytes 1544 | tf_op jit(solution)/shard_map/ppermute | solution.py:39
  32.3 6.5 %collective-permute-start.5 = (f32[2,16,1024]{2,1,0:T(8,128)S(1)}, f32[2,16,1024]{2,1,0:T(8,128)S(1)}, u32[]{:S(2)}, u32[]{:S(2)}) collective-permute-start(f32[2,16,1024]{2,1,0:T(8,128)S(1)} %pad_maximum_fusion.3), channel_id=1, source_target_pairs={{0,8},{4,12},{8,0},{12,4},{16,24},{20,28},{24,16},{28,20},{32,40},... | collective-permute-start | bytes 393224 | tf_op jit(solution)/shard_map/ppermute | solution.py:39
  32.4 6.7 %collective-permute-start.6 = (f32[2,16,1024]{2,1,0:T(8,128)S(1)}, f32[2,16,1024]{2,1,0:T(8,128)S(1)}, u32[]{:S(2)}, u32[]{:S(2)}) collective-permute-start(f32[2,16,1024]{2,1,0:T(8,128)S(1)} %pad_maximum_fusion.3), channel_id=1, source_target_pairs={{0,4},{4,8},{8,12},{12,0},{16,20},{20,24},{24,28},{28,16},{32,36},... | collective-permute-start | bytes 393224 | tf_op jit(solution)/shard_map/ppermute | solution.py:39
  32.5 6.6 %collective-permute-start.4 = (f32[2,16,1024]{2,1,0:T(8,128)S(1)}, f32[2,16,1024]{2,1,0:T(8,128)S(1)}, u32[]{:S(2)}, u32[]{:S(2)}) collective-permute-start(f32[2,16,1024]{2,1,0:T(8,128)S(1)} %pad_maximum_fusion.3), channel_id=1, source_target_pairs={{0,12},{4,0},{8,4},{12,8},{16,28},{20,16},{24,20},{28,24},{32,44},... | collective-permute-start | bytes 393224 | tf_op jit(solution)/shard_map/ppermute | solution.py:39
  39.4 11.7 %collective-permute-start.8 = (f32[2,16,1024]{2,1,0:T(8,128)S(1)}, f32[2,16,1024]{2,1,0:T(8,128)S(1)}, u32[]{:S(2)}, u32[]{:S(2)}) collective-permute-start(f32[2,16,1024]{2,1,0:T(8,128)S(1)} %pad_maximum_fusion.4), channel_id=1, source_target_pairs={{0,32},{4,36},{8,40},{12,44},{16,48},{20,52},{24,56},{28,60},{32,0... | collective-permute-start | bytes 393224 | tf_op jit(solution)/shard_map/ppermute | solution.py:39
  46.9 12.7 %collective-permute-start.9 = (f32[2,16,1024]{2,1,0:T(8,128)S(1)}, f32[2,16,1024]{2,1,0:T(8,128)S(1)}, u32[]{:S(2)}, u32[]{:S(2)}) collective-permute-start(f32[2,16,1024]{2,1,0:T(8,128)S(1)} %pad_maximum_fusion.4), channel_id=1, source_target_pairs={{0,16},{4,20},{8,24},{12,28},{16,32},{20,36},{24,40},{28,44},{32,4... | collective-permute-start | bytes 393224 | tf_op jit(solution)/shard_map/ppermute | solution.py:39
  47.4 12.2 %collective-permute-start.7 = (f32[2,16,1024]{2,1,0:T(8,128)S(1)}, f32[2,16,1024]{2,1,0:T(8,128)S(1)}, u32[]{:S(2)}, u32[]{:S(2)}) collective-permute-start(f32[2,16,1024]{2,1,0:T(8,128)S(1)} %pad_maximum_fusion.4), channel_id=1, source_target_pairs={{0,48},{4,52},{8,56},{12,60},{16,0},{20,4},{24,8},{28,12},{32,16},... | collective-permute-start | bytes 393224 | tf_op jit(solution)/shard_map/ppermute | solution.py:39
  59.8 7.6 %collective-permute-start.11 = (f32[2,16,1024]{2,1,0:T(8,128)S(1)}, f32[2,16,1024]{2,1,0:T(8,128)S(1)}, u32[]{:S(2)}, u32[]{:S(2)}) collective-permute-start(f32[2,16,1024]{2,1,0:T(8,128)S(1)} %pad_maximum_fusion.5), channel_id=1, source_target_pairs={{0,128},{4,132},{8,136},{12,140},{16,144},{20,148},{24,152},{28,15... | collective-permute-start | bytes 393224 | tf_op jit(solution)/shard_map/ppermute | solution.py:39
  63.3 6.3 %collective-permute-start.12 = (f32[2,16,1024]{2,1,0:T(8,128)S(1)}, f32[2,16,1024]{2,1,0:T(8,128)S(1)}, u32[]{:S(2)}, u32[]{:S(2)}) collective-permute-start(f32[2,16,1024]{2,1,0:T(8,128)S(1)} %pad_maximum_fusion.5), channel_id=1, source_target_pairs={{0,64},{4,68},{8,72},{12,76},{16,80},{20,84},{24,88},{28,92},{32,9... | collective-permute-start | bytes 393224 | tf_op jit(solution)/shard_map/ppermute | solution.py:39
  64.2 5.7 %collective-permute-start.10 = (f32[2,16,1024]{2,1,0:T(8,128)S(1)}, f32[2,16,1024]{2,1,0:T(8,128)S(1)}, u32[]{:S(2)}, u32[]{:S(2)}) collective-permute-start(f32[2,16,1024]{2,1,0:T(8,128)S(1)} %pad_maximum_fusion.5), channel_id=1, source_target_pairs={{0,192},{4,196},{8,200},{12,204},{16,208},{20,212},{24,216},{28,22... | collective-permute-start | bytes 393224 | tf_op jit(solution)/shard_map/ppermute | solution.py:39
  79.3 6.4 %collective-permute-start.18 = (f32[25,1024]{1,0:T(8,128)S(1)}, f32[25,1024]{1,0:T(8,128)S(1)}, u32[]{:S(2)}, u32[]{:S(2)}) collective-permute-start(f32[25,1024]{1,0:T(8,128)S(1)} %pad_maximum_fusion.6), channel_id=1, source_target_pairs={{0,8},{4,12},{8,0},{12,4},{16,24},{20,28},{24,16},{28,20},{32,40},... | collective-permute-start | bytes 307208 | tf_op jit(solution)/shard_map/ppermute | solution.py:39
  80.0 7.7 %collective-permute-start.19 = (f32[25,1024]{1,0:T(8,128)S(1)}, f32[25,1024]{1,0:T(8,128)S(1)}, u32[]{:S(2)}, u32[]{:S(2)}) collective-permute-start(f32[25,1024]{1,0:T(8,128)S(1)} %pad_maximum_fusion.6), channel_id=1, source_target_pairs={{0,4},{4,8},{8,12},{12,0},{16,20},{20,24},{24,28},{28,16},{32,36},... | collective-permute-start | bytes 307208 | tf_op jit(solution)/shard_map/ppermute | solution.py:39
  80.8 6.8 %collective-permute-start.17 = (f32[25,1024]{1,0:T(8,128)S(1)}, f32[25,1024]{1,0:T(8,128)S(1)}, u32[]{:S(2)}, u32[]{:S(2)}) collective-permute-start(f32[25,1024]{1,0:T(8,128)S(1)} %pad_maximum_fusion.6), channel_id=1, source_target_pairs={{0,12},{4,0},{8,4},{12,8},{16,28},{20,16},{24,20},{28,24},{32,44},... | collective-permute-start | bytes 307208 | tf_op jit(solution)/shard_map/ppermute | solution.py:39
  82.4 10.7 %collective-permute-start.15 = (f32[128]{0:T(128)S(1)}, f32[128]{0:T(128)S(1)}, u32[]{:S(2)}, u32[]{:S(2)}) collective-permute-start(f32[128]{0:T(128)S(1)} %get-tuple-element.48), channel_id=1, source_target_pairs={{0,2},{1,3},{2,0},{3,1},{4,6},{5,7},{6,4},{7,5},{8,10},{9,11},{10,... | collective-permute-start | bytes 1544 | tf_op jit(solution)/shard_map/ppermute | solution.py:39
  82.7 12.9 %collective-permute-start.16 = (f32[128]{0:T(128)S(1)}, f32[128]{0:T(128)S(1)}, u32[]{:S(2)}, u32[]{:S(2)}) collective-permute-start(f32[128]{0:T(128)S(1)} %get-tuple-element.48), channel_id=1, source_target_pairs={{0,1},{1,2},{2,3},{3,0},{4,5},{5,6},{6,7},{7,4},{8,9},{9,10},{10,1... | collective-permute-start | bytes 1544 | tf_op jit(solution)/shard_map/ppermute | solution.py:39
  85.7 9.9 %collective-permute-start.14 = (f32[128]{0:T(128)S(1)}, f32[128]{0:T(128)S(1)}, u32[]{:S(2)}, u32[]{:S(2)}) collective-permute-start(f32[128]{0:T(128)S(1)} %get-tuple-element.48), channel_id=1, source_target_pairs={{0,3},{1,0},{2,1},{3,2},{4,7},{5,4},{6,5},{7,6},{8,11},{9,8},{10,9... | collective-permute-start | bytes 1544 | tf_op jit(solution)/shard_map/ppermute | solution.py:39
  87.7 11.2 %collective-permute-start.21 = (f32[25,1024]{1,0:T(8,128)S(1)}, f32[25,1024]{1,0:T(8,128)S(1)}, u32[]{:S(2)}, u32[]{:S(2)}) collective-permute-start(f32[25,1024]{1,0:T(8,128)S(1)} %add_add_fusion.3), channel_id=1, source_target_pairs={{0,32},{4,36},{8,40},{12,44},{16,48},{20,52},{24,56},{28,60},{32,0... | collective-permute-start | bytes 307208 | tf_op jit(solution)/shard_map/ppermute | solution.py:39
  91.5 15.0 %collective-permute-start.22 = (f32[25,1024]{1,0:T(8,128)S(1)}, f32[25,1024]{1,0:T(8,128)S(1)}, u32[]{:S(2)}, u32[]{:S(2)}) collective-permute-start(f32[25,1024]{1,0:T(8,128)S(1)} %add_add_fusion.3), channel_id=1, source_target_pairs={{0,16},{4,20},{8,24},{12,28},{16,32},{20,36},{24,40},{28,44},{32,4... | collective-permute-start | bytes 307208 | tf_op jit(solution)/shard_map/ppermute | solution.py:39
  93.2 13.3 %collective-permute-start.20 = (f32[25,1024]{1,0:T(8,128)S(1)}, f32[25,1024]{1,0:T(8,128)S(1)}, u32[]{:S(2)}, u32[]{:S(2)}) collective-permute-start(f32[25,1024]{1,0:T(8,128)S(1)} %add_add_fusion.3), channel_id=1, source_target_pairs={{0,48},{4,52},{8,56},{12,60},{16,0},{20,4},{24,8},{28,12},{32,16},... | collective-permute-start | bytes 307208 | tf_op jit(solution)/shard_map/ppermute | solution.py:39
  106.5 7.9 %collective-permute-start.24 = (f32[25,1024]{1,0:T(8,128)S(1)}, f32[25,1024]{1,0:T(8,128)S(1)}, u32[]{:S(2)}, u32[]{:S(2)}) collective-permute-start(f32[25,1024]{1,0:T(8,128)S(1)} %add_add_fusion.2), channel_id=1, source_target_pairs={{0,128},{4,132},{8,136},{12,140},{16,144},{20,148},{24,152},{28,15... | collective-permute-start | bytes 307208 | tf_op jit(solution)/shard_map/ppermute | solution.py:39
  108.6 7.7 %collective-permute-start.25 = (f32[25,1024]{1,0:T(8,128)S(1)}, f32[25,1024]{1,0:T(8,128)S(1)}, u32[]{:S(2)}, u32[]{:S(2)}) collective-permute-start(f32[25,1024]{1,0:T(8,128)S(1)} %add_add_fusion.2), channel_id=1, source_target_pairs={{0,64},{4,68},{8,72},{12,76},{16,80},{20,84},{24,88},{28,92},{32,9... | collective-permute-start | bytes 307208 | tf_op jit(solution)/shard_map/ppermute | solution.py:39
  110.2 6.2 %collective-permute-start.23 = (f32[25,1024]{1,0:T(8,128)S(1)}, f32[25,1024]{1,0:T(8,128)S(1)}, u32[]{:S(2)}, u32[]{:S(2)}) collective-permute-start(f32[25,1024]{1,0:T(8,128)S(1)} %add_add_fusion.2), channel_id=1, source_target_pairs={{0,192},{4,196},{8,200},{12,204},{16,208},{20,212},{24,216},{28,22... | collective-permute-start | bytes 307208 | tf_op jit(solution)/shard_map/ppermute | solution.py:39
  (15 other events, 167.0 us)

commit v4 on v3

--- a/solution.py
+++ b/solution.py
@@ -83,17 +83,14 @@
 
 def summed(value, axis):
     count = lax.axis_size(axis)
-    if not power_of_two(count):
-        return lax.psum(value, axis)
-    stride = 1
-    for radix in radices(count):
-        group, _ = members(value, axis, stride, radix)
-        if radix == 4:
-            value = (group[0] + group[1]) + (group[2] + group[3])
-        else:
-            value = group[0] + group[1]
-        stride *= radix
-    return value
+    flat = value.reshape(-1)
+    width = -(-flat.size // count)
+    width = -(-width // 128) * 128
+    flat = jnp.pad(flat, (0, count * width - flat.size)).reshape(count, width)
+    pieces = lax.all_to_all(flat, axis, 0, 0)
+    own = jnp.sum(pieces, axis=0)
+    whole = lax.all_to_all(jnp.broadcast_to(own[None], (count, width)), axis, 0, 0)
+    return whole.reshape(-1)[: value.size].reshape(value.shape)
 
 
 def per_device(stream, norm_gain, short_filters, mode_rates, residues, grad_out):

time: 119 us -> 147 us (1.24)
  waiting for transfers between devices: 36.6 us -> 52.2 us
  starting transfers between devices: 47.9 us -> 54.4 us
  local copies, waits for them, and re-layouts: 3.43 us -> 7.82 us
    all_to_all x0 -> x6, waiting for transfers between devices: none -> 33.2 us  [the longest x3 18.8 us: summed(): lax.all_to_all(jnp.broadcast_to(own[None], (count, width)), axis, 0, 0)]
    all_to_all x0 -> x6, starting transfers between devices: none -> 30.1 us  [the longest x3 16.9 us: summed(): pieces = lax.all_to_all(flat, axis, 0, 0)]
    ppermute x24 -> x9, starting transfers between devices: 44 us -> 19.9 us  [members(): received.append(lax.ppermute(value, axis, pairs))]
    ppermute x24 -> x9, waiting for transfers between devices: 33.8 us -> 15.7 us  [members(): received.append(lax.ppermute(value, axis, pairs))]
    broadcast_in_dim x0 -> x3, local copies, waits for them, and re-layouts: none -> 1.87 us  [summed(): jnp.broadcast_to(own[None], (count, width))]
    pad x0 -> x3, local copies, waits for them, and re-layouts: none -> 1.84 us  [summed(): flat = jnp.pad(flat, (0, count * width - flat.size)).reshape(count, width)]
  transfers between devices with their start and end apart: 26 -> 17, of which waited for: 14 -> 12; matrix products, arithmetic and copies ran while one was open for 8% -> 7% of each run, Pallas kernels for 0% -> 0%
where the time goes in v4:
time: 147 us; the launch traced here: 145 us
  starting transfers between devices  54.4 us (37%)
  waiting for transfers between devices  52.2 us (36%)
  other arithmetic  28.6 us (19%)
  local copies, waits for them, and re-layouts  7.82 us (5%)
    ppermute x9, starting transfers between devices, members(): received.append(lax.ppermute(value, axis, pairs))  19.9 us
    all_to_all x3, waiting for transfers between devices, summed(): lax.all_to_all(jnp.broadcast_to(own[None], (count, width)), axis, 0, 0)  18.8 us
    all_to_all x3, starting transfers between devices, summed(): pieces = lax.all_to_all(flat, axis, 0, 0)  16.9 us
    ppermute x9, waiting for transfers between devices, members(): received.append(lax.ppermute(value, axis, pairs))  15.7 us
    all_to_all x3, waiting for transfers between devices, summed(): pieces = lax.all_to_all(flat, axis, 0, 0)  14.4 us
    all_to_all x3, starting transfers between devices, summed(): lax.all_to_all(jnp.broadcast_to(own[None], (count, width)), axis, 0, 0)  13.2 us
    reduce_sum x1, other arithmetic, per_device(): weighted = jnp.sum(shifted[None] * grad_blocks[:, None], axis=2)  5.26 us
    ppermute x2, starting transfers between devices, passed_along(): lax.ppermute(value, axis, [(source, source + steps) for source in range(f...  4.33 us
  transfers between devices with their start and end apart: 17, of which 12 were waited for; matrix products, arithmetic and copies ran while one was open for 7% of the time, Pallas kernels for 0%

profile of v4, /device:TPU:32, one launch (start us, length us, event | category | flops | bytes accessed | tf_op | source)
XLA Modules:
  0.0 144.5 jit_solution(6867965532039100237)
XLA Ops:
  2.3 4.3 %all-to-all-start = ((f32[4,1,128]{2,1,0:T(1,128)}), f32[4,1,128]{2,1,0:T(1,128)S(1)}, u32[]{:S(2)}, u32[]{:S(2)}) async-start(f32[4,1,128]{2,1,0:T(1,128)} %bitcast.7), calls=%async_computation | async-start | bytes 4096 | tf_op jit(solution)/shard_map/all_to_all | solution.py:90
  13.1 4.8 %all-to-all-start.1 = ((f32[4,1,128]{2,1,0:T(1,128)}), f32[4,1,128]{2,1,0:T(1,128)S(1)}, u32[]{:S(2)}, u32[]{:S(2)}) async-start(f32[4,1,128]{2,1,0:T(1,128)} %broadcast_in_dim.6), calls=%async_computation.1 | async-start | bytes 4096 | tf_op jit(solution)/shard_map/all_to_all | solution.py:92
  17.9 5.2 %all-to-all-done.1 = f32[4,1,128]{2,1,0:T(1,128)S(1)} async-done(((f32[4,1,128]{2,1,0:T(1,128)}), f32[4,1,128]{2,1,0:T(1,128)S(1)}, u32[]{:S(2)}, u32[]{:S(2)}) %all-to-all-start.1) | async-done | bytes 2080 | tf_op jit(solution)/shard_map/all_to_all | solution.py:92
  24.2 1.9 %collective-permute-start = (bf16[2,1024]{1,0:T(2,128)(2,1)S(1)}, bf16[2,1024]{1,0:T(2,128)(2,1)S(1)}, u32[]{:S(2)}, u32[]{:S(2)}) collective-permute-start(bf16[2,1024]{1,0:T(2,128)(2,1)S(1)} %slice.699), channel_id=1, source_target_pairs={{0,4},{4,8},{8,12},{12,16},{16,20},{20,24},{24,28},{28,32},{32,36}... | collective-permute-start | bytes 12296 | tf_op jit(solution)/shard_map/ppermute | solution.py:17
  26.4 2.7 %collective-permute-done = bf16[2,1024]{1,0:T(2,128)(2,1)S(1)} collective-permute-done((bf16[2,1024]{1,0:T(2,128)(2,1)S(1)}, bf16[2,1024]{1,0:T(2,128)(2,1)S(1)}, u32[]{:S(2)}, u32[]{:S(2)}) %collective-permute-start) | collective-permute-done | bytes 4128 | tf_op jit(solution)/shard_map/ppermute | solution.py:17
  33.7 2.2 %multiply_reduce_fusion.5 = (f32[16,1024]{1,0:T(8,128)S(1)}, f32[32,1024]{1,0:T(8,128)S(1)}, f32[16,32,1024]{2,1,0:T(8,128)S(1)}, f32[16,32,1024]{2,1,0:T(8,128)...) fusion(f32[32,1024]{1,0:T(8,128)S(1)} %stack.195, ...), kind=kLoop, calls=%fused_computation.75 | loop fusion | flops 5193728 | bytes 10945024 | tf_op jit(solution)/shard_map/reduce_sum | solution.py:198
  35.9 5.3 %multiply_reduce_fusion = (f32[4,16,1024]{2,1,0:T(8,128)S(1)}, f32[4,16,1024]{2,1,0:T(8,128)S(1)}, f32[4,16,1024]{2,1,0:T(8,128)S(1)}) fusion(f32[16,32,1024]{2,1,0:T(8,128)S(1)} %get-tuple-element.110, f32[4,32,1024]{2,1,0:T(8,128)S(1)} %bitcast.400, f32[16,32,1024]{2,1,0:T(8,128)S(1)} %get-tuple-element.109, f32[4,32,1024]{2,1,0:T(8,128)S(1)} %bitcast_convert_fusion.1, ...), kind=kLoop, calls=%fused_computation | loop fusion | flops 12386304 | bytes 8126464 | tf_op jit(solution)/shard_map/reduce_sum | solution.py:187
  43.6 4.3 %collective-permute-done.2 = f32[2,16,1024]{2,1,0:T(8,128)S(1)} collective-permute-done((f32[2,16,1024]{2,1,0:T(8,128)S(1)}, f32[2,16,1024]{2,1,0:T(8,128)S(1)}, u32[]{:S(2)}, u32[]{:S(2)}) %collective-permute-start.2) | collective-permute-done | bytes 131104 | tf_op jit(solution)/shard_map/ppermute | solution.py:39
  48.5 7.3 %collective-permute-start.5 = (f32[2,16,1024]{2,1,0:T(8,128)S(1)}, f32[2,16,1024]{2,1,0:T(8,128)S(1)}, u32[]{:S(2)}, u32[]{:S(2)}) collective-permute-start(f32[2,16,1024]{2,1,0:T(8,128)S(1)} %pad_maximum_fusion.4), channel_id=1, source_target_pairs={{0,32},{4,36},{8,40},{12,44},{16,48},{20,52},{24,56},{28,60},{32,0... | collective-permute-start | bytes 393224 | tf_op jit(solution)/shard_map/ppermute | solution.py:39
  56.3 3.7 %collective-permute-start.4 = (f32[2,16,1024]{2,1,0:T(8,128)S(1)}, f32[2,16,1024]{2,1,0:T(8,128)S(1)}, u32[]{:S(2)}, u32[]{:S(2)}) collective-permute-start(f32[2,16,1024]{2,1,0:T(8,128)S(1)} %pad_maximum_fusion.4), channel_id=1, source_target_pairs={{0,48},{4,52},{8,56},{12,60},{16,0},{20,4},{24,8},{28,12},{32,16},... | collective-permute-start | bytes 393224 | tf_op jit(solution)/shard_map/ppermute | solution.py:39
  60.0 8.5 %collective-permute-done.6 = f32[2,16,1024]{2,1,0:T(8,128)S(1)} collective-permute-done((f32[2,16,1024]{2,1,0:T(8,128)S(1)}, f32[2,16,1024]{2,1,0:T(8,128)S(1)}, u32[]{:S(2)}, u32[]{:S(2)}) %collective-permute-start.6) | collective-permute-done | bytes 131104 | tf_op jit(solution)/shard_map/ppermute | solution.py:39
  68.7 3.3 %collective-permute-start.8 = (f32[2,16,1024]{2,1,0:T(8,128)S(1)}, f32[2,16,1024]{2,1,0:T(8,128)S(1)}, u32[]{:S(2)}, u32[]{:S(2)}) collective-permute-start(f32[2,16,1024]{2,1,0:T(8,128)S(1)} %pad_maximum_fusion.5), channel_id=1, source_target_pairs={{0,128},{4,132},{8,136},{12,140},{16,144},{20,148},{24,152},{28,15... | collective-permute-start | bytes 393224 | tf_op jit(solution)/shard_map/ppermute | solution.py:39
  72.7 2.6 %collective-permute-start.7 = (f32[2,16,1024]{2,1,0:T(8,128)S(1)}, f32[2,16,1024]{2,1,0:T(8,128)S(1)}, u32[]{:S(2)}, u32[]{:S(2)}) collective-permute-start(f32[2,16,1024]{2,1,0:T(8,128)S(1)} %pad_maximum_fusion.5), channel_id=1, source_target_pairs={{0,192},{4,196},{8,200},{12,204},{16,208},{20,212},{24,216},{28,22... | collective-permute-start | bytes 393224 | tf_op jit(solution)/shard_map/ppermute | solution.py:39
  76.3 2.2 %collective-permute-done.9 = f32[2,16,1024]{2,1,0:T(8,128)S(1)} collective-permute-done((f32[2,16,1024]{2,1,0:T(8,128)S(1)}, f32[2,16,1024]{2,1,0:T(8,128)S(1)}, u32[]{:S(2)}, u32[]{:S(2)}) %collective-permute-start.9) | collective-permute-done | bytes 131104 | tf_op jit(solution)/shard_map/ppermute | solution.py:39
  82.1 1.9 %fusion.87 = f32[4,32,1024]{2,1,0:T(8,128)S(1)} fusion(f32[4,32,1024]{2,1,0:T(8,128)S(1)} %multiply_reduce_fusion.1, f32[4,32,1024]{2,1,0:T(8,128)S(1)} %bitcast.401, f32[1024]{0:T(1024)S(1)} %bitcast.417, f32[1024]{0:T(1024)S(1)} %bitcast.419, f32[1024]{0:T(1024)S(1)} %bitcast.421, f32[1024]{0:T(1024)S(1)} %bitcast.423, f32[1024]{0:T(1024)S(1)} %bitcast.425, ...), kind=kLoop, calls=%fused_computation.183 | loop fusion | flops 8388608 | bytes 1703936 | tf_op jit(solution)/shard_map/add | solution.py:183
  85.1 2.4 %collective-permute-start.10 = (bf16[3,2,1024]{2,1,0:T(2,128)(2,1)S(1)}, bf16[3,2,1024]{2,1,0:T(2,128)(2,1)S(1)}, u32[]{:S(2)}, u32[]{:S(2)}) collective-permute-start(bf16[3,2,1024]{2,1,0:T(2,128)(2,1)S(1)} %slice.760), channel_id=1, source_target_pairs={{4,0},{8,4},{12,8},{16,12},{20,16},{24,20},{28,24},{32,28},{36,32}... | collective-permute-start | bytes 36872 | tf_op jit(solution)/shard_map/ppermute | solution.py:17
  90.2 3.2 %all-to-all-start.2 = ((f32[4,1,128]{2,1,0:T(1,128)}), f32[4,1,128]{2,1,0:T(1,128)S(1)}, u32[]{:S(2)}, u32[]{:S(2)}) async-start(f32[4,1,128]{2,1,0:T(1,128)} %bitcast.96), calls=%async_computation.2 | async-start | bytes 4096 | tf_op jit(solution)/shard_map/all_to_all | solution.py:90
  94.1 4.4 %all-to-all-done.2 = f32[4,1,128]{2,1,0:T(1,128)S(1)} async-done(((f32[4,1,128]{2,1,0:T(1,128)}), f32[4,1,128]{2,1,0:T(1,128)S(1)}, u32[]{:S(2)}, u32[]{:S(2)}) %all-to-all-start.2) | async-done | bytes 2080 | tf_op jit(solution)/shard_map/all_to_all | solution.py:90
  98.6 9.4 %all-to-all-start.4 = ((f32[64,1,512]{2,1,0:T(1,128)}), f32[64,1,512]{2,1,0:T(1,128)S(1)}, u32[]{:S(2)}, u32[]{:S(2)}) async-start(f32[64,1,512]{2,1,0:T(1,128)} %bitcast.134), calls=%async_computation.4 | async-start | bytes 262144 | tf_op jit(solution)/shard_map/all_to_all | solution.py:90
  108.0 10.0 %all-to-all-done.4 = f32[64,1,512]{2,1,0:T(1,128)S(1)} async-done(((f32[64,1,512]{2,1,0:T(1,128)}), f32[64,1,512]{2,1,0:T(1,128)S(1)}, u32[]{:S(2)}, u32[]{:S(2)}) %all-to-all-start.4) | async-done | bytes 131104 | tf_op jit(solution)/shard_map/all_to_all | solution.py:90
  118.6 3.2 %all-to-all-start.3 = ((f32[4,1,128]{2,1,0:T(1,128)}), f32[4,1,128]{2,1,0:T(1,128)S(1)}, u32[]{:S(2)}, u32[]{:S(2)}) async-start(f32[4,1,128]{2,1,0:T(1,128)} %broadcast_in_dim.7), calls=%async_computation.3 | async-start | bytes 4096 | tf_op jit(solution)/shard_map/all_to_all | solution.py:92
  121.9 5.0 %all-to-all-done.3 = f32[4,1,128]{2,1,0:T(1,128)S(1)} async-done(((f32[4,1,128]{2,1,0:T(1,128)}), f32[4,1,128]{2,1,0:T(1,128)S(1)}, u32[]{:S(2)}, u32[]{:S(2)}) %all-to-all-start.3) | async-done | bytes 2080 | tf_op jit(solution)/shard_map/all_to_all | solution.py:92
  127.7 5.2 %all-to-all-start.5 = ((f32[64,1,512]{2,1,0:T(1,128)}), f32[64,1,512]{2,1,0:T(1,128)S(1)}, u32[]{:S(2)}, u32[]{:S(2)}) async-start(f32[64,1,512]{2,1,0:T(1,128)} %broadcast_in_dim.8), calls=%async_computation.5 | async-start | bytes 262144 | tf_op jit(solution)/shard_map/all_to_all | solution.py:92
  134.4 8.5 %all-to-all-done.5 = f32[64,1,512]{2,1,0:T(1,128)S(1)} async-done(((f32[64,1,512]{2,1,0:T(1,128)}), f32[64,1,512]{2,1,0:T(1,128)S(1)}, u32[]{:S(2)}, u32[]{:S(2)}) %all-to-all-start.5) | async-done | bytes 131104 | tf_op jit(solution)/shard_map/all_to_all | solution.py:92
  (115 shorter events, 31.5 us)
Async XLA Ops:
  2.3 10.2 %all-to-all-start = ((f32[4,1,128]{2,1,0:T(1,128)}), f32[4,1,128]{2,1,0:T(1,128)S(1)}, u32[]{:S(2)}, u32[]{:S(2)}) async-start(f32[4,1,128]{2,1,0:T(1,128)} %bitcast.7), calls=%async_computation | async-start | bytes 4096 | tf_op jit(solution)/shard_map/all_to_all | solution.py:90
  13.1 10.0 %all-to-all-start.1 = ((f32[4,1,128]{2,1,0:T(1,128)}), f32[4,1,128]{2,1,0:T(1,128)S(1)}, u32[]{:S(2)}, u32[]{:S(2)}) async-start(f32[4,1,128]{2,1,0:T(1,128)} %broadcast_in_dim.6), calls=%async_computation.1 | async-start | bytes 4096 | tf_op jit(solution)/shard_map/all_to_all | solution.py:92
  24.2 4.9 %collective-permute-start = (bf16[2,1024]{1,0:T(2,128)(2,1)S(1)}, bf16[2,1024]{1,0:T(2,128)(2,1)S(1)}, u32[]{:S(2)}, u32[]{:S(2)}) collective-permute-start(bf16[2,1024]{1,0:T(2,128)(2,1)S(1)} %slice.699), channel_id=1, source_target_pairs={{0,4},{4,8},{8,12},{12,16},{16,20},{20,24},{24,28},{28,32},{32,36}... | collective-permute-start | bytes 12296 | tf_op jit(solution)/shard_map/ppermute | solution.py:17
  35.9 5.3 %copy-start.12 = (f32[4]{0:T(128)S(1)}, f32[4]{0:T(128)}, u32[]{:S(2)}) copy-start(f32[4]{0:T(128)} %get-tuple-element.127) | copy-start | bytes 52
  41.4 7.0 %copy-start.1 = (f32[16,1024]{1,0:T(8,128)S(1)}, f32[16,1024]{1,0:T(8,128)}, u32[]{:S(2)}) copy-start(f32[16,1024]{1,0:T(8,128)} %param.9) | copy-start | bytes 196612
  41.4 6.5 %collective-permute-start.2 = (f32[2,16,1024]{2,1,0:T(8,128)S(1)}, f32[2,16,1024]{2,1,0:T(8,128)S(1)}, u32[]{:S(2)}, u32[]{:S(2)}) collective-permute-start(f32[2,16,1024]{2,1,0:T(8,128)S(1)} %pad_maximum_fusion.3), channel_id=1, source_target_pairs={{0,8},{4,12},{8,0},{12,4},{16,24},{20,28},{24,16},{28,20},{32,40},... | collective-permute-start | bytes 393224 | tf_op jit(solution)/shard_map/ppermute | solution.py:39
  41.5 6.7 %collective-permute-start.3 = (f32[2,16,1024]{2,1,0:T(8,128)S(1)}, f32[2,16,1024]{2,1,0:T(8,128)S(1)}, u32[]{:S(2)}, u32[]{:S(2)}) collective-permute-start(f32[2,16,1024]{2,1,0:T(8,128)S(1)} %pad_maximum_fusion.3), channel_id=1, source_target_pairs={{0,4},{4,8},{8,12},{12,0},{16,20},{20,24},{24,28},{28,16},{32,36},... | collective-permute-start | bytes 393224 | tf_op jit(solution)/shard_map/ppermute | solution.py:39
  41.6 6.7 %collective-permute-start.1 = (f32[2,16,1024]{2,1,0:T(8,128)S(1)}, f32[2,16,1024]{2,1,0:T(8,128)S(1)}, u32[]{:S(2)}, u32[]{:S(2)}) collective-permute-start(f32[2,16,1024]{2,1,0:T(8,128)S(1)} %pad_maximum_fusion.3), channel_id=1, source_target_pairs={{0,12},{4,0},{8,4},{12,8},{16,28},{20,16},{24,20},{28,24},{32,44},... | collective-permute-start | bytes 393224 | tf_op jit(solution)/shard_map/ppermute | solution.py:39
  48.3 26.9 %copy-start.5 = (f32[4,4]{1,0:T(4,128)S(1)}, f32[4,4]{1,0:T(4,128)}, u32[]{:S(2)}) copy-start(f32[4,4]{1,0:T(4,128)} %get-tuple-element.124) | copy-start | bytes 196
  48.3 26.9 %copy-start.6 = (f32[4,4]{1,0:T(4,128)S(1)}, f32[4,4]{1,0:T(4,128)}, u32[]{:S(2)}) copy-start(f32[4,4]{1,0:T(4,128)} %get-tuple-element.125) | copy-start | bytes 196
  48.3 26.9 %copy-start.7 = (f32[4,4]{1,0:T(4,128)S(1)}, f32[4,4]{1,0:T(4,128)}, u32[]{:S(2)}) copy-start(f32[4,4]{1,0:T(4,128)} %get-tuple-element.122) | copy-start | bytes 196
  48.3 26.9 %copy-start.8 = (f32[4,4]{1,0:T(4,128)S(1)}, f32[4,4]{1,0:T(4,128)}, u32[]{:S(2)}) copy-start(f32[4,4]{1,0:T(4,128)} %get-tuple-element.123) | copy-start | bytes 196
  48.5 11.5 %collective-permute-start.5 = (f32[2,16,1024]{2,1,0:T(8,128)S(1)}, f32[2,16,1024]{2,1,0:T(8,128)S(1)}, u32[]{:S(2)}, u32[]{:S(2)}) collective-permute-start(f32[2,16,1024]{2,1,0:T(8,128)S(1)} %pad_maximum_fusion.4), channel_id=1, source_target_pairs={{0,32},{4,36},{8,40},{12,44},{16,48},{20,52},{24,56},{28,60},{32,0... | collective-permute-start | bytes 393224 | tf_op jit(solution)/shard_map/ppermute | solution.py:39
  55.8 12.7 %collective-permute-start.6 = (f32[2,16,1024]{2,1,0:T(8,128)S(1)}, f32[2,16,1024]{2,1,0:T(8,128)S(1)}, u32[]{:S(2)}, u32[]{:S(2)}) collective-permute-start(f32[2,16,1024]{2,1,0:T(8,128)S(1)} %pad_maximum_fusion.4), channel_id=1, source_target_pairs={{0,16},{4,20},{8,24},{12,28},{16,32},{20,36},{24,40},{28,44},{32,4... | collective-permute-start | bytes 393224 | tf_op jit(solution)/shard_map/ppermute | solution.py:39
  56.3 12.2 %collective-permute-start.4 = (f32[2,16,1024]{2,1,0:T(8,128)S(1)}, f32[2,16,1024]{2,1,0:T(8,128)S(1)}, u32[]{:S(2)}, u32[]{:S(2)}) collective-permute-start(f32[2,16,1024]{2,1,0:T(8,128)S(1)} %pad_maximum_fusion.4), channel_id=1, source_target_pairs={{0,48},{4,52},{8,56},{12,60},{16,0},{20,4},{24,8},{28,12},{32,16},... | collective-permute-start | bytes 393224 | tf_op jit(solution)/shard_map/ppermute | solution.py:39
  68.7 7.6 %collective-permute-start.8 = (f32[2,16,1024]{2,1,0:T(8,128)S(1)}, f32[2,16,1024]{2,1,0:T(8,128)S(1)}, u32[]{:S(2)}, u32[]{:S(2)}) collective-permute-start(f32[2,16,1024]{2,1,0:T(8,128)S(1)} %pad_maximum_fusion.5), channel_id=1, source_target_pairs={{0,128},{4,132},{8,136},{12,140},{16,144},{20,148},{24,152},{28,15... | collective-permute-start | bytes 393224 | tf_op jit(solution)/shard_map/ppermute | solution.py:39
  72.0 6.5 %collective-permute-start.9 = (f32[2,16,1024]{2,1,0:T(8,128)S(1)}, f32[2,16,1024]{2,1,0:T(8,128)S(1)}, u32[]{:S(2)}, u32[]{:S(2)}) collective-permute-start(f32[2,16,1024]{2,1,0:T(8,128)S(1)} %pad_maximum_fusion.5), channel_id=1, source_target_pairs={{0,64},{4,68},{8,72},{12,76},{16,80},{20,84},{24,88},{28,92},{32,9... | collective-permute-start | bytes 393224 | tf_op jit(solution)/shard_map/ppermute | solution.py:39
  72.7 5.8 %collective-permute-start.7 = (f32[2,16,1024]{2,1,0:T(8,128)S(1)}, f32[2,16,1024]{2,1,0:T(8,128)S(1)}, u32[]{:S(2)}, u32[]{:S(2)}) collective-permute-start(f32[2,16,1024]{2,1,0:T(8,128)S(1)} %pad_maximum_fusion.5), channel_id=1, source_target_pairs={{0,192},{4,196},{8,200},{12,204},{16,208},{20,212},{24,216},{28,22... | collective-permute-start | bytes 393224 | tf_op jit(solution)/shard_map/ppermute | solution.py:39
  85.1 3.8 %collective-permute-start.10 = (bf16[3,2,1024]{2,1,0:T(2,128)(2,1)S(1)}, bf16[3,2,1024]{2,1,0:T(2,128)(2,1)S(1)}, u32[]{:S(2)}, u32[]{:S(2)}) collective-permute-start(bf16[3,2,1024]{2,1,0:T(2,128)(2,1)S(1)} %slice.760), channel_id=1, source_target_pairs={{4,0},{8,4},{12,8},{16,12},{20,16},{24,20},{28,24},{32,28},{36,32}... | collective-permute-start | bytes 36872 | tf_op jit(solution)/shard_map/ppermute | solution.py:17
  88.9 44.6 %copy-start.10 = (f32[128]{0:T(128)S(1)}, f32[128]{0:T(128)}, u32[]{:S(2)}) copy-start(f32[128]{0:T(128)} %copy-done.9) | copy-start | bytes 1540
  90.2 8.4 %all-to-all-start.2 = ((f32[4,1,128]{2,1,0:T(1,128)}), f32[4,1,128]{2,1,0:T(1,128)S(1)}, u32[]{:S(2)}, u32[]{:S(2)}) async-start(f32[4,1,128]{2,1,0:T(1,128)} %bitcast.96), calls=%async_computation.2 | async-start | bytes 4096 | tf_op jit(solution)/shard_map/all_to_all | solution.py:90
  98.6 19.4 %all-to-all-start.4 = ((f32[64,1,512]{2,1,0:T(1,128)}), f32[64,1,512]{2,1,0:T(1,128)S(1)}, u32[]{:S(2)}, u32[]{:S(2)}) async-start(f32[64,1,512]{2,1,0:T(1,128)} %bitcast.134), calls=%async_computation.4 | async-start | bytes 262144 | tf_op jit(solution)/shard_map/all_to_all | solution.py:90
  118.6 8.4 %all-to-all-start.3 = ((f32[4,1,128]{2,1,0:T(1,128)}), f32[4,1,128]{2,1,0:T(1,128)S(1)}, u32[]{:S(2)}, u32[]{:S(2)}) async-start(f32[4,1,128]{2,1,0:T(1,128)} %broadcast_in_dim.7), calls=%async_computation.3 | async-start | bytes 4096 | tf_op jit(solution)/shard_map/all_to_all | solution.py:92
  127.7 15.2 %all-to-all-start.5 = ((f32[64,1,512]{2,1,0:T(1,128)}), f32[64,1,512]{2,1,0:T(1,128)S(1)}, u32[]{:S(2)}, u32[]{:S(2)}) async-start(f32[64,1,512]{2,1,0:T(1,128)} %broadcast_in_dim.8), calls=%async_computation.5 | async-start | bytes 262144 | tf_op jit(solution)/shard_map/all_to_all | solution.py:92
  (7 other events, 22.0 us)

commit v5 on v3

--- a/solution.py
+++ b/solution.py
@@ -102,11 +102,14 @@
     total_chans = chan_count * lax.axis_size("ch")
     total_rows = row_count * lax.axis_size("ctx")
     stream_wide = stream.astype(jnp.float32)
-    squares = summed(jnp.sum(stream_wide * stream_wide, axis=1), "ch")
-    row_scale = lax.rsqrt(squares / total_chans + EPSILON)
-    normed = (stream_wide * row_scale[:, None] * norm_gain[None, :]).astype(jnp.bfloat16)
-    rim_rows = passed_along(normed[row_count - (KS - 1) :], "ctx", 1)
-    padded_half = jnp.concatenate([rim_rows, lax.optimization_barrier(normed)], 0)
+    rim_rows = passed_along(stream[row_count - (KS - 1) :], "ctx", 1)
+    with_rim = jnp.concatenate([rim_rows, stream], 0).astype(jnp.float32)
+    squares = summed(jnp.sum(with_rim * with_rim, axis=1), "ch")
+    scale_with_rim = lax.rsqrt(squares / total_chans + EPSILON)
+    row_scale = scale_with_rim[KS - 1 :]
+    padded_half = lax.optimization_barrier(
+        (with_rim * scale_with_rim[:, None] * norm_gain[None, :]).astype(jnp.bfloat16)
+    )
     padded = padded_half.astype(jnp.float32)
     branches = [
         sum(
@@ -187,7 +190,7 @@
     grad_key = (grad_product * value_part).astype(jnp.bfloat16)
     grad_value = (grad_product * key_part).astype(jnp.bfloat16)
 
-    weighted = jnp.sum(shifted[None] * grad_blocks[:, None], axis=2)
+    weighted = jnp.exp(-mode_rates)[None] * block_heads
     cross_part = jnp.sum(weighted * starts, axis=0)
     by_lag = jnp.stack(
         [

time: 119 us -> 119 us (level)
  waiting for transfers between devices: 36.6 us -> 32.6 us
  local copies, waits for them, and re-layouts: 3.43 us -> 5.95 us
  starting transfers between devices: 47.9 us -> 50.2 us
  other arithmetic: 28.5 us -> 26.5 us
    reduce_sum x4 -> x3, other arithmetic: 9.13 us -> 3.38 us  [the longest x1 1.13 us: per_device(): squares = summed(jnp.sum(with_rim * with_rim, axis=1), 'ch')]
    mul x0 -> x2, other arithmetic: none -> 2.78 us  [the longest x1 2.23 us: per_device(): jnp.exp(-mode_rates[:, None, :] * (P_SIZE - steps)[None, :, None])]
    ppermute x2, waiting for transfers between devices: 2.76 us -> 0.01 us  [passed_along(): lax.ppermute(value, axis, [(source, source + steps) for source in range(f...]
    ppermute x24, starting transfers between devices: 44 us -> 46.2 us  [members(): received.append(lax.ppermute(value, axis, pairs))]
    ppermute x24, waiting for transfers between devices: 33.8 us -> 32.6 us  [members(): received.append(lax.ppermute(value, axis, pairs))]
  transfers between devices with their start and end apart: 26 -> 26, of which waited for: 14 -> 12; matrix products, arithmetic and copies ran while one was open for 8% -> 8% of each run, Pallas kernels for 0% -> 0%
where the time goes in v5:
time: 119 us; the launch traced here: 117 us
  starting transfers between devices  50.2 us (42%)
  waiting for transfers between devices  32.6 us (27%)
  other arithmetic  26.5 us (22%)
  local copies, waits for them, and re-layouts  5.95 us (5%)
  between operations  1.42 us (1%)
    ppermute x24, starting transfers between devices, members(): received.append(lax.ppermute(value, axis, pairs))  46.2 us
    ppermute x24, waiting for transfers between devices, members(): received.append(lax.ppermute(value, axis, pairs))  32.6 us
    ppermute x2, starting transfers between devices, passed_along(): lax.ppermute(value, axis, [(source, source + steps) for source in range(f...  4.07 us
    reduce_sum x3, other arithmetic, per_device(): jnp.sum(blocks_padded[:, P_SIZE - 1 - lag:2 * P_SIZE - 1 - lag] * grad_bl...  2.5 us
  transfers between devices with their start and end apart: 26, of which 12 were waited for; matrix products, arithmetic and copies ran while one was open for 8% of the time, Pallas kernels for 0%

profile of v5, /device:TPU:32, one launch (start us, length us, event | category | flops | bytes accessed | tf_op | source)
XLA Modules:
  0.0 116.7 jit_solution(16325340630670450191)
XLA Ops:
  1.4 1.9 %collective-permute-start = (bf16[2,1024]{1,0:T(2,128)(2,1)S(1)}, bf16[2,1024]{1,0:T(2,128)(2,1)S(1)}, u32[]{:S(2)}, u32[]{:S(2)}) collective-permute-start(bf16[2,1024]{1,0:T(2,128)(2,1)S(1)} %slice.536), channel_id=1, source_target_pairs={{0,4},{4,8},{8,12},{12,16},{16,20},{20,24},{24,28},{28,32},{32,36}... | collective-permute-start | bytes 12296 | tf_op jit(solution)/shard_map/ppermute | solution.py:17
  11.1 3.1 %collective-permute-start.2 = (f32[130]{0:T(256)S(1)}, f32[130]{0:T(256)S(1)}, u32[]{:S(2)}, u32[]{:S(2)}) collective-permute-start(f32[130]{0:T(256)S(1)} %fusion.3), channel_id=1, source_target_pairs={{0,2},{1,3},{2,0},{3,1},{4,6},{5,7},{6,4},{7,5},{8,10},{9,11},{10,... | collective-permute-start | bytes 1568 | tf_op jit(solution)/shard_map/ppermute | solution.py:39
  14.8 2.6 %collective-permute-start.1 = (f32[130]{0:T(256)S(1)}, f32[130]{0:T(256)S(1)}, u32[]{:S(2)}, u32[]{:S(2)}) collective-permute-start(f32[130]{0:T(256)S(1)} %fusion.3), channel_id=1, source_target_pairs={{0,3},{1,0},{2,1},{3,2},{4,7},{5,4},{6,5},{7,6},{8,11},{9,8},{10,9... | collective-permute-start | bytes 1568 | tf_op jit(solution)/shard_map/ppermute | solution.py:39
  24.1 2.3 %stack.195 = f32[32,1024]{1,0:T(8,128)S(1)} concatenate(f32[1,1024]{1,0:T(1,128)S(1)} %bitcast.501, f32[1,1024]{1,0:T(1,128)} %bitcast.514, f32[1,1024]{1,0:T(1,128)S(1)} %bitcast.484, f32[1,1024]{1,0:T(1,128)S(1)} %bitcast.485, f32[1,1024]{1,0:T(1,128)S(1)} %bitcast.486, f32[1,1024]{1,0:T(1,128)S(1)} %bitcast.487, f32[1,1024]{1,0:T(1,128)S(1)} %bitcast.488, ...), dimensions={0} | concatenate | bytes 262144 | tf_op jit(solution)/shard_map/stack | solution.py:195
  26.5 2.2 %exponential_multiply_fusion = (f32[16,32,1024]{2,1,0:T(8,128)S(1)}, f32[16,32,1024]{2,1,0:T(8,128)S(1)}, f32[32,1024]{1,0:T(8,128)S(1)}, f32[16,1024]{1,0:T(8,1...) fusion(f32[32]{0:T(128)} %broadcast_subtract_fusion, f32[16,1024]{1,0:T(8,128)S(1)} %neg.5, ...), kind=kLoop, calls=%fused_computation.75 | loop fusion | flops 5193728 | bytes 8847872 | tf_op jit(solution)/shard_map/mul | solution.py:138
  33.5 4.1 %collective-permute-done.5 = f32[2,16,1024]{2,1,0:T(8,128)S(1)} collective-permute-done((f32[2,16,1024]{2,1,0:T(8,128)S(1)}, f32[2,16,1024]{2,1,0:T(8,128)S(1)}, u32[]{:S(2)}, u32[]{:S(2)}) %collective-permute-start.5) | collective-permute-done | bytes 131104 | tf_op jit(solution)/shard_map/ppermute | solution.py:39
  37.6 2.2 %collective-permute-done.6 = f32[2,16,1024]{2,1,0:T(8,128)S(1)} collective-permute-done((f32[2,16,1024]{2,1,0:T(8,128)S(1)}, f32[2,16,1024]{2,1,0:T(8,128)S(1)}, u32[]{:S(2)}, u32[]{:S(2)}) %collective-permute-start.6) | collective-permute-done | bytes 131104 | tf_op jit(solution)/shard_map/ppermute | solution.py:39
  40.0 4.9 %collective-permute-start.8 = (f32[2,16,1024]{2,1,0:T(8,128)S(1)}, f32[2,16,1024]{2,1,0:T(8,128)S(1)}, u32[]{:S(2)}, u32[]{:S(2)}) collective-permute-start(f32[2,16,1024]{2,1,0:T(8,128)S(1)} %pad_maximum_fusion.4), channel_id=1, source_target_pairs={{0,32},{4,36},{8,40},{12,44},{16,48},{20,52},{24,56},{28,60},{32,0... | collective-permute-start | bytes 393224 | tf_op jit(solution)/shard_map/ppermute | solution.py:39
  46.3 2.7 %collective-permute-start.7 = (f32[2,16,1024]{2,1,0:T(8,128)S(1)}, f32[2,16,1024]{2,1,0:T(8,128)S(1)}, u32[]{:S(2)}, u32[]{:S(2)}) collective-permute-start(f32[2,16,1024]{2,1,0:T(8,128)S(1)} %pad_maximum_fusion.4), channel_id=1, source_target_pairs={{0,48},{4,52},{8,56},{12,60},{16,0},{20,4},{24,8},{28,12},{32,16},... | collective-permute-start | bytes 393224 | tf_op jit(solution)/shard_map/ppermute | solution.py:39
  49.1 2.9 %collective-permute-done.8 = f32[2,16,1024]{2,1,0:T(8,128)S(1)} collective-permute-done((f32[2,16,1024]{2,1,0:T(8,128)S(1)}, f32[2,16,1024]{2,1,0:T(8,128)S(1)}, u32[]{:S(2)}, u32[]{:S(2)}) %collective-permute-start.8) | collective-permute-done | bytes 131104 | tf_op jit(solution)/shard_map/ppermute | solution.py:39
  52.0 6.5 %collective-permute-done.9 = f32[2,16,1024]{2,1,0:T(8,128)S(1)} collective-permute-done((f32[2,16,1024]{2,1,0:T(8,128)S(1)}, f32[2,16,1024]{2,1,0:T(8,128)S(1)}, u32[]{:S(2)}, u32[]{:S(2)}) %collective-permute-start.9) | collective-permute-done | bytes 131104 | tf_op jit(solution)/shard_map/ppermute | solution.py:39
  58.7 3.3 %collective-permute-start.11 = (f32[2,16,1024]{2,1,0:T(8,128)S(1)}, f32[2,16,1024]{2,1,0:T(8,128)S(1)}, u32[]{:S(2)}, u32[]{:S(2)}) collective-permute-start(f32[2,16,1024]{2,1,0:T(8,128)S(1)} %pad_maximum_fusion.5), channel_id=1, source_target_pairs={{0,128},{4,132},{8,136},{12,140},{16,144},{20,148},{24,152},{28,15... | collective-permute-start | bytes 393224 | tf_op jit(solution)/shard_map/ppermute | solution.py:39
  62.7 2.6 %collective-permute-start.10 = (f32[2,16,1024]{2,1,0:T(8,128)S(1)}, f32[2,16,1024]{2,1,0:T(8,128)S(1)}, u32[]{:S(2)}, u32[]{:S(2)}) collective-permute-start(f32[2,16,1024]{2,1,0:T(8,128)S(1)} %pad_maximum_fusion.5), channel_id=1, source_target_pairs={{0,192},{4,196},{8,200},{12,204},{16,208},{20,212},{24,216},{28,22... | collective-permute-start | bytes 393224 | tf_op jit(solution)/shard_map/ppermute | solution.py:39
  66.6 2.3 %collective-permute-done.12 = f32[2,16,1024]{2,1,0:T(8,128)S(1)} collective-permute-done((f32[2,16,1024]{2,1,0:T(8,128)S(1)}, f32[2,16,1024]{2,1,0:T(8,128)S(1)}, u32[]{:S(2)}, u32[]{:S(2)}) %collective-permute-start.12) | collective-permute-done | bytes 131104 | tf_op jit(solution)/shard_map/ppermute | solution.py:39
  72.9 1.9 %fusion.87 = f32[4,32,1024]{2,1,0:T(8,128)S(1)} fusion(f32[4,32,1024]{2,1,0:T(8,128)S(1)} %get-tuple-element.128, f32[4,32,1024]{2,1,0:T(8,128)S(1)} %bitcast.388, f32[1024]{0:T(1024)S(1)} %bitcast.404, f32[1024]{0:T(1024)S(1)} %bitcast.406, f32[1024]{0:T(1024)S(1)} %bitcast.408, f32[1024]{0:T(1024)S(1)} %bitcast.410, f32[1024]{0:T(1024)S(1)} %bitcast.412, ...), kind=kLoop, calls=%fused_computation.181 | loop fusion | flops 8388608 | bytes 1703936 | tf_op jit(solution)/shard_map/add | solution.py:189
  75.8 2.2 %collective-permute-start.13 = (bf16[3,2,1024]{2,1,0:T(2,128)(2,1)S(1)}, bf16[3,2,1024]{2,1,0:T(2,128)(2,1)S(1)}, u32[]{:S(2)}, u32[]{:S(2)}) collective-permute-start(bf16[3,2,1024]{2,1,0:T(2,128)(2,1)S(1)} %slice.742), channel_id=1, source_target_pairs={{4,0},{8,4},{12,8},{16,12},{20,16},{24,20},{28,24},{32,28},{36,32}... | collective-permute-start | bytes 36872 | tf_op jit(solution)/shard_map/ppermute | solution.py:17
  83.5 2.3 %collective-permute-start.16 = (f32[128]{0:T(128)S(1)}, f32[128]{0:T(128)S(1)}, u32[]{:S(2)}, u32[]{:S(2)}) collective-permute-start(f32[128]{0:T(128)S(1)} %get-tuple-element.46), channel_id=1, source_target_pairs={{0,1},{1,2},{2,3},{3,0},{4,5},{5,6},{6,7},{7,4},{8,9},{9,10},{10,1... | collective-permute-start | bytes 1544 | tf_op jit(solution)/shard_map/ppermute | solution.py:39
  85.8 2.3 %collective-permute-start.14 = (f32[128]{0:T(128)S(1)}, f32[128]{0:T(128)S(1)}, u32[]{:S(2)}, u32[]{:S(2)}) collective-permute-start(f32[128]{0:T(128)S(1)} %get-tuple-element.46), channel_id=1, source_target_pairs={{0,3},{1,0},{2,1},{3,2},{4,7},{5,4},{6,5},{7,6},{8,11},{9,8},{10,9... | collective-permute-start | bytes 1544 | tf_op jit(solution)/shard_map/ppermute | solution.py:39
  88.2 4.1 %collective-permute-start.21 = (f32[25,1024]{1,0:T(8,128)S(1)}, f32[25,1024]{1,0:T(8,128)S(1)}, u32[]{:S(2)}, u32[]{:S(2)}) collective-permute-start(f32[25,1024]{1,0:T(8,128)S(1)} %add_add_fusion.3), channel_id=1, source_target_pairs={{0,32},{4,36},{8,40},{12,44},{16,48},{20,52},{24,56},{28,60},{32,0... | collective-permute-start | bytes 307208 | tf_op jit(solution)/shard_map/ppermute | solution.py:39
  92.4 1.9 %collective-permute-start.22 = (f32[25,1024]{1,0:T(8,128)S(1)}, f32[25,1024]{1,0:T(8,128)S(1)}, u32[]{:S(2)}, u32[]{:S(2)}) collective-permute-start(f32[25,1024]{1,0:T(8,128)S(1)} %add_add_fusion.3), channel_id=1, source_target_pairs={{0,16},{4,20},{8,24},{12,28},{16,32},{20,36},{24,40},{28,44},{32,4... | collective-permute-start | bytes 307208 | tf_op jit(solution)/shard_map/ppermute | solution.py:39
  94.3 2.2 %collective-permute-start.20 = (f32[25,1024]{1,0:T(8,128)S(1)}, f32[25,1024]{1,0:T(8,128)S(1)}, u32[]{:S(2)}, u32[]{:S(2)}) collective-permute-start(f32[25,1024]{1,0:T(8,128)S(1)} %add_add_fusion.3), channel_id=1, source_target_pairs={{0,48},{4,52},{8,56},{12,60},{16,0},{20,4},{24,8},{28,12},{32,16},... | collective-permute-start | bytes 307208 | tf_op jit(solution)/shard_map/ppermute | solution.py:39
  96.6 3.6 %collective-permute-done.21 = f32[25,1024]{1,0:T(8,128)S(1)} collective-permute-done((f32[25,1024]{1,0:T(8,128)S(1)}, f32[25,1024]{1,0:T(8,128)S(1)}, u32[]{:S(2)}, u32[]{:S(2)}) %collective-permute-start.21) | collective-permute-done | bytes 102432 | tf_op jit(solution)/shard_map/ppermute | solution.py:39
  100.2 5.4 %collective-permute-done.22 = f32[25,1024]{1,0:T(8,128)S(1)} collective-permute-done((f32[25,1024]{1,0:T(8,128)S(1)}, f32[25,1024]{1,0:T(8,128)S(1)}, u32[]{:S(2)}, u32[]{:S(2)}) %collective-permute-start.22) | collective-permute-done | bytes 102432 | tf_op jit(solution)/shard_map/ppermute | solution.py:39
  105.7 2.1 %collective-permute-start.24 = (f32[25,1024]{1,0:T(8,128)S(1)}, f32[25,1024]{1,0:T(8,128)S(1)}, u32[]{:S(2)}, u32[]{:S(2)}) collective-permute-start(f32[25,1024]{1,0:T(8,128)S(1)} %add_add_fusion.2), channel_id=1, source_target_pairs={{0,128},{4,132},{8,136},{12,140},{16,144},{20,148},{24,152},{28,15... | collective-permute-start | bytes 307208 | tf_op jit(solution)/shard_map/ppermute | solution.py:39
  (124 shorter events, 43.5 us)
Async XLA Ops:
  1.4 8.6 %collective-permute-start = (bf16[2,1024]{1,0:T(2,128)(2,1)S(1)}, bf16[2,1024]{1,0:T(2,128)(2,1)S(1)}, u32[]{:S(2)}, u32[]{:S(2)}) collective-permute-start(bf16[2,1024]{1,0:T(2,128)(2,1)S(1)} %slice.536), channel_id=1, source_target_pairs={{0,4},{4,8},{8,12},{12,16},{16,20},{20,24},{24,28},{28,32},{32,36}... | collective-permute-start | bytes 12296 | tf_op jit(solution)/shard_map/ppermute | solution.py:17
  11.1 6.3 %collective-permute-start.2 = (f32[130]{0:T(256)S(1)}, f32[130]{0:T(256)S(1)}, u32[]{:S(2)}, u32[]{:S(2)}) collective-permute-start(f32[130]{0:T(256)S(1)} %fusion.3), channel_id=1, source_target_pairs={{0,2},{1,3},{2,0},{3,1},{4,6},{5,7},{6,4},{7,5},{8,10},{9,11},{10,... | collective-permute-start | bytes 1568 | tf_op jit(solution)/shard_map/ppermute | solution.py:39
  31.2 6.4 %collective-permute-start.5 = (f32[2,16,1024]{2,1,0:T(8,128)S(1)}, f32[2,16,1024]{2,1,0:T(8,128)S(1)}, u32[]{:S(2)}, u32[]{:S(2)}) collective-permute-start(f32[2,16,1024]{2,1,0:T(8,128)S(1)} %pad_maximum_fusion.3), channel_id=1, source_target_pairs={{0,8},{4,12},{8,0},{12,4},{16,24},{20,28},{24,16},{28,20},{32,40},... | collective-permute-start | bytes 393224 | tf_op jit(solution)/shard_map/ppermute | solution.py:39
  31.3 8.5 %collective-permute-start.6 = (f32[2,16,1024]{2,1,0:T(8,128)S(1)}, f32[2,16,1024]{2,1,0:T(8,128)S(1)}, u32[]{:S(2)}, u32[]{:S(2)}) collective-permute-start(f32[2,16,1024]{2,1,0:T(8,128)S(1)} %pad_maximum_fusion.3), channel_id=1, source_target_pairs={{0,4},{4,8},{8,12},{12,0},{16,20},{20,24},{24,28},{28,16},{32,36},... | collective-permute-start | bytes 393224 | tf_op jit(solution)/shard_map/ppermute | solution.py:39
  32.0 7.8 %collective-permute-start.4 = (f32[2,16,1024]{2,1,0:T(8,128)S(1)}, f32[2,16,1024]{2,1,0:T(8,128)S(1)}, u32[]{:S(2)}, u32[]{:S(2)}) collective-permute-start(f32[2,16,1024]{2,1,0:T(8,128)S(1)} %pad_maximum_fusion.3), channel_id=1, source_target_pairs={{0,12},{4,0},{8,4},{12,8},{16,28},{20,16},{24,20},{28,24},{32,44},... | collective-permute-start | bytes 393224 | tf_op jit(solution)/shard_map/ppermute | solution.py:39
  40.0 11.9 %collective-permute-start.8 = (f32[2,16,1024]{2,1,0:T(8,128)S(1)}, f32[2,16,1024]{2,1,0:T(8,128)S(1)}, u32[]{:S(2)}, u32[]{:S(2)}) collective-permute-start(f32[2,16,1024]{2,1,0:T(8,128)S(1)} %pad_maximum_fusion.4), channel_id=1, source_target_pairs={{0,32},{4,36},{8,40},{12,44},{16,48},{20,52},{24,56},{28,60},{32,0... | collective-permute-start | bytes 393224 | tf_op jit(solution)/shard_map/ppermute | solution.py:39
  44.9 13.6 %collective-permute-start.9 = (f32[2,16,1024]{2,1,0:T(8,128)S(1)}, f32[2,16,1024]{2,1,0:T(8,128)S(1)}, u32[]{:S(2)}, u32[]{:S(2)}) collective-permute-start(f32[2,16,1024]{2,1,0:T(8,128)S(1)} %pad_maximum_fusion.4), channel_id=1, source_target_pairs={{0,16},{4,20},{8,24},{12,28},{16,32},{20,36},{24,40},{28,44},{32,4... | collective-permute-start | bytes 393224 | tf_op jit(solution)/shard_map/ppermute | solution.py:39
  46.3 12.2 %collective-permute-start.7 = (f32[2,16,1024]{2,1,0:T(8,128)S(1)}, f32[2,16,1024]{2,1,0:T(8,128)S(1)}, u32[]{:S(2)}, u32[]{:S(2)}) collective-permute-start(f32[2,16,1024]{2,1,0:T(8,128)S(1)} %pad_maximum_fusion.4), channel_id=1, source_target_pairs={{0,48},{4,52},{8,56},{12,60},{16,0},{20,4},{24,8},{28,12},{32,16},... | collective-permute-start | bytes 393224 | tf_op jit(solution)/shard_map/ppermute | solution.py:39
  58.7 7.9 %collective-permute-start.11 = (f32[2,16,1024]{2,1,0:T(8,128)S(1)}, f32[2,16,1024]{2,1,0:T(8,128)S(1)}, u32[]{:S(2)}, u32[]{:S(2)}) collective-permute-start(f32[2,16,1024]{2,1,0:T(8,128)S(1)} %pad_maximum_fusion.5), channel_id=1, source_target_pairs={{0,128},{4,132},{8,136},{12,140},{16,144},{20,148},{24,152},{28,15... | collective-permute-start | bytes 393224 | tf_op jit(solution)/shard_map/ppermute | solution.py:39
  62.0 6.9 %collective-permute-start.12 = (f32[2,16,1024]{2,1,0:T(8,128)S(1)}, f32[2,16,1024]{2,1,0:T(8,128)S(1)}, u32[]{:S(2)}, u32[]{:S(2)}) collective-permute-start(f32[2,16,1024]{2,1,0:T(8,128)S(1)} %pad_maximum_fusion.5), channel_id=1, source_target_pairs={{0,64},{4,68},{8,72},{12,76},{16,80},{20,84},{24,88},{28,92},{32,9... | collective-permute-start | bytes 393224 | tf_op jit(solution)/shard_map/ppermute | solution.py:39
  62.7 6.2 %collective-permute-start.10 = (f32[2,16,1024]{2,1,0:T(8,128)S(1)}, f32[2,16,1024]{2,1,0:T(8,128)S(1)}, u32[]{:S(2)}, u32[]{:S(2)}) collective-permute-start(f32[2,16,1024]{2,1,0:T(8,128)S(1)} %pad_maximum_fusion.5), channel_id=1, source_target_pairs={{0,192},{4,196},{8,200},{12,204},{16,208},{20,212},{24,216},{28,22... | collective-permute-start | bytes 393224 | tf_op jit(solution)/shard_map/ppermute | solution.py:39
  75.8 5.2 %collective-permute-start.13 = (bf16[3,2,1024]{2,1,0:T(2,128)(2,1)S(1)}, bf16[3,2,1024]{2,1,0:T(2,128)(2,1)S(1)}, u32[]{:S(2)}, u32[]{:S(2)}) collective-permute-start(bf16[3,2,1024]{2,1,0:T(2,128)(2,1)S(1)} %slice.742), channel_id=1, source_target_pairs={{4,0},{8,4},{12,8},{16,12},{20,16},{24,20},{28,24},{32,28},{36,32}... | collective-permute-start | bytes 36872 | tf_op jit(solution)/shard_map/ppermute | solution.py:17
  78.8 7.0 %collective-permute-start.18 = (f32[25,1024]{1,0:T(8,128)S(1)}, f32[25,1024]{1,0:T(8,128)S(1)}, u32[]{:S(2)}, u32[]{:S(2)}) collective-permute-start(f32[25,1024]{1,0:T(8,128)S(1)} %pad_maximum_fusion.6), channel_id=1, source_target_pairs={{0,8},{4,12},{8,0},{12,4},{16,24},{20,28},{24,16},{28,20},{32,40},... | collective-permute-start | bytes 307208 | tf_op jit(solution)/shard_map/ppermute | solution.py:39
  79.2 8.9 %collective-permute-start.19 = (f32[25,1024]{1,0:T(8,128)S(1)}, f32[25,1024]{1,0:T(8,128)S(1)}, u32[]{:S(2)}, u32[]{:S(2)}) collective-permute-start(f32[25,1024]{1,0:T(8,128)S(1)} %pad_maximum_fusion.6), channel_id=1, source_target_pairs={{0,4},{4,8},{8,12},{12,0},{16,20},{20,24},{24,28},{28,16},{32,36},... | collective-permute-start | bytes 307208 | tf_op jit(solution)/shard_map/ppermute | solution.py:39
  80.1 8.1 %collective-permute-start.17 = (f32[25,1024]{1,0:T(8,128)S(1)}, f32[25,1024]{1,0:T(8,128)S(1)}, u32[]{:S(2)}, u32[]{:S(2)}) collective-permute-start(f32[25,1024]{1,0:T(8,128)S(1)} %pad_maximum_fusion.6), channel_id=1, source_target_pairs={{0,12},{4,0},{8,4},{12,8},{16,28},{20,16},{24,20},{28,24},{32,44},... | collective-permute-start | bytes 307208 | tf_op jit(solution)/shard_map/ppermute | solution.py:39
  81.7 12.6 %collective-permute-start.15 = (f32[128]{0:T(128)S(1)}, f32[128]{0:T(128)S(1)}, u32[]{:S(2)}, u32[]{:S(2)}) collective-permute-start(f32[128]{0:T(128)S(1)} %get-tuple-element.46), channel_id=1, source_target_pairs={{0,2},{1,3},{2,0},{3,1},{4,6},{5,7},{6,4},{7,5},{8,10},{9,11},{10,... | collective-permute-start | bytes 1544 | tf_op jit(solution)/shard_map/ppermute | solution.py:39
  83.5 13.1 %collective-permute-start.16 = (f32[128]{0:T(128)S(1)}, f32[128]{0:T(128)S(1)}, u32[]{:S(2)}, u32[]{:S(2)}) collective-permute-start(f32[128]{0:T(128)S(1)} %get-tuple-element.46), channel_id=1, source_target_pairs={{0,1},{1,2},{2,3},{3,0},{4,5},{5,6},{6,7},{7,4},{8,9},{9,10},{10,1... | collective-permute-start | bytes 1544 | tf_op jit(solution)/shard_map/ppermute | solution.py:39
  85.8 10.7 %collective-permute-start.14 = (f32[128]{0:T(128)S(1)}, f32[128]{0:T(128)S(1)}, u32[]{:S(2)}, u32[]{:S(2)}) collective-permute-start(f32[128]{0:T(128)S(1)} %get-tuple-element.46), channel_id=1, source_target_pairs={{0,3},{1,0},{2,1},{3,2},{4,7},{5,4},{6,5},{7,6},{8,11},{9,8},{10,9... | collective-permute-start | bytes 1544 | tf_op jit(solution)/shard_map/ppermute | solution.py:39
  88.2 12.0 %collective-permute-start.21 = (f32[25,1024]{1,0:T(8,128)S(1)}, f32[25,1024]{1,0:T(8,128)S(1)}, u32[]{:S(2)}, u32[]{:S(2)}) collective-permute-start(f32[25,1024]{1,0:T(8,128)S(1)} %add_add_fusion.3), channel_id=1, source_target_pairs={{0,32},{4,36},{8,40},{12,44},{16,48},{20,52},{24,56},{28,60},{32,0... | collective-permute-start | bytes 307208 | tf_op jit(solution)/shard_map/ppermute | solution.py:39
  92.4 13.2 %collective-permute-start.22 = (f32[25,1024]{1,0:T(8,128)S(1)}, f32[25,1024]{1,0:T(8,128)S(1)}, u32[]{:S(2)}, u32[]{:S(2)}) collective-permute-start(f32[25,1024]{1,0:T(8,128)S(1)} %add_add_fusion.3), channel_id=1, source_target_pairs={{0,16},{4,20},{8,24},{12,28},{16,32},{20,36},{24,40},{28,44},{32,4... | collective-permute-start | bytes 307208 | tf_op jit(solution)/shard_map/ppermute | solution.py:39
  94.3 11.3 %collective-permute-start.20 = (f32[25,1024]{1,0:T(8,128)S(1)}, f32[25,1024]{1,0:T(8,128)S(1)}, u32[]{:S(2)}, u32[]{:S(2)}) collective-permute-start(f32[25,1024]{1,0:T(8,128)S(1)} %add_add_fusion.3), channel_id=1, source_target_pairs={{0,48},{4,52},{8,56},{12,60},{16,0},{20,4},{24,8},{28,12},{32,16},... | collective-permute-start | bytes 307208 | tf_op jit(solution)/shard_map/ppermute | solution.py:39
  105.7 7.7 %collective-permute-start.24 = (f32[25,1024]{1,0:T(8,128)S(1)}, f32[25,1024]{1,0:T(8,128)S(1)}, u32[]{:S(2)}, u32[]{:S(2)}) collective-permute-start(f32[25,1024]{1,0:T(8,128)S(1)} %add_add_fusion.2), channel_id=1, source_target_pairs={{0,128},{4,132},{8,136},{12,140},{16,144},{20,148},{24,152},{28,15... | collective-permute-start | bytes 307208 | tf_op jit(solution)/shard_map/ppermute | solution.py:39
  107.8 7.4 %collective-permute-start.25 = (f32[25,1024]{1,0:T(8,128)S(1)}, f32[25,1024]{1,0:T(8,128)S(1)}, u32[]{:S(2)}, u32[]{:S(2)}) collective-permute-start(f32[25,1024]{1,0:T(8,128)S(1)} %add_add_fusion.2), channel_id=1, source_target_pairs={{0,64},{4,68},{8,72},{12,76},{16,80},{20,84},{24,88},{28,92},{32,9... | collective-permute-start | bytes 307208 | tf_op jit(solution)/shard_map/ppermute | solution.py:39
  109.6 5.8 %collective-permute-start.23 = (f32[25,1024]{1,0:T(8,128)S(1)}, f32[25,1024]{1,0:T(8,128)S(1)}, u32[]{:S(2)}, u32[]{:S(2)}) collective-permute-start(f32[25,1024]{1,0:T(8,128)S(1)} %add_add_fusion.2), channel_id=1, source_target_pairs={{0,192},{4,196},{8,200},{12,204},{16,208},{20,212},{24,216},{28,22... | collective-permute-start | bytes 307208 | tf_op jit(solution)/shard_map/ppermute | solution.py:39
  (15 other events, 148.3 us)

commit v6 on v5

--- a/solution.py
+++ b/solution.py
@@ -26,16 +26,41 @@
     return levels
 
 
+PLACES = {}
+
+
+def hops(first, second):
+    rings = PLACES.get("rings")
+    return sum(min(abs(a - b), ring - abs(a - b)) for a, b, ring in zip(first, second, rings))
+
+
+def source_of(target, step, stride, radix, count, flip):
+    digit = (target // stride) % radix
+    position = (target % stride) ^ flip
+    base = target - target % (stride * radix)
+    return base + ((digit + step) % radix) * stride + position
+
+
+def best_flip(axis, step, stride, radix, count):
+    places = PLACES.get(axis)
+    if places is None or len(places) != count:
+        return 0
+    best, flip_of_best = None, 0
+    for flip in range(stride):
+        far = [hops(places[source_of(t, step, stride, radix, count, flip)], places[t]) for t in range(count)]
+        score = (max(far), sum(far))
+        if best is None or score < best:
+            best, flip_of_best = score, flip
+    return flip_of_best
+
+
 def members(value, axis, stride, radix):
     count = lax.axis_size(axis)
     digit = (lax.axis_index(axis) // stride) % radix
     received = [value]
     for step in range(1, radix):
-        pairs = []
-        for source in range(count):
-            source_digit = (source // stride) % radix
-            target = source + (((source_digit - step) % radix) - source_digit) * stride
-            pairs.append((source, target))
+        flip = best_flip(axis, step, stride, radix, count)
+        pairs = [(source_of(t, step, stride, radix, count, flip), t) for t in range(count)]
         received.append(lax.ppermute(value, axis, pairs))
     ordered = [
         lax.select_n(((position - digit) % radix).astype(jnp.int32), *received)
@@ -242,6 +267,12 @@
 
 
 def solution(mesh):
+    devices = mesh.devices
+    if all(hasattr(d, "coords") for d in devices.flat):
+        coords = [tuple(d.coords) for d in devices.flat]
+        PLACES["rings"] = tuple(max(c[k] for c in coords) + 1 for k in range(len(coords[0])))
+        PLACES["ctx"] = [tuple(d.coords) for d in devices[:, 0]]
+        PLACES["ch"] = [tuple(d.coords) for d in devices[0, :]]
     return jax.shard_map(
         per_device,
         mesh=mesh,

time: 119 us -> 117 us (0.983)
  the two profiles are of different devices: /device:TPU:32 before, /device:TPU:6 now
where the time goes in v6:
time: 117 us; the launch traced here: 116 us
  starting transfers between devices  45.3 us (39%)
  waiting for transfers between devices  37.2 us (32%)
  other arithmetic  26.5 us (23%)
  local copies, waits for them, and re-layouts  5.95 us (5%)
  between operations  1.41 us (1%)
    ppermute x24, starting transfers between devices, members(): received.append(lax.ppermute(value, axis, pairs))  42.3 us
    ppermute x24, waiting for transfers between devices, members(): received.append(lax.ppermute(value, axis, pairs))  37.2 us
    ppermute x2, starting transfers between devices, passed_along(): lax.ppermute(value, axis, [(source, source + steps) for source in range(f...  3.02 us
    reduce_sum x3, other arithmetic, per_device(): jnp.sum(blocks_padded[:, P_SIZE - 1 - lag:2 * P_SIZE - 1 - lag] * grad_bl...  2.5 us
  transfers between devices with their start and end apart: 26, of which 17 were waited for; matrix products, arithmetic and copies ran while one was open for 8% of the time, Pallas kernels for 0%

profile of v6, /device:TPU:6, one launch (start us, length us, event | category | flops | bytes accessed | tf_op | source)
XLA Modules:
  0.0 116.4 jit_solution(5228310742895700426)
XLA Ops:
  12.4 2.1 %collective-permute-start.3 = (f32[130]{0:T(256)S(1)}, f32[130]{0:T(256)S(1)}, u32[]{:S(2)}, u32[]{:S(2)}) collective-permute-start(f32[130]{0:T(256)S(1)} %fusion.3), channel_id=1, source_target_pairs={{3,0},{0,1},{1,2},{2,3},{7,4},{4,5},{5,6},{6,7},{11,8},{8,9},{9,10... | collective-permute-start | bytes 1568 | tf_op jit(solution)/shard_map/ppermute | solution.py:64
  16.0 3.2 %collective-permute-done.1 = f32[130]{0:T(256)S(1)} collective-permute-done((f32[130]{0:T(256)S(1)}, f32[130]{0:T(256)S(1)}, u32[]{:S(2)}, u32[]{:S(2)}) %collective-permute-start.1) | collective-permute-done | bytes 552 | tf_op jit(solution)/shard_map/ppermute | solution.py:64
  24.4 2.3 %stack.195 = f32[32,1024]{1,0:T(8,128)S(1)} concatenate(f32[1,1024]{1,0:T(1,128)S(1)} %bitcast.501, f32[1,1024]{1,0:T(1,128)} %bitcast.514, f32[1,1024]{1,0:T(1,128)S(1)} %bitcast.484, f32[1,1024]{1,0:T(1,128)S(1)} %bitcast.485, f32[1,1024]{1,0:T(1,128)S(1)} %bitcast.486, f32[1,1024]{1,0:T(1,128)S(1)} %bitcast.487, f32[1,1024]{1,0:T(1,128)S(1)} %bitcast.488, ...), dimensions={0} | concatenate | bytes 262144 | tf_op jit(solution)/shard_map/stack | solution.py:220
  26.8 2.2 %exponential_multiply_fusion = (f32[16,32,1024]{2,1,0:T(8,128)S(1)}, f32[16,32,1024]{2,1,0:T(8,128)S(1)}, f32[32,1024]{1,0:T(8,128)S(1)}, f32[16,1024]{1,0:T(8,1...) fusion(f32[32]{0:T(128)} %broadcast_subtract_fusion, f32[16,1024]{1,0:T(8,128)S(1)} %neg.5, ...), kind=kLoop, calls=%fused_computation.75 | loop fusion | flops 5193728 | bytes 8847872 | tf_op jit(solution)/shard_map/mul | solution.py:163
  31.5 2.2 %collective-permute-start.5 = (f32[2,16,1024]{2,1,0:T(8,128)S(1)}, f32[2,16,1024]{2,1,0:T(8,128)S(1)}, u32[]{:S(2)}, u32[]{:S(2)}) collective-permute-start(f32[2,16,1024]{2,1,0:T(8,128)S(1)} %pad_maximum_fusion.3), channel_id=1, source_target_pairs={{8,0},{12,4},{0,8},{4,12},{24,16},{28,20},{16,24},{20,28},{40,32},... | collective-permute-start | bytes 393224 | tf_op jit(solution)/shard_map/ppermute | solution.py:64
  35.7 2.3 %collective-permute-done.5 = f32[2,16,1024]{2,1,0:T(8,128)S(1)} collective-permute-done((f32[2,16,1024]{2,1,0:T(8,128)S(1)}, f32[2,16,1024]{2,1,0:T(8,128)S(1)}, u32[]{:S(2)}, u32[]{:S(2)}) %collective-permute-start.5) | collective-permute-done | bytes 131104 | tf_op jit(solution)/shard_map/ppermute | solution.py:64
  38.0 2.2 %collective-permute-done.6 = f32[2,16,1024]{2,1,0:T(8,128)S(1)} collective-permute-done((f32[2,16,1024]{2,1,0:T(8,128)S(1)}, f32[2,16,1024]{2,1,0:T(8,128)S(1)}, u32[]{:S(2)}, u32[]{:S(2)}) %collective-permute-start.6) | collective-permute-done | bytes 131104 | tf_op jit(solution)/shard_map/ppermute | solution.py:64
  40.4 5.3 %collective-permute-start.8 = (f32[2,16,1024]{2,1,0:T(8,128)S(1)}, f32[2,16,1024]{2,1,0:T(8,128)S(1)}, u32[]{:S(2)}, u32[]{:S(2)}) collective-permute-start(f32[2,16,1024]{2,1,0:T(8,128)S(1)} %pad_maximum_fusion.4), channel_id=1, source_target_pairs={{40,0},{44,4},{32,8},{36,12},{56,16},{60,20},{48,24},{52,28},{8,32... | collective-permute-start | bytes 393224 | tf_op jit(solution)/shard_map/ppermute | solution.py:64
  47.2 2.7 %collective-permute-start.7 = (f32[2,16,1024]{2,1,0:T(8,128)S(1)}, f32[2,16,1024]{2,1,0:T(8,128)S(1)}, u32[]{:S(2)}, u32[]{:S(2)}) collective-permute-start(f32[2,16,1024]{2,1,0:T(8,128)S(1)} %pad_maximum_fusion.4), channel_id=1, source_target_pairs={{16,0},{20,4},{24,8},{28,12},{32,16},{36,20},{40,24},{44,28},{48,3... | collective-permute-start | bytes 393224 | tf_op jit(solution)/shard_map/ppermute | solution.py:64
  50.0 3.9 %collective-permute-done.9 = f32[2,16,1024]{2,1,0:T(8,128)S(1)} collective-permute-done((f32[2,16,1024]{2,1,0:T(8,128)S(1)}, f32[2,16,1024]{2,1,0:T(8,128)S(1)}, u32[]{:S(2)}, u32[]{:S(2)}) %collective-permute-start.9) | collective-permute-done | bytes 131104 | tf_op jit(solution)/shard_map/ppermute | solution.py:64
  54.0 5.3 %collective-permute-done.7 = f32[2,16,1024]{2,1,0:T(8,128)S(1)} collective-permute-done((f32[2,16,1024]{2,1,0:T(8,128)S(1)}, f32[2,16,1024]{2,1,0:T(8,128)S(1)}, u32[]{:S(2)}, u32[]{:S(2)}) %collective-permute-start.7) | collective-permute-done | bytes 131104 | tf_op jit(solution)/shard_map/ppermute | solution.py:64
  59.4 3.3 %collective-permute-start.11 = (f32[2,16,1024]{2,1,0:T(8,128)S(1)}, f32[2,16,1024]{2,1,0:T(8,128)S(1)}, u32[]{:S(2)}, u32[]{:S(2)}) collective-permute-start(f32[2,16,1024]{2,1,0:T(8,128)S(1)} %pad_maximum_fusion.5), channel_id=1, source_target_pairs={{128,0},{132,4},{136,8},{140,12},{144,16},{148,20},{152,24},{156,2... | collective-permute-start | bytes 393224 | tf_op jit(solution)/shard_map/ppermute | solution.py:64
  63.4 2.6 %collective-permute-start.10 = (f32[2,16,1024]{2,1,0:T(8,128)S(1)}, f32[2,16,1024]{2,1,0:T(8,128)S(1)}, u32[]{:S(2)}, u32[]{:S(2)}) collective-permute-start(f32[2,16,1024]{2,1,0:T(8,128)S(1)} %pad_maximum_fusion.5), channel_id=1, source_target_pairs={{64,0},{68,4},{72,8},{76,12},{80,16},{84,20},{88,24},{92,28},{96,3... | collective-permute-start | bytes 393224 | tf_op jit(solution)/shard_map/ppermute | solution.py:64
  67.4 2.3 %collective-permute-done.12 = f32[2,16,1024]{2,1,0:T(8,128)S(1)} collective-permute-done((f32[2,16,1024]{2,1,0:T(8,128)S(1)}, f32[2,16,1024]{2,1,0:T(8,128)S(1)}, u32[]{:S(2)}, u32[]{:S(2)}) %collective-permute-start.12) | collective-permute-done | bytes 131104 | tf_op jit(solution)/shard_map/ppermute | solution.py:64
  73.7 1.9 %fusion.87 = f32[4,32,1024]{2,1,0:T(8,128)S(1)} fusion(f32[4,32,1024]{2,1,0:T(8,128)S(1)} %get-tuple-element.128, f32[4,32,1024]{2,1,0:T(8,128)S(1)} %bitcast.388, f32[1024]{0:T(1024)S(1)} %bitcast.404, f32[1024]{0:T(1024)S(1)} %bitcast.406, f32[1024]{0:T(1024)S(1)} %bitcast.408, f32[1024]{0:T(1024)S(1)} %bitcast.410, f32[1024]{0:T(1024)S(1)} %bitcast.412, ...), kind=kLoop, calls=%fused_computation.181 | loop fusion | flops 8388608 | bytes 1703936 | tf_op jit(solution)/shard_map/add | solution.py:214
  78.7 1.8 %collective-permute-start.18 = (f32[25,1024]{1,0:T(8,128)S(1)}, f32[25,1024]{1,0:T(8,128)S(1)}, u32[]{:S(2)}, u32[]{:S(2)}) collective-permute-start(f32[25,1024]{1,0:T(8,128)S(1)} %pad_maximum_fusion.6), channel_id=1, source_target_pairs={{8,0},{12,4},{0,8},{4,12},{24,16},{28,20},{16,24},{20,28},{40,32},... | collective-permute-start | bytes 307208 | tf_op jit(solution)/shard_map/ppermute | solution.py:64
  85.4 2.6 %collective-permute-done.19 = f32[25,1024]{1,0:T(8,128)S(1)} collective-permute-done((f32[25,1024]{1,0:T(8,128)S(1)}, f32[25,1024]{1,0:T(8,128)S(1)}, u32[]{:S(2)}, u32[]{:S(2)}) %collective-permute-start.19) | collective-permute-done | bytes 102432 | tf_op jit(solution)/shard_map/ppermute | solution.py:64
  88.1 3.6 %collective-permute-start.21 = (f32[25,1024]{1,0:T(8,128)S(1)}, f32[25,1024]{1,0:T(8,128)S(1)}, u32[]{:S(2)}, u32[]{:S(2)}) collective-permute-start(f32[25,1024]{1,0:T(8,128)S(1)} %add_add_fusion.3), channel_id=1, source_target_pairs={{40,0},{44,4},{32,8},{36,12},{56,16},{60,20},{48,24},{52,28},{8,32... | collective-permute-start | bytes 307208 | tf_op jit(solution)/shard_map/ppermute | solution.py:64
  92.0 3.8 %collective-permute-start.20 = (f32[25,1024]{1,0:T(8,128)S(1)}, f32[25,1024]{1,0:T(8,128)S(1)}, u32[]{:S(2)}, u32[]{:S(2)}) collective-permute-start(f32[25,1024]{1,0:T(8,128)S(1)} %add_add_fusion.3), channel_id=1, source_target_pairs={{16,0},{20,4},{24,8},{28,12},{32,16},{36,20},{40,24},{44,28},{48,3... | collective-permute-start | bytes 307208 | tf_op jit(solution)/shard_map/ppermute | solution.py:64
  95.9 4.9 %collective-permute-done.21 = f32[25,1024]{1,0:T(8,128)S(1)} collective-permute-done((f32[25,1024]{1,0:T(8,128)S(1)}, f32[25,1024]{1,0:T(8,128)S(1)}, u32[]{:S(2)}, u32[]{:S(2)}) %collective-permute-start.21) | collective-permute-done | bytes 102432 | tf_op jit(solution)/shard_map/ppermute | solution.py:64
  101.1 3.6 %collective-permute-done.20 = f32[25,1024]{1,0:T(8,128)S(1)} collective-permute-done((f32[25,1024]{1,0:T(8,128)S(1)}, f32[25,1024]{1,0:T(8,128)S(1)}, u32[]{:S(2)}, u32[]{:S(2)}) %collective-permute-start.20) | collective-permute-done | bytes 102432 | tf_op jit(solution)/shard_map/ppermute | solution.py:64
  104.7 2.1 %collective-permute-start.24 = (f32[25,1024]{1,0:T(8,128)S(1)}, f32[25,1024]{1,0:T(8,128)S(1)}, u32[]{:S(2)}, u32[]{:S(2)}) collective-permute-start(f32[25,1024]{1,0:T(8,128)S(1)} %add_add_fusion.2), channel_id=1, source_target_pairs={{128,0},{132,4},{136,8},{140,12},{144,16},{148,20},{152,24},{156,2... | collective-permute-start | bytes 307208 | tf_op jit(solution)/shard_map/ppermute | solution.py:64
  106.9 2.0 %collective-permute-start.25 = (f32[25,1024]{1,0:T(8,128)S(1)}, f32[25,1024]{1,0:T(8,128)S(1)}, u32[]{:S(2)}, u32[]{:S(2)}) collective-permute-start(f32[25,1024]{1,0:T(8,128)S(1)} %add_add_fusion.2), channel_id=1, source_target_pairs={{192,0},{196,4},{200,8},{204,12},{208,16},{212,20},{216,24},{220,2... | collective-permute-start | bytes 307208 | tf_op jit(solution)/shard_map/ppermute | solution.py:64
  112.7 1.8 %collective-permute-done.25 = f32[25,1024]{1,0:T(8,128)S(1)} collective-permute-done((f32[25,1024]{1,0:T(8,128)S(1)}, f32[25,1024]{1,0:T(8,128)S(1)}, u32[]{:S(2)}, u32[]{:S(2)}) %collective-permute-start.25) | collective-permute-done | bytes 102432 | tf_op jit(solution)/shard_map/ppermute | solution.py:64
  (124 shorter events, 45.0 us)
Async XLA Ops:
  1.4 8.4 %collective-permute-start = (bf16[2,1024]{1,0:T(2,128)(2,1)S(1)}, bf16[2,1024]{1,0:T(2,128)(2,1)S(1)}, u32[]{:S(2)}, u32[]{:S(2)}) collective-permute-start(bf16[2,1024]{1,0:T(2,128)(2,1)S(1)} %slice.536), channel_id=1, source_target_pairs={{0,4},{4,8},{8,12},{12,16},{16,20},{20,24},{24,28},{28,32},{32,36}... | collective-permute-start | bytes 12296 | tf_op jit(solution)/shard_map/ppermute | solution.py:17
  10.9 5.2 %collective-permute-start.2 = (f32[130]{0:T(256)S(1)}, f32[130]{0:T(256)S(1)}, u32[]{:S(2)}, u32[]{:S(2)}) collective-permute-start(f32[130]{0:T(256)S(1)} %fusion.3), channel_id=1, source_target_pairs={{2,0},{3,1},{0,2},{1,3},{6,4},{7,5},{4,6},{5,7},{10,8},{11,9},{8,1... | collective-permute-start | bytes 1568 | tf_op jit(solution)/shard_map/ppermute | solution.py:64
  31.5 6.5 %collective-permute-start.5 = (f32[2,16,1024]{2,1,0:T(8,128)S(1)}, f32[2,16,1024]{2,1,0:T(8,128)S(1)}, u32[]{:S(2)}, u32[]{:S(2)}) collective-permute-start(f32[2,16,1024]{2,1,0:T(8,128)S(1)} %pad_maximum_fusion.3), channel_id=1, source_target_pairs={{8,0},{12,4},{0,8},{4,12},{24,16},{28,20},{16,24},{20,28},{40,32},... | collective-permute-start | bytes 393224 | tf_op jit(solution)/shard_map/ppermute | solution.py:64
  33.7 6.5 %collective-permute-start.6 = (f32[2,16,1024]{2,1,0:T(8,128)S(1)}, f32[2,16,1024]{2,1,0:T(8,128)S(1)}, u32[]{:S(2)}, u32[]{:S(2)}) collective-permute-start(f32[2,16,1024]{2,1,0:T(8,128)S(1)} %pad_maximum_fusion.3), channel_id=1, source_target_pairs={{12,0},{0,4},{4,8},{8,12},{28,16},{16,20},{20,24},{24,28},{44,32},... | collective-permute-start | bytes 393224 | tf_op jit(solution)/shard_map/ppermute | solution.py:64
  33.7 6.5 %collective-permute-start.4 = (f32[2,16,1024]{2,1,0:T(8,128)S(1)}, f32[2,16,1024]{2,1,0:T(8,128)S(1)}, u32[]{:S(2)}, u32[]{:S(2)}) collective-permute-start(f32[2,16,1024]{2,1,0:T(8,128)S(1)} %pad_maximum_fusion.3), channel_id=1, source_target_pairs={{4,0},{8,4},{12,8},{0,12},{20,16},{24,20},{28,24},{16,28},{36,32},... | collective-permute-start | bytes 393224 | tf_op jit(solution)/shard_map/ppermute | solution.py:64
  40.4 9.6 %collective-permute-start.8 = (f32[2,16,1024]{2,1,0:T(8,128)S(1)}, f32[2,16,1024]{2,1,0:T(8,128)S(1)}, u32[]{:S(2)}, u32[]{:S(2)}) collective-permute-start(f32[2,16,1024]{2,1,0:T(8,128)S(1)} %pad_maximum_fusion.4), channel_id=1, source_target_pairs={{40,0},{44,4},{32,8},{36,12},{56,16},{60,20},{48,24},{52,28},{8,32... | collective-permute-start | bytes 393224 | tf_op jit(solution)/shard_map/ppermute | solution.py:64
  45.8 8.2 %collective-permute-start.9 = (f32[2,16,1024]{2,1,0:T(8,128)S(1)}, f32[2,16,1024]{2,1,0:T(8,128)S(1)}, u32[]{:S(2)}, u32[]{:S(2)}) collective-permute-start(f32[2,16,1024]{2,1,0:T(8,128)S(1)} %pad_maximum_fusion.4), channel_id=1, source_target_pairs={{48,0},{52,4},{56,8},{60,12},{0,16},{4,20},{8,24},{12,28},{16,32},... | collective-permute-start | bytes 393224 | tf_op jit(solution)/shard_map/ppermute | solution.py:64
  47.2 12.0 %collective-permute-start.7 = (f32[2,16,1024]{2,1,0:T(8,128)S(1)}, f32[2,16,1024]{2,1,0:T(8,128)S(1)}, u32[]{:S(2)}, u32[]{:S(2)}) collective-permute-start(f32[2,16,1024]{2,1,0:T(8,128)S(1)} %pad_maximum_fusion.4), channel_id=1, source_target_pairs={{16,0},{20,4},{24,8},{28,12},{32,16},{36,20},{40,24},{44,28},{48,3... | collective-permute-start | bytes 393224 | tf_op jit(solution)/shard_map/ppermute | solution.py:64
  59.4 7.9 %collective-permute-start.11 = (f32[2,16,1024]{2,1,0:T(8,128)S(1)}, f32[2,16,1024]{2,1,0:T(8,128)S(1)}, u32[]{:S(2)}, u32[]{:S(2)}) collective-permute-start(f32[2,16,1024]{2,1,0:T(8,128)S(1)} %pad_maximum_fusion.5), channel_id=1, source_target_pairs={{128,0},{132,4},{136,8},{140,12},{144,16},{148,20},{152,24},{156,2... | collective-permute-start | bytes 393224 | tf_op jit(solution)/shard_map/ppermute | solution.py:64
  62.7 6.9 %collective-permute-start.12 = (f32[2,16,1024]{2,1,0:T(8,128)S(1)}, f32[2,16,1024]{2,1,0:T(8,128)S(1)}, u32[]{:S(2)}, u32[]{:S(2)}) collective-permute-start(f32[2,16,1024]{2,1,0:T(8,128)S(1)} %pad_maximum_fusion.5), channel_id=1, source_target_pairs={{192,0},{196,4},{200,8},{204,12},{208,16},{212,20},{216,24},{220,2... | collective-permute-start | bytes 393224 | tf_op jit(solution)/shard_map/ppermute | solution.py:64
  63.4 6.3 %collective-permute-start.10 = (f32[2,16,1024]{2,1,0:T(8,128)S(1)}, f32[2,16,1024]{2,1,0:T(8,128)S(1)}, u32[]{:S(2)}, u32[]{:S(2)}) collective-permute-start(f32[2,16,1024]{2,1,0:T(8,128)S(1)} %pad_maximum_fusion.5), channel_id=1, source_target_pairs={{64,0},{68,4},{72,8},{76,12},{80,16},{84,20},{88,24},{92,28},{96,3... | collective-permute-start | bytes 393224 | tf_op jit(solution)/shard_map/ppermute | solution.py:64
  76.6 5.6 %collective-permute-start.13 = (bf16[3,2,1024]{2,1,0:T(2,128)(2,1)S(1)}, bf16[3,2,1024]{2,1,0:T(2,128)(2,1)S(1)}, u32[]{:S(2)}, u32[]{:S(2)}) collective-permute-start(bf16[3,2,1024]{2,1,0:T(2,128)(2,1)S(1)} %slice.742), channel_id=1, source_target_pairs={{4,0},{8,4},{12,8},{16,12},{20,16},{24,20},{28,24},{32,28},{36,32}... | collective-permute-start | bytes 36872 | tf_op jit(solution)/shard_map/ppermute | solution.py:17
  78.7 6.3 %collective-permute-start.18 = (f32[25,1024]{1,0:T(8,128)S(1)}, f32[25,1024]{1,0:T(8,128)S(1)}, u32[]{:S(2)}, u32[]{:S(2)}) collective-permute-start(f32[25,1024]{1,0:T(8,128)S(1)} %pad_maximum_fusion.6), channel_id=1, source_target_pairs={{8,0},{12,4},{0,8},{4,12},{24,16},{28,20},{16,24},{20,28},{40,32},... | collective-permute-start | bytes 307208 | tf_op jit(solution)/shard_map/ppermute | solution.py:64
  80.5 7.5 %collective-permute-start.19 = (f32[25,1024]{1,0:T(8,128)S(1)}, f32[25,1024]{1,0:T(8,128)S(1)}, u32[]{:S(2)}, u32[]{:S(2)}) collective-permute-start(f32[25,1024]{1,0:T(8,128)S(1)} %pad_maximum_fusion.6), channel_id=1, source_target_pairs={{12,0},{0,4},{4,8},{8,12},{28,16},{16,20},{20,24},{24,28},{44,32},... | collective-permute-start | bytes 307208 | tf_op jit(solution)/shard_map/ppermute | solution.py:64
  80.5 7.5 %collective-permute-start.17 = (f32[25,1024]{1,0:T(8,128)S(1)}, f32[25,1024]{1,0:T(8,128)S(1)}, u32[]{:S(2)}, u32[]{:S(2)}) collective-permute-start(f32[25,1024]{1,0:T(8,128)S(1)} %pad_maximum_fusion.6), channel_id=1, source_target_pairs={{4,0},{8,4},{12,8},{0,12},{20,16},{24,20},{28,24},{16,28},{36,32},... | collective-permute-start | bytes 307208 | tf_op jit(solution)/shard_map/ppermute | solution.py:64
  83.0 9.0 %collective-permute-start.15 = (f32[128]{0:T(128)S(1)}, f32[128]{0:T(128)S(1)}, u32[]{:S(2)}, u32[]{:S(2)}) collective-permute-start(f32[128]{0:T(128)S(1)} %get-tuple-element.46), channel_id=1, source_target_pairs={{2,0},{3,1},{0,2},{1,3},{6,4},{7,5},{4,6},{5,7},{10,8},{11,9},{8,1... | collective-permute-start | bytes 1544 | tf_op jit(solution)/shard_map/ppermute | solution.py:64
  83.3 12.5 %collective-permute-start.16 = (f32[128]{0:T(128)S(1)}, f32[128]{0:T(128)S(1)}, u32[]{:S(2)}, u32[]{:S(2)}) collective-permute-start(f32[128]{0:T(128)S(1)} %get-tuple-element.46), channel_id=1, source_target_pairs={{3,0},{0,1},{1,2},{2,3},{7,4},{4,5},{5,6},{6,7},{11,8},{8,9},{9,10... | collective-permute-start | bytes 1544 | tf_op jit(solution)/shard_map/ppermute | solution.py:64
  85.0 10.8 %collective-permute-start.14 = (f32[128]{0:T(128)S(1)}, f32[128]{0:T(128)S(1)}, u32[]{:S(2)}, u32[]{:S(2)}) collective-permute-start(f32[128]{0:T(128)S(1)} %get-tuple-element.46), channel_id=1, source_target_pairs={{1,0},{2,1},{3,2},{0,3},{5,4},{6,5},{7,6},{4,7},{9,8},{10,9},{11,1... | collective-permute-start | bytes 1544 | tf_op jit(solution)/shard_map/ppermute | solution.py:64
  88.1 12.7 %collective-permute-start.21 = (f32[25,1024]{1,0:T(8,128)S(1)}, f32[25,1024]{1,0:T(8,128)S(1)}, u32[]{:S(2)}, u32[]{:S(2)}) collective-permute-start(f32[25,1024]{1,0:T(8,128)S(1)} %add_add_fusion.3), channel_id=1, source_target_pairs={{40,0},{44,4},{32,8},{36,12},{56,16},{60,20},{48,24},{52,28},{8,32... | collective-permute-start | bytes 307208 | tf_op jit(solution)/shard_map/ppermute | solution.py:64
  91.6 9.4 %collective-permute-start.22 = (f32[25,1024]{1,0:T(8,128)S(1)}, f32[25,1024]{1,0:T(8,128)S(1)}, u32[]{:S(2)}, u32[]{:S(2)}) collective-permute-start(f32[25,1024]{1,0:T(8,128)S(1)} %add_add_fusion.3), channel_id=1, source_target_pairs={{48,0},{52,4},{56,8},{60,12},{0,16},{4,20},{8,24},{12,28},{16,32},... | collective-permute-start | bytes 307208 | tf_op jit(solution)/shard_map/ppermute | solution.py:64
  92.0 12.7 %collective-permute-start.20 = (f32[25,1024]{1,0:T(8,128)S(1)}, f32[25,1024]{1,0:T(8,128)S(1)}, u32[]{:S(2)}, u32[]{:S(2)}) collective-permute-start(f32[25,1024]{1,0:T(8,128)S(1)} %add_add_fusion.3), channel_id=1, source_target_pairs={{16,0},{20,4},{24,8},{28,12},{32,16},{36,20},{40,24},{44,28},{48,3... | collective-permute-start | bytes 307208 | tf_op jit(solution)/shard_map/ppermute | solution.py:64
  104.7 8.0 %collective-permute-start.24 = (f32[25,1024]{1,0:T(8,128)S(1)}, f32[25,1024]{1,0:T(8,128)S(1)}, u32[]{:S(2)}, u32[]{:S(2)}) collective-permute-start(f32[25,1024]{1,0:T(8,128)S(1)} %add_add_fusion.2), channel_id=1, source_target_pairs={{128,0},{132,4},{136,8},{140,12},{144,16},{148,20},{152,24},{156,2... | collective-permute-start | bytes 307208 | tf_op jit(solution)/shard_map/ppermute | solution.py:64
  106.9 7.7 %collective-permute-start.25 = (f32[25,1024]{1,0:T(8,128)S(1)}, f32[25,1024]{1,0:T(8,128)S(1)}, u32[]{:S(2)}, u32[]{:S(2)}) collective-permute-start(f32[25,1024]{1,0:T(8,128)S(1)} %add_add_fusion.2), channel_id=1, source_target_pairs={{192,0},{196,4},{200,8},{204,12},{208,16},{212,20},{216,24},{220,2... | collective-permute-start | bytes 307208 | tf_op jit(solution)/shard_map/ppermute | solution.py:64
  108.8 6.2 %collective-permute-start.23 = (f32[25,1024]{1,0:T(8,128)S(1)}, f32[25,1024]{1,0:T(8,128)S(1)}, u32[]{:S(2)}, u32[]{:S(2)}) collective-permute-start(f32[25,1024]{1,0:T(8,128)S(1)} %add_add_fusion.2), channel_id=1, source_target_pairs={{64,0},{68,4},{72,8},{76,12},{80,16},{84,20},{88,24},{92,28},{96,3... | collective-permute-start | bytes 307208 | tf_op jit(solution)/shard_map/ppermute | solution.py:64
  (15 other events, 150.0 us)

commit v7 on v6

--- a/solution.py
+++ b/solution.py
@@ -73,7 +73,7 @@
     return count & (count - 1) == 0
 
 
-def entering(own_state, own_back, rates, rows, axis):
+def entering(own_state, own_back, rates, rows, axis, riders):
     count = lax.axis_size(axis)
     place = lax.axis_index(axis)
     incoming = jnp.zeros_like(own_state)
@@ -82,6 +82,8 @@
     stride = 1
     for radix in radices(count):
         group, digit = members(totals, axis, stride, radix)
+        if stride == 1:
+            group, riders = lax.optimization_barrier((group, riders))
         position = (place % stride).astype(jnp.float32)
         for other in range(radix):
             before = (digit > other).astype(jnp.float32)
@@ -103,7 +105,7 @@
             ) * group[other][1]
         totals = jnp.stack([forward_total, backward_total], 0)
         stride *= radix
-    return incoming, later
+    return incoming, later, riders
 
 
 def summed(value, axis):
@@ -176,7 +178,11 @@
     own_back = jnp.sum(
         jnp.exp(-mode_rates[None] * (P_SIZE * block_steps)[:, None, None]) * block_heads, axis=0
     )
-    incoming, later_state = entering(own_state, own_back, mode_rates, row_count, "ctx")
+    lead = jnp.zeros((block_count, P_SIZE - 1, chan_count), jnp.float32)
+    incoming, later_state, (late_blocks, late_grads) = entering(
+        own_state, own_back, mode_rates, row_count, "ctx", (blocks, grad_blocks)
+    )
+    late_padded = jnp.concatenate([lead, late_blocks], 1)
 
     gap = block_steps[:, None] - block_steps[None, :] - 1.0
     earlier = (gap >= 0).astype(jnp.float32)
@@ -220,7 +226,7 @@
     by_lag = jnp.stack(
         [
             jnp.sum(
-                blocks_padded[:, P_SIZE - 1 - lag : 2 * P_SIZE - 1 - lag] * grad_blocks, axis=(0, 1)
+                late_padded[:, P_SIZE - 1 - lag : 2 * P_SIZE - 1 - lag] * late_grads, axis=(0, 1)
             )
             for lag in range(P_SIZE)
         ],

time: 117 us -> 107 us (0.915)
  the two profiles are of different devices: /device:TPU:6 before, /device:TPU:32 now
where the time goes in v7:
time: 107 us
  waiting for transfers between devices  43 us (40%)
  starting transfers between devices  36.3 us (34%)
  other arithmetic  22 us (21%)
  local copies, waits for them, and re-layouts  3.68 us (3%)
  between operations  1.76 us (2%)
    ppermute x24, waiting for transfers between devices, members(): received.append(lax.ppermute(value, axis, pairs))  43 us
    ppermute x24, starting transfers between devices, members(): received.append(lax.ppermute(value, axis, pairs))  32.5 us
    ppermute x2, starting transfers between devices, passed_along(): lax.ppermute(value, axis, [(source, source + steps) for source in range(f...  3.83 us
  transfers between devices with their start and end apart: 26, of which 18 were waited for; matrix products, arithmetic and copies ran while one was open for 10% of the time, Pallas kernels for 0%

profile of v7, /device:TPU:32, one launch (start us, length us, event | category | flops | bytes accessed | tf_op | source)
XLA Modules:
  0.0 106.8 jit_solution(2962980030794209021)
XLA Ops:
  1.4 1.9 %collective-permute-start = (bf16[2,1024]{1,0:T(2,128)(2,1)S(1)}, bf16[2,1024]{1,0:T(2,128)(2,1)S(1)}, u32[]{:S(2)}, u32[]{:S(2)}) collective-permute-start(bf16[2,1024]{1,0:T(2,128)(2,1)S(1)} %slice.598), channel_id=1, source_target_pairs={{0,4},{4,8},{8,12},{12,16},{16,20},{20,24},{24,28},{28,32},{32,36}... | collective-permute-start | bytes 12296 | tf_op jit(solution)/shard_map/ppermute | solution.py:17
  5.8 2.0 %multiply_exponential_fusion = (f32[16,32,1024]{2,1,0:T(8,128)}, f32[16,32,1024]{2,1,0:T(8,128)S(1)}) fusion(f32[32]{0:T(128)S(1)} %broadcast_subtract_fusion.1, f32[16,1024]{1,0:T(8,128)S(1)} %neg.5, f32[32]{0:T(128)S(1)} %iota_convert_fusion.1), kind=kLoop, calls=%fused_computation.108 | loop fusion | flops 1048576 | bytes 4260096 | tf_op jit(solution)/shard_map/exp | solution.py:160
  8.0 2.8 %collective-permute-start.1 = (f32[130]{0:T(256)S(1)}, f32[130]{0:T(256)S(1)}, u32[]{:S(2)}, u32[]{:S(2)}) collective-permute-start(f32[130]{0:T(256)S(1)} %fusion.3), channel_id=1, source_target_pairs={{1,0},{2,1},{3,2},{0,3},{5,4},{6,5},{7,6},{4,7},{9,8},{10,9},{11,1... | collective-permute-start | bytes 1568 | tf_op jit(solution)/shard_map/ppermute | solution.py:64
  12.5 3.4 %collective-permute-done.2 = f32[130]{0:T(256)S(1)} collective-permute-done((f32[130]{0:T(256)S(1)}, f32[130]{0:T(256)S(1)}, u32[]{:S(2)}, u32[]{:S(2)}) %collective-permute-start.2) | collective-permute-done | bytes 552 | tf_op jit(solution)/shard_map/ppermute | solution.py:64
  21.3 1.9 %collective-permute-start.5 = (f32[2,16,1024]{2,1,0:T(8,128)S(1)}, f32[2,16,1024]{2,1,0:T(8,128)S(1)}, u32[]{:S(2)}, u32[]{:S(2)}) collective-permute-start(f32[2,16,1024]{2,1,0:T(8,128)S(1)} %pad_maximum_fusion.3), channel_id=1, source_target_pairs={{8,0},{12,4},{0,8},{4,12},{24,16},{28,20},{16,24},{20,28},{40,32},... | collective-permute-start | bytes 393224 | tf_op jit(solution)/shard_map/ppermute | solution.py:64
  25.2 4.8 %collective-permute-done.5 = f32[2,16,1024]{2,1,0:T(8,128)S(1)} collective-permute-done((f32[2,16,1024]{2,1,0:T(8,128)S(1)}, f32[2,16,1024]{2,1,0:T(8,128)S(1)}, u32[]{:S(2)}, u32[]{:S(2)}) %collective-permute-start.5) | collective-permute-done | bytes 131104 | tf_op jit(solution)/shard_map/ppermute | solution.py:64
  30.2 4.9 %collective-permute-start.7 = (f32[2,16,1024]{2,1,0:T(8,128)S(1)}, f32[2,16,1024]{2,1,0:T(8,128)S(1)}, u32[]{:S(2)}, u32[]{:S(2)}) collective-permute-start(f32[2,16,1024]{2,1,0:T(8,128)S(1)} %pad_maximum_fusion.4), channel_id=1, source_target_pairs={{16,0},{20,4},{24,8},{28,12},{32,16},{36,20},{40,24},{44,28},{48,3... | collective-permute-start | bytes 393224 | tf_op jit(solution)/shard_map/ppermute | solution.py:64
  36.3 2.4 %collective-permute-start.9 = (f32[2,16,1024]{2,1,0:T(8,128)S(1)}, f32[2,16,1024]{2,1,0:T(8,128)S(1)}, u32[]{:S(2)}, u32[]{:S(2)}) collective-permute-start(f32[2,16,1024]{2,1,0:T(8,128)S(1)} %pad_maximum_fusion.4), channel_id=1, source_target_pairs={{48,0},{52,4},{56,8},{60,12},{0,16},{4,20},{8,24},{12,28},{16,32},... | collective-permute-start | bytes 393224 | tf_op jit(solution)/shard_map/ppermute | solution.py:64
  42.1 5.7 %collective-permute-done.8 = f32[2,16,1024]{2,1,0:T(8,128)S(1)} collective-permute-done((f32[2,16,1024]{2,1,0:T(8,128)S(1)}, f32[2,16,1024]{2,1,0:T(8,128)S(1)}, u32[]{:S(2)}, u32[]{:S(2)}) %collective-permute-start.8) | collective-permute-done | bytes 131104 | tf_op jit(solution)/shard_map/ppermute | solution.py:64
  48.3 3.1 %collective-permute-start.10 = (f32[2,16,1024]{2,1,0:T(8,128)S(1)}, f32[2,16,1024]{2,1,0:T(8,128)S(1)}, u32[]{:S(2)}, u32[]{:S(2)}) collective-permute-start(f32[2,16,1024]{2,1,0:T(8,128)S(1)} %pad_maximum_fusion.5), channel_id=1, source_target_pairs={{64,0},{68,4},{72,8},{76,12},{80,16},{84,20},{88,24},{92,28},{96,3... | collective-permute-start | bytes 393224 | tf_op jit(solution)/shard_map/ppermute | solution.py:64
  53.1 4.1 %collective-permute-done.10 = f32[2,16,1024]{2,1,0:T(8,128)S(1)} collective-permute-done((f32[2,16,1024]{2,1,0:T(8,128)S(1)}, f32[2,16,1024]{2,1,0:T(8,128)S(1)}, u32[]{:S(2)}, u32[]{:S(2)}) %collective-permute-start.10) | collective-permute-done | bytes 131104 | tf_op jit(solution)/shard_map/ppermute | solution.py:64
  57.2 2.1 %collective-permute-done.11 = f32[2,16,1024]{2,1,0:T(8,128)S(1)} collective-permute-done((f32[2,16,1024]{2,1,0:T(8,128)S(1)}, f32[2,16,1024]{2,1,0:T(8,128)S(1)}, u32[]{:S(2)}, u32[]{:S(2)}) %collective-permute-start.11) | collective-permute-done | bytes 131104 | tf_op jit(solution)/shard_map/ppermute | solution.py:64
  62.9 1.9 %fusion.150 = f32[4,32,1024]{2,1,0:T(8,128)S(1)} fusion(f32[4,32,1024]{2,1,0:T(8,128)S(1)} %multiply_reduce_fusion, f32[4,32,1024]{2,1,0:T(8,128)S(1)} %bitcast.403, f32[1024]{0:T(1024)S(1)} %bitcast.418, f32[1024]{0:T(1024)S(1)} %bitcast.420, f32[1024]{0:T(1024)S(1)} %bitcast.422, f32[1024]{0:T(1024)S(1)} %bitcast.424, f32[1024]{0:T(1024)S(1)} %bitcast.426, ...), kind=kLoop, calls=%fused_computation.275 | loop fusion | flops 8388608 | bytes 1703936 | tf_op jit(solution)/shard_map/add | solution.py:220
  64.7 1.7 %fusion.87 = f32[4,32,1024]{2,1,0:T(8,128)S(1)} fusion(f32[4,32,1024]{2,1,0:T(8,128)S(1)} %multiply_reduce_fusion.1, f32[4,32,1024]{2,1,0:T(8,128)S(1)} %bitcast_convert_fusion, f32[1024]{0:T(1024)S(1)} %bitcast.419, f32[1024]{0:T(1024)S(1)} %bitcast.421, f32[1024]{0:T(1024)S(1)} %bitcast.423, f32[1024]{0:T(1024)S(1)} %bitcast.425, f32[1024]{0:T(1024)S(1)} %bitcast.427, ...), kind=kLoop, calls=%fused_computation.212 | loop fusion | flops 8388608 | bytes 1703936 | tf_op jit(solution)/shard_map/add | solution.py:212
  68.5 1.9 %collective-permute-start.13 = (bf16[3,2,1024]{2,1,0:T(2,128)(2,1)S(1)}, bf16[3,2,1024]{2,1,0:T(2,128)(2,1)S(1)}, u32[]{:S(2)}, u32[]{:S(2)}) collective-permute-start(bf16[3,2,1024]{2,1,0:T(2,128)(2,1)S(1)} %slice.827), channel_id=1, source_target_pairs={{4,0},{8,4},{12,8},{16,12},{20,16},{24,20},{28,24},{32,28},{36,32}... | collective-permute-start | bytes 36872 | tf_op jit(solution)/shard_map/ppermute | solution.py:17
  70.6 2.1 %collective-permute-start.18 = (f32[25,1024]{1,0:T(8,128)S(1)}, f32[25,1024]{1,0:T(8,128)S(1)}, u32[]{:S(2)}, u32[]{:S(2)}) collective-permute-start(f32[25,1024]{1,0:T(8,128)S(1)} %pad_maximum_fusion.6), channel_id=1, source_target_pairs={{8,0},{12,4},{0,8},{4,12},{24,16},{28,20},{16,24},{20,28},{40,32},... | collective-permute-start | bytes 307208 | tf_op jit(solution)/shard_map/ppermute | solution.py:64
  75.7 3.6 %collective-permute-done.18 = f32[25,1024]{1,0:T(8,128)S(1)} collective-permute-done((f32[25,1024]{1,0:T(8,128)S(1)}, f32[25,1024]{1,0:T(8,128)S(1)}, u32[]{:S(2)}, u32[]{:S(2)}) %collective-permute-start.18) | collective-permute-done | bytes 102432 | tf_op jit(solution)/shard_map/ppermute | solution.py:64
  79.4 1.7 %collective-permute-start.20 = (f32[25,1024]{1,0:T(8,128)S(1)}, f32[25,1024]{1,0:T(8,128)S(1)}, u32[]{:S(2)}, u32[]{:S(2)}) collective-permute-start(f32[25,1024]{1,0:T(8,128)S(1)} %add_add_fusion.2), channel_id=1, source_target_pairs={{16,0},{20,4},{24,8},{28,12},{32,16},{36,20},{40,24},{44,28},{48,3... | collective-permute-start | bytes 307208 | tf_op jit(solution)/shard_map/ppermute | solution.py:64
  81.2 2.8 %collective-permute-start.21 = (f32[25,1024]{1,0:T(8,128)S(1)}, f32[25,1024]{1,0:T(8,128)S(1)}, u32[]{:S(2)}, u32[]{:S(2)}) collective-permute-start(f32[25,1024]{1,0:T(8,128)S(1)} %add_add_fusion.2), channel_id=1, source_target_pairs={{40,0},{44,4},{32,8},{36,12},{56,16},{60,20},{48,24},{52,28},{8,32... | collective-permute-start | bytes 307208 | tf_op jit(solution)/shard_map/ppermute | solution.py:64
  86.9 7.7 %collective-permute-done.21 = f32[25,1024]{1,0:T(8,128)S(1)} collective-permute-done((f32[25,1024]{1,0:T(8,128)S(1)}, f32[25,1024]{1,0:T(8,128)S(1)}, u32[]{:S(2)}, u32[]{:S(2)}) %collective-permute-start.21) | collective-permute-done | bytes 102432 | tf_op jit(solution)/shard_map/ppermute | solution.py:64
  96.0 2.1 %collective-permute-start.24 = (f32[25,1024]{1,0:T(8,128)S(1)}, f32[25,1024]{1,0:T(8,128)S(1)}, u32[]{:S(2)}, u32[]{:S(2)}) collective-permute-start(f32[25,1024]{1,0:T(8,128)S(1)} %add_add_fusion.1), channel_id=1, source_target_pairs={{128,0},{132,4},{136,8},{140,12},{144,16},{148,20},{152,24},{156,2... | collective-permute-start | bytes 307208 | tf_op jit(solution)/shard_map/ppermute | solution.py:64
  99.0 2.1 %collective-permute-done.23 = f32[25,1024]{1,0:T(8,128)S(1)} collective-permute-done((f32[25,1024]{1,0:T(8,128)S(1)}, f32[25,1024]{1,0:T(8,128)S(1)}, u32[]{:S(2)}, u32[]{:S(2)}) %collective-permute-start.23) | collective-permute-done | bytes 102432 | tf_op jit(solution)/shard_map/ppermute | solution.py:64
  101.2 2.3 %collective-permute-done.24 = f32[25,1024]{1,0:T(8,128)S(1)} collective-permute-done((f32[25,1024]{1,0:T(8,128)S(1)}, f32[25,1024]{1,0:T(8,128)S(1)}, u32[]{:S(2)}, u32[]{:S(2)}) %collective-permute-start.24) | collective-permute-done | bytes 102432 | tf_op jit(solution)/shard_map/ppermute | solution.py:64
  103.5 1.9 %collective-permute-done.25 = f32[25,1024]{1,0:T(8,128)S(1)} collective-permute-done((f32[25,1024]{1,0:T(8,128)S(1)}, f32[25,1024]{1,0:T(8,128)S(1)}, u32[]{:S(2)}, u32[]{:S(2)}) %collective-permute-start.25) | collective-permute-done | bytes 102432 | tf_op jit(solution)/shard_map/ppermute | solution.py:64
  (128 shorter events, 33.8 us)
Async XLA Ops:
  1.4 6.4 %collective-permute-start = (bf16[2,1024]{1,0:T(2,128)(2,1)S(1)}, bf16[2,1024]{1,0:T(2,128)(2,1)S(1)}, u32[]{:S(2)}, u32[]{:S(2)}) collective-permute-start(bf16[2,1024]{1,0:T(2,128)(2,1)S(1)} %slice.598), channel_id=1, source_target_pairs={{0,4},{4,8},{8,12},{12,16},{16,20},{20,24},{24,28},{28,32},{32,36}... | collective-permute-start | bytes 12296 | tf_op jit(solution)/shard_map/ppermute | solution.py:17
  8.0 4.5 %collective-permute-start.1 = (f32[130]{0:T(256)S(1)}, f32[130]{0:T(256)S(1)}, u32[]{:S(2)}, u32[]{:S(2)}) collective-permute-start(f32[130]{0:T(256)S(1)} %fusion.3), channel_id=1, source_target_pairs={{1,0},{2,1},{3,2},{0,3},{5,4},{6,5},{7,6},{4,7},{9,8},{10,9},{11,1... | collective-permute-start | bytes 1568 | tf_op jit(solution)/shard_map/ppermute | solution.py:64
  10.8 5.1 %collective-permute-start.2 = (f32[130]{0:T(256)S(1)}, f32[130]{0:T(256)S(1)}, u32[]{:S(2)}, u32[]{:S(2)}) collective-permute-start(f32[130]{0:T(256)S(1)} %fusion.3), channel_id=1, source_target_pairs={{2,0},{3,1},{0,2},{1,3},{6,4},{7,5},{4,6},{5,7},{10,8},{11,9},{8,1... | collective-permute-start | bytes 1568 | tf_op jit(solution)/shard_map/ppermute | solution.py:64
  11.6 4.8 %collective-permute-start.3 = (f32[130]{0:T(256)S(1)}, f32[130]{0:T(256)S(1)}, u32[]{:S(2)}, u32[]{:S(2)}) collective-permute-start(f32[130]{0:T(256)S(1)} %fusion.3), channel_id=1, source_target_pairs={{3,0},{0,1},{1,2},{2,3},{7,4},{4,5},{5,6},{6,7},{11,8},{8,9},{9,10... | collective-permute-start | bytes 1568 | tf_op jit(solution)/shard_map/ppermute | solution.py:64
  21.3 8.7 %collective-permute-start.5 = (f32[2,16,1024]{2,1,0:T(8,128)S(1)}, f32[2,16,1024]{2,1,0:T(8,128)S(1)}, u32[]{:S(2)}, u32[]{:S(2)}) collective-permute-start(f32[2,16,1024]{2,1,0:T(8,128)S(1)} %pad_maximum_fusion.3), channel_id=1, source_target_pairs={{8,0},{12,4},{0,8},{4,12},{24,16},{28,20},{16,24},{20,28},{40,32},... | collective-permute-start | bytes 393224 | tf_op jit(solution)/shard_map/ppermute | solution.py:64
  23.2 6.8 %collective-permute-start.6 = (f32[2,16,1024]{2,1,0:T(8,128)S(1)}, f32[2,16,1024]{2,1,0:T(8,128)S(1)}, u32[]{:S(2)}, u32[]{:S(2)}) collective-permute-start(f32[2,16,1024]{2,1,0:T(8,128)S(1)} %pad_maximum_fusion.3), channel_id=1, source_target_pairs={{12,0},{0,4},{4,8},{8,12},{28,16},{16,20},{20,24},{24,28},{44,32},... | collective-permute-start | bytes 393224 | tf_op jit(solution)/shard_map/ppermute | solution.py:64
  30.2 11.9 %collective-permute-start.7 = (f32[2,16,1024]{2,1,0:T(8,128)S(1)}, f32[2,16,1024]{2,1,0:T(8,128)S(1)}, u32[]{:S(2)}, u32[]{:S(2)}) collective-permute-start(f32[2,16,1024]{2,1,0:T(8,128)S(1)} %pad_maximum_fusion.4), channel_id=1, source_target_pairs={{16,0},{20,4},{24,8},{28,12},{32,16},{36,20},{40,24},{44,28},{48,3... | collective-permute-start | bytes 393224 | tf_op jit(solution)/shard_map/ppermute | solution.py:64
  35.1 12.6 %collective-permute-start.8 = (f32[2,16,1024]{2,1,0:T(8,128)S(1)}, f32[2,16,1024]{2,1,0:T(8,128)S(1)}, u32[]{:S(2)}, u32[]{:S(2)}) collective-permute-start(f32[2,16,1024]{2,1,0:T(8,128)S(1)} %pad_maximum_fusion.4), channel_id=1, source_target_pairs={{40,0},{44,4},{32,8},{36,12},{56,16},{60,20},{48,24},{52,28},{8,32... | collective-permute-start | bytes 393224 | tf_op jit(solution)/shard_map/ppermute | solution.py:64
  36.3 11.9 %collective-permute-start.9 = (f32[2,16,1024]{2,1,0:T(8,128)S(1)}, f32[2,16,1024]{2,1,0:T(8,128)S(1)}, u32[]{:S(2)}, u32[]{:S(2)}) collective-permute-start(f32[2,16,1024]{2,1,0:T(8,128)S(1)} %pad_maximum_fusion.4), channel_id=1, source_target_pairs={{48,0},{52,4},{56,8},{60,12},{0,16},{4,20},{8,24},{12,28},{16,32},... | collective-permute-start | bytes 393224 | tf_op jit(solution)/shard_map/ppermute | solution.py:64
  48.3 8.9 %collective-permute-start.10 = (f32[2,16,1024]{2,1,0:T(8,128)S(1)}, f32[2,16,1024]{2,1,0:T(8,128)S(1)}, u32[]{:S(2)}, u32[]{:S(2)}) collective-permute-start(f32[2,16,1024]{2,1,0:T(8,128)S(1)} %pad_maximum_fusion.5), channel_id=1, source_target_pairs={{64,0},{68,4},{72,8},{76,12},{80,16},{84,20},{88,24},{92,28},{96,3... | collective-permute-start | bytes 393224 | tf_op jit(solution)/shard_map/ppermute | solution.py:64
  51.4 7.9 %collective-permute-start.11 = (f32[2,16,1024]{2,1,0:T(8,128)S(1)}, f32[2,16,1024]{2,1,0:T(8,128)S(1)}, u32[]{:S(2)}, u32[]{:S(2)}) collective-permute-start(f32[2,16,1024]{2,1,0:T(8,128)S(1)} %pad_maximum_fusion.5), channel_id=1, source_target_pairs={{128,0},{132,4},{136,8},{140,12},{144,16},{148,20},{152,24},{156,2... | collective-permute-start | bytes 393224 | tf_op jit(solution)/shard_map/ppermute | solution.py:64
  52.1 8.9 %collective-permute-start.12 = (f32[2,16,1024]{2,1,0:T(8,128)S(1)}, f32[2,16,1024]{2,1,0:T(8,128)S(1)}, u32[]{:S(2)}, u32[]{:S(2)}) collective-permute-start(f32[2,16,1024]{2,1,0:T(8,128)S(1)} %pad_maximum_fusion.5), channel_id=1, source_target_pairs={{192,0},{196,4},{200,8},{204,12},{208,16},{212,20},{216,24},{220,2... | collective-permute-start | bytes 393224 | tf_op jit(solution)/shard_map/ppermute | solution.py:64
  68.5 4.4 %collective-permute-start.13 = (bf16[3,2,1024]{2,1,0:T(2,128)(2,1)S(1)}, bf16[3,2,1024]{2,1,0:T(2,128)(2,1)S(1)}, u32[]{:S(2)}, u32[]{:S(2)}) collective-permute-start(bf16[3,2,1024]{2,1,0:T(2,128)(2,1)S(1)} %slice.827), channel_id=1, source_target_pairs={{4,0},{8,4},{12,8},{16,12},{20,16},{24,20},{28,24},{32,28},{36,32}... | collective-permute-start | bytes 36872 | tf_op jit(solution)/shard_map/ppermute | solution.py:17
  70.6 8.8 %collective-permute-start.18 = (f32[25,1024]{1,0:T(8,128)S(1)}, f32[25,1024]{1,0:T(8,128)S(1)}, u32[]{:S(2)}, u32[]{:S(2)}) collective-permute-start(f32[25,1024]{1,0:T(8,128)S(1)} %pad_maximum_fusion.6), channel_id=1, source_target_pairs={{8,0},{12,4},{0,8},{4,12},{24,16},{28,20},{16,24},{20,28},{40,32},... | collective-permute-start | bytes 307208 | tf_op jit(solution)/shard_map/ppermute | solution.py:64
  72.7 6.7 %collective-permute-start.19 = (f32[25,1024]{1,0:T(8,128)S(1)}, f32[25,1024]{1,0:T(8,128)S(1)}, u32[]{:S(2)}, u32[]{:S(2)}) collective-permute-start(f32[25,1024]{1,0:T(8,128)S(1)} %pad_maximum_fusion.6), channel_id=1, source_target_pairs={{12,0},{0,4},{4,8},{8,12},{28,16},{16,20},{20,24},{24,28},{44,32},... | collective-permute-start | bytes 307208 | tf_op jit(solution)/shard_map/ppermute | solution.py:64
  73.6 10.4 %collective-permute-start.14 = (f32[128]{0:T(128)S(1)}, f32[128]{0:T(128)S(1)}, u32[]{:S(2)}, u32[]{:S(2)}) collective-permute-start(f32[128]{0:T(128)S(1)} %get-tuple-element.59), channel_id=1, source_target_pairs={{1,0},{2,1},{3,2},{0,3},{5,4},{6,5},{7,6},{4,7},{9,8},{10,9},{11,1... | collective-permute-start | bytes 1544 | tf_op jit(solution)/shard_map/ppermute | solution.py:64
  74.0 11.1 %collective-permute-start.15 = (f32[128]{0:T(128)S(1)}, f32[128]{0:T(128)S(1)}, u32[]{:S(2)}, u32[]{:S(2)}) collective-permute-start(f32[128]{0:T(128)S(1)} %get-tuple-element.59), channel_id=1, source_target_pairs={{2,0},{3,1},{0,2},{1,3},{6,4},{7,5},{4,6},{5,7},{10,8},{11,9},{8,1... | collective-permute-start | bytes 1544 | tf_op jit(solution)/shard_map/ppermute | solution.py:64
  74.5 10.7 %collective-permute-start.16 = (f32[128]{0:T(128)S(1)}, f32[128]{0:T(128)S(1)}, u32[]{:S(2)}, u32[]{:S(2)}) collective-permute-start(f32[128]{0:T(128)S(1)} %get-tuple-element.59), channel_id=1, source_target_pairs={{3,0},{0,1},{1,2},{2,3},{7,4},{4,5},{5,6},{6,7},{11,8},{8,9},{9,10... | collective-permute-start | bytes 1544 | tf_op jit(solution)/shard_map/ppermute | solution.py:64
  79.4 7.5 %collective-permute-start.20 = (f32[25,1024]{1,0:T(8,128)S(1)}, f32[25,1024]{1,0:T(8,128)S(1)}, u32[]{:S(2)}, u32[]{:S(2)}) collective-permute-start(f32[25,1024]{1,0:T(8,128)S(1)} %add_add_fusion.2), channel_id=1, source_target_pairs={{16,0},{20,4},{24,8},{28,12},{32,16},{36,20},{40,24},{44,28},{48,3... | collective-permute-start | bytes 307208 | tf_op jit(solution)/shard_map/ppermute | solution.py:64
  81.2 13.5 %collective-permute-start.21 = (f32[25,1024]{1,0:T(8,128)S(1)}, f32[25,1024]{1,0:T(8,128)S(1)}, u32[]{:S(2)}, u32[]{:S(2)}) collective-permute-start(f32[25,1024]{1,0:T(8,128)S(1)} %add_add_fusion.2), channel_id=1, source_target_pairs={{40,0},{44,4},{32,8},{36,12},{56,16},{60,20},{48,24},{52,28},{8,32... | collective-permute-start | bytes 307208 | tf_op jit(solution)/shard_map/ppermute | solution.py:64
  84.0 11.3 %collective-permute-start.22 = (f32[25,1024]{1,0:T(8,128)S(1)}, f32[25,1024]{1,0:T(8,128)S(1)}, u32[]{:S(2)}, u32[]{:S(2)}) collective-permute-start(f32[25,1024]{1,0:T(8,128)S(1)} %add_add_fusion.2), channel_id=1, source_target_pairs={{48,0},{52,4},{56,8},{60,12},{0,16},{4,20},{8,24},{12,28},{16,32},... | collective-permute-start | bytes 307208 | tf_op jit(solution)/shard_map/ppermute | solution.py:64
  95.4 5.8 %collective-permute-start.23 = (f32[25,1024]{1,0:T(8,128)S(1)}, f32[25,1024]{1,0:T(8,128)S(1)}, u32[]{:S(2)}, u32[]{:S(2)}) collective-permute-start(f32[25,1024]{1,0:T(8,128)S(1)} %add_add_fusion.1), channel_id=1, source_target_pairs={{64,0},{68,4},{72,8},{76,12},{80,16},{84,20},{88,24},{92,28},{96,3... | collective-permute-start | bytes 307208 | tf_op jit(solution)/shard_map/ppermute | solution.py:64
  96.0 7.4 %collective-permute-start.24 = (f32[25,1024]{1,0:T(8,128)S(1)}, f32[25,1024]{1,0:T(8,128)S(1)}, u32[]{:S(2)}, u32[]{:S(2)}) collective-permute-start(f32[25,1024]{1,0:T(8,128)S(1)} %add_add_fusion.1), channel_id=1, source_target_pairs={{128,0},{132,4},{136,8},{140,12},{144,16},{148,20},{152,24},{156,2... | collective-permute-start | bytes 307208 | tf_op jit(solution)/shard_map/ppermute | solution.py:64
  98.2 7.2 %collective-permute-start.25 = (f32[25,1024]{1,0:T(8,128)S(1)}, f32[25,1024]{1,0:T(8,128)S(1)}, u32[]{:S(2)}, u32[]{:S(2)}) collective-permute-start(f32[25,1024]{1,0:T(8,128)S(1)} %add_add_fusion.1), channel_id=1, source_target_pairs={{192,0},{196,4},{200,8},{204,12},{208,16},{212,20},{216,24},{220,2... | collective-permute-start | bytes 307208 | tf_op jit(solution)/shard_map/ppermute | solution.py:64
  (17 other events, 88.7 us)

commit v8 on v7

--- a/solution.py
+++ b/solution.py
@@ -129,11 +129,37 @@
     total_chans = chan_count * lax.axis_size("ch")
     total_rows = row_count * lax.axis_size("ctx")
     stream_wide = stream.astype(jnp.float32)
-    rim_rows = passed_along(stream[row_count - (KS - 1) :], "ctx", 1)
-    with_rim = jnp.concatenate([rim_rows, stream], 0).astype(jnp.float32)
-    squares = summed(jnp.sum(with_rim * with_rim, axis=1), "ch")
-    scale_with_rim = lax.rsqrt(squares / total_chans + EPSILON)
-    row_scale = scale_with_rim[KS - 1 :]
+    ch_count = lax.axis_size("ch")
+    ctx_count = lax.axis_size("ctx")
+    ch_place = lax.axis_index("ch")
+    rim_raw = stream[row_count - (KS - 1) :]
+    shards = []
+    for step in range(ch_count):
+        pairs = [
+            ((place - 1) * ch_count + (shard + step) % ch_count, place * ch_count + shard)
+            for place in range(1, ctx_count)
+            for shard in range(ch_count)
+        ]
+        shards.append(lax.ppermute(rim_raw, ("ctx", "ch"), pairs))
+    shard_sums = [jnp.sum(jnp.square(s.astype(jnp.float32)), axis=1) for s in shards]
+    ordered = [
+        lax.select_n(((position - ch_place) % ch_count).astype(jnp.int32), *shard_sums)
+        for position in range(ch_count)
+    ]
+    while len(ordered) > 1:
+        radix = radices(len(ordered))[0]
+        ordered = [
+            (ordered[i] + ordered[i + 1]) + (ordered[i + 2] + ordered[i + 3])
+            if radix == 4
+            else ordered[i] + ordered[i + 1]
+            for i in range(0, len(ordered), radix)
+        ]
+    rim_squares = ordered[0]
+    rim_scale = lax.rsqrt(rim_squares / total_chans + EPSILON)
+    squares = summed(jnp.sum(stream_wide * stream_wide, axis=1), "ch")
+    row_scale = lax.rsqrt(squares / total_chans + EPSILON)
+    with_rim = jnp.concatenate([shards[0].astype(jnp.float32), stream_wide], 0)
+    scale_with_rim = jnp.concatenate([rim_scale, row_scale], 0)
     padded_half = lax.optimization_barrier(
         (with_rim * scale_with_rim[:, None] * norm_gain[None, :]).astype(jnp.bfloat16)
     )

time: 107 us -> 126 us (1.18); the launches traced: 107 us -> 124 us
  starting transfers between devices: 36.3 us -> 50.4 us
  waiting for transfers between devices: 43 us -> 31.5 us
  other arithmetic: 22 us -> 31.8 us
  local copies, waits for them, and re-layouts: 3.68 us -> 9.3 us
    ppermute x0 -> x4, starting transfers between devices: none -> 15.6 us  [per_device(): shards.append(lax.ppermute(rim_raw, ('ctx', 'ch'), pairs))]
    ppermute x24, waiting for transfers between devices: 43 us -> 30.6 us  [members(): received.append(lax.ppermute(value, axis, pairs))]
    another operation x1, local copies, waits for them, and re-layouts: 0.24 us -> 5.49 us  [per_device(): jnp.stack([jnp.sum(late_padded[:, P_SIZE - 1 - lag:2 * P_SIZE - 1 - lag]...]
    select_n x6, other arithmetic: 0.24 us -> 2.23 us  [members(): lax.select_n(((position - digit) % radix).astype(jnp.int32), *received)]
    ppermute x2 -> x1, starting transfers between devices: 3.83 us -> 1.92 us  [passed_along(): lax.ppermute(value, axis, [(source, source + steps) for source in range(f...]
    mul x1, other arithmetic: 1.2 us -> 2.81 us  [per_device(): jnp.exp(-mode_rates[:, None, :] * (P_SIZE - steps)[None, :, None])]
    reduce_sum x1 -> x5, other arithmetic: 0.18 us -> 1.57 us  [the longest x1 1.08 us: per_device(): squares = summed(jnp.sum(stream_wide * stream_wide, axis=1), 'ch')]
  transfers between devices with their start and end apart: 26 -> 29, of which waited for: 18 -> 13; matrix products, arithmetic and copies ran while one was open for 10% -> 19% of each run, Pallas kernels for 0% -> 0%
where the time goes in v8:
time: 126 us; the launch traced here: 124 us
  starting transfers between devices  50.4 us (40%)
  other arithmetic  31.8 us (25%)
  waiting for transfers between devices  31.5 us (25%)
  local copies, waits for them, and re-layouts  9.3 us (7%)
  between operations  1.51 us (1%)
    ppermute x24, starting transfers between devices, members(): received.append(lax.ppermute(value, axis, pairs))  32.9 us
    ppermute x24, waiting for transfers between devices, members(): received.append(lax.ppermute(value, axis, pairs))  30.6 us
    ppermute x4, starting transfers between devices, per_device(): shards.append(lax.ppermute(rim_raw, ('ctx', 'ch'), pairs))  15.6 us
    another operation x1, local copies, waits for them, and re-layouts, per_device(): jnp.stack([jnp.sum(late_padded[:, P_SIZE - 1 - lag:2 * P_SIZE - 1 - lag]...  5.49 us
    reduce_sum x2, other arithmetic, per_device(): jnp.sum(late_padded[:, P_SIZE - 1 - lag:2 * P_SIZE - 1 - lag] * late_grad...  2.91 us
    mul x1, other arithmetic, per_device(): jnp.exp(-mode_rates[:, None, :] * (P_SIZE - steps)[None, :, None])  2.81 us
  transfers between devices with their start and end apart: 29, of which 13 were waited for; matrix products, arithmetic and copies ran while one was open for 19% of the time, Pallas kernels for 0%

profile of v8, /device:TPU:32, one launch (start us, length us, event | category | flops | bytes accessed | tf_op | source)
XLA Modules:
  0.0 124.5 jit_solution(5249366762218833272)
XLA Ops:
  1.4 1.9 %collective-permute-start = (bf16[2,1024]{1,0:T(2,128)(2,1)S(1)}, bf16[2,1024]{1,0:T(2,128)(2,1)S(1)}, u32[]{:S(2)}, u32[]{:S(2)}) collective-permute-start(bf16[2,1024]{1,0:T(2,128)(2,1)S(1)} %slice.595), channel_id=1, source_target_pairs={{0,4},{1,5},{2,6},{3,7},{4,8},{5,9},{6,10},{7,11},{8,12},{9,13},{1... | collective-permute-start | bytes 12296 | tf_op jit(solution)/shard_map/ppermute | solution.py:143
  3.3 5.0 %collective-permute-start.3 = (bf16[2,1024]{1,0:T(2,128)(2,1)S(1)}, bf16[2,1024]{1,0:T(2,128)(2,1)S(1)}, u32[]{:S(2)}, u32[]{:S(2)}) collective-permute-start(bf16[2,1024]{1,0:T(2,128)(2,1)S(1)} %slice.595), channel_id=1, source_target_pairs={{3,4},{0,5},{1,6},{2,7},{7,8},{4,9},{5,10},{6,11},{11,12},{8,13},{... | collective-permute-start | bytes 12296 | tf_op jit(solution)/shard_map/ppermute | solution.py:143
  9.4 1.8 %collective-permute-start.4 = (f32[128]{0:T(128)S(1)}, f32[128]{0:T(128)S(1)}, u32[]{:S(2)}, u32[]{:S(2)}) collective-permute-start(f32[128]{0:T(128)S(1)} %multiply_reduce_fusion.10), channel_id=1, source_target_pairs={{1,0},{2,1},{3,2},{0,3},{5,4},{6,5},{7,6},{4,7},{9,8},{10,9},{11,1... | collective-permute-start | bytes 1544 | tf_op jit(solution)/shard_map/ppermute | solution.py:64
  18.7 2.0 %multiply_exponential_fusion = (f32[16,32,1024]{2,1,0:T(8,128)}, f32[16,32,1024]{2,1,0:T(8,128)S(1)}) fusion(f32[32]{0:T(128)S(1)} %broadcast_subtract_fusion.1, f32[16,1024]{1,0:T(8,128)S(1)} %neg.5, f32[32]{0:T(128)S(1)} %iota_convert_fusion.1), kind=kLoop, calls=%fused_computation.108 | loop fusion | flops 1048576 | bytes 4260096 | tf_op jit(solution)/shard_map/exp | solution.py:186
  20.7 2.5 %collective-permute-start.2 = (bf16[2,1024]{1,0:T(2,128)(2,1)S(1)}, bf16[2,1024]{1,0:T(2,128)(2,1)S(1)}, u32[]{:S(2)}, u32[]{:S(2)}) collective-permute-start(bf16[2,1024]{1,0:T(2,128)(2,1)S(1)} %slice.595), channel_id=1, source_target_pairs={{2,4},{3,5},{0,6},{1,7},{6,8},{7,9},{4,10},{5,11},{10,12},{11,13},... | collective-permute-start | bytes 12296 | tf_op jit(solution)/shard_map/ppermute | solution.py:143
  23.3 6.1 %collective-permute-start.1 = (bf16[2,1024]{1,0:T(2,128)(2,1)S(1)}, bf16[2,1024]{1,0:T(2,128)(2,1)S(1)}, u32[]{:S(2)}, u32[]{:S(2)}) collective-permute-start(bf16[2,1024]{1,0:T(2,128)(2,1)S(1)} %slice.595), channel_id=1, source_target_pairs={{1,4},{2,5},{3,6},{0,7},{5,8},{6,9},{7,10},{4,11},{9,12},{10,13},{... | collective-permute-start | bytes 12296 | tf_op jit(solution)/shard_map/ppermute | solution.py:143
  35.9 1.9 %collective-permute-start.8 = (f32[2,16,1024]{2,1,0:T(8,128)S(1)}, f32[2,16,1024]{2,1,0:T(8,128)S(1)}, u32[]{:S(2)}, u32[]{:S(2)}) collective-permute-start(f32[2,16,1024]{2,1,0:T(8,128)S(1)} %pad_maximum_fusion.2), channel_id=1, source_target_pairs={{8,0},{12,4},{0,8},{4,12},{24,16},{28,20},{16,24},{20,28},{40,32},... | collective-permute-start | bytes 393224 | tf_op jit(solution)/shard_map/ppermute | solution.py:64
  39.8 4.8 %collective-permute-done.8 = f32[2,16,1024]{2,1,0:T(8,128)S(1)} collective-permute-done((f32[2,16,1024]{2,1,0:T(8,128)S(1)}, f32[2,16,1024]{2,1,0:T(8,128)S(1)}, u32[]{:S(2)}, u32[]{:S(2)}) %collective-permute-start.8) | collective-permute-done | bytes 131104 | tf_op jit(solution)/shard_map/ppermute | solution.py:64
  46.0 3.0 %collective-permute-start.10 = (f32[2,16,1024]{2,1,0:T(8,128)}, f32[2,16,1024]{2,1,0:T(8,128)}, u32[]{:S(2)}, u32[]{:S(2)}) collective-permute-start(f32[2,16,1024]{2,1,0:T(8,128)} %pad_maximum_fusion.3), channel_id=1, source_target_pairs={{16,0},{20,4},{24,8},{28,12},{32,16},{36,20},{40,24},{44,28},{48,3... | collective-permute-start | bytes 393224 | tf_op jit(solution)/shard_map/ppermute | solution.py:64
  49.0 3.7 %collective-permute-start.11 = (f32[2,16,1024]{2,1,0:T(8,128)}, f32[2,16,1024]{2,1,0:T(8,128)}, u32[]{:S(2)}, u32[]{:S(2)}) collective-permute-start(f32[2,16,1024]{2,1,0:T(8,128)} %pad_maximum_fusion.3), channel_id=1, source_target_pairs={{40,0},{44,4},{32,8},{36,12},{56,16},{60,20},{48,24},{52,28},{8,32... | collective-permute-start | bytes 393224 | tf_op jit(solution)/shard_map/ppermute | solution.py:64
  56.6 5.5 %stack.195 = f32[32,1024]{1,0:T(8,128)} concatenate(f32[1,1024]{1,0:T(1,128)} %bitcast.529, f32[1,1024]{1,0:T(1,128)} %bitcast.528, f32[1,1024]{1,0:T(1,128)} %bitcast.527, f32[1,1024]{1,0:T(1,128)} %bitcast.526, f32[1,1024]{1,0:T(1,128)} %bitcast.525, f32[1,1024]{1,0:T(1,128)} %bitcast.524, f32[1,1024]{1,0:T(1,128)} %bitcast.523, f32[1,1024]{1,0:T(1,128)} %bitcast.522, ...), dimensions={0} | concatenate | bytes 262144 | tf_op jit(solution)/shard_map/stack | solution.py:252
  62.1 2.8 %exponential_multiply_fusion = (f32[16,32,1024]{2,1,0:T(8,128)S(1)}, f32[16,32,1024]{2,1,0:T(8,128)S(1)}, f32[32,1024]{1,0:T(8,128)S(1)}, f32[16,1024]{1,0:T(8,128)}) fusion(f32[32]{0:T(128)} %broadcast_subtract_fusion, f32[16,1024]{1,0:T(8,128)S(1)} %neg.5, f32[16,1024]{1,0:T(8,128)} %param.10, f32[32]{0:T(128)} %broadcast_add_fusion, f32[32]{0:T(128)} %copy-done.32, ...), kind=kLoop, calls=%fused_computation.106 | loop fusion | flops 4669440 | bytes 4653440 | tf_op jit(solution)/shard_map/mul | solution.py:191
  67.2 3.1 %collective-permute-start.13 = (f32[2,16,1024]{2,1,0:T(8,128)S(1)}, f32[2,16,1024]{2,1,0:T(8,128)S(1)}, u32[]{:S(2)}, u32[]{:S(2)}) collective-permute-start(f32[2,16,1024]{2,1,0:T(8,128)S(1)} %pad_maximum_fusion.4), channel_id=1, source_target_pairs={{64,0},{68,4},{72,8},{76,12},{80,16},{84,20},{88,24},{92,28},{96,3... | collective-permute-start | bytes 393224 | tf_op jit(solution)/shard_map/ppermute | solution.py:64
  71.9 2.3 %collective-permute-done.13 = f32[2,16,1024]{2,1,0:T(8,128)S(1)} collective-permute-done((f32[2,16,1024]{2,1,0:T(8,128)S(1)}, f32[2,16,1024]{2,1,0:T(8,128)S(1)}, u32[]{:S(2)}, u32[]{:S(2)}) %collective-permute-start.13) | collective-permute-done | bytes 131104 | tf_op jit(solution)/shard_map/ppermute | solution.py:64
  74.2 2.7 %collective-permute-done.14 = f32[2,16,1024]{2,1,0:T(8,128)S(1)} collective-permute-done((f32[2,16,1024]{2,1,0:T(8,128)S(1)}, f32[2,16,1024]{2,1,0:T(8,128)S(1)}, u32[]{:S(2)}, u32[]{:S(2)}) %collective-permute-start.14) | collective-permute-done | bytes 131104 | tf_op jit(solution)/shard_map/ppermute | solution.py:64
  80.1 1.9 %fusion.146 = f32[4,32,1024]{2,1,0:T(8,128)S(1)} fusion(f32[4,32,1024]{2,1,0:T(8,128)S(1)} %multiply_reduce_fusion, f32[4,32,1024]{2,1,0:T(8,128)S(1)} %bitcast.403, f32[1024]{0:T(1024)S(1)} %bitcast.418, f32[1024]{0:T(1024)S(1)} %bitcast.420, f32[1024]{0:T(1024)S(1)} %bitcast.422, f32[1024]{0:T(1024)S(1)} %bitcast.424, f32[1024]{0:T(1024)S(1)} %bitcast.426, ...), kind=kLoop, calls=%fused_computation.268 | loop fusion | flops 8388608 | bytes 1703936 | tf_op jit(solution)/shard_map/add | solution.py:246
  85.5 1.9 %collective-permute-start.16 = (bf16[3,2,1024]{2,1,0:T(2,128)(2,1)S(1)}, bf16[3,2,1024]{2,1,0:T(2,128)(2,1)S(1)}, u32[]{:S(2)}, u32[]{:S(2)}) collective-permute-start(bf16[3,2,1024]{2,1,0:T(2,128)(2,1)S(1)} %slice.823), channel_id=1, source_target_pairs={{4,0},{8,4},{12,8},{16,12},{20,16},{24,20},{28,24},{32,28},{36,32}... | collective-permute-start | bytes 36872 | tf_op jit(solution)/shard_map/ppermute | solution.py:17
  90.7 3.0 %collective-permute-start.17 = (f32[128]{0:T(128)S(1)}, f32[128]{0:T(128)S(1)}, u32[]{:S(2)}, u32[]{:S(2)}) collective-permute-start(f32[128]{0:T(128)S(1)} %get-tuple-element.59), channel_id=1, source_target_pairs={{1,0},{2,1},{3,2},{0,3},{5,4},{6,5},{7,6},{4,7},{9,8},{10,9},{11,1... | collective-permute-start | bytes 1544 | tf_op jit(solution)/shard_map/ppermute | solution.py:64
  96.5 3.3 %collective-permute-start.23 = (f32[25,1024]{1,0:T(8,128)S(1)}, f32[25,1024]{1,0:T(8,128)S(1)}, u32[]{:S(2)}, u32[]{:S(2)}) collective-permute-start(f32[25,1024]{1,0:T(8,128)S(1)} %add_add_fusion.2), channel_id=1, source_target_pairs={{16,0},{20,4},{24,8},{28,12},{32,16},{36,20},{40,24},{44,28},{48,3... | collective-permute-start | bytes 307208 | tf_op jit(solution)/shard_map/ppermute | solution.py:64
  102.5 3.5 %collective-permute-done.23 = f32[25,1024]{1,0:T(8,128)S(1)} collective-permute-done((f32[25,1024]{1,0:T(8,128)S(1)}, f32[25,1024]{1,0:T(8,128)S(1)}, u32[]{:S(2)}, u32[]{:S(2)}) %collective-permute-start.23) | collective-permute-done | bytes 102432 | tf_op jit(solution)/shard_map/ppermute | solution.py:64
  106.0 6.0 %collective-permute-done.24 = f32[25,1024]{1,0:T(8,128)S(1)} collective-permute-done((f32[25,1024]{1,0:T(8,128)S(1)}, f32[25,1024]{1,0:T(8,128)S(1)}, u32[]{:S(2)}, u32[]{:S(2)}) %collective-permute-start.24) | collective-permute-done | bytes 102432 | tf_op jit(solution)/shard_map/ppermute | solution.py:64
  112.0 1.9 %collective-permute-done.25 = f32[25,1024]{1,0:T(8,128)S(1)} collective-permute-done((f32[25,1024]{1,0:T(8,128)S(1)}, f32[25,1024]{1,0:T(8,128)S(1)}, u32[]{:S(2)}, u32[]{:S(2)}) %collective-permute-start.25) | collective-permute-done | bytes 102432 | tf_op jit(solution)/shard_map/ppermute | solution.py:64
  117.0 2.4 %collective-permute-done.26 = f32[25,1024]{1,0:T(8,128)S(1)} collective-permute-done((f32[25,1024]{1,0:T(8,128)S(1)}, f32[25,1024]{1,0:T(8,128)S(1)}, u32[]{:S(2)}, u32[]{:S(2)}) %collective-permute-start.26) | collective-permute-done | bytes 102432 | tf_op jit(solution)/shard_map/ppermute | solution.py:64
  119.4 2.4 %collective-permute-done.27 = f32[25,1024]{1,0:T(8,128)S(1)} collective-permute-done((f32[25,1024]{1,0:T(8,128)S(1)}, f32[25,1024]{1,0:T(8,128)S(1)}, u32[]{:S(2)}, u32[]{:S(2)}) %collective-permute-start.27) | collective-permute-done | bytes 102432 | tf_op jit(solution)/shard_map/ppermute | solution.py:64
  (178 shorter events, 47.6 us)
Async XLA Ops:
  1.4 28.1 %collective-permute-start = (bf16[2,1024]{1,0:T(2,128)(2,1)S(1)}, bf16[2,1024]{1,0:T(2,128)(2,1)S(1)}, u32[]{:S(2)}, u32[]{:S(2)}) collective-permute-start(bf16[2,1024]{1,0:T(2,128)(2,1)S(1)} %slice.595), channel_id=1, source_target_pairs={{0,4},{1,5},{2,6},{3,7},{4,8},{5,9},{6,10},{7,11},{8,12},{9,13},{1... | collective-permute-start | bytes 12296 | tf_op jit(solution)/shard_map/ppermute | solution.py:143
  3.3 26.3 %collective-permute-start.3 = (bf16[2,1024]{1,0:T(2,128)(2,1)S(1)}, bf16[2,1024]{1,0:T(2,128)(2,1)S(1)}, u32[]{:S(2)}, u32[]{:S(2)}) collective-permute-start(bf16[2,1024]{1,0:T(2,128)(2,1)S(1)} %slice.595), channel_id=1, source_target_pairs={{3,4},{0,5},{1,6},{2,7},{7,8},{4,9},{5,10},{6,11},{11,12},{8,13},{... | collective-permute-start | bytes 12296 | tf_op jit(solution)/shard_map/ppermute | solution.py:143
  9.4 11.3 %collective-permute-start.4 = (f32[128]{0:T(128)S(1)}, f32[128]{0:T(128)S(1)}, u32[]{:S(2)}, u32[]{:S(2)}) collective-permute-start(f32[128]{0:T(128)S(1)} %multiply_reduce_fusion.10), channel_id=1, source_target_pairs={{1,0},{2,1},{3,2},{0,3},{5,4},{6,5},{7,6},{4,7},{9,8},{10,9},{11,1... | collective-permute-start | bytes 1544 | tf_op jit(solution)/shard_map/ppermute | solution.py:64
  11.2 12.0 %collective-permute-start.5 = (f32[128]{0:T(128)S(1)}, f32[128]{0:T(128)S(1)}, u32[]{:S(2)}, u32[]{:S(2)}) collective-permute-start(f32[128]{0:T(128)S(1)} %multiply_reduce_fusion.10), channel_id=1, source_target_pairs={{2,0},{3,1},{0,2},{1,3},{6,4},{7,5},{4,6},{5,7},{10,8},{11,9},{8,1... | collective-permute-start | bytes 1544 | tf_op jit(solution)/shard_map/ppermute | solution.py:64
  13.0 16.4 %collective-permute-start.6 = (f32[128]{0:T(128)S(1)}, f32[128]{0:T(128)S(1)}, u32[]{:S(2)}, u32[]{:S(2)}) collective-permute-start(f32[128]{0:T(128)S(1)} %multiply_reduce_fusion.10), channel_id=1, source_target_pairs={{3,0},{0,1},{1,2},{2,3},{7,4},{4,5},{5,6},{6,7},{11,8},{8,9},{9,10... | collective-permute-start | bytes 1544 | tf_op jit(solution)/shard_map/ppermute | solution.py:64
  20.7 9.0 %collective-permute-start.2 = (bf16[2,1024]{1,0:T(2,128)(2,1)S(1)}, bf16[2,1024]{1,0:T(2,128)(2,1)S(1)}, u32[]{:S(2)}, u32[]{:S(2)}) collective-permute-start(bf16[2,1024]{1,0:T(2,128)(2,1)S(1)} %slice.595), channel_id=1, source_target_pairs={{2,4},{3,5},{0,6},{1,7},{6,8},{7,9},{4,10},{5,11},{10,12},{11,13},... | collective-permute-start | bytes 12296 | tf_op jit(solution)/shard_map/ppermute | solution.py:143
  23.3 7.4 %collective-permute-start.1 = (bf16[2,1024]{1,0:T(2,128)(2,1)S(1)}, bf16[2,1024]{1,0:T(2,128)(2,1)S(1)}, u32[]{:S(2)}, u32[]{:S(2)}) collective-permute-start(bf16[2,1024]{1,0:T(2,128)(2,1)S(1)} %slice.595), channel_id=1, source_target_pairs={{1,4},{2,5},{3,6},{0,7},{5,8},{6,9},{7,10},{4,11},{9,12},{10,13},{... | collective-permute-start | bytes 12296 | tf_op jit(solution)/shard_map/ppermute | solution.py:143
  35.9 8.7 %collective-permute-start.8 = (f32[2,16,1024]{2,1,0:T(8,128)S(1)}, f32[2,16,1024]{2,1,0:T(8,128)S(1)}, u32[]{:S(2)}, u32[]{:S(2)}) collective-permute-start(f32[2,16,1024]{2,1,0:T(8,128)S(1)} %pad_maximum_fusion.2), channel_id=1, source_target_pairs={{8,0},{12,4},{0,8},{4,12},{24,16},{28,20},{16,24},{20,28},{40,32},... | collective-permute-start | bytes 393224 | tf_op jit(solution)/shard_map/ppermute | solution.py:64
  37.8 6.8 %collective-permute-start.9 = (f32[2,16,1024]{2,1,0:T(8,128)S(1)}, f32[2,16,1024]{2,1,0:T(8,128)S(1)}, u32[]{:S(2)}, u32[]{:S(2)}) collective-permute-start(f32[2,16,1024]{2,1,0:T(8,128)S(1)} %pad_maximum_fusion.2), channel_id=1, source_target_pairs={{12,0},{0,4},{4,8},{8,12},{28,16},{16,20},{20,24},{24,28},{44,32},... | collective-permute-start | bytes 393224 | tf_op jit(solution)/shard_map/ppermute | solution.py:64
  46.0 18.9 %collective-permute-start.10 = (f32[2,16,1024]{2,1,0:T(8,128)}, f32[2,16,1024]{2,1,0:T(8,128)}, u32[]{:S(2)}, u32[]{:S(2)}) collective-permute-start(f32[2,16,1024]{2,1,0:T(8,128)} %pad_maximum_fusion.3), channel_id=1, source_target_pairs={{16,0},{20,4},{24,8},{28,12},{32,16},{36,20},{40,24},{44,28},{48,3... | collective-permute-start | bytes 393224 | tf_op jit(solution)/shard_map/ppermute | solution.py:64
  49.0 15.9 %collective-permute-start.11 = (f32[2,16,1024]{2,1,0:T(8,128)}, f32[2,16,1024]{2,1,0:T(8,128)}, u32[]{:S(2)}, u32[]{:S(2)}) collective-permute-start(f32[2,16,1024]{2,1,0:T(8,128)} %pad_maximum_fusion.3), channel_id=1, source_target_pairs={{40,0},{44,4},{32,8},{36,12},{56,16},{60,20},{48,24},{52,28},{8,32... | collective-permute-start | bytes 393224 | tf_op jit(solution)/shard_map/ppermute | solution.py:64
  52.7 12.3 %collective-permute-start.12 = (f32[2,16,1024]{2,1,0:T(8,128)}, f32[2,16,1024]{2,1,0:T(8,128)}, u32[]{:S(2)}, u32[]{:S(2)}) collective-permute-start(f32[2,16,1024]{2,1,0:T(8,128)} %pad_maximum_fusion.3), channel_id=1, source_target_pairs={{48,0},{52,4},{56,8},{60,12},{0,16},{4,20},{8,24},{12,28},{16,32},... | collective-permute-start | bytes 393224 | tf_op jit(solution)/shard_map/ppermute | solution.py:64
  67.2 7.0 %collective-permute-start.13 = (f32[2,16,1024]{2,1,0:T(8,128)S(1)}, f32[2,16,1024]{2,1,0:T(8,128)S(1)}, u32[]{:S(2)}, u32[]{:S(2)}) collective-permute-start(f32[2,16,1024]{2,1,0:T(8,128)S(1)} %pad_maximum_fusion.4), channel_id=1, source_target_pairs={{64,0},{68,4},{72,8},{76,12},{80,16},{84,20},{88,24},{92,28},{96,3... | collective-permute-start | bytes 393224 | tf_op jit(solution)/shard_map/ppermute | solution.py:64
  70.9 7.2 %collective-permute-start.15 = (f32[2,16,1024]{2,1,0:T(8,128)S(1)}, f32[2,16,1024]{2,1,0:T(8,128)S(1)}, u32[]{:S(2)}, u32[]{:S(2)}) collective-permute-start(f32[2,16,1024]{2,1,0:T(8,128)S(1)} %pad_maximum_fusion.4), channel_id=1, source_target_pairs={{192,0},{196,4},{200,8},{204,12},{208,16},{212,20},{216,24},{220,2... | collective-permute-start | bytes 393224 | tf_op jit(solution)/shard_map/ppermute | solution.py:64
  88.6 7.8 %collective-permute-start.21 = (f32[25,1024]{1,0:T(8,128)S(1)}, f32[25,1024]{1,0:T(8,128)S(1)}, u32[]{:S(2)}, u32[]{:S(2)}) collective-permute-start(f32[25,1024]{1,0:T(8,128)S(1)} %pad_maximum_fusion.5), channel_id=1, source_target_pairs={{8,0},{12,4},{0,8},{4,12},{24,16},{28,20},{16,24},{20,28},{40,32},... | collective-permute-start | bytes 307208 | tf_op jit(solution)/shard_map/ppermute | solution.py:64
  89.7 6.7 %collective-permute-start.22 = (f32[25,1024]{1,0:T(8,128)S(1)}, f32[25,1024]{1,0:T(8,128)S(1)}, u32[]{:S(2)}, u32[]{:S(2)}) collective-permute-start(f32[25,1024]{1,0:T(8,128)S(1)} %pad_maximum_fusion.5), channel_id=1, source_target_pairs={{12,0},{0,4},{4,8},{8,12},{28,16},{16,20},{20,24},{24,28},{44,32},... | collective-permute-start | bytes 307208 | tf_op jit(solution)/shard_map/ppermute | solution.py:64
  90.7 10.7 %collective-permute-start.17 = (f32[128]{0:T(128)S(1)}, f32[128]{0:T(128)S(1)}, u32[]{:S(2)}, u32[]{:S(2)}) collective-permute-start(f32[128]{0:T(128)S(1)} %get-tuple-element.59), channel_id=1, source_target_pairs={{1,0},{2,1},{3,2},{0,3},{5,4},{6,5},{7,6},{4,7},{9,8},{10,9},{11,1... | collective-permute-start | bytes 1544 | tf_op jit(solution)/shard_map/ppermute | solution.py:64
  93.7 8.7 %collective-permute-start.18 = (f32[128]{0:T(128)S(1)}, f32[128]{0:T(128)S(1)}, u32[]{:S(2)}, u32[]{:S(2)}) collective-permute-start(f32[128]{0:T(128)S(1)} %get-tuple-element.59), channel_id=1, source_target_pairs={{2,0},{3,1},{0,2},{1,3},{6,4},{7,5},{4,6},{5,7},{10,8},{11,9},{8,1... | collective-permute-start | bytes 1544 | tf_op jit(solution)/shard_map/ppermute | solution.py:64
  94.1 8.3 %collective-permute-start.19 = (f32[128]{0:T(128)S(1)}, f32[128]{0:T(128)S(1)}, u32[]{:S(2)}, u32[]{:S(2)}) collective-permute-start(f32[128]{0:T(128)S(1)} %get-tuple-element.59), channel_id=1, source_target_pairs={{3,0},{0,1},{1,2},{2,3},{7,4},{4,5},{5,6},{6,7},{11,8},{8,9},{9,10... | collective-permute-start | bytes 1544 | tf_op jit(solution)/shard_map/ppermute | solution.py:64
  96.5 9.5 %collective-permute-start.23 = (f32[25,1024]{1,0:T(8,128)S(1)}, f32[25,1024]{1,0:T(8,128)S(1)}, u32[]{:S(2)}, u32[]{:S(2)}) collective-permute-start(f32[25,1024]{1,0:T(8,128)S(1)} %add_add_fusion.2), channel_id=1, source_target_pairs={{16,0},{20,4},{24,8},{28,12},{32,16},{36,20},{40,24},{44,28},{48,3... | collective-permute-start | bytes 307208 | tf_op jit(solution)/shard_map/ppermute | solution.py:64
  99.8 12.3 %collective-permute-start.24 = (f32[25,1024]{1,0:T(8,128)S(1)}, f32[25,1024]{1,0:T(8,128)S(1)}, u32[]{:S(2)}, u32[]{:S(2)}) collective-permute-start(f32[25,1024]{1,0:T(8,128)S(1)} %add_add_fusion.2), channel_id=1, source_target_pairs={{40,0},{44,4},{32,8},{36,12},{56,16},{60,20},{48,24},{52,28},{8,32... | collective-permute-start | bytes 307208 | tf_op jit(solution)/shard_map/ppermute | solution.py:64
  101.3 12.6 %collective-permute-start.25 = (f32[25,1024]{1,0:T(8,128)S(1)}, f32[25,1024]{1,0:T(8,128)S(1)}, u32[]{:S(2)}, u32[]{:S(2)}) collective-permute-start(f32[25,1024]{1,0:T(8,128)S(1)} %add_add_fusion.2), channel_id=1, source_target_pairs={{48,0},{52,4},{56,8},{60,12},{0,16},{4,20},{8,24},{12,28},{16,32},... | collective-permute-start | bytes 307208 | tf_op jit(solution)/shard_map/ppermute | solution.py:64
  114.6 7.1 %collective-permute-start.27 = (f32[25,1024]{1,0:T(8,128)S(1)}, f32[25,1024]{1,0:T(8,128)S(1)}, u32[]{:S(2)}, u32[]{:S(2)}) collective-permute-start(f32[25,1024]{1,0:T(8,128)S(1)} %add_add_fusion.1), channel_id=1, source_target_pairs={{128,0},{132,4},{136,8},{140,12},{144,16},{148,20},{152,24},{156,2... | collective-permute-start | bytes 307208 | tf_op jit(solution)/shard_map/ppermute | solution.py:64
  115.6 7.5 %collective-permute-start.28 = (f32[25,1024]{1,0:T(8,128)S(1)}, f32[25,1024]{1,0:T(8,128)S(1)}, u32[]{:S(2)}, u32[]{:S(2)}) collective-permute-start(f32[25,1024]{1,0:T(8,128)S(1)} %add_add_fusion.1), channel_id=1, source_target_pairs={{192,0},{196,4},{200,8},{204,12},{208,16},{212,20},{216,24},{220,2... | collective-permute-start | bytes 307208 | tf_op jit(solution)/shard_map/ppermute | solution.py:64
  (38 other events, 274.6 us)

commit v9 on v7

--- a/solution.py
+++ b/solution.py
@@ -73,7 +73,7 @@
     return count & (count - 1) == 0
 
 
-def entering(own_state, own_back, rates, rows, axis, riders):
+def entering(own_state, own_back, rates, rows, axis, riders, work):
     count = lax.axis_size(axis)
     place = lax.axis_index(axis)
     incoming = jnp.zeros_like(own_state)
@@ -83,7 +83,8 @@
     for radix in radices(count):
         group, digit = members(totals, axis, stride, radix)
         if stride == 1:
-            group, riders = lax.optimization_barrier((group, riders))
+            _, riders = lax.optimization_barrier((group, riders))
+            riders = work(*riders)
         position = (place % stride).astype(jnp.float32)
         for other in range(radix):
             before = (digit > other).astype(jnp.float32)
@@ -105,7 +106,7 @@
             ) * group[other][1]
         totals = jnp.stack([forward_total, backward_total], 0)
         stride *= radix
-    return incoming, later, riders
+    return lax.optimization_barrier((incoming, later, riders))
 
 
 def summed(value, axis):
@@ -179,10 +180,35 @@
         jnp.exp(-mode_rates[None] * (P_SIZE * block_steps)[:, None, None]) * block_heads, axis=0
     )
     lead = jnp.zeros((block_count, P_SIZE - 1, chan_count), jnp.float32)
-    incoming, later_state, (late_blocks, late_grads) = entering(
-        own_state, own_back, mode_rates, row_count, "ctx", (blocks, grad_blocks)
-    )
-    late_padded = jnp.concatenate([lead, late_blocks], 1)
+
+    def local_work(some_blocks, some_grads):
+        blocks_padded = jnp.concatenate([lead, some_blocks], 1)
+        grads_padded = jnp.concatenate([some_grads, lead], 1)
+        local_part = sum(
+            response[lag][None, None, :]
+            * blocks_padded[:, P_SIZE - 1 - lag : 2 * P_SIZE - 1 - lag]
+            for lag in range(P_SIZE)
+        )
+        back_local = sum(
+            response[lag][None, None, :] * grads_padded[:, lag : lag + P_SIZE]
+            for lag in range(P_SIZE)
+        )
+        by_lag = jnp.stack(
+            [
+                jnp.sum(
+                    blocks_padded[:, P_SIZE - 1 - lag : 2 * P_SIZE - 1 - lag] * some_grads,
+                    axis=(0, 1),
+                )
+                for lag in range(P_SIZE)
+            ],
+            0,
+        )
+        local_terms = jnp.sum(by_lag[None] * decay_table, axis=1)
+        return local_part, back_local, local_terms
+
+    incoming, later_state, (local_part, back_local, local_terms) = entering(
+        own_state, own_back, mode_rates, row_count, "ctx", (blocks, grad_blocks), local_work
+    )
 
     gap = block_steps[:, None] - block_steps[None, :] - 1.0
     earlier = (gap >= 0).astype(jnp.float32)
@@ -201,21 +227,11 @@
         -mode_rates[None] * (P_SIZE * (block_count - 1 - block_steps))[:, None, None]
     ) * later_state[None]
 
-    lead = jnp.zeros((block_count, P_SIZE - 1, chan_count), jnp.float32)
-    blocks_padded = jnp.concatenate([lead, blocks], 1)
-    grads_padded = jnp.concatenate([grad_blocks, lead], 1)
-    local_part = sum(
-        response[lag][None, None, :] * blocks_padded[:, P_SIZE - 1 - lag : 2 * P_SIZE - 1 - lag]
-        for lag in range(P_SIZE)
-    )
     carried = jnp.sum(starts[:, :, None, :] * carried_table[None], axis=1)
     long_conv = (local_part + carried).reshape(row_count, chan_count)
     output = (query_part * long_conv).astype(jnp.bfloat16)
     grad_query = (cotangent * long_conv).astype(jnp.bfloat16)
 
-    back_local = sum(
-        response[lag][None, None, :] * grads_padded[:, lag : lag + P_SIZE] for lag in range(P_SIZE)
-    )
     back_carried = jnp.sum(ends_back[:, :, None, :] * carried_reversed[None], axis=1)
     grad_product = (back_local + back_carried).reshape(row_count, chan_count)
     grad_key = (grad_product * value_part).astype(jnp.bfloat16)
@@ -223,16 +239,6 @@
 
     weighted = jnp.exp(-mode_rates)[None] * block_heads
     cross_part = jnp.sum(weighted * starts, axis=0)
-    by_lag = jnp.stack(
-        [
-            jnp.sum(
-                late_padded[:, P_SIZE - 1 - lag : 2 * P_SIZE - 1 - lag] * late_grads, axis=(0, 1)
-            )
-            for lag in range(P_SIZE)
-        ],
-        0,
-    )
-    local_terms = jnp.sum(by_lag[None] * decay_table, axis=1)
 
     stacked_half = lax.optimization_barrier(jnp.stack([grad_query, grad_key, grad_value], 0))
     next_rows = passed_along(stacked_half[:, : KS - 1], "ctx", -1)

time: 107 us -> 108 us (level); the launches traced: 107 us -> 106 us
  waiting for transfers between devices: 43 us -> 23.4 us
  starting transfers between devices: 36.3 us -> 50 us
  other arithmetic: 22 us -> 26.7 us
    ppermute x24, waiting for transfers between devices: 43 us -> 23.4 us  [members(): received.append(lax.ppermute(value, axis, pairs))]
    ppermute x24, starting transfers between devices: 32.5 us -> 45.9 us  [members(): received.append(lax.ppermute(value, axis, pairs))]
    add x0 -> x2, other arithmetic: none -> 3.41 us  [the longest x1 1.74 us: local_work(): sum((response[lag][None, None, :] * grads_padded[:, lag:lag + P_SIZE] for...]
    add x1, other arithmetic: 1.86 us -> 0.06 us  [per_device(): grad_product = (back_local + back_carried).reshape(row_count, chan_count)]
    add x1, other arithmetic: 1.7 us -> 0.06 us  [per_device(): long_conv = (local_part + carried).reshape(row_count, chan_count)]
    another operation x4, other arithmetic: 0.15 us -> 1.43 us  [entering(): totals = jnp.stack([forward_total, backward_total], 0)]
  transfers between devices with their start and end apart: 26 -> 26, of which waited for: 18 -> 10; matrix products, arithmetic and copies ran while one was open for 10% -> 16% of each run, Pallas kernels for 0% -> 0%
where the time goes in v9:
time: 108 us; the launch traced here: 106 us
  starting transfers between devices  50 us (46%)
  other arithmetic  26.7 us (25%)
  waiting for transfers between devices  23.4 us (22%)
  local copies, waits for them, and re-layouts  4.27 us (4%)
  between operations  2.07 us (2%)
    ppermute x24, starting transfers between devices, members(): received.append(lax.ppermute(value, axis, pairs))  45.9 us
    ppermute x24, waiting for transfers between devices, members(): received.append(lax.ppermute(value, axis, pairs))  23.4 us
    ppermute x2, starting transfers between devices, passed_along(): lax.ppermute(value, axis, [(source, source + steps) for source in range(f...  4.02 us
  transfers between devices with their start and end apart: 26, of which 10 were waited for; matrix products, arithmetic and copies ran while one was open for 16% of the time, Pallas kernels for 0%

profile of v9, /device:TPU:32, one launch (start us, length us, event | category | flops | bytes accessed | tf_op | source)
XLA Modules:
  0.0 106.5 jit_solution(3660963532499711695)
XLA Ops:
  1.4 1.9 %collective-permute-start = (bf16[2,1024]{1,0:T(2,128)(2,1)S(1)}, bf16[2,1024]{1,0:T(2,128)(2,1)S(1)}, u32[]{:S(2)}, u32[]{:S(2)}) collective-permute-start(bf16[2,1024]{1,0:T(2,128)(2,1)S(1)} %slice.536), channel_id=1, source_target_pairs={{0,4},{4,8},{8,12},{12,16},{16,20},{20,24},{24,28},{28,32},{32,36}... | collective-permute-start | bytes 12296 | tf_op jit(solution)/shard_map/ppermute | solution.py:17
  7.0 2.0 %multiply_exponential_fusion = (f32[16,32,1024]{2,1,0:T(8,128)S(1)}, f32[16,32,1024]{2,1,0:T(8,128)}) fusion(f32[32]{0:T(128)S(1)} %iota_convert_fusion, f32[16,1024]{1,0:T(8,128)S(1)} %neg.5, f32[32]{0:T(128)S(1)} %broadcast_subtract_fusion.1), kind=kLoop, calls=%fused_computation.78 | loop fusion | flops 1048576 | bytes 4260096 | tf_op jit(solution)/shard_map/exp | solution.py:160
  9.1 3.1 %collective-permute-start.2 = (f32[130]{0:T(256)S(1)}, f32[130]{0:T(256)S(1)}, u32[]{:S(2)}, u32[]{:S(2)}) collective-permute-start(f32[130]{0:T(256)S(1)} %fusion.3), channel_id=1, source_target_pairs={{2,0},{3,1},{0,2},{1,3},{6,4},{7,5},{4,6},{5,7},{10,8},{11,9},{8,1... | collective-permute-start | bytes 1568 | tf_op jit(solution)/shard_map/ppermute | solution.py:64
  12.8 2.6 %collective-permute-start.1 = (f32[130]{0:T(256)S(1)}, f32[130]{0:T(256)S(1)}, u32[]{:S(2)}, u32[]{:S(2)}) collective-permute-start(f32[130]{0:T(256)S(1)} %fusion.3), channel_id=1, source_target_pairs={{1,0},{2,1},{3,2},{0,3},{5,4},{6,5},{7,6},{4,7},{9,8},{10,9},{11,1... | collective-permute-start | bytes 1568 | tf_op jit(solution)/shard_map/ppermute | solution.py:64
  26.6 1.7 %collective-permute-done.5 = f32[2,16,1024]{2,1,0:T(8,128)S(1)} collective-permute-done((f32[2,16,1024]{2,1,0:T(8,128)S(1)}, f32[2,16,1024]{2,1,0:T(8,128)S(1)}, u32[]{:S(2)}, u32[]{:S(2)}) %collective-permute-start.5) | collective-permute-done | bytes 131104 | tf_op jit(solution)/shard_map/ppermute | solution.py:64
  28.3 2.2 %collective-permute-done.6 = f32[2,16,1024]{2,1,0:T(8,128)S(1)} collective-permute-done((f32[2,16,1024]{2,1,0:T(8,128)S(1)}, f32[2,16,1024]{2,1,0:T(8,128)S(1)}, u32[]{:S(2)}, u32[]{:S(2)}) %collective-permute-start.6) | collective-permute-done | bytes 131104 | tf_op jit(solution)/shard_map/ppermute | solution.py:64
  32.0 4.1 %collective-permute-start.8 = (f32[2,16,1024]{2,1,0:T(8,128)}, f32[2,16,1024]{2,1,0:T(8,128)S(1)}, u32[]{:S(2)}, u32[]{:S(2)}) collective-permute-start(f32[2,16,1024]{2,1,0:T(8,128)} %pad_maximum_fusion.4), channel_id=1, source_target_pairs={{40,0},{44,4},{32,8},{36,12},{56,16},{60,20},{48,24},{52,28},{8,32... | collective-permute-start | bytes 393224 | tf_op jit(solution)/shard_map/ppermute | solution.py:64
  37.6 2.7 %collective-permute-start.7 = (f32[2,16,1024]{2,1,0:T(8,128)}, f32[2,16,1024]{2,1,0:T(8,128)}, u32[]{:S(2)}, u32[]{:S(2)}) collective-permute-start(f32[2,16,1024]{2,1,0:T(8,128)} %pad_maximum_fusion.4), channel_id=1, source_target_pairs={{16,0},{20,4},{24,8},{28,12},{32,16},{36,20},{40,24},{44,28},{48,3... | collective-permute-start | bytes 393224 | tf_op jit(solution)/shard_map/ppermute | solution.py:64
  46.1 3.9 %collective-permute-done.9 = f32[2,16,1024]{2,1,0:T(8,128)} collective-permute-done((f32[2,16,1024]{2,1,0:T(8,128)}, f32[2,16,1024]{2,1,0:T(8,128)}, u32[]{:S(2)}, u32[]{:S(2)}) %collective-permute-start.9) | collective-permute-done | bytes 131104 | tf_op jit(solution)/shard_map/ppermute | solution.py:64
  51.2 3.1 %collective-permute-start.11 = (f32[2,16,1024]{2,1,0:T(8,128)S(1)}, f32[2,16,1024]{2,1,0:T(8,128)S(1)}, u32[]{:S(2)}, u32[]{:S(2)}) collective-permute-start(f32[2,16,1024]{2,1,0:T(8,128)S(1)} %pad_maximum_fusion.5), channel_id=1, source_target_pairs={{128,0},{132,4},{136,8},{140,12},{144,16},{148,20},{152,24},{156,2... | collective-permute-start | bytes 393224 | tf_op jit(solution)/shard_map/ppermute | solution.py:64
  54.9 2.6 %collective-permute-start.10 = (f32[2,16,1024]{2,1,0:T(8,128)S(1)}, f32[2,16,1024]{2,1,0:T(8,128)S(1)}, u32[]{:S(2)}, u32[]{:S(2)}) collective-permute-start(f32[2,16,1024]{2,1,0:T(8,128)S(1)} %pad_maximum_fusion.5), channel_id=1, source_target_pairs={{64,0},{68,4},{72,8},{76,12},{80,16},{84,20},{88,24},{92,28},{96,3... | collective-permute-start | bytes 393224 | tf_op jit(solution)/shard_map/ppermute | solution.py:64
  57.5 1.7 %fusion.86 = f32[4,32,1024]{2,1,0:T(8,128)S(1)} fusion(f32[4,32,1024]{2,1,0:T(8,128)S(1)} %bitcast.359, f32[1024]{0:T(1024)S(1)} %bitcast.375, f32[1024]{0:T(1024)S(1)} %bitcast.377, f32[1024]{0:T(1024)S(1)} %bitcast.379, f32[1024]{0:T(1024)S(1)} %bitcast.381, f32[1024]{0:T(1024)S(1)} %bitcast.383, f32[1024]{0:T(1024)S(1)} %bitcast.385, ...), kind=kLoop, calls=%fused_computation.180 | loop fusion | flops 8257536 | bytes 1179648 | tf_op jit(solution)/shard_map/add | solution.py:192
  59.3 2.0 %collective-permute-done.12 = f32[2,16,1024]{2,1,0:T(8,128)S(1)} collective-permute-done((f32[2,16,1024]{2,1,0:T(8,128)S(1)}, f32[2,16,1024]{2,1,0:T(8,128)S(1)}, u32[]{:S(2)}, u32[]{:S(2)}) %collective-permute-start.12) | collective-permute-done | bytes 131104 | tf_op jit(solution)/shard_map/ppermute | solution.py:64
  65.9 2.1 %collective-permute-start.13 = (bf16[3,2,1024]{2,1,0:T(2,128)(2,1)S(1)}, bf16[3,2,1024]{2,1,0:T(2,128)(2,1)S(1)}, u32[]{:S(2)}, u32[]{:S(2)}) collective-permute-start(bf16[3,2,1024]{2,1,0:T(2,128)(2,1)S(1)} %slice.742), channel_id=1, source_target_pairs={{4,0},{8,4},{12,8},{16,12},{20,16},{24,20},{28,24},{32,28},{36,32}... | collective-permute-start | bytes 36872 | tf_op jit(solution)/shard_map/ppermute | solution.py:17
  73.4 2.6 %collective-permute-start.16 = (f32[128]{0:T(128)S(1)}, f32[128]{0:T(128)S(1)}, u32[]{:S(2)}, u32[]{:S(2)}) collective-permute-start(f32[128]{0:T(128)S(1)} %get-tuple-element.61), channel_id=1, source_target_pairs={{3,0},{0,1},{1,2},{2,3},{7,4},{4,5},{5,6},{6,7},{11,8},{8,9},{9,10... | collective-permute-start | bytes 1544 | tf_op jit(solution)/shard_map/ppermute | solution.py:64
  76.0 2.5 %collective-permute-start.14 = (f32[128]{0:T(128)S(1)}, f32[128]{0:T(128)S(1)}, u32[]{:S(2)}, u32[]{:S(2)}) collective-permute-start(f32[128]{0:T(128)S(1)} %get-tuple-element.61), channel_id=1, source_target_pairs={{1,0},{2,1},{3,2},{0,3},{5,4},{6,5},{7,6},{4,7},{9,8},{10,9},{11,1... | collective-permute-start | bytes 1544 | tf_op jit(solution)/shard_map/ppermute | solution.py:64
  78.6 4.7 %collective-permute-start.21 = (f32[25,1024]{1,0:T(8,128)S(1)}, f32[25,1024]{1,0:T(8,128)S(1)}, u32[]{:S(2)}, u32[]{:S(2)}) collective-permute-start(f32[25,1024]{1,0:T(8,128)S(1)} %add_add_fusion.2), channel_id=1, source_target_pairs={{40,0},{44,4},{32,8},{36,12},{56,16},{60,20},{48,24},{52,28},{8,32... | collective-permute-start | bytes 307208 | tf_op jit(solution)/shard_map/ppermute | solution.py:64
  84.7 2.7 %collective-permute-start.20 = (f32[25,1024]{1,0:T(8,128)S(1)}, f32[25,1024]{1,0:T(8,128)S(1)}, u32[]{:S(2)}, u32[]{:S(2)}) collective-permute-start(f32[25,1024]{1,0:T(8,128)S(1)} %add_add_fusion.2), channel_id=1, source_target_pairs={{16,0},{20,4},{24,8},{28,12},{32,16},{36,20},{40,24},{44,28},{48,3... | collective-permute-start | bytes 307208 | tf_op jit(solution)/shard_map/ppermute | solution.py:64
  87.5 4.4 %collective-permute-done.21 = f32[25,1024]{1,0:T(8,128)S(1)} collective-permute-done((f32[25,1024]{1,0:T(8,128)S(1)}, f32[25,1024]{1,0:T(8,128)S(1)}, u32[]{:S(2)}, u32[]{:S(2)}) %collective-permute-start.21) | collective-permute-done | bytes 102432 | tf_op jit(solution)/shard_map/ppermute | solution.py:64
  91.9 3.3 %collective-permute-done.22 = f32[25,1024]{1,0:T(8,128)S(1)} collective-permute-done((f32[25,1024]{1,0:T(8,128)S(1)}, f32[25,1024]{1,0:T(8,128)S(1)}, u32[]{:S(2)}, u32[]{:S(2)}) %collective-permute-start.22) | collective-permute-done | bytes 102432 | tf_op jit(solution)/shard_map/ppermute | solution.py:64
  95.3 2.2 %collective-permute-start.24 = (f32[25,1024]{1,0:T(8,128)S(1)}, f32[25,1024]{1,0:T(8,128)S(1)}, u32[]{:S(2)}, u32[]{:S(2)}) collective-permute-start(f32[25,1024]{1,0:T(8,128)S(1)} %add_add_fusion.1), channel_id=1, source_target_pairs={{128,0},{132,4},{136,8},{140,12},{144,16},{148,20},{152,24},{156,2... | collective-permute-start | bytes 307208 | tf_op jit(solution)/shard_map/ppermute | solution.py:64
  98.9 1.7 %collective-permute-start.23 = (f32[25,1024]{1,0:T(8,128)S(1)}, f32[25,1024]{1,0:T(8,128)S(1)}, u32[]{:S(2)}, u32[]{:S(2)}) collective-permute-start(f32[25,1024]{1,0:T(8,128)S(1)} %add_add_fusion.1), channel_id=1, source_target_pairs={{64,0},{68,4},{72,8},{76,12},{80,16},{84,20},{88,24},{92,28},{96,3... | collective-permute-start | bytes 307208 | tf_op jit(solution)/shard_map/ppermute | solution.py:64
  101.5 1.7 %collective-permute-done.24 = f32[25,1024]{1,0:T(8,128)S(1)} collective-permute-done((f32[25,1024]{1,0:T(8,128)S(1)}, f32[25,1024]{1,0:T(8,128)S(1)}, u32[]{:S(2)}, u32[]{:S(2)}) %collective-permute-start.24) | collective-permute-done | bytes 102432 | tf_op jit(solution)/shard_map/ppermute | solution.py:64
  103.2 1.9 %collective-permute-done.25 = f32[25,1024]{1,0:T(8,128)S(1)} collective-permute-done((f32[25,1024]{1,0:T(8,128)S(1)}, f32[25,1024]{1,0:T(8,128)S(1)}, u32[]{:S(2)}, u32[]{:S(2)}) %collective-permute-start.25) | collective-permute-done | bytes 102432 | tf_op jit(solution)/shard_map/ppermute | solution.py:64
  (184 shorter events, 41.0 us)
Async XLA Ops:
  1.4 7.6 %collective-permute-start = (bf16[2,1024]{1,0:T(2,128)(2,1)S(1)}, bf16[2,1024]{1,0:T(2,128)(2,1)S(1)}, u32[]{:S(2)}, u32[]{:S(2)}) collective-permute-start(bf16[2,1024]{1,0:T(2,128)(2,1)S(1)} %slice.536), channel_id=1, source_target_pairs={{0,4},{4,8},{8,12},{12,16},{16,20},{20,24},{24,28},{28,32},{32,36}... | collective-permute-start | bytes 12296 | tf_op jit(solution)/shard_map/ppermute | solution.py:17
  9.1 6.3 %collective-permute-start.2 = (f32[130]{0:T(256)S(1)}, f32[130]{0:T(256)S(1)}, u32[]{:S(2)}, u32[]{:S(2)}) collective-permute-start(f32[130]{0:T(256)S(1)} %fusion.3), channel_id=1, source_target_pairs={{2,0},{3,1},{0,2},{1,3},{6,4},{7,5},{4,6},{5,7},{10,8},{11,9},{8,1... | collective-permute-start | bytes 1568 | tf_op jit(solution)/shard_map/ppermute | solution.py:64
  21.9 6.4 %collective-permute-start.5 = (f32[2,16,1024]{2,1,0:T(8,128)S(1)}, f32[2,16,1024]{2,1,0:T(8,128)S(1)}, u32[]{:S(2)}, u32[]{:S(2)}) collective-permute-start(f32[2,16,1024]{2,1,0:T(8,128)S(1)} %pad_maximum_fusion.3), channel_id=1, source_target_pairs={{8,0},{12,4},{0,8},{4,12},{24,16},{28,20},{16,24},{20,28},{40,32},... | collective-permute-start | bytes 393224 | tf_op jit(solution)/shard_map/ppermute | solution.py:64
  22.0 8.5 %collective-permute-start.6 = (f32[2,16,1024]{2,1,0:T(8,128)S(1)}, f32[2,16,1024]{2,1,0:T(8,128)S(1)}, u32[]{:S(2)}, u32[]{:S(2)}) collective-permute-start(f32[2,16,1024]{2,1,0:T(8,128)S(1)} %pad_maximum_fusion.3), channel_id=1, source_target_pairs={{12,0},{0,4},{4,8},{8,12},{28,16},{16,20},{20,24},{24,28},{44,32},... | collective-permute-start | bytes 393224 | tf_op jit(solution)/shard_map/ppermute | solution.py:64
  22.7 7.8 %collective-permute-start.4 = (f32[2,16,1024]{2,1,0:T(8,128)S(1)}, f32[2,16,1024]{2,1,0:T(8,128)S(1)}, u32[]{:S(2)}, u32[]{:S(2)}) collective-permute-start(f32[2,16,1024]{2,1,0:T(8,128)S(1)} %pad_maximum_fusion.3), channel_id=1, source_target_pairs={{4,0},{8,4},{12,8},{0,12},{20,16},{24,20},{28,24},{16,28},{36,32},... | collective-permute-start | bytes 393224 | tf_op jit(solution)/shard_map/ppermute | solution.py:64
  32.0 14.1 %collective-permute-start.8 = (f32[2,16,1024]{2,1,0:T(8,128)}, f32[2,16,1024]{2,1,0:T(8,128)S(1)}, u32[]{:S(2)}, u32[]{:S(2)}) collective-permute-start(f32[2,16,1024]{2,1,0:T(8,128)} %pad_maximum_fusion.4), channel_id=1, source_target_pairs={{40,0},{44,4},{32,8},{36,12},{56,16},{60,20},{48,24},{52,28},{8,32... | collective-permute-start | bytes 393224 | tf_op jit(solution)/shard_map/ppermute | solution.py:64
  36.2 13.8 %collective-permute-start.9 = (f32[2,16,1024]{2,1,0:T(8,128)}, f32[2,16,1024]{2,1,0:T(8,128)}, u32[]{:S(2)}, u32[]{:S(2)}) collective-permute-start(f32[2,16,1024]{2,1,0:T(8,128)} %pad_maximum_fusion.4), channel_id=1, source_target_pairs={{48,0},{52,4},{56,8},{60,12},{0,16},{4,20},{8,24},{12,28},{16,32},... | collective-permute-start | bytes 393224 | tf_op jit(solution)/shard_map/ppermute | solution.py:64
  37.6 12.3 %collective-permute-start.7 = (f32[2,16,1024]{2,1,0:T(8,128)}, f32[2,16,1024]{2,1,0:T(8,128)}, u32[]{:S(2)}, u32[]{:S(2)}) collective-permute-start(f32[2,16,1024]{2,1,0:T(8,128)} %pad_maximum_fusion.4), channel_id=1, source_target_pairs={{16,0},{20,4},{24,8},{28,12},{32,16},{36,20},{40,24},{44,28},{48,3... | collective-permute-start | bytes 393224 | tf_op jit(solution)/shard_map/ppermute | solution.py:64
  51.2 8.0 %collective-permute-start.11 = (f32[2,16,1024]{2,1,0:T(8,128)S(1)}, f32[2,16,1024]{2,1,0:T(8,128)S(1)}, u32[]{:S(2)}, u32[]{:S(2)}) collective-permute-start(f32[2,16,1024]{2,1,0:T(8,128)S(1)} %pad_maximum_fusion.5), channel_id=1, source_target_pairs={{128,0},{132,4},{136,8},{140,12},{144,16},{148,20},{152,24},{156,2... | collective-permute-start | bytes 393224 | tf_op jit(solution)/shard_map/ppermute | solution.py:64
  54.3 7.0 %collective-permute-start.12 = (f32[2,16,1024]{2,1,0:T(8,128)S(1)}, f32[2,16,1024]{2,1,0:T(8,128)S(1)}, u32[]{:S(2)}, u32[]{:S(2)}) collective-permute-start(f32[2,16,1024]{2,1,0:T(8,128)S(1)} %pad_maximum_fusion.5), channel_id=1, source_target_pairs={{192,0},{196,4},{200,8},{204,12},{208,16},{212,20},{216,24},{220,2... | collective-permute-start | bytes 393224 | tf_op jit(solution)/shard_map/ppermute | solution.py:64
  54.9 6.3 %collective-permute-start.10 = (f32[2,16,1024]{2,1,0:T(8,128)S(1)}, f32[2,16,1024]{2,1,0:T(8,128)S(1)}, u32[]{:S(2)}, u32[]{:S(2)}) collective-permute-start(f32[2,16,1024]{2,1,0:T(8,128)S(1)} %pad_maximum_fusion.5), channel_id=1, source_target_pairs={{64,0},{68,4},{72,8},{76,12},{80,16},{84,20},{88,24},{92,28},{96,3... | collective-permute-start | bytes 393224 | tf_op jit(solution)/shard_map/ppermute | solution.py:64
  65.9 5.1 %collective-permute-start.13 = (bf16[3,2,1024]{2,1,0:T(2,128)(2,1)S(1)}, bf16[3,2,1024]{2,1,0:T(2,128)(2,1)S(1)}, u32[]{:S(2)}, u32[]{:S(2)}) collective-permute-start(bf16[3,2,1024]{2,1,0:T(2,128)(2,1)S(1)} %slice.742), channel_id=1, source_target_pairs={{4,0},{8,4},{12,8},{16,12},{20,16},{24,20},{28,24},{32,28},{36,32}... | collective-permute-start | bytes 36872 | tf_op jit(solution)/shard_map/ppermute | solution.py:17
  68.9 7.0 %collective-permute-start.18 = (f32[25,1024]{1,0:T(8,128)S(1)}, f32[25,1024]{1,0:T(8,128)S(1)}, u32[]{:S(2)}, u32[]{:S(2)}) collective-permute-start(f32[25,1024]{1,0:T(8,128)S(1)} %pad_maximum_fusion.6), channel_id=1, source_target_pairs={{8,0},{12,4},{0,8},{4,12},{24,16},{28,20},{16,24},{20,28},{40,32},... | collective-permute-start | bytes 307208 | tf_op jit(solution)/shard_map/ppermute | solution.py:64
  69.3 9.2 %collective-permute-start.19 = (f32[25,1024]{1,0:T(8,128)S(1)}, f32[25,1024]{1,0:T(8,128)S(1)}, u32[]{:S(2)}, u32[]{:S(2)}) collective-permute-start(f32[25,1024]{1,0:T(8,128)S(1)} %pad_maximum_fusion.6), channel_id=1, source_target_pairs={{12,0},{0,4},{4,8},{8,12},{28,16},{16,20},{20,24},{24,28},{44,32},... | collective-permute-start | bytes 307208 | tf_op jit(solution)/shard_map/ppermute | solution.py:64
  70.2 8.3 %collective-permute-start.17 = (f32[25,1024]{1,0:T(8,128)S(1)}, f32[25,1024]{1,0:T(8,128)S(1)}, u32[]{:S(2)}, u32[]{:S(2)}) collective-permute-start(f32[25,1024]{1,0:T(8,128)S(1)} %pad_maximum_fusion.6), channel_id=1, source_target_pairs={{4,0},{8,4},{12,8},{0,12},{20,16},{24,20},{28,24},{16,28},{36,32},... | collective-permute-start | bytes 307208 | tf_op jit(solution)/shard_map/ppermute | solution.py:64
  71.9 12.8 %collective-permute-start.15 = (f32[128]{0:T(128)S(1)}, f32[128]{0:T(128)S(1)}, u32[]{:S(2)}, u32[]{:S(2)}) collective-permute-start(f32[128]{0:T(128)S(1)} %get-tuple-element.61), channel_id=1, source_target_pairs={{2,0},{3,1},{0,2},{1,3},{6,4},{7,5},{4,6},{5,7},{10,8},{11,9},{8,1... | collective-permute-start | bytes 1544 | tf_op jit(solution)/shard_map/ppermute | solution.py:64
  73.4 14.0 %collective-permute-start.16 = (f32[128]{0:T(128)S(1)}, f32[128]{0:T(128)S(1)}, u32[]{:S(2)}, u32[]{:S(2)}) collective-permute-start(f32[128]{0:T(128)S(1)} %get-tuple-element.61), channel_id=1, source_target_pairs={{3,0},{0,1},{1,2},{2,3},{7,4},{4,5},{5,6},{6,7},{11,8},{8,9},{9,10... | collective-permute-start | bytes 1544 | tf_op jit(solution)/shard_map/ppermute | solution.py:64
  76.0 11.4 %collective-permute-start.14 = (f32[128]{0:T(128)S(1)}, f32[128]{0:T(128)S(1)}, u32[]{:S(2)}, u32[]{:S(2)}) collective-permute-start(f32[128]{0:T(128)S(1)} %get-tuple-element.61), channel_id=1, source_target_pairs={{1,0},{2,1},{3,2},{0,3},{5,4},{6,5},{7,6},{4,7},{9,8},{10,9},{11,1... | collective-permute-start | bytes 1544 | tf_op jit(solution)/shard_map/ppermute | solution.py:64
  78.6 13.3 %collective-permute-start.21 = (f32[25,1024]{1,0:T(8,128)S(1)}, f32[25,1024]{1,0:T(8,128)S(1)}, u32[]{:S(2)}, u32[]{:S(2)}) collective-permute-start(f32[25,1024]{1,0:T(8,128)S(1)} %add_add_fusion.2), channel_id=1, source_target_pairs={{40,0},{44,4},{32,8},{36,12},{56,16},{60,20},{48,24},{52,28},{8,32... | collective-permute-start | bytes 307208 | tf_op jit(solution)/shard_map/ppermute | solution.py:64
  83.2 11.9 %collective-permute-start.22 = (f32[25,1024]{1,0:T(8,128)S(1)}, f32[25,1024]{1,0:T(8,128)S(1)}, u32[]{:S(2)}, u32[]{:S(2)}) collective-permute-start(f32[25,1024]{1,0:T(8,128)S(1)} %add_add_fusion.2), channel_id=1, source_target_pairs={{48,0},{52,4},{56,8},{60,12},{0,16},{4,20},{8,24},{12,28},{16,32},... | collective-permute-start | bytes 307208 | tf_op jit(solution)/shard_map/ppermute | solution.py:64
  84.7 10.5 %collective-permute-start.20 = (f32[25,1024]{1,0:T(8,128)S(1)}, f32[25,1024]{1,0:T(8,128)S(1)}, u32[]{:S(2)}, u32[]{:S(2)}) collective-permute-start(f32[25,1024]{1,0:T(8,128)S(1)} %add_add_fusion.2), channel_id=1, source_target_pairs={{16,0},{20,4},{24,8},{28,12},{32,16},{36,20},{40,24},{44,28},{48,3... | collective-permute-start | bytes 307208 | tf_op jit(solution)/shard_map/ppermute | solution.py:64
  95.3 7.9 %collective-permute-start.24 = (f32[25,1024]{1,0:T(8,128)S(1)}, f32[25,1024]{1,0:T(8,128)S(1)}, u32[]{:S(2)}, u32[]{:S(2)}) collective-permute-start(f32[25,1024]{1,0:T(8,128)S(1)} %add_add_fusion.1), channel_id=1, source_target_pairs={{128,0},{132,4},{136,8},{140,12},{144,16},{148,20},{152,24},{156,2... | collective-permute-start | bytes 307208 | tf_op jit(solution)/shard_map/ppermute | solution.py:64
  97.4 7.7 %collective-permute-start.25 = (f32[25,1024]{1,0:T(8,128)S(1)}, f32[25,1024]{1,0:T(8,128)S(1)}, u32[]{:S(2)}, u32[]{:S(2)}) collective-permute-start(f32[25,1024]{1,0:T(8,128)S(1)} %add_add_fusion.1), channel_id=1, source_target_pairs={{192,0},{196,4},{200,8},{204,12},{208,16},{212,20},{216,24},{220,2... | collective-permute-start | bytes 307208 | tf_op jit(solution)/shard_map/ppermute | solution.py:64
  98.9 6.1 %collective-permute-start.23 = (f32[25,1024]{1,0:T(8,128)S(1)}, f32[25,1024]{1,0:T(8,128)S(1)}, u32[]{:S(2)}, u32[]{:S(2)}) collective-permute-start(f32[25,1024]{1,0:T(8,128)S(1)} %add_add_fusion.1), channel_id=1, source_target_pairs={{64,0},{68,4},{72,8},{76,12},{80,16},{84,20},{88,24},{92,28},{96,3... | collective-permute-start | bytes 307208 | tf_op jit(solution)/shard_map/ppermute | solution.py:64
  (44 other events, 336.9 us)

commit v10 on v7

--- a/solution.py
+++ b/solution.py
@@ -123,6 +123,28 @@
     return value
 
 
+def summed_apart(first, second, axis):
+    count = lax.axis_size(axis)
+    levels = radices(count)
+    if not power_of_two(count) or len(levels) < 2:
+        return summed(first, axis), summed(second, axis)
+
+    def level(value, stride, radix):
+        group, _ = members(value, axis, stride, radix)
+        if radix == 4:
+            return (group[0] + group[1]) + (group[2] + group[3])
+        return group[0] + group[1]
+
+    first = level(first, 1, levels[0])
+    second = level(second, 1, levels[0])
+    value = jnp.concatenate([first, second], 0)
+    stride = levels[0]
+    for radix in levels[1:]:
+        value = level(value, stride, radix)
+        stride *= radix
+    return value[: first.shape[0]], value[first.shape[0] :]
+
+
 def per_device(stream, norm_gain, short_filters, mode_rates, residues, grad_out):
     row_count, chan_count = stream.shape
     block_count = row_count // P_SIZE
@@ -257,13 +279,12 @@
         ],
         1,
     )
-    partial_sums = jnp.concatenate(
-        [cross_part + local_terms, short_terms.reshape(3 * KS, chan_count)], 0
-    )
-    whole_sums = summed(partial_sums, "ctx")
+    residue_sum, short_sum = summed_apart(
+        cross_part + local_terms, short_terms.reshape(3 * KS, chan_count), "ctx"
+    )
     norm_factor = 1.0 / jnp.sqrt(jnp.float32(total_rows))
-    grad_residues = whole_sums[:M] * norm_factor
-    grad_short = whole_sums[M:].reshape(3, KS, chan_count) * norm_factor
+    grad_residues = residue_sum * norm_factor
+    grad_short = short_sum.reshape(3, KS, chan_count) * norm_factor
     row_dot = summed(jnp.sum(norm_gain[None, :] * grad_normed * stream_wide, axis=1), "ch")
     grad_stream = (
         row_scale[:, None] * norm_gain[None, :] * grad_normed

time: 107 us -> 109 us (1.019)
  starting transfers between devices: 36.3 us -> 40.3 us
  waiting for transfers between devices: 43 us -> 40.5 us
    ppermute x24 -> x27, starting transfers between devices: 32.5 us -> 36.2 us  [members(): received.append(lax.ppermute(value, axis, pairs))]
    ppermute x24 -> x27, waiting for transfers between devices: 43 us -> 40.5 us  [members(): received.append(lax.ppermute(value, axis, pairs))]
  transfers between devices with their start and end apart: 26 -> 29, of which waited for: 18 -> 18; matrix products, arithmetic and copies ran while one was open for 10% -> 16% of each run, Pallas kernels for 0% -> 0%
where the time goes in v10:
time: 109 us; the launch traced here: 108 us
  waiting for transfers between devices  40.5 us (37%)
  starting transfers between devices  40.3 us (37%)
  other arithmetic  22 us (20%)
  local copies, waits for them, and re-layouts  3.68 us (3%)
  between operations  1.78 us (2%)
    ppermute x27, waiting for transfers between devices, members(): received.append(lax.ppermute(value, axis, pairs))  40.5 us
    ppermute x27, starting transfers between devices, members(): received.append(lax.ppermute(value, axis, pairs))  36.2 us
    ppermute x2, starting transfers between devices, passed_along(): lax.ppermute(value, axis, [(source, source + steps) for source in range(f...  4.05 us
  transfers between devices with their start and end apart: 29, of which 18 were waited for; matrix products, arithmetic and copies ran while one was open for 16% of the time, Pallas kernels for 0%

profile of v10, /device:TPU:32, one launch (start us, length us, event | category | flops | bytes accessed | tf_op | source)
XLA Modules:
  0.0 108.3 jit_solution(5187727594142348366)
XLA Ops:
  1.4 1.9 %collective-permute-start = (bf16[2,1024]{1,0:T(2,128)(2,1)S(1)}, bf16[2,1024]{1,0:T(2,128)(2,1)S(1)}, u32[]{:S(2)}, u32[]{:S(2)}) collective-permute-start(bf16[2,1024]{1,0:T(2,128)(2,1)S(1)} %slice.598), channel_id=1, source_target_pairs={{0,4},{4,8},{8,12},{12,16},{16,20},{20,24},{24,28},{28,32},{32,36}... | collective-permute-start | bytes 12296 | tf_op jit(solution)/shard_map/ppermute | solution.py:17
  5.8 2.0 %multiply_exponential_fusion = (f32[16,32,1024]{2,1,0:T(8,128)}, f32[16,32,1024]{2,1,0:T(8,128)S(1)}) fusion(f32[32]{0:T(128)S(1)} %broadcast_subtract_fusion.1, f32[16,1024]{1,0:T(8,128)S(1)} %neg.5, f32[32]{0:T(128)S(1)} %iota_convert_fusion.1), kind=kLoop, calls=%fused_computation.108 | loop fusion | flops 1048576 | bytes 4260096 | tf_op jit(solution)/shard_map/exp | solution.py:182
  8.0 2.8 %collective-permute-start.1 = (f32[130]{0:T(256)S(1)}, f32[130]{0:T(256)S(1)}, u32[]{:S(2)}, u32[]{:S(2)}) collective-permute-start(f32[130]{0:T(256)S(1)} %fusion.3), channel_id=1, source_target_pairs={{1,0},{2,1},{3,2},{0,3},{5,4},{6,5},{7,6},{4,7},{9,8},{10,9},{11,1... | collective-permute-start | bytes 1568 | tf_op jit(solution)/shard_map/ppermute | solution.py:64
  12.5 3.4 %collective-permute-done.2 = f32[130]{0:T(256)S(1)} collective-permute-done((f32[130]{0:T(256)S(1)}, f32[130]{0:T(256)S(1)}, u32[]{:S(2)}, u32[]{:S(2)}) %collective-permute-start.2) | collective-permute-done | bytes 552 | tf_op jit(solution)/shard_map/ppermute | solution.py:64
  21.3 1.9 %collective-permute-start.5 = (f32[2,16,1024]{2,1,0:T(8,128)S(1)}, f32[2,16,1024]{2,1,0:T(8,128)S(1)}, u32[]{:S(2)}, u32[]{:S(2)}) collective-permute-start(f32[2,16,1024]{2,1,0:T(8,128)S(1)} %pad_maximum_fusion.3), channel_id=1, source_target_pairs={{8,0},{12,4},{0,8},{4,12},{24,16},{28,20},{16,24},{20,28},{40,32},... | collective-permute-start | bytes 393224 | tf_op jit(solution)/shard_map/ppermute | solution.py:64
  25.2 4.8 %collective-permute-done.5 = f32[2,16,1024]{2,1,0:T(8,128)S(1)} collective-permute-done((f32[2,16,1024]{2,1,0:T(8,128)S(1)}, f32[2,16,1024]{2,1,0:T(8,128)S(1)}, u32[]{:S(2)}, u32[]{:S(2)}) %collective-permute-start.5) | collective-permute-done | bytes 131104 | tf_op jit(solution)/shard_map/ppermute | solution.py:64
  30.2 4.9 %collective-permute-start.7 = (f32[2,16,1024]{2,1,0:T(8,128)S(1)}, f32[2,16,1024]{2,1,0:T(8,128)S(1)}, u32[]{:S(2)}, u32[]{:S(2)}) collective-permute-start(f32[2,16,1024]{2,1,0:T(8,128)S(1)} %pad_maximum_fusion.4), channel_id=1, source_target_pairs={{16,0},{20,4},{24,8},{28,12},{32,16},{36,20},{40,24},{44,28},{48,3... | collective-permute-start | bytes 393224 | tf_op jit(solution)/shard_map/ppermute | solution.py:64
  36.3 2.4 %collective-permute-start.9 = (f32[2,16,1024]{2,1,0:T(8,128)S(1)}, f32[2,16,1024]{2,1,0:T(8,128)S(1)}, u32[]{:S(2)}, u32[]{:S(2)}) collective-permute-start(f32[2,16,1024]{2,1,0:T(8,128)S(1)} %pad_maximum_fusion.4), channel_id=1, source_target_pairs={{48,0},{52,4},{56,8},{60,12},{0,16},{4,20},{8,24},{12,28},{16,32},... | collective-permute-start | bytes 393224 | tf_op jit(solution)/shard_map/ppermute | solution.py:64
  42.1 5.7 %collective-permute-done.8 = f32[2,16,1024]{2,1,0:T(8,128)S(1)} collective-permute-done((f32[2,16,1024]{2,1,0:T(8,128)S(1)}, f32[2,16,1024]{2,1,0:T(8,128)S(1)}, u32[]{:S(2)}, u32[]{:S(2)}) %collective-permute-start.8) | collective-permute-done | bytes 131104 | tf_op jit(solution)/shard_map/ppermute | solution.py:64
  48.3 3.1 %collective-permute-start.10 = (f32[2,16,1024]{2,1,0:T(8,128)S(1)}, f32[2,16,1024]{2,1,0:T(8,128)S(1)}, u32[]{:S(2)}, u32[]{:S(2)}) collective-permute-start(f32[2,16,1024]{2,1,0:T(8,128)S(1)} %pad_maximum_fusion.5), channel_id=1, source_target_pairs={{64,0},{68,4},{72,8},{76,12},{80,16},{84,20},{88,24},{92,28},{96,3... | collective-permute-start | bytes 393224 | tf_op jit(solution)/shard_map/ppermute | solution.py:64
  53.1 4.1 %collective-permute-done.10 = f32[2,16,1024]{2,1,0:T(8,128)S(1)} collective-permute-done((f32[2,16,1024]{2,1,0:T(8,128)S(1)}, f32[2,16,1024]{2,1,0:T(8,128)S(1)}, u32[]{:S(2)}, u32[]{:S(2)}) %collective-permute-start.10) | collective-permute-done | bytes 131104 | tf_op jit(solution)/shard_map/ppermute | solution.py:64
  57.2 2.1 %collective-permute-done.11 = f32[2,16,1024]{2,1,0:T(8,128)S(1)} collective-permute-done((f32[2,16,1024]{2,1,0:T(8,128)S(1)}, f32[2,16,1024]{2,1,0:T(8,128)S(1)}, u32[]{:S(2)}, u32[]{:S(2)}) %collective-permute-start.11) | collective-permute-done | bytes 131104 | tf_op jit(solution)/shard_map/ppermute | solution.py:64
  59.3 1.6 %collective-permute-done.12 = f32[2,16,1024]{2,1,0:T(8,128)S(1)} collective-permute-done((f32[2,16,1024]{2,1,0:T(8,128)S(1)}, f32[2,16,1024]{2,1,0:T(8,128)S(1)}, u32[]{:S(2)}, u32[]{:S(2)}) %collective-permute-start.12) | collective-permute-done | bytes 131104 | tf_op jit(solution)/shard_map/ppermute | solution.py:64
  61.7 1.6 %collective-permute-start.18 = (f32[16,1024]{1,0:T(8,128)S(1)}, f32[16,1024]{1,0:T(8,128)S(1)}, u32[]{:S(2)}, u32[]{:S(2)}) collective-permute-start(f32[16,1024]{1,0:T(8,128)S(1)} %add.788), channel_id=1, source_target_pairs={{8,0},{12,4},{0,8},{4,12},{24,16},{28,20},{16,24},{20,28},{40,32},... | collective-permute-start | bytes 196616 | tf_op jit(solution)/shard_map/ppermute | solution.py:64
  64.6 1.9 %fusion.150 = f32[4,32,1024]{2,1,0:T(8,128)S(1)} fusion(f32[4,32,1024]{2,1,0:T(8,128)S(1)} %multiply_reduce_fusion, f32[4,32,1024]{2,1,0:T(8,128)S(1)} %bitcast.403, f32[1024]{0:T(1024)S(1)} %bitcast.418, f32[1024]{0:T(1024)S(1)} %bitcast.420, f32[1024]{0:T(1024)S(1)} %bitcast.422, f32[1024]{0:T(1024)S(1)} %bitcast.424, f32[1024]{0:T(1024)S(1)} %bitcast.426, ...), kind=kLoop, calls=%fused_computation.275 | loop fusion | flops 8388608 | bytes 1703936 | tf_op jit(solution)/shard_map/add | solution.py:242
  66.5 1.7 %fusion.87 = f32[4,32,1024]{2,1,0:T(8,128)S(1)} fusion(f32[4,32,1024]{2,1,0:T(8,128)S(1)} %multiply_reduce_fusion.1, f32[4,32,1024]{2,1,0:T(8,128)S(1)} %bitcast_convert_fusion, f32[1024]{0:T(1024)S(1)} %bitcast.419, f32[1024]{0:T(1024)S(1)} %bitcast.421, f32[1024]{0:T(1024)S(1)} %bitcast.423, f32[1024]{0:T(1024)S(1)} %bitcast.425, f32[1024]{0:T(1024)S(1)} %bitcast.427, ...), kind=kLoop, calls=%fused_computation.212 | loop fusion | flops 8388608 | bytes 1703936 | tf_op jit(solution)/shard_map/add | solution.py:234
  70.2 2.1 %collective-permute-start.13 = (bf16[3,2,1024]{2,1,0:T(2,128)(2,1)S(1)}, bf16[3,2,1024]{2,1,0:T(2,128)(2,1)S(1)}, u32[]{:S(2)}, u32[]{:S(2)}) collective-permute-start(bf16[3,2,1024]{2,1,0:T(2,128)(2,1)S(1)} %slice.827), channel_id=1, source_target_pairs={{4,0},{8,4},{12,8},{16,12},{20,16},{24,20},{28,24},{32,28},{36,32}... | collective-permute-start | bytes 36872 | tf_op jit(solution)/shard_map/ppermute | solution.py:17
  73.1 1.5 %collective-permute-start.21 = (f32[9,1024]{1,0:T(8,128)S(1)}, f32[9,1024]{1,0:T(8,128)S(1)}, u32[]{:S(2)}, u32[]{:S(2)}) collective-permute-start(f32[9,1024]{1,0:T(8,128)S(1)} %reshape.260), channel_id=1, source_target_pairs={{8,0},{12,4},{0,8},{4,12},{24,16},{28,20},{16,24},{20,28},{40,32},... | collective-permute-start | bytes 110600 | tf_op jit(solution)/shard_map/ppermute | solution.py:64
  80.2 3.1 %collective-permute-start.23 = (f32[25,1024]{1,0:T(8,128)S(1)}, f32[25,1024]{1,0:T(8,128)S(1)}, u32[]{:S(2)}, u32[]{:S(2)}) collective-permute-start(f32[25,1024]{1,0:T(8,128)S(1)} %pad_maximum_fusion.6), channel_id=1, source_target_pairs={{16,0},{20,4},{24,8},{28,12},{32,16},{36,20},{40,24},{44,28},{48,3... | collective-permute-start | bytes 307208 | tf_op jit(solution)/shard_map/ppermute | solution.py:64
  83.3 3.6 %collective-permute-start.24 = (f32[25,1024]{1,0:T(8,128)S(1)}, f32[25,1024]{1,0:T(8,128)S(1)}, u32[]{:S(2)}, u32[]{:S(2)}) collective-permute-start(f32[25,1024]{1,0:T(8,128)S(1)} %pad_maximum_fusion.6), channel_id=1, source_target_pairs={{40,0},{44,4},{32,8},{36,12},{56,16},{60,20},{48,24},{52,28},{8,32... | collective-permute-start | bytes 307208 | tf_op jit(solution)/shard_map/ppermute | solution.py:64
  87.7 8.9 %collective-permute-done.24 = f32[25,1024]{1,0:T(8,128)S(1)} collective-permute-done((f32[25,1024]{1,0:T(8,128)S(1)}, f32[25,1024]{1,0:T(8,128)S(1)}, u32[]{:S(2)}, u32[]{:S(2)}) %collective-permute-start.24) | collective-permute-done | bytes 102432 | tf_op jit(solution)/shard_map/ppermute | solution.py:64
  98.1 2.3 %collective-permute-start.27 = (f32[25,1024]{1,0:T(8,128)S(1)}, f32[25,1024]{1,0:T(8,128)S(1)}, u32[]{:S(2)}, u32[]{:S(2)}) collective-permute-start(f32[25,1024]{1,0:T(8,128)S(1)} %add_add_fusion.1), channel_id=1, source_target_pairs={{128,0},{132,4},{136,8},{140,12},{144,16},{148,20},{152,24},{156,2... | collective-permute-start | bytes 307208 | tf_op jit(solution)/shard_map/ppermute | solution.py:64
  101.2 2.3 %collective-permute-done.26 = f32[25,1024]{1,0:T(8,128)S(1)} collective-permute-done((f32[25,1024]{1,0:T(8,128)S(1)}, f32[25,1024]{1,0:T(8,128)S(1)}, u32[]{:S(2)}, u32[]{:S(2)}) %collective-permute-start.26) | collective-permute-done | bytes 102432 | tf_op jit(solution)/shard_map/ppermute | solution.py:64
  103.5 2.3 %collective-permute-done.27 = f32[25,1024]{1,0:T(8,128)S(1)} collective-permute-done((f32[25,1024]{1,0:T(8,128)S(1)}, f32[25,1024]{1,0:T(8,128)S(1)}, u32[]{:S(2)}, u32[]{:S(2)}) %collective-permute-start.27) | collective-permute-done | bytes 102432 | tf_op jit(solution)/shard_map/ppermute | solution.py:64
  (135 shorter events, 34.5 us)
Async XLA Ops:
  1.4 6.4 %collective-permute-start = (bf16[2,1024]{1,0:T(2,128)(2,1)S(1)}, bf16[2,1024]{1,0:T(2,128)(2,1)S(1)}, u32[]{:S(2)}, u32[]{:S(2)}) collective-permute-start(bf16[2,1024]{1,0:T(2,128)(2,1)S(1)} %slice.598), channel_id=1, source_target_pairs={{0,4},{4,8},{8,12},{12,16},{16,20},{20,24},{24,28},{28,32},{32,36}... | collective-permute-start | bytes 12296 | tf_op jit(solution)/shard_map/ppermute | solution.py:17
  10.8 5.1 %collective-permute-start.2 = (f32[130]{0:T(256)S(1)}, f32[130]{0:T(256)S(1)}, u32[]{:S(2)}, u32[]{:S(2)}) collective-permute-start(f32[130]{0:T(256)S(1)} %fusion.3), channel_id=1, source_target_pairs={{2,0},{3,1},{0,2},{1,3},{6,4},{7,5},{4,6},{5,7},{10,8},{11,9},{8,1... | collective-permute-start | bytes 1568 | tf_op jit(solution)/shard_map/ppermute | solution.py:64
  11.6 4.8 %collective-permute-start.3 = (f32[130]{0:T(256)S(1)}, f32[130]{0:T(256)S(1)}, u32[]{:S(2)}, u32[]{:S(2)}) collective-permute-start(f32[130]{0:T(256)S(1)} %fusion.3), channel_id=1, source_target_pairs={{3,0},{0,1},{1,2},{2,3},{7,4},{4,5},{5,6},{6,7},{11,8},{8,9},{9,10... | collective-permute-start | bytes 1568 | tf_op jit(solution)/shard_map/ppermute | solution.py:64
  21.3 8.7 %collective-permute-start.5 = (f32[2,16,1024]{2,1,0:T(8,128)S(1)}, f32[2,16,1024]{2,1,0:T(8,128)S(1)}, u32[]{:S(2)}, u32[]{:S(2)}) collective-permute-start(f32[2,16,1024]{2,1,0:T(8,128)S(1)} %pad_maximum_fusion.3), channel_id=1, source_target_pairs={{8,0},{12,4},{0,8},{4,12},{24,16},{28,20},{16,24},{20,28},{40,32},... | collective-permute-start | bytes 393224 | tf_op jit(solution)/shard_map/ppermute | solution.py:64
  23.2 6.8 %collective-permute-start.6 = (f32[2,16,1024]{2,1,0:T(8,128)S(1)}, f32[2,16,1024]{2,1,0:T(8,128)S(1)}, u32[]{:S(2)}, u32[]{:S(2)}) collective-permute-start(f32[2,16,1024]{2,1,0:T(8,128)S(1)} %pad_maximum_fusion.3), channel_id=1, source_target_pairs={{12,0},{0,4},{4,8},{8,12},{28,16},{16,20},{20,24},{24,28},{44,32},... | collective-permute-start | bytes 393224 | tf_op jit(solution)/shard_map/ppermute | solution.py:64
  30.2 11.9 %collective-permute-start.7 = (f32[2,16,1024]{2,1,0:T(8,128)S(1)}, f32[2,16,1024]{2,1,0:T(8,128)S(1)}, u32[]{:S(2)}, u32[]{:S(2)}) collective-permute-start(f32[2,16,1024]{2,1,0:T(8,128)S(1)} %pad_maximum_fusion.4), channel_id=1, source_target_pairs={{16,0},{20,4},{24,8},{28,12},{32,16},{36,20},{40,24},{44,28},{48,3... | collective-permute-start | bytes 393224 | tf_op jit(solution)/shard_map/ppermute | solution.py:64
  35.1 12.6 %collective-permute-start.8 = (f32[2,16,1024]{2,1,0:T(8,128)S(1)}, f32[2,16,1024]{2,1,0:T(8,128)S(1)}, u32[]{:S(2)}, u32[]{:S(2)}) collective-permute-start(f32[2,16,1024]{2,1,0:T(8,128)S(1)} %pad_maximum_fusion.4), channel_id=1, source_target_pairs={{40,0},{44,4},{32,8},{36,12},{56,16},{60,20},{48,24},{52,28},{8,32... | collective-permute-start | bytes 393224 | tf_op jit(solution)/shard_map/ppermute | solution.py:64
  36.3 11.9 %collective-permute-start.9 = (f32[2,16,1024]{2,1,0:T(8,128)S(1)}, f32[2,16,1024]{2,1,0:T(8,128)S(1)}, u32[]{:S(2)}, u32[]{:S(2)}) collective-permute-start(f32[2,16,1024]{2,1,0:T(8,128)S(1)} %pad_maximum_fusion.4), channel_id=1, source_target_pairs={{48,0},{52,4},{56,8},{60,12},{0,16},{4,20},{8,24},{12,28},{16,32},... | collective-permute-start | bytes 393224 | tf_op jit(solution)/shard_map/ppermute | solution.py:64
  48.3 8.9 %collective-permute-start.10 = (f32[2,16,1024]{2,1,0:T(8,128)S(1)}, f32[2,16,1024]{2,1,0:T(8,128)S(1)}, u32[]{:S(2)}, u32[]{:S(2)}) collective-permute-start(f32[2,16,1024]{2,1,0:T(8,128)S(1)} %pad_maximum_fusion.5), channel_id=1, source_target_pairs={{64,0},{68,4},{72,8},{76,12},{80,16},{84,20},{88,24},{92,28},{96,3... | collective-permute-start | bytes 393224 | tf_op jit(solution)/shard_map/ppermute | solution.py:64
  51.4 7.9 %collective-permute-start.11 = (f32[2,16,1024]{2,1,0:T(8,128)S(1)}, f32[2,16,1024]{2,1,0:T(8,128)S(1)}, u32[]{:S(2)}, u32[]{:S(2)}) collective-permute-start(f32[2,16,1024]{2,1,0:T(8,128)S(1)} %pad_maximum_fusion.5), channel_id=1, source_target_pairs={{128,0},{132,4},{136,8},{140,12},{144,16},{148,20},{152,24},{156,2... | collective-permute-start | bytes 393224 | tf_op jit(solution)/shard_map/ppermute | solution.py:64
  52.1 8.9 %collective-permute-start.12 = (f32[2,16,1024]{2,1,0:T(8,128)S(1)}, f32[2,16,1024]{2,1,0:T(8,128)S(1)}, u32[]{:S(2)}, u32[]{:S(2)}) collective-permute-start(f32[2,16,1024]{2,1,0:T(8,128)S(1)} %pad_maximum_fusion.5), channel_id=1, source_target_pairs={{192,0},{196,4},{200,8},{204,12},{208,16},{212,20},{216,24},{220,2... | collective-permute-start | bytes 393224 | tf_op jit(solution)/shard_map/ppermute | solution.py:64
  61.6 17.3 %collective-permute-start.17 = (f32[16,1024]{1,0:T(8,128)S(1)}, f32[16,1024]{1,0:T(8,128)S(1)}, u32[]{:S(2)}, u32[]{:S(2)}) collective-permute-start(f32[16,1024]{1,0:T(8,128)S(1)} %add.788), channel_id=1, source_target_pairs={{4,0},{8,4},{12,8},{0,12},{20,16},{24,20},{28,24},{16,28},{36,32},... | collective-permute-start | bytes 196616 | tf_op jit(solution)/shard_map/ppermute | solution.py:64
  61.7 18.4 %collective-permute-start.18 = (f32[16,1024]{1,0:T(8,128)S(1)}, f32[16,1024]{1,0:T(8,128)S(1)}, u32[]{:S(2)}, u32[]{:S(2)}) collective-permute-start(f32[16,1024]{1,0:T(8,128)S(1)} %add.788), channel_id=1, source_target_pairs={{8,0},{12,4},{0,8},{4,12},{24,16},{28,20},{16,24},{20,28},{40,32},... | collective-permute-start | bytes 196616 | tf_op jit(solution)/shard_map/ppermute | solution.py:64
  70.2 4.6 %collective-permute-start.13 = (bf16[3,2,1024]{2,1,0:T(2,128)(2,1)S(1)}, bf16[3,2,1024]{2,1,0:T(2,128)(2,1)S(1)}, u32[]{:S(2)}, u32[]{:S(2)}) collective-permute-start(bf16[3,2,1024]{2,1,0:T(2,128)(2,1)S(1)} %slice.827), channel_id=1, source_target_pairs={{4,0},{8,4},{12,8},{16,12},{20,16},{24,20},{28,24},{32,28},{36,32}... | collective-permute-start | bytes 36872 | tf_op jit(solution)/shard_map/ppermute | solution.py:17
  73.1 4.8 %collective-permute-start.21 = (f32[9,1024]{1,0:T(8,128)S(1)}, f32[9,1024]{1,0:T(8,128)S(1)}, u32[]{:S(2)}, u32[]{:S(2)}) collective-permute-start(f32[9,1024]{1,0:T(8,128)S(1)} %reshape.260), channel_id=1, source_target_pairs={{8,0},{12,4},{0,8},{4,12},{24,16},{28,20},{16,24},{20,28},{40,32},... | collective-permute-start | bytes 110600 | tf_op jit(solution)/shard_map/ppermute | solution.py:64
  77.9 9.0 %collective-permute-start.14 = (f32[128]{0:T(128)S(1)}, f32[128]{0:T(128)S(1)}, u32[]{:S(2)}, u32[]{:S(2)}) collective-permute-start(f32[128]{0:T(128)S(1)} %get-tuple-element.59), channel_id=1, source_target_pairs={{1,0},{2,1},{3,2},{0,3},{5,4},{6,5},{7,6},{4,7},{9,8},{10,9},{11,1... | collective-permute-start | bytes 1544 | tf_op jit(solution)/shard_map/ppermute | solution.py:64
  78.6 8.4 %collective-permute-start.15 = (f32[128]{0:T(128)S(1)}, f32[128]{0:T(128)S(1)}, u32[]{:S(2)}, u32[]{:S(2)}) collective-permute-start(f32[128]{0:T(128)S(1)} %get-tuple-element.59), channel_id=1, source_target_pairs={{2,0},{3,1},{0,2},{1,3},{6,4},{7,5},{4,6},{5,7},{10,8},{11,9},{8,1... | collective-permute-start | bytes 1544 | tf_op jit(solution)/shard_map/ppermute | solution.py:64
  78.9 8.1 %collective-permute-start.16 = (f32[128]{0:T(128)S(1)}, f32[128]{0:T(128)S(1)}, u32[]{:S(2)}, u32[]{:S(2)}) collective-permute-start(f32[128]{0:T(128)S(1)} %get-tuple-element.59), channel_id=1, source_target_pairs={{3,0},{0,1},{1,2},{2,3},{7,4},{4,5},{5,6},{6,7},{11,8},{8,9},{9,10... | collective-permute-start | bytes 1544 | tf_op jit(solution)/shard_map/ppermute | solution.py:64
  80.2 7.5 %collective-permute-start.23 = (f32[25,1024]{1,0:T(8,128)S(1)}, f32[25,1024]{1,0:T(8,128)S(1)}, u32[]{:S(2)}, u32[]{:S(2)}) collective-permute-start(f32[25,1024]{1,0:T(8,128)S(1)} %pad_maximum_fusion.6), channel_id=1, source_target_pairs={{16,0},{20,4},{24,8},{28,12},{32,16},{36,20},{40,24},{44,28},{48,3... | collective-permute-start | bytes 307208 | tf_op jit(solution)/shard_map/ppermute | solution.py:64
  83.3 13.3 %collective-permute-start.24 = (f32[25,1024]{1,0:T(8,128)S(1)}, f32[25,1024]{1,0:T(8,128)S(1)}, u32[]{:S(2)}, u32[]{:S(2)}) collective-permute-start(f32[25,1024]{1,0:T(8,128)S(1)} %pad_maximum_fusion.6), channel_id=1, source_target_pairs={{40,0},{44,4},{32,8},{36,12},{56,16},{60,20},{48,24},{52,28},{8,32... | collective-permute-start | bytes 307208 | tf_op jit(solution)/shard_map/ppermute | solution.py:64
  86.9 10.9 %collective-permute-start.25 = (f32[25,1024]{1,0:T(8,128)S(1)}, f32[25,1024]{1,0:T(8,128)S(1)}, u32[]{:S(2)}, u32[]{:S(2)}) collective-permute-start(f32[25,1024]{1,0:T(8,128)S(1)} %pad_maximum_fusion.6), channel_id=1, source_target_pairs={{48,0},{52,4},{56,8},{60,12},{0,16},{4,20},{8,24},{12,28},{16,32},... | collective-permute-start | bytes 307208 | tf_op jit(solution)/shard_map/ppermute | solution.py:64
  97.9 5.7 %collective-permute-start.26 = (f32[25,1024]{1,0:T(8,128)S(1)}, f32[25,1024]{1,0:T(8,128)S(1)}, u32[]{:S(2)}, u32[]{:S(2)}) collective-permute-start(f32[25,1024]{1,0:T(8,128)S(1)} %add_add_fusion.1), channel_id=1, source_target_pairs={{64,0},{68,4},{72,8},{76,12},{80,16},{84,20},{88,24},{92,28},{96,3... | collective-permute-start | bytes 307208 | tf_op jit(solution)/shard_map/ppermute | solution.py:64
  98.1 7.7 %collective-permute-start.27 = (f32[25,1024]{1,0:T(8,128)S(1)}, f32[25,1024]{1,0:T(8,128)S(1)}, u32[]{:S(2)}, u32[]{:S(2)}) collective-permute-start(f32[25,1024]{1,0:T(8,128)S(1)} %add_add_fusion.1), channel_id=1, source_target_pairs={{128,0},{132,4},{136,8},{140,12},{144,16},{148,20},{152,24},{156,2... | collective-permute-start | bytes 307208 | tf_op jit(solution)/shard_map/ppermute | solution.py:64
  100.3 6.6 %collective-permute-start.28 = (f32[25,1024]{1,0:T(8,128)S(1)}, f32[25,1024]{1,0:T(8,128)S(1)}, u32[]{:S(2)}, u32[]{:S(2)}) collective-permute-start(f32[25,1024]{1,0:T(8,128)S(1)} %add_add_fusion.1), channel_id=1, source_target_pairs={{192,0},{196,4},{200,8},{204,12},{208,16},{212,20},{216,24},{220,2... | collective-permute-start | bytes 307208 | tf_op jit(solution)/shard_map/ppermute | solution.py:64
  (20 other events, 100.7 us)

commit v11 on v7

--- a/solution.py
+++ b/solution.py
@@ -179,8 +179,17 @@
         jnp.exp(-mode_rates[None] * (P_SIZE * block_steps)[:, None, None]) * block_heads, axis=0
     )
     lead = jnp.zeros((block_count, P_SIZE - 1, chan_count), jnp.float32)
-    incoming, later_state, (late_blocks, late_grads) = entering(
-        own_state, own_back, mode_rates, row_count, "ctx", (blocks, grad_blocks)
+    blocks_padded = jnp.concatenate([lead, blocks], 1)
+    grads_padded = jnp.concatenate([grad_blocks, lead], 1)
+    local_part = sum(
+        response[lag][None, None, :] * blocks_padded[:, P_SIZE - 1 - lag : 2 * P_SIZE - 1 - lag]
+        for lag in range(P_SIZE)
+    )
+    back_local = sum(
+        response[lag][None, None, :] * grads_padded[:, lag : lag + P_SIZE] for lag in range(P_SIZE)
+    )
+    incoming, later_state, (late_blocks, late_grads, local_part, back_local) = entering(
+        own_state, own_back, mode_rates, row_count, "ctx", (blocks, grad_blocks, local_part, back_local)
     )
     late_padded = jnp.concatenate([lead, late_blocks], 1)
 
@@ -201,21 +210,11 @@
         -mode_rates[None] * (P_SIZE * (block_count - 1 - block_steps))[:, None, None]
     ) * later_state[None]
 
-    lead = jnp.zeros((block_count, P_SIZE - 1, chan_count), jnp.float32)
-    blocks_padded = jnp.concatenate([lead, blocks], 1)
-    grads_padded = jnp.concatenate([grad_blocks, lead], 1)
-    local_part = sum(
-        response[lag][None, None, :] * blocks_padded[:, P_SIZE - 1 - lag : 2 * P_SIZE - 1 - lag]
-        for lag in range(P_SIZE)
-    )
     carried = jnp.sum(starts[:, :, None, :] * carried_table[None], axis=1)
     long_conv = (local_part + carried).reshape(row_count, chan_count)
     output = (query_part * long_conv).astype(jnp.bfloat16)
     grad_query = (cotangent * long_conv).astype(jnp.bfloat16)
 
-    back_local = sum(
-        response[lag][None, None, :] * grads_padded[:, lag : lag + P_SIZE] for lag in range(P_SIZE)
-    )
     back_carried = jnp.sum(ends_back[:, :, None, :] * carried_reversed[None], axis=1)
     grad_product = (back_local + back_carried).reshape(row_count, chan_count)
     grad_key = (grad_product * value_part).astype(jnp.bfloat16)

time: 107 us -> 112 us (1.047)
  the two profiles are of different devices: /device:TPU:32 before, /device:TPU:6 now
where the time goes in v11:
time: 112 us; the launch traced here: 111 us
  starting transfers between devices  44.9 us (40%)
  other arithmetic  30.6 us (27%)
  waiting for transfers between devices  23.1 us (21%)
  local copies, waits for them, and re-layouts  10.5 us (9%)
  between operations  2.27 us (2%)
    ppermute x24, starting transfers between devices, members(): received.append(lax.ppermute(value, axis, pairs))  41.6 us
    ppermute x24, waiting for transfers between devices, members(): received.append(lax.ppermute(value, axis, pairs))  23.1 us
    another operation x1, local copies, waits for them, and re-layouts, per_device(): jnp.stack([jnp.sum(late_padded[:, P_SIZE - 1 - lag:2 * P_SIZE - 1 - lag]...  5.49 us
    mul x1, other arithmetic, per_device(): jnp.exp(-mode_rates[:, None, :] * (P_SIZE - steps)[None, :, None])  4.53 us
    unnamed x92, local copies, waits for them, and re-layouts  3.46 us
    ppermute x2, starting transfers between devices, passed_along(): lax.ppermute(value, axis, [(source, source + steps) for source in range(f...  3.24 us
    reduce_sum x2, other arithmetic, per_device(): jnp.sum(late_padded[:, P_SIZE - 1 - lag:2 * P_SIZE - 1 - lag] * late_grad...  2.93 us
    add x1, other arithmetic, per_device(): sum((response[lag][None, None, :] * grads_padded[:, lag:lag + P_SIZE] for...  2.5 us
  transfers between devices with their start and end apart: 26, of which 11 were waited for; matrix products, arithmetic and copies ran while one was open for 23% of the time, Pallas kernels for 0%

profile of v11, /device:TPU:6, one launch (start us, length us, event | category | flops | bytes accessed | tf_op | source)
XLA Modules:
  0.0 111.4 jit_solution(16123284139732924301)
XLA Ops:
  1.4 1.7 %collective-permute-start = (bf16[2,1024]{1,0:T(2,128)(2,1)S(1)}, bf16[2,1024]{1,0:T(2,128)(2,1)S(1)}, u32[]{:S(2)}, u32[]{:S(2)}) collective-permute-start(bf16[2,1024]{1,0:T(2,128)(2,1)S(1)} %slice.598), channel_id=1, source_target_pairs={{0,4},{4,8},{8,12},{12,16},{16,20},{20,24},{24,28},{28,32},{32,36}... | collective-permute-start | bytes 12296 | tf_op jit(solution)/shard_map/ppermute | solution.py:17
  4.3 4.5 %exponential_multiply_fusion = (f32[16,32,1024]{2,1,0:T(8,128)S(1)}, f32[16,32,1024]{2,1,0:T(8,128)}, f32[32,1024]{1,0:T(8,128)S(1)}, f32[16,32,1024]{2,1,0:T(8,128)}, f32[16,32,1024]{2,1,0:T(8,128)}) fusion(f32[32]{0:T(128)S(1)} %broadcast_subtract_fusion, f32[16,1024]{1,0:T(8,128)} %param.10, f32[16,1024]{1,0:T(8,128)S(1)} %neg.5, ...), kind=kLoop, calls=%fused_computation.106 | loop fusion | flops 4161536 | bytes 8651264 | tf_op jit(solution)/shard_map/mul | solution.py:165
  11.4 2.1 %collective-permute-start.3 = (f32[130]{0:T(256)S(1)}, f32[130]{0:T(256)S(1)}, u32[]{:S(2)}, u32[]{:S(2)}) collective-permute-start(f32[130]{0:T(256)S(1)} %fusion.3), channel_id=1, source_target_pairs={{3,0},{0,1},{1,2},{2,3},{7,4},{4,5},{5,6},{6,7},{11,8},{8,9},{9,10... | collective-permute-start | bytes 1568 | tf_op jit(solution)/shard_map/ppermute | solution.py:64
  15.0 3.2 %collective-permute-done.1 = f32[130]{0:T(256)S(1)} collective-permute-done((f32[130]{0:T(256)S(1)}, f32[130]{0:T(256)S(1)}, u32[]{:S(2)}, u32[]{:S(2)}) %collective-permute-start.1) | collective-permute-done | bytes 552 | tf_op jit(solution)/shard_map/ppermute | solution.py:64
  23.0 2.2 %collective-permute-start.5 = (f32[2,16,1024]{2,1,0:T(8,128)S(1)}, f32[2,16,1024]{2,1,0:T(8,128)S(1)}, u32[]{:S(2)}, u32[]{:S(2)}) collective-permute-start(f32[2,16,1024]{2,1,0:T(8,128)S(1)} %pad_maximum_fusion.3), channel_id=1, source_target_pairs={{8,0},{12,4},{0,8},{4,12},{24,16},{28,20},{16,24},{20,28},{40,32},... | collective-permute-start | bytes 393224 | tf_op jit(solution)/shard_map/ppermute | solution.py:64
  25.2 1.7 %collective-permute-start.4 = (f32[2,16,1024]{2,1,0:T(8,128)S(1)}, f32[2,16,1024]{2,1,0:T(8,128)S(1)}, u32[]{:S(2)}, u32[]{:S(2)}) collective-permute-start(f32[2,16,1024]{2,1,0:T(8,128)S(1)} %pad_maximum_fusion.3), channel_id=1, source_target_pairs={{4,0},{8,4},{12,8},{0,12},{20,16},{24,20},{28,24},{16,28},{36,32},... | collective-permute-start | bytes 393224 | tf_op jit(solution)/shard_map/ppermute | solution.py:64
  26.9 2.3 %fusion.86 = f32[4,32,1024]{2,1,0:T(8,128)} fusion(f32[4,32,1024]{2,1,0:T(8,128)S(1)} %bitcast_convert_fusion, f32[1024]{0:T(1024)S(1)} %bitcast.418, f32[1024]{0:T(1024)S(1)} %bitcast.420, f32[1024]{0:T(1024)S(1)} %bitcast.422, f32[1024]{0:T(1024)S(1)} %bitcast.424, f32[1024]{0:T(1024)S(1)} %bitcast.426, f32[1024]{0:T(1024)S(1)} %bitcast.428, ...), kind=kLoop, calls=%fused_computation.211 | loop fusion | flops 8257536 | bytes 1179648 | tf_op jit(solution)/shard_map/add | solution.py:184
  29.2 2.5 %fusion.148 = f32[4,32,1024]{2,1,0:T(8,128)} fusion(f32[4,32,1024]{2,1,0:T(8,128)S(1)} %bitcast.401, f32[1024]{0:T(1024)S(1)} %bitcast.419, f32[1024]{0:T(1024)S(1)} %bitcast.421, f32[1024]{0:T(1024)S(1)} %bitcast.423, f32[1024]{0:T(1024)S(1)} %bitcast.425, f32[1024]{0:T(1024)S(1)} %bitcast.427, f32[1024]{0:T(1024)S(1)} %bitcast.429, ...), kind=kLoop, calls=%fused_computation.273 | loop fusion | flops 8257536 | bytes 1179648 | tf_op jit(solution)/shard_map/add | solution.py:188
  36.5 5.8 %collective-permute-start.8 = (f32[2,16,1024]{2,1,0:T(8,128)}, f32[2,16,1024]{2,1,0:T(8,128)}, u32[]{:S(2)}, u32[]{:S(2)}) collective-permute-start(f32[2,16,1024]{2,1,0:T(8,128)} %pad_maximum_fusion.4), channel_id=1, source_target_pairs={{40,0},{44,4},{32,8},{36,12},{56,16},{60,20},{48,24},{52,28},{8,32... | collective-permute-start | bytes 393224 | tf_op jit(solution)/shard_map/ppermute | solution.py:64
  43.8 2.7 %collective-permute-start.7 = (f32[2,16,1024]{2,1,0:T(8,128)}, f32[2,16,1024]{2,1,0:T(8,128)}, u32[]{:S(2)}, u32[]{:S(2)}) collective-permute-start(f32[2,16,1024]{2,1,0:T(8,128)} %pad_maximum_fusion.4), channel_id=1, source_target_pairs={{16,0},{20,4},{24,8},{28,12},{32,16},{36,20},{40,24},{44,28},{48,3... | collective-permute-start | bytes 393224 | tf_op jit(solution)/shard_map/ppermute | solution.py:64
  49.4 5.5 %stack.195 = f32[32,1024]{1,0:T(8,128)} concatenate(f32[1,1024]{1,0:T(1,128)} %bitcast.529, f32[1,1024]{1,0:T(1,128)} %bitcast.528, f32[1,1024]{1,0:T(1,128)} %bitcast.527, f32[1,1024]{1,0:T(1,128)} %bitcast.526, f32[1,1024]{1,0:T(1,128)} %bitcast.525, f32[1,1024]{1,0:T(1,128)} %bitcast.524, f32[1,1024]{1,0:T(1,128)} %bitcast.523, f32[1,1024]{1,0:T(1,128)} %bitcast.522, ...), dimensions={0} | concatenate | bytes 262144 | tf_op jit(solution)/shard_map/stack | solution.py:225
  57.3 3.3 %collective-permute-start.11 = (f32[2,16,1024]{2,1,0:T(8,128)S(1)}, f32[2,16,1024]{2,1,0:T(8,128)S(1)}, u32[]{:S(2)}, u32[]{:S(2)}) collective-permute-start(f32[2,16,1024]{2,1,0:T(8,128)S(1)} %pad_maximum_fusion.5), channel_id=1, source_target_pairs={{128,0},{132,4},{136,8},{140,12},{144,16},{148,20},{152,24},{156,2... | collective-permute-start | bytes 393224 | tf_op jit(solution)/shard_map/ppermute | solution.py:64
  61.3 2.6 %collective-permute-start.10 = (f32[2,16,1024]{2,1,0:T(8,128)S(1)}, f32[2,16,1024]{2,1,0:T(8,128)S(1)}, u32[]{:S(2)}, u32[]{:S(2)}) collective-permute-start(f32[2,16,1024]{2,1,0:T(8,128)S(1)} %pad_maximum_fusion.5), channel_id=1, source_target_pairs={{64,0},{68,4},{72,8},{76,12},{80,16},{84,20},{88,24},{92,28},{96,3... | collective-permute-start | bytes 393224 | tf_op jit(solution)/shard_map/ppermute | solution.py:64
  74.2 1.8 %collective-permute-start.18 = (f32[25,1024]{1,0:T(8,128)S(1)}, f32[25,1024]{1,0:T(8,128)S(1)}, u32[]{:S(2)}, u32[]{:S(2)}) collective-permute-start(f32[25,1024]{1,0:T(8,128)S(1)} %pad_maximum_fusion.6), channel_id=1, source_target_pairs={{8,0},{12,4},{0,8},{4,12},{24,16},{28,20},{16,24},{20,28},{40,32},... | collective-permute-start | bytes 307208 | tf_op jit(solution)/shard_map/ppermute | solution.py:64
  76.1 1.8 %collective-permute-start.17 = (f32[25,1024]{1,0:T(8,128)S(1)}, f32[25,1024]{1,0:T(8,128)S(1)}, u32[]{:S(2)}, u32[]{:S(2)}) collective-permute-start(f32[25,1024]{1,0:T(8,128)S(1)} %pad_maximum_fusion.6), channel_id=1, source_target_pairs={{4,0},{8,4},{12,8},{0,12},{20,16},{24,20},{28,24},{16,28},{36,32},... | collective-permute-start | bytes 307208 | tf_op jit(solution)/shard_map/ppermute | solution.py:64
  80.8 2.6 %collective-permute-done.19 = f32[25,1024]{1,0:T(8,128)S(1)} collective-permute-done((f32[25,1024]{1,0:T(8,128)S(1)}, f32[25,1024]{1,0:T(8,128)S(1)}, u32[]{:S(2)}, u32[]{:S(2)}) %collective-permute-start.19) | collective-permute-done | bytes 102432 | tf_op jit(solution)/shard_map/ppermute | solution.py:64
  83.5 3.0 %collective-permute-start.21 = (f32[25,1024]{1,0:T(8,128)S(1)}, f32[25,1024]{1,0:T(8,128)S(1)}, u32[]{:S(2)}, u32[]{:S(2)}) collective-permute-start(f32[25,1024]{1,0:T(8,128)S(1)} %add_add_fusion.2), channel_id=1, source_target_pairs={{40,0},{44,4},{32,8},{36,12},{56,16},{60,20},{48,24},{52,28},{8,32... | collective-permute-start | bytes 307208 | tf_op jit(solution)/shard_map/ppermute | solution.py:64
  87.3 3.3 %collective-permute-start.20 = (f32[25,1024]{1,0:T(8,128)S(1)}, f32[25,1024]{1,0:T(8,128)S(1)}, u32[]{:S(2)}, u32[]{:S(2)}) collective-permute-start(f32[25,1024]{1,0:T(8,128)S(1)} %add_add_fusion.2), channel_id=1, source_target_pairs={{16,0},{20,4},{24,8},{28,12},{32,16},{36,20},{40,24},{44,28},{48,3... | collective-permute-start | bytes 307208 | tf_op jit(solution)/shard_map/ppermute | solution.py:64
  90.7 7.4 %collective-permute-done.21 = f32[25,1024]{1,0:T(8,128)S(1)} collective-permute-done((f32[25,1024]{1,0:T(8,128)S(1)}, f32[25,1024]{1,0:T(8,128)S(1)}, u32[]{:S(2)}, u32[]{:S(2)}) %collective-permute-start.21) | collective-permute-done | bytes 102432 | tf_op jit(solution)/shard_map/ppermute | solution.py:64
  98.1 1.8 %collective-permute-done.20 = f32[25,1024]{1,0:T(8,128)S(1)} collective-permute-done((f32[25,1024]{1,0:T(8,128)S(1)}, f32[25,1024]{1,0:T(8,128)S(1)}, u32[]{:S(2)}, u32[]{:S(2)}) %collective-permute-start.20) | collective-permute-done | bytes 102432 | tf_op jit(solution)/shard_map/ppermute | solution.py:64
  100.0 1.9 %collective-permute-start.24 = (f32[25,1024]{1,0:T(8,128)S(1)}, f32[25,1024]{1,0:T(8,128)S(1)}, u32[]{:S(2)}, u32[]{:S(2)}) collective-permute-start(f32[25,1024]{1,0:T(8,128)S(1)} %add_add_fusion.1), channel_id=1, source_target_pairs={{128,0},{132,4},{136,8},{140,12},{144,16},{148,20},{152,24},{156,2... | collective-permute-start | bytes 307208 | tf_op jit(solution)/shard_map/ppermute | solution.py:64
  101.9 2.2 %collective-permute-start.25 = (f32[25,1024]{1,0:T(8,128)S(1)}, f32[25,1024]{1,0:T(8,128)S(1)}, u32[]{:S(2)}, u32[]{:S(2)}) collective-permute-start(f32[25,1024]{1,0:T(8,128)S(1)} %add_add_fusion.1), channel_id=1, source_target_pairs={{192,0},{196,4},{200,8},{204,12},{208,16},{212,20},{216,24},{220,2... | collective-permute-start | bytes 307208 | tf_op jit(solution)/shard_map/ppermute | solution.py:64
  106.0 2.0 %collective-permute-done.24 = f32[25,1024]{1,0:T(8,128)S(1)} collective-permute-done((f32[25,1024]{1,0:T(8,128)S(1)}, f32[25,1024]{1,0:T(8,128)S(1)}, u32[]{:S(2)}, u32[]{:S(2)}) %collective-permute-start.24) | collective-permute-done | bytes 102432 | tf_op jit(solution)/shard_map/ppermute | solution.py:64
  107.9 1.8 %collective-permute-done.25 = f32[25,1024]{1,0:T(8,128)S(1)} collective-permute-done((f32[25,1024]{1,0:T(8,128)S(1)}, f32[25,1024]{1,0:T(8,128)S(1)}, u32[]{:S(2)}, u32[]{:S(2)}) %collective-permute-start.25) | collective-permute-done | bytes 102432 | tf_op jit(solution)/shard_map/ppermute | solution.py:64
  (192 shorter events, 39.5 us)
Async XLA Ops:
  1.4 8.3 %collective-permute-start = (bf16[2,1024]{1,0:T(2,128)(2,1)S(1)}, bf16[2,1024]{1,0:T(2,128)(2,1)S(1)}, u32[]{:S(2)}, u32[]{:S(2)}) collective-permute-start(bf16[2,1024]{1,0:T(2,128)(2,1)S(1)} %slice.598), channel_id=1, source_target_pairs={{0,4},{4,8},{8,12},{12,16},{16,20},{20,24},{24,28},{28,32},{32,36}... | collective-permute-start | bytes 12296 | tf_op jit(solution)/shard_map/ppermute | solution.py:17
  9.9 5.2 %collective-permute-start.2 = (f32[130]{0:T(256)S(1)}, f32[130]{0:T(256)S(1)}, u32[]{:S(2)}, u32[]{:S(2)}) collective-permute-start(f32[130]{0:T(256)S(1)} %fusion.3), channel_id=1, source_target_pairs={{2,0},{3,1},{0,2},{1,3},{6,4},{7,5},{4,6},{5,7},{10,8},{11,9},{8,1... | collective-permute-start | bytes 1568 | tf_op jit(solution)/shard_map/ppermute | solution.py:64
  23.0 11.4 %collective-permute-start.5 = (f32[2,16,1024]{2,1,0:T(8,128)S(1)}, f32[2,16,1024]{2,1,0:T(8,128)S(1)}, u32[]{:S(2)}, u32[]{:S(2)}) collective-permute-start(f32[2,16,1024]{2,1,0:T(8,128)S(1)} %pad_maximum_fusion.3), channel_id=1, source_target_pairs={{8,0},{12,4},{0,8},{4,12},{24,16},{28,20},{16,24},{20,28},{40,32},... | collective-permute-start | bytes 393224 | tf_op jit(solution)/shard_map/ppermute | solution.py:64
  25.2 9.2 %collective-permute-start.6 = (f32[2,16,1024]{2,1,0:T(8,128)S(1)}, f32[2,16,1024]{2,1,0:T(8,128)S(1)}, u32[]{:S(2)}, u32[]{:S(2)}) collective-permute-start(f32[2,16,1024]{2,1,0:T(8,128)S(1)} %pad_maximum_fusion.3), channel_id=1, source_target_pairs={{12,0},{0,4},{4,8},{8,12},{28,16},{16,20},{20,24},{24,28},{44,32},... | collective-permute-start | bytes 393224 | tf_op jit(solution)/shard_map/ppermute | solution.py:64
  25.2 9.2 %collective-permute-start.4 = (f32[2,16,1024]{2,1,0:T(8,128)S(1)}, f32[2,16,1024]{2,1,0:T(8,128)S(1)}, u32[]{:S(2)}, u32[]{:S(2)}) collective-permute-start(f32[2,16,1024]{2,1,0:T(8,128)S(1)} %pad_maximum_fusion.3), channel_id=1, source_target_pairs={{4,0},{8,4},{12,8},{0,12},{20,16},{24,20},{28,24},{16,28},{36,32},... | collective-permute-start | bytes 393224 | tf_op jit(solution)/shard_map/ppermute | solution.py:64
  36.5 18.4 %collective-permute-start.8 = (f32[2,16,1024]{2,1,0:T(8,128)}, f32[2,16,1024]{2,1,0:T(8,128)}, u32[]{:S(2)}, u32[]{:S(2)}) collective-permute-start(f32[2,16,1024]{2,1,0:T(8,128)} %pad_maximum_fusion.4), channel_id=1, source_target_pairs={{40,0},{44,4},{32,8},{36,12},{56,16},{60,20},{48,24},{52,28},{8,32... | collective-permute-start | bytes 393224 | tf_op jit(solution)/shard_map/ppermute | solution.py:64
  42.4 12.6 %collective-permute-start.9 = (f32[2,16,1024]{2,1,0:T(8,128)}, f32[2,16,1024]{2,1,0:T(8,128)}, u32[]{:S(2)}, u32[]{:S(2)}) collective-permute-start(f32[2,16,1024]{2,1,0:T(8,128)} %pad_maximum_fusion.4), channel_id=1, source_target_pairs={{48,0},{52,4},{56,8},{60,12},{0,16},{4,20},{8,24},{12,28},{16,32},... | collective-permute-start | bytes 393224 | tf_op jit(solution)/shard_map/ppermute | solution.py:64
  43.8 11.1 %collective-permute-start.7 = (f32[2,16,1024]{2,1,0:T(8,128)}, f32[2,16,1024]{2,1,0:T(8,128)}, u32[]{:S(2)}, u32[]{:S(2)}) collective-permute-start(f32[2,16,1024]{2,1,0:T(8,128)} %pad_maximum_fusion.4), channel_id=1, source_target_pairs={{16,0},{20,4},{24,8},{28,12},{32,16},{36,20},{40,24},{44,28},{48,3... | collective-permute-start | bytes 393224 | tf_op jit(solution)/shard_map/ppermute | solution.py:64
  57.3 8.0 %collective-permute-start.11 = (f32[2,16,1024]{2,1,0:T(8,128)S(1)}, f32[2,16,1024]{2,1,0:T(8,128)S(1)}, u32[]{:S(2)}, u32[]{:S(2)}) collective-permute-start(f32[2,16,1024]{2,1,0:T(8,128)S(1)} %pad_maximum_fusion.5), channel_id=1, source_target_pairs={{128,0},{132,4},{136,8},{140,12},{144,16},{148,20},{152,24},{156,2... | collective-permute-start | bytes 393224 | tf_op jit(solution)/shard_map/ppermute | solution.py:64
  60.6 6.4 %collective-permute-start.12 = (f32[2,16,1024]{2,1,0:T(8,128)S(1)}, f32[2,16,1024]{2,1,0:T(8,128)S(1)}, u32[]{:S(2)}, u32[]{:S(2)}) collective-permute-start(f32[2,16,1024]{2,1,0:T(8,128)S(1)} %pad_maximum_fusion.5), channel_id=1, source_target_pairs={{192,0},{196,4},{200,8},{204,12},{208,16},{212,20},{216,24},{220,2... | collective-permute-start | bytes 393224 | tf_op jit(solution)/shard_map/ppermute | solution.py:64
  61.3 5.8 %collective-permute-start.10 = (f32[2,16,1024]{2,1,0:T(8,128)S(1)}, f32[2,16,1024]{2,1,0:T(8,128)S(1)}, u32[]{:S(2)}, u32[]{:S(2)}) collective-permute-start(f32[2,16,1024]{2,1,0:T(8,128)S(1)} %pad_maximum_fusion.5), channel_id=1, source_target_pairs={{64,0},{68,4},{72,8},{76,12},{80,16},{84,20},{88,24},{92,28},{96,3... | collective-permute-start | bytes 393224 | tf_op jit(solution)/shard_map/ppermute | solution.py:64
  71.8 6.0 %collective-permute-start.13 = (bf16[3,2,1024]{2,1,0:T(2,128)(2,1)S(1)}, bf16[3,2,1024]{2,1,0:T(2,128)(2,1)S(1)}, u32[]{:S(2)}, u32[]{:S(2)}) collective-permute-start(bf16[3,2,1024]{2,1,0:T(2,128)(2,1)S(1)} %slice.827), channel_id=1, source_target_pairs={{4,0},{8,4},{12,8},{16,12},{20,16},{24,20},{28,24},{32,28},{36,32}... | collective-permute-start | bytes 36872 | tf_op jit(solution)/shard_map/ppermute | solution.py:17
  74.2 6.5 %collective-permute-start.18 = (f32[25,1024]{1,0:T(8,128)S(1)}, f32[25,1024]{1,0:T(8,128)S(1)}, u32[]{:S(2)}, u32[]{:S(2)}) collective-permute-start(f32[25,1024]{1,0:T(8,128)S(1)} %pad_maximum_fusion.6), channel_id=1, source_target_pairs={{8,0},{12,4},{0,8},{4,12},{24,16},{28,20},{16,24},{20,28},{40,32},... | collective-permute-start | bytes 307208 | tf_op jit(solution)/shard_map/ppermute | solution.py:64
  76.1 7.3 %collective-permute-start.19 = (f32[25,1024]{1,0:T(8,128)S(1)}, f32[25,1024]{1,0:T(8,128)S(1)}, u32[]{:S(2)}, u32[]{:S(2)}) collective-permute-start(f32[25,1024]{1,0:T(8,128)S(1)} %pad_maximum_fusion.6), channel_id=1, source_target_pairs={{12,0},{0,4},{4,8},{8,12},{28,16},{16,20},{20,24},{24,28},{44,32},... | collective-permute-start | bytes 307208 | tf_op jit(solution)/shard_map/ppermute | solution.py:64
  76.1 7.3 %collective-permute-start.17 = (f32[25,1024]{1,0:T(8,128)S(1)}, f32[25,1024]{1,0:T(8,128)S(1)}, u32[]{:S(2)}, u32[]{:S(2)}) collective-permute-start(f32[25,1024]{1,0:T(8,128)S(1)} %pad_maximum_fusion.6), channel_id=1, source_target_pairs={{4,0},{8,4},{12,8},{0,12},{20,16},{24,20},{28,24},{16,28},{36,32},... | collective-permute-start | bytes 307208 | tf_op jit(solution)/shard_map/ppermute | solution.py:64
  78.6 8.7 %collective-permute-start.15 = (f32[128]{0:T(128)S(1)}, f32[128]{0:T(128)S(1)}, u32[]{:S(2)}, u32[]{:S(2)}) collective-permute-start(f32[128]{0:T(128)S(1)} %get-tuple-element.61), channel_id=1, source_target_pairs={{2,0},{3,1},{0,2},{1,3},{6,4},{7,5},{4,6},{5,7},{10,8},{11,9},{8,1... | collective-permute-start | bytes 1544 | tf_op jit(solution)/shard_map/ppermute | solution.py:64
  78.7 11.9 %collective-permute-start.16 = (f32[128]{0:T(128)S(1)}, f32[128]{0:T(128)S(1)}, u32[]{:S(2)}, u32[]{:S(2)}) collective-permute-start(f32[128]{0:T(128)S(1)} %get-tuple-element.61), channel_id=1, source_target_pairs={{3,0},{0,1},{1,2},{2,3},{7,4},{4,5},{5,6},{6,7},{11,8},{8,9},{9,10... | collective-permute-start | bytes 1544 | tf_op jit(solution)/shard_map/ppermute | solution.py:64
  80.7 10.0 %collective-permute-start.14 = (f32[128]{0:T(128)S(1)}, f32[128]{0:T(128)S(1)}, u32[]{:S(2)}, u32[]{:S(2)}) collective-permute-start(f32[128]{0:T(128)S(1)} %get-tuple-element.61), channel_id=1, source_target_pairs={{1,0},{2,1},{3,2},{0,3},{5,4},{6,5},{7,6},{4,7},{9,8},{10,9},{11,1... | collective-permute-start | bytes 1544 | tf_op jit(solution)/shard_map/ppermute | solution.py:64
  83.5 14.7 %collective-permute-start.21 = (f32[25,1024]{1,0:T(8,128)S(1)}, f32[25,1024]{1,0:T(8,128)S(1)}, u32[]{:S(2)}, u32[]{:S(2)}) collective-permute-start(f32[25,1024]{1,0:T(8,128)S(1)} %add_add_fusion.2), channel_id=1, source_target_pairs={{40,0},{44,4},{32,8},{36,12},{56,16},{60,20},{48,24},{52,28},{8,32... | collective-permute-start | bytes 307208 | tf_op jit(solution)/shard_map/ppermute | solution.py:64
  86.5 11.6 %collective-permute-start.22 = (f32[25,1024]{1,0:T(8,128)S(1)}, f32[25,1024]{1,0:T(8,128)S(1)}, u32[]{:S(2)}, u32[]{:S(2)}) collective-permute-start(f32[25,1024]{1,0:T(8,128)S(1)} %add_add_fusion.2), channel_id=1, source_target_pairs={{48,0},{52,4},{56,8},{60,12},{0,16},{4,20},{8,24},{12,28},{16,32},... | collective-permute-start | bytes 307208 | tf_op jit(solution)/shard_map/ppermute | solution.py:64
  87.3 12.6 %collective-permute-start.20 = (f32[25,1024]{1,0:T(8,128)S(1)}, f32[25,1024]{1,0:T(8,128)S(1)}, u32[]{:S(2)}, u32[]{:S(2)}) collective-permute-start(f32[25,1024]{1,0:T(8,128)S(1)} %add_add_fusion.2), channel_id=1, source_target_pairs={{16,0},{20,4},{24,8},{28,12},{32,16},{36,20},{40,24},{44,28},{48,3... | collective-permute-start | bytes 307208 | tf_op jit(solution)/shard_map/ppermute | solution.py:64
  100.0 8.0 %collective-permute-start.24 = (f32[25,1024]{1,0:T(8,128)S(1)}, f32[25,1024]{1,0:T(8,128)S(1)}, u32[]{:S(2)}, u32[]{:S(2)}) collective-permute-start(f32[25,1024]{1,0:T(8,128)S(1)} %add_add_fusion.1), channel_id=1, source_target_pairs={{128,0},{132,4},{136,8},{140,12},{144,16},{148,20},{152,24},{156,2... | collective-permute-start | bytes 307208 | tf_op jit(solution)/shard_map/ppermute | solution.py:64
  101.9 7.8 %collective-permute-start.25 = (f32[25,1024]{1,0:T(8,128)S(1)}, f32[25,1024]{1,0:T(8,128)S(1)}, u32[]{:S(2)}, u32[]{:S(2)}) collective-permute-start(f32[25,1024]{1,0:T(8,128)S(1)} %add_add_fusion.1), channel_id=1, source_target_pairs={{192,0},{196,4},{200,8},{204,12},{208,16},{212,20},{216,24},{220,2... | collective-permute-start | bytes 307208 | tf_op jit(solution)/shard_map/ppermute | solution.py:64
  104.0 6.0 %collective-permute-start.23 = (f32[25,1024]{1,0:T(8,128)S(1)}, f32[25,1024]{1,0:T(8,128)S(1)}, u32[]{:S(2)}, u32[]{:S(2)}) collective-permute-start(f32[25,1024]{1,0:T(8,128)S(1)} %add_add_fusion.1), channel_id=1, source_target_pairs={{64,0},{68,4},{72,8},{76,12},{80,16},{84,20},{88,24},{92,28},{96,3... | collective-permute-start | bytes 307208 | tf_op jit(solution)/shard_map/ppermute | solution.py:64
  (48 other events, 299.2 us)

commit v12 on v7

--- a/solution.py
+++ b/solution.py
@@ -260,10 +260,10 @@
     partial_sums = jnp.concatenate(
         [cross_part + local_terms, short_terms.reshape(3 * KS, chan_count)], 0
     )
-    whole_sums = summed(partial_sums, "ctx")
     norm_factor = 1.0 / jnp.sqrt(jnp.float32(total_rows))
-    grad_residues = whole_sums[:M] * norm_factor
-    grad_short = whole_sums[M:].reshape(3, KS, chan_count) * norm_factor
+    whole_sums = summed(partial_sums * norm_factor, "ctx")
+    grad_residues = whole_sums[:M]
+    grad_short = whole_sums[M:].reshape(3, KS, chan_count)
     row_dot = summed(jnp.sum(norm_gain[None, :] * grad_normed * stream_wide, axis=1), "ch")
     grad_stream = (
         row_scale[:, None] * norm_gain[None, :] * grad_normed

time: 107 us -> 107 us (level)
  no operation moved by 1% of the time
where the time goes in v12:
time: 107 us
  waiting for transfers between devices  43 us (40%)
  starting transfers between devices  36.3 us (34%)
  other arithmetic  21.4 us (20%)
  local copies, waits for them, and re-layouts  4.32 us (4%)
  between operations  1.76 us (2%)
    ppermute x24, waiting for transfers between devices, members(): received.append(lax.ppermute(value, axis, pairs))  43 us
    ppermute x24, starting transfers between devices, members(): received.append(lax.ppermute(value, axis, pairs))  32.5 us
    ppermute x2, starting transfers between devices, passed_along(): lax.ppermute(value, axis, [(source, source + steps) for source in range(f...  3.83 us
  transfers between devices with their start and end apart: 26, of which 18 were waited for; matrix products, arithmetic and copies ran while one was open for 10% of the time, Pallas kernels for 0%

profile of v12, /device:TPU:32, one launch (start us, length us, event | category | flops | bytes accessed | tf_op | source)
XLA Modules:
  0.0 106.8 jit_solution(18047409281874915979)
XLA Ops:
  1.4 1.9 %collective-permute-start = (bf16[2,1024]{1,0:T(2,128)(2,1)S(1)}, bf16[2,1024]{1,0:T(2,128)(2,1)S(1)}, u32[]{:S(2)}, u32[]{:S(2)}) collective-permute-start(bf16[2,1024]{1,0:T(2,128)(2,1)S(1)} %slice.598), channel_id=1, source_target_pairs={{0,4},{4,8},{8,12},{12,16},{16,20},{20,24},{24,28},{28,32},{32,36}... | collective-permute-start | bytes 12296 | tf_op jit(solution)/shard_map/ppermute | solution.py:17
  5.8 2.0 %multiply_exponential_fusion = (f32[16,32,1024]{2,1,0:T(8,128)}, f32[16,32,1024]{2,1,0:T(8,128)S(1)}) fusion(f32[32]{0:T(128)S(1)} %broadcast_subtract_fusion.1, f32[16,1024]{1,0:T(8,128)S(1)} %neg.5, f32[32]{0:T(128)S(1)} %iota_convert_fusion.1), kind=kLoop, calls=%fused_computation.108 | loop fusion | flops 1048576 | bytes 4260096 | tf_op jit(solution)/shard_map/exp | solution.py:160
  8.0 2.8 %collective-permute-start.1 = (f32[130]{0:T(256)S(1)}, f32[130]{0:T(256)S(1)}, u32[]{:S(2)}, u32[]{:S(2)}) collective-permute-start(f32[130]{0:T(256)S(1)} %fusion.3), channel_id=1, source_target_pairs={{1,0},{2,1},{3,2},{0,3},{5,4},{6,5},{7,6},{4,7},{9,8},{10,9},{11,1... | collective-permute-start | bytes 1568 | tf_op jit(solution)/shard_map/ppermute | solution.py:64
  12.5 3.4 %collective-permute-done.2 = f32[130]{0:T(256)S(1)} collective-permute-done((f32[130]{0:T(256)S(1)}, f32[130]{0:T(256)S(1)}, u32[]{:S(2)}, u32[]{:S(2)}) %collective-permute-start.2) | collective-permute-done | bytes 552 | tf_op jit(solution)/shard_map/ppermute | solution.py:64
  21.3 1.9 %collective-permute-start.5 = (f32[2,16,1024]{2,1,0:T(8,128)S(1)}, f32[2,16,1024]{2,1,0:T(8,128)S(1)}, u32[]{:S(2)}, u32[]{:S(2)}) collective-permute-start(f32[2,16,1024]{2,1,0:T(8,128)S(1)} %pad_maximum_fusion.3), channel_id=1, source_target_pairs={{8,0},{12,4},{0,8},{4,12},{24,16},{28,20},{16,24},{20,28},{40,32},... | collective-permute-start | bytes 393224 | tf_op jit(solution)/shard_map/ppermute | solution.py:64
  25.2 4.8 %collective-permute-done.5 = f32[2,16,1024]{2,1,0:T(8,128)S(1)} collective-permute-done((f32[2,16,1024]{2,1,0:T(8,128)S(1)}, f32[2,16,1024]{2,1,0:T(8,128)S(1)}, u32[]{:S(2)}, u32[]{:S(2)}) %collective-permute-start.5) | collective-permute-done | bytes 131104 | tf_op jit(solution)/shard_map/ppermute | solution.py:64
  30.2 4.9 %collective-permute-start.7 = (f32[2,16,1024]{2,1,0:T(8,128)S(1)}, f32[2,16,1024]{2,1,0:T(8,128)S(1)}, u32[]{:S(2)}, u32[]{:S(2)}) collective-permute-start(f32[2,16,1024]{2,1,0:T(8,128)S(1)} %pad_maximum_fusion.4), channel_id=1, source_target_pairs={{16,0},{20,4},{24,8},{28,12},{32,16},{36,20},{40,24},{44,28},{48,3... | collective-permute-start | bytes 393224 | tf_op jit(solution)/shard_map/ppermute | solution.py:64
  36.3 2.4 %collective-permute-start.9 = (f32[2,16,1024]{2,1,0:T(8,128)S(1)}, f32[2,16,1024]{2,1,0:T(8,128)S(1)}, u32[]{:S(2)}, u32[]{:S(2)}) collective-permute-start(f32[2,16,1024]{2,1,0:T(8,128)S(1)} %pad_maximum_fusion.4), channel_id=1, source_target_pairs={{48,0},{52,4},{56,8},{60,12},{0,16},{4,20},{8,24},{12,28},{16,32},... | collective-permute-start | bytes 393224 | tf_op jit(solution)/shard_map/ppermute | solution.py:64
  42.1 5.7 %collective-permute-done.8 = f32[2,16,1024]{2,1,0:T(8,128)S(1)} collective-permute-done((f32[2,16,1024]{2,1,0:T(8,128)S(1)}, f32[2,16,1024]{2,1,0:T(8,128)S(1)}, u32[]{:S(2)}, u32[]{:S(2)}) %collective-permute-start.8) | collective-permute-done | bytes 131104 | tf_op jit(solution)/shard_map/ppermute | solution.py:64
  48.3 3.1 %collective-permute-start.10 = (f32[2,16,1024]{2,1,0:T(8,128)S(1)}, f32[2,16,1024]{2,1,0:T(8,128)S(1)}, u32[]{:S(2)}, u32[]{:S(2)}) collective-permute-start(f32[2,16,1024]{2,1,0:T(8,128)S(1)} %pad_maximum_fusion.5), channel_id=1, source_target_pairs={{64,0},{68,4},{72,8},{76,12},{80,16},{84,20},{88,24},{92,28},{96,3... | collective-permute-start | bytes 393224 | tf_op jit(solution)/shard_map/ppermute | solution.py:64
  53.1 4.1 %collective-permute-done.10 = f32[2,16,1024]{2,1,0:T(8,128)S(1)} collective-permute-done((f32[2,16,1024]{2,1,0:T(8,128)S(1)}, f32[2,16,1024]{2,1,0:T(8,128)S(1)}, u32[]{:S(2)}, u32[]{:S(2)}) %collective-permute-start.10) | collective-permute-done | bytes 131104 | tf_op jit(solution)/shard_map/ppermute | solution.py:64
  57.2 2.1 %collective-permute-done.11 = f32[2,16,1024]{2,1,0:T(8,128)S(1)} collective-permute-done((f32[2,16,1024]{2,1,0:T(8,128)S(1)}, f32[2,16,1024]{2,1,0:T(8,128)S(1)}, u32[]{:S(2)}, u32[]{:S(2)}) %collective-permute-start.11) | collective-permute-done | bytes 131104 | tf_op jit(solution)/shard_map/ppermute | solution.py:64
  62.9 1.9 %fusion.150 = f32[4,32,1024]{2,1,0:T(8,128)S(1)} fusion(f32[4,32,1024]{2,1,0:T(8,128)S(1)} %multiply_reduce_fusion, f32[4,32,1024]{2,1,0:T(8,128)S(1)} %bitcast.403, f32[1024]{0:T(1024)S(1)} %bitcast.418, f32[1024]{0:T(1024)S(1)} %bitcast.420, f32[1024]{0:T(1024)S(1)} %bitcast.422, f32[1024]{0:T(1024)S(1)} %bitcast.424, f32[1024]{0:T(1024)S(1)} %bitcast.426, ...), kind=kLoop, calls=%fused_computation.275 | loop fusion | flops 8388608 | bytes 1703936 | tf_op jit(solution)/shard_map/add | solution.py:220
  64.7 1.7 %fusion.87 = f32[4,32,1024]{2,1,0:T(8,128)S(1)} fusion(f32[4,32,1024]{2,1,0:T(8,128)S(1)} %multiply_reduce_fusion.1, f32[4,32,1024]{2,1,0:T(8,128)S(1)} %bitcast_convert_fusion, f32[1024]{0:T(1024)S(1)} %bitcast.419, f32[1024]{0:T(1024)S(1)} %bitcast.421, f32[1024]{0:T(1024)S(1)} %bitcast.423, f32[1024]{0:T(1024)S(1)} %bitcast.425, f32[1024]{0:T(1024)S(1)} %bitcast.427, ...), kind=kLoop, calls=%fused_computation.212 | loop fusion | flops 8388608 | bytes 1703936 | tf_op jit(solution)/shard_map/add | solution.py:212
  68.5 1.9 %collective-permute-start.13 = (bf16[3,2,1024]{2,1,0:T(2,128)(2,1)S(1)}, bf16[3,2,1024]{2,1,0:T(2,128)(2,1)S(1)}, u32[]{:S(2)}, u32[]{:S(2)}) collective-permute-start(bf16[3,2,1024]{2,1,0:T(2,128)(2,1)S(1)} %slice.827), channel_id=1, source_target_pairs={{4,0},{8,4},{12,8},{16,12},{20,16},{24,20},{28,24},{32,28},{36,32}... | collective-permute-start | bytes 36872 | tf_op jit(solution)/shard_map/ppermute | solution.py:17
  70.6 2.1 %collective-permute-start.18 = (f32[25,1024]{1,0:T(8,128)S(1)}, f32[25,1024]{1,0:T(8,128)S(1)}, u32[]{:S(2)}, u32[]{:S(2)}) collective-permute-start(f32[25,1024]{1,0:T(8,128)S(1)} %maximum_multiply_fusion), channel_id=1, source_target_pairs={{8,0},{12,4},{0,8},{4,12},{24,16},{28,20},{16,24},{20,28},{40,32},... | collective-permute-start | bytes 307208 | tf_op jit(solution)/shard_map/ppermute | solution.py:64
  75.7 3.7 %collective-permute-done.18 = f32[25,1024]{1,0:T(8,128)S(1)} collective-permute-done((f32[25,1024]{1,0:T(8,128)S(1)}, f32[25,1024]{1,0:T(8,128)S(1)}, u32[]{:S(2)}, u32[]{:S(2)}) %collective-permute-start.18) | collective-permute-done | bytes 102432 | tf_op jit(solution)/shard_map/ppermute | solution.py:64
  79.5 1.7 %collective-permute-start.20 = (f32[25,1024]{1,0:T(8,128)S(1)}, f32[25,1024]{1,0:T(8,128)S(1)}, u32[]{:S(2)}, u32[]{:S(2)}) collective-permute-start(f32[25,1024]{1,0:T(8,128)S(1)} %add_add_fusion.2), channel_id=1, source_target_pairs={{16,0},{20,4},{24,8},{28,12},{32,16},{36,20},{40,24},{44,28},{48,3... | collective-permute-start | bytes 307208 | tf_op jit(solution)/shard_map/ppermute | solution.py:64
  81.2 2.8 %collective-permute-start.21 = (f32[25,1024]{1,0:T(8,128)S(1)}, f32[25,1024]{1,0:T(8,128)S(1)}, u32[]{:S(2)}, u32[]{:S(2)}) collective-permute-start(f32[25,1024]{1,0:T(8,128)S(1)} %add_add_fusion.2), channel_id=1, source_target_pairs={{40,0},{44,4},{32,8},{36,12},{56,16},{60,20},{48,24},{52,28},{8,32... | collective-permute-start | bytes 307208 | tf_op jit(solution)/shard_map/ppermute | solution.py:64
  86.9 7.7 %collective-permute-done.21 = f32[25,1024]{1,0:T(8,128)S(1)} collective-permute-done((f32[25,1024]{1,0:T(8,128)S(1)}, f32[25,1024]{1,0:T(8,128)S(1)}, u32[]{:S(2)}, u32[]{:S(2)}) %collective-permute-start.21) | collective-permute-done | bytes 102432 | tf_op jit(solution)/shard_map/ppermute | solution.py:64
  96.0 2.1 %collective-permute-start.24 = (f32[25,1024]{1,0:T(8,128)S(1)}, f32[25,1024]{1,0:T(8,128)S(1)}, u32[]{:S(2)}, u32[]{:S(2)}) collective-permute-start(f32[25,1024]{1,0:T(8,128)S(1)} %add_add_fusion.1), channel_id=1, source_target_pairs={{128,0},{132,4},{136,8},{140,12},{144,16},{148,20},{152,24},{156,2... | collective-permute-start | bytes 307208 | tf_op jit(solution)/shard_map/ppermute | solution.py:64
  99.0 2.1 %collective-permute-done.23 = f32[25,1024]{1,0:T(8,128)S(1)} collective-permute-done((f32[25,1024]{1,0:T(8,128)S(1)}, f32[25,1024]{1,0:T(8,128)S(1)}, u32[]{:S(2)}, u32[]{:S(2)}) %collective-permute-start.23) | collective-permute-done | bytes 102432 | tf_op jit(solution)/shard_map/ppermute | solution.py:64
  101.2 2.3 %collective-permute-done.24 = f32[25,1024]{1,0:T(8,128)S(1)} collective-permute-done((f32[25,1024]{1,0:T(8,128)S(1)}, f32[25,1024]{1,0:T(8,128)S(1)}, u32[]{:S(2)}, u32[]{:S(2)}) %collective-permute-start.24) | collective-permute-done | bytes 102432 | tf_op jit(solution)/shard_map/ppermute | solution.py:64
  103.5 1.9 %collective-permute-done.25 = f32[25,1024]{1,0:T(8,128)S(1)} collective-permute-done((f32[25,1024]{1,0:T(8,128)S(1)}, f32[25,1024]{1,0:T(8,128)S(1)}, u32[]{:S(2)}, u32[]{:S(2)}) %collective-permute-start.25) | collective-permute-done | bytes 102432 | tf_op jit(solution)/shard_map/ppermute | solution.py:64
  (128 shorter events, 33.8 us)
Async XLA Ops:
  1.4 6.4 %collective-permute-start = (bf16[2,1024]{1,0:T(2,128)(2,1)S(1)}, bf16[2,1024]{1,0:T(2,128)(2,1)S(1)}, u32[]{:S(2)}, u32[]{:S(2)}) collective-permute-start(bf16[2,1024]{1,0:T(2,128)(2,1)S(1)} %slice.598), channel_id=1, source_target_pairs={{0,4},{4,8},{8,12},{12,16},{16,20},{20,24},{24,28},{28,32},{32,36}... | collective-permute-start | bytes 12296 | tf_op jit(solution)/shard_map/ppermute | solution.py:17
  8.0 4.5 %collective-permute-start.1 = (f32[130]{0:T(256)S(1)}, f32[130]{0:T(256)S(1)}, u32[]{:S(2)}, u32[]{:S(2)}) collective-permute-start(f32[130]{0:T(256)S(1)} %fusion.3), channel_id=1, source_target_pairs={{1,0},{2,1},{3,2},{0,3},{5,4},{6,5},{7,6},{4,7},{9,8},{10,9},{11,1... | collective-permute-start | bytes 1568 | tf_op jit(solution)/shard_map/ppermute | solution.py:64
  10.8 5.1 %collective-permute-start.2 = (f32[130]{0:T(256)S(1)}, f32[130]{0:T(256)S(1)}, u32[]{:S(2)}, u32[]{:S(2)}) collective-permute-start(f32[130]{0:T(256)S(1)} %fusion.3), channel_id=1, source_target_pairs={{2,0},{3,1},{0,2},{1,3},{6,4},{7,5},{4,6},{5,7},{10,8},{11,9},{8,1... | collective-permute-start | bytes 1568 | tf_op jit(solution)/shard_map/ppermute | solution.py:64
  11.6 4.8 %collective-permute-start.3 = (f32[130]{0:T(256)S(1)}, f32[130]{0:T(256)S(1)}, u32[]{:S(2)}, u32[]{:S(2)}) collective-permute-start(f32[130]{0:T(256)S(1)} %fusion.3), channel_id=1, source_target_pairs={{3,0},{0,1},{1,2},{2,3},{7,4},{4,5},{5,6},{6,7},{11,8},{8,9},{9,10... | collective-permute-start | bytes 1568 | tf_op jit(solution)/shard_map/ppermute | solution.py:64
  21.3 8.7 %collective-permute-start.5 = (f32[2,16,1024]{2,1,0:T(8,128)S(1)}, f32[2,16,1024]{2,1,0:T(8,128)S(1)}, u32[]{:S(2)}, u32[]{:S(2)}) collective-permute-start(f32[2,16,1024]{2,1,0:T(8,128)S(1)} %pad_maximum_fusion.3), channel_id=1, source_target_pairs={{8,0},{12,4},{0,8},{4,12},{24,16},{28,20},{16,24},{20,28},{40,32},... | collective-permute-start | bytes 393224 | tf_op jit(solution)/shard_map/ppermute | solution.py:64
  23.2 6.8 %collective-permute-start.6 = (f32[2,16,1024]{2,1,0:T(8,128)S(1)}, f32[2,16,1024]{2,1,0:T(8,128)S(1)}, u32[]{:S(2)}, u32[]{:S(2)}) collective-permute-start(f32[2,16,1024]{2,1,0:T(8,128)S(1)} %pad_maximum_fusion.3), channel_id=1, source_target_pairs={{12,0},{0,4},{4,8},{8,12},{28,16},{16,20},{20,24},{24,28},{44,32},... | collective-permute-start | bytes 393224 | tf_op jit(solution)/shard_map/ppermute | solution.py:64
  30.2 11.9 %collective-permute-start.7 = (f32[2,16,1024]{2,1,0:T(8,128)S(1)}, f32[2,16,1024]{2,1,0:T(8,128)S(1)}, u32[]{:S(2)}, u32[]{:S(2)}) collective-permute-start(f32[2,16,1024]{2,1,0:T(8,128)S(1)} %pad_maximum_fusion.4), channel_id=1, source_target_pairs={{16,0},{20,4},{24,8},{28,12},{32,16},{36,20},{40,24},{44,28},{48,3... | collective-permute-start | bytes 393224 | tf_op jit(solution)/shard_map/ppermute | solution.py:64
  35.1 12.6 %collective-permute-start.8 = (f32[2,16,1024]{2,1,0:T(8,128)S(1)}, f32[2,16,1024]{2,1,0:T(8,128)S(1)}, u32[]{:S(2)}, u32[]{:S(2)}) collective-permute-start(f32[2,16,1024]{2,1,0:T(8,128)S(1)} %pad_maximum_fusion.4), channel_id=1, source_target_pairs={{40,0},{44,4},{32,8},{36,12},{56,16},{60,20},{48,24},{52,28},{8,32... | collective-permute-start | bytes 393224 | tf_op jit(solution)/shard_map/ppermute | solution.py:64
  36.3 11.9 %collective-permute-start.9 = (f32[2,16,1024]{2,1,0:T(8,128)S(1)}, f32[2,16,1024]{2,1,0:T(8,128)S(1)}, u32[]{:S(2)}, u32[]{:S(2)}) collective-permute-start(f32[2,16,1024]{2,1,0:T(8,128)S(1)} %pad_maximum_fusion.4), channel_id=1, source_target_pairs={{48,0},{52,4},{56,8},{60,12},{0,16},{4,20},{8,24},{12,28},{16,32},... | collective-permute-start | bytes 393224 | tf_op jit(solution)/shard_map/ppermute | solution.py:64
  48.3 8.9 %collective-permute-start.10 = (f32[2,16,1024]{2,1,0:T(8,128)S(1)}, f32[2,16,1024]{2,1,0:T(8,128)S(1)}, u32[]{:S(2)}, u32[]{:S(2)}) collective-permute-start(f32[2,16,1024]{2,1,0:T(8,128)S(1)} %pad_maximum_fusion.5), channel_id=1, source_target_pairs={{64,0},{68,4},{72,8},{76,12},{80,16},{84,20},{88,24},{92,28},{96,3... | collective-permute-start | bytes 393224 | tf_op jit(solution)/shard_map/ppermute | solution.py:64
  51.4 7.9 %collective-permute-start.11 = (f32[2,16,1024]{2,1,0:T(8,128)S(1)}, f32[2,16,1024]{2,1,0:T(8,128)S(1)}, u32[]{:S(2)}, u32[]{:S(2)}) collective-permute-start(f32[2,16,1024]{2,1,0:T(8,128)S(1)} %pad_maximum_fusion.5), channel_id=1, source_target_pairs={{128,0},{132,4},{136,8},{140,12},{144,16},{148,20},{152,24},{156,2... | collective-permute-start | bytes 393224 | tf_op jit(solution)/shard_map/ppermute | solution.py:64
  52.1 8.9 %collective-permute-start.12 = (f32[2,16,1024]{2,1,0:T(8,128)S(1)}, f32[2,16,1024]{2,1,0:T(8,128)S(1)}, u32[]{:S(2)}, u32[]{:S(2)}) collective-permute-start(f32[2,16,1024]{2,1,0:T(8,128)S(1)} %pad_maximum_fusion.5), channel_id=1, source_target_pairs={{192,0},{196,4},{200,8},{204,12},{208,16},{212,20},{216,24},{220,2... | collective-permute-start | bytes 393224 | tf_op jit(solution)/shard_map/ppermute | solution.py:64
  68.5 4.4 %collective-permute-start.13 = (bf16[3,2,1024]{2,1,0:T(2,128)(2,1)S(1)}, bf16[3,2,1024]{2,1,0:T(2,128)(2,1)S(1)}, u32[]{:S(2)}, u32[]{:S(2)}) collective-permute-start(bf16[3,2,1024]{2,1,0:T(2,128)(2,1)S(1)} %slice.827), channel_id=1, source_target_pairs={{4,0},{8,4},{12,8},{16,12},{20,16},{24,20},{28,24},{32,28},{36,32}... | collective-permute-start | bytes 36872 | tf_op jit(solution)/shard_map/ppermute | solution.py:17
  70.6 8.8 %collective-permute-start.18 = (f32[25,1024]{1,0:T(8,128)S(1)}, f32[25,1024]{1,0:T(8,128)S(1)}, u32[]{:S(2)}, u32[]{:S(2)}) collective-permute-start(f32[25,1024]{1,0:T(8,128)S(1)} %maximum_multiply_fusion), channel_id=1, source_target_pairs={{8,0},{12,4},{0,8},{4,12},{24,16},{28,20},{16,24},{20,28},{40,32},... | collective-permute-start | bytes 307208 | tf_op jit(solution)/shard_map/ppermute | solution.py:64
  72.7 6.7 %collective-permute-start.19 = (f32[25,1024]{1,0:T(8,128)S(1)}, f32[25,1024]{1,0:T(8,128)S(1)}, u32[]{:S(2)}, u32[]{:S(2)}) collective-permute-start(f32[25,1024]{1,0:T(8,128)S(1)} %maximum_multiply_fusion), channel_id=1, source_target_pairs={{12,0},{0,4},{4,8},{8,12},{28,16},{16,20},{20,24},{24,28},{44,32},... | collective-permute-start | bytes 307208 | tf_op jit(solution)/shard_map/ppermute | solution.py:64
  73.6 10.4 %collective-permute-start.14 = (f32[128]{0:T(128)S(1)}, f32[128]{0:T(128)S(1)}, u32[]{:S(2)}, u32[]{:S(2)}) collective-permute-start(f32[128]{0:T(128)S(1)} %get-tuple-element.59), channel_id=1, source_target_pairs={{1,0},{2,1},{3,2},{0,3},{5,4},{6,5},{7,6},{4,7},{9,8},{10,9},{11,1... | collective-permute-start | bytes 1544 | tf_op jit(solution)/shard_map/ppermute | solution.py:64
  74.0 11.2 %collective-permute-start.15 = (f32[128]{0:T(128)S(1)}, f32[128]{0:T(128)S(1)}, u32[]{:S(2)}, u32[]{:S(2)}) collective-permute-start(f32[128]{0:T(128)S(1)} %get-tuple-element.59), channel_id=1, source_target_pairs={{2,0},{3,1},{0,2},{1,3},{6,4},{7,5},{4,6},{5,7},{10,8},{11,9},{8,1... | collective-permute-start | bytes 1544 | tf_op jit(solution)/shard_map/ppermute | solution.py:64
  74.5 10.7 %collective-permute-start.16 = (f32[128]{0:T(128)S(1)}, f32[128]{0:T(128)S(1)}, u32[]{:S(2)}, u32[]{:S(2)}) collective-permute-start(f32[128]{0:T(128)S(1)} %get-tuple-element.59), channel_id=1, source_target_pairs={{3,0},{0,1},{1,2},{2,3},{7,4},{4,5},{5,6},{6,7},{11,8},{8,9},{9,10... | collective-permute-start | bytes 1544 | tf_op jit(solution)/shard_map/ppermute | solution.py:64
  79.5 7.4 %collective-permute-start.20 = (f32[25,1024]{1,0:T(8,128)S(1)}, f32[25,1024]{1,0:T(8,128)S(1)}, u32[]{:S(2)}, u32[]{:S(2)}) collective-permute-start(f32[25,1024]{1,0:T(8,128)S(1)} %add_add_fusion.2), channel_id=1, source_target_pairs={{16,0},{20,4},{24,8},{28,12},{32,16},{36,20},{40,24},{44,28},{48,3... | collective-permute-start | bytes 307208 | tf_op jit(solution)/shard_map/ppermute | solution.py:64
  81.2 13.5 %collective-permute-start.21 = (f32[25,1024]{1,0:T(8,128)S(1)}, f32[25,1024]{1,0:T(8,128)S(1)}, u32[]{:S(2)}, u32[]{:S(2)}) collective-permute-start(f32[25,1024]{1,0:T(8,128)S(1)} %add_add_fusion.2), channel_id=1, source_target_pairs={{40,0},{44,4},{32,8},{36,12},{56,16},{60,20},{48,24},{52,28},{8,32... | collective-permute-start | bytes 307208 | tf_op jit(solution)/shard_map/ppermute | solution.py:64
  84.0 11.3 %collective-permute-start.22 = (f32[25,1024]{1,0:T(8,128)S(1)}, f32[25,1024]{1,0:T(8,128)S(1)}, u32[]{:S(2)}, u32[]{:S(2)}) collective-permute-start(f32[25,1024]{1,0:T(8,128)S(1)} %add_add_fusion.2), channel_id=1, source_target_pairs={{48,0},{52,4},{56,8},{60,12},{0,16},{4,20},{8,24},{12,28},{16,32},... | collective-permute-start | bytes 307208 | tf_op jit(solution)/shard_map/ppermute | solution.py:64
  95.4 5.8 %collective-permute-start.23 = (f32[25,1024]{1,0:T(8,128)S(1)}, f32[25,1024]{1,0:T(8,128)S(1)}, u32[]{:S(2)}, u32[]{:S(2)}) collective-permute-start(f32[25,1024]{1,0:T(8,128)S(1)} %add_add_fusion.1), channel_id=1, source_target_pairs={{64,0},{68,4},{72,8},{76,12},{80,16},{84,20},{88,24},{92,28},{96,3... | collective-permute-start | bytes 307208 | tf_op jit(solution)/shard_map/ppermute | solution.py:64
  96.0 7.4 %collective-permute-start.24 = (f32[25,1024]{1,0:T(8,128)S(1)}, f32[25,1024]{1,0:T(8,128)S(1)}, u32[]{:S(2)}, u32[]{:S(2)}) collective-permute-start(f32[25,1024]{1,0:T(8,128)S(1)} %add_add_fusion.1), channel_id=1, source_target_pairs={{128,0},{132,4},{136,8},{140,12},{144,16},{148,20},{152,24},{156,2... | collective-permute-start | bytes 307208 | tf_op jit(solution)/shard_map/ppermute | solution.py:64
  98.2 7.2 %collective-permute-start.25 = (f32[25,1024]{1,0:T(8,128)S(1)}, f32[25,1024]{1,0:T(8,128)S(1)}, u32[]{:S(2)}, u32[]{:S(2)}) collective-permute-start(f32[25,1024]{1,0:T(8,128)S(1)} %add_add_fusion.1), channel_id=1, source_target_pairs={{192,0},{196,4},{200,8},{204,12},{208,16},{212,20},{216,24},{220,2... | collective-permute-start | bytes 307208 | tf_op jit(solution)/shard_map/ppermute | solution.py:64
  (17 other events, 88.6 us)

commit v13 on v7

--- a/solution.py
+++ b/solution.py
@@ -108,12 +108,12 @@
     return incoming, later, riders
 
 
-def summed(value, axis):
+def summed(value, axis, pairwise=False):
     count = lax.axis_size(axis)
     if not power_of_two(count):
         return lax.psum(value, axis)
     stride = 1
-    for radix in radices(count):
+    for radix in [2] * (count.bit_length() - 1) if pairwise else radices(count):
         group, _ = members(value, axis, stride, radix)
         if radix == 4:
             value = (group[0] + group[1]) + (group[2] + group[3])
@@ -264,7 +264,9 @@
     norm_factor = 1.0 / jnp.sqrt(jnp.float32(total_rows))
     grad_residues = whole_sums[:M] * norm_factor
     grad_short = whole_sums[M:].reshape(3, KS, chan_count) * norm_factor
-    row_dot = summed(jnp.sum(norm_gain[None, :] * grad_normed * stream_wide, axis=1), "ch")
+    row_dot = summed(
+        jnp.sum(norm_gain[None, :] * grad_normed * stream_wide, axis=1), "ch", pairwise=True
+    )
     grad_stream = (
         row_scale[:, None] * norm_gain[None, :] * grad_normed
         - stream_wide * (row_scale**3 * row_dot / total_chans)[:, None]

time: 107 us -> 112 us (1.047)
  waiting for transfers between devices: 43 us -> 48.2 us
    ppermute x24 -> x23, waiting for transfers between devices: 43 us -> 47.1 us  [members(): received.append(lax.ppermute(value, axis, pairs))]
    ppermute x24 -> x23, starting transfers between devices: 32.5 us -> 31.7 us  [members(): received.append(lax.ppermute(value, axis, pairs))]
  transfers between devices with their start and end apart: 26 -> 25, of which waited for: 18 -> 19; matrix products, arithmetic and copies ran while one was open for 10% -> 9% of each run, Pallas kernels for 0% -> 0%
where the time goes in v13:
time: 112 us; the launch traced here: 111 us
  waiting for transfers between devices  48.2 us (43%)
  starting transfers between devices  35.6 us (32%)
  other arithmetic  22 us (20%)
  local copies, waits for them, and re-layouts  3.69 us (3%)
  between operations  1.82 us (2%)
    ppermute x23, waiting for transfers between devices, members(): received.append(lax.ppermute(value, axis, pairs))  47.1 us
    ppermute x23, starting transfers between devices, members(): received.append(lax.ppermute(value, axis, pairs))  31.7 us
    ppermute x2, starting transfers between devices, passed_along(): lax.ppermute(value, axis, [(source, source + steps) for source in range(f...  3.83 us
  transfers between devices with their start and end apart: 25, of which 19 were waited for; matrix products, arithmetic and copies ran while one was open for 9% of the time, Pallas kernels for 0%

profile of v13, /device:TPU:32, one launch (start us, length us, event | category | flops | bytes accessed | tf_op | source)
XLA Modules:
  0.0 111.3 jit_solution(16910466057622635908)
XLA Ops:
  1.4 1.9 %collective-permute-start = (bf16[2,1024]{1,0:T(2,128)(2,1)S(1)}, bf16[2,1024]{1,0:T(2,128)(2,1)S(1)}, u32[]{:S(2)}, u32[]{:S(2)}) collective-permute-start(bf16[2,1024]{1,0:T(2,128)(2,1)S(1)} %slice.598), channel_id=1, source_target_pairs={{0,4},{4,8},{8,12},{12,16},{16,20},{20,24},{24,28},{28,32},{32,36}... | collective-permute-start | bytes 12296 | tf_op jit(solution)/shard_map/ppermute | solution.py:17
  5.9 2.0 %multiply_exponential_fusion = (f32[16,32,1024]{2,1,0:T(8,128)}, f32[16,32,1024]{2,1,0:T(8,128)S(1)}) fusion(f32[32]{0:T(128)S(1)} %broadcast_subtract_fusion.1, f32[16,1024]{1,0:T(8,128)S(1)} %neg.5, f32[32]{0:T(128)S(1)} %iota_convert_fusion.1), kind=kLoop, calls=%fused_computation.108 | loop fusion | flops 1048576 | bytes 4260096 | tf_op jit(solution)/shard_map/exp | solution.py:160
  8.0 2.8 %collective-permute-start.1 = (f32[130]{0:T(256)S(1)}, f32[130]{0:T(256)S(1)}, u32[]{:S(2)}, u32[]{:S(2)}) collective-permute-start(f32[130]{0:T(256)S(1)} %fusion.3), channel_id=1, source_target_pairs={{1,0},{2,1},{3,2},{0,3},{5,4},{6,5},{7,6},{4,7},{9,8},{10,9},{11,1... | collective-permute-start | bytes 1568 | tf_op jit(solution)/shard_map/ppermute | solution.py:64
  12.6 3.4 %collective-permute-done.2 = f32[130]{0:T(256)S(1)} collective-permute-done((f32[130]{0:T(256)S(1)}, f32[130]{0:T(256)S(1)}, u32[]{:S(2)}, u32[]{:S(2)}) %collective-permute-start.2) | collective-permute-done | bytes 552 | tf_op jit(solution)/shard_map/ppermute | solution.py:64
  21.3 1.9 %collective-permute-start.5 = (f32[2,16,1024]{2,1,0:T(8,128)S(1)}, f32[2,16,1024]{2,1,0:T(8,128)S(1)}, u32[]{:S(2)}, u32[]{:S(2)}) collective-permute-start(f32[2,16,1024]{2,1,0:T(8,128)S(1)} %pad_maximum_fusion.3), channel_id=1, source_target_pairs={{8,0},{12,4},{0,8},{4,12},{24,16},{28,20},{16,24},{20,28},{40,32},... | collective-permute-start | bytes 393224 | tf_op jit(solution)/shard_map/ppermute | solution.py:64
  25.2 4.8 %collective-permute-done.5 = f32[2,16,1024]{2,1,0:T(8,128)S(1)} collective-permute-done((f32[2,16,1024]{2,1,0:T(8,128)S(1)}, f32[2,16,1024]{2,1,0:T(8,128)S(1)}, u32[]{:S(2)}, u32[]{:S(2)}) %collective-permute-start.5) | collective-permute-done | bytes 131104 | tf_op jit(solution)/shard_map/ppermute | solution.py:64
  30.3 4.9 %collective-permute-start.7 = (f32[2,16,1024]{2,1,0:T(8,128)S(1)}, f32[2,16,1024]{2,1,0:T(8,128)S(1)}, u32[]{:S(2)}, u32[]{:S(2)}) collective-permute-start(f32[2,16,1024]{2,1,0:T(8,128)S(1)} %pad_maximum_fusion.4), channel_id=1, source_target_pairs={{16,0},{20,4},{24,8},{28,12},{32,16},{36,20},{40,24},{44,28},{48,3... | collective-permute-start | bytes 393224 | tf_op jit(solution)/shard_map/ppermute | solution.py:64
  36.4 2.4 %collective-permute-start.9 = (f32[2,16,1024]{2,1,0:T(8,128)S(1)}, f32[2,16,1024]{2,1,0:T(8,128)S(1)}, u32[]{:S(2)}, u32[]{:S(2)}) collective-permute-start(f32[2,16,1024]{2,1,0:T(8,128)S(1)} %pad_maximum_fusion.4), channel_id=1, source_target_pairs={{48,0},{52,4},{56,8},{60,12},{0,16},{4,20},{8,24},{12,28},{16,32},... | collective-permute-start | bytes 393224 | tf_op jit(solution)/shard_map/ppermute | solution.py:64
  42.1 5.7 %collective-permute-done.8 = f32[2,16,1024]{2,1,0:T(8,128)S(1)} collective-permute-done((f32[2,16,1024]{2,1,0:T(8,128)S(1)}, f32[2,16,1024]{2,1,0:T(8,128)S(1)}, u32[]{:S(2)}, u32[]{:S(2)}) %collective-permute-start.8) | collective-permute-done | bytes 131104 | tf_op jit(solution)/shard_map/ppermute | solution.py:64
  48.4 3.1 %collective-permute-start.10 = (f32[2,16,1024]{2,1,0:T(8,128)S(1)}, f32[2,16,1024]{2,1,0:T(8,128)S(1)}, u32[]{:S(2)}, u32[]{:S(2)}) collective-permute-start(f32[2,16,1024]{2,1,0:T(8,128)S(1)} %pad_maximum_fusion.5), channel_id=1, source_target_pairs={{64,0},{68,4},{72,8},{76,12},{80,16},{84,20},{88,24},{92,28},{96,3... | collective-permute-start | bytes 393224 | tf_op jit(solution)/shard_map/ppermute | solution.py:64
  53.1 4.1 %collective-permute-done.10 = f32[2,16,1024]{2,1,0:T(8,128)S(1)} collective-permute-done((f32[2,16,1024]{2,1,0:T(8,128)S(1)}, f32[2,16,1024]{2,1,0:T(8,128)S(1)}, u32[]{:S(2)}, u32[]{:S(2)}) %collective-permute-start.10) | collective-permute-done | bytes 131104 | tf_op jit(solution)/shard_map/ppermute | solution.py:64
  57.3 2.1 %collective-permute-done.11 = f32[2,16,1024]{2,1,0:T(8,128)S(1)} collective-permute-done((f32[2,16,1024]{2,1,0:T(8,128)S(1)}, f32[2,16,1024]{2,1,0:T(8,128)S(1)}, u32[]{:S(2)}, u32[]{:S(2)}) %collective-permute-start.11) | collective-permute-done | bytes 131104 | tf_op jit(solution)/shard_map/ppermute | solution.py:64
  62.9 1.9 %fusion.150 = f32[4,32,1024]{2,1,0:T(8,128)S(1)} fusion(f32[4,32,1024]{2,1,0:T(8,128)S(1)} %multiply_reduce_fusion, f32[4,32,1024]{2,1,0:T(8,128)S(1)} %bitcast.403, f32[1024]{0:T(1024)S(1)} %bitcast.418, f32[1024]{0:T(1024)S(1)} %bitcast.420, f32[1024]{0:T(1024)S(1)} %bitcast.422, f32[1024]{0:T(1024)S(1)} %bitcast.424, f32[1024]{0:T(1024)S(1)} %bitcast.426, ...), kind=kLoop, calls=%fused_computation.275 | loop fusion | flops 8388608 | bytes 1703936 | tf_op jit(solution)/shard_map/add | solution.py:220
  64.8 1.7 %fusion.87 = f32[4,32,1024]{2,1,0:T(8,128)S(1)} fusion(f32[4,32,1024]{2,1,0:T(8,128)S(1)} %multiply_reduce_fusion.1, f32[4,32,1024]{2,1,0:T(8,128)S(1)} %bitcast_convert_fusion, f32[1024]{0:T(1024)S(1)} %bitcast.419, f32[1024]{0:T(1024)S(1)} %bitcast.421, f32[1024]{0:T(1024)S(1)} %bitcast.423, f32[1024]{0:T(1024)S(1)} %bitcast.425, f32[1024]{0:T(1024)S(1)} %bitcast.427, ...), kind=kLoop, calls=%fused_computation.212 | loop fusion | flops 8388608 | bytes 1703936 | tf_op jit(solution)/shard_map/add | solution.py:212
  68.5 1.9 %collective-permute-start.13 = (bf16[3,2,1024]{2,1,0:T(2,128)(2,1)S(1)}, bf16[3,2,1024]{2,1,0:T(2,128)(2,1)S(1)}, u32[]{:S(2)}, u32[]{:S(2)}) collective-permute-start(bf16[3,2,1024]{2,1,0:T(2,128)(2,1)S(1)} %slice.827), channel_id=1, source_target_pairs={{4,0},{8,4},{12,8},{16,12},{20,16},{24,20},{28,24},{32,28},{36,32}... | collective-permute-start | bytes 36872 | tf_op jit(solution)/shard_map/ppermute | solution.py:17
  72.6 2.0 %collective-permute-start.16 = (f32[25,1024]{1,0:T(8,128)S(1)}, f32[25,1024]{1,0:T(8,128)S(1)}, u32[]{:S(2)}, u32[]{:S(2)}) collective-permute-start(f32[25,1024]{1,0:T(8,128)S(1)} %pad_maximum_fusion.6), channel_id=1, source_target_pairs={{4,0},{8,4},{12,8},{0,12},{20,16},{24,20},{28,24},{16,28},{36,32},... | collective-permute-start | bytes 307208 | tf_op jit(solution)/shard_map/ppermute | solution.py:64
  74.6 1.6 %collective-permute-start.17 = (f32[25,1024]{1,0:T(8,128)S(1)}, f32[25,1024]{1,0:T(8,128)S(1)}, u32[]{:S(2)}, u32[]{:S(2)}) collective-permute-start(f32[25,1024]{1,0:T(8,128)S(1)} %pad_maximum_fusion.6), channel_id=1, source_target_pairs={{8,0},{12,4},{0,8},{4,12},{24,16},{28,20},{16,24},{20,28},{40,32},... | collective-permute-start | bytes 307208 | tf_op jit(solution)/shard_map/ppermute | solution.py:64
  76.7 1.7 %collective-permute-done.16 = f32[25,1024]{1,0:T(8,128)S(1)} collective-permute-done((f32[25,1024]{1,0:T(8,128)S(1)}, f32[25,1024]{1,0:T(8,128)S(1)}, u32[]{:S(2)}, u32[]{:S(2)}) %collective-permute-start.16) | collective-permute-done | bytes 102432 | tf_op jit(solution)/shard_map/ppermute | solution.py:64
  78.4 4.5 %collective-permute-done.17 = f32[25,1024]{1,0:T(8,128)S(1)} collective-permute-done((f32[25,1024]{1,0:T(8,128)S(1)}, f32[25,1024]{1,0:T(8,128)S(1)}, u32[]{:S(2)}, u32[]{:S(2)}) %collective-permute-start.17) | collective-permute-done | bytes 102432 | tf_op jit(solution)/shard_map/ppermute | solution.py:64
  83.0 3.0 %collective-permute-start.19 = (f32[25,1024]{1,0:T(8,128)S(1)}, f32[25,1024]{1,0:T(8,128)S(1)}, u32[]{:S(2)}, u32[]{:S(2)}) collective-permute-start(f32[25,1024]{1,0:T(8,128)S(1)} %add_add_fusion.2), channel_id=1, source_target_pairs={{16,0},{20,4},{24,8},{28,12},{32,16},{36,20},{40,24},{44,28},{48,3... | collective-permute-start | bytes 307208 | tf_op jit(solution)/shard_map/ppermute | solution.py:64
  86.0 2.1 %collective-permute-start.20 = (f32[25,1024]{1,0:T(8,128)S(1)}, f32[25,1024]{1,0:T(8,128)S(1)}, u32[]{:S(2)}, u32[]{:S(2)}) collective-permute-start(f32[25,1024]{1,0:T(8,128)S(1)} %add_add_fusion.2), channel_id=1, source_target_pairs={{40,0},{44,4},{32,8},{36,12},{56,16},{60,20},{48,24},{52,28},{8,32... | collective-permute-start | bytes 307208 | tf_op jit(solution)/shard_map/ppermute | solution.py:64
  89.3 10.0 %collective-permute-done.20 = f32[25,1024]{1,0:T(8,128)S(1)} collective-permute-done((f32[25,1024]{1,0:T(8,128)S(1)}, f32[25,1024]{1,0:T(8,128)S(1)}, u32[]{:S(2)}, u32[]{:S(2)}) %collective-permute-start.20) | collective-permute-done | bytes 102432 | tf_op jit(solution)/shard_map/ppermute | solution.py:64
  103.0 3.5 %collective-permute-done.22 = f32[25,1024]{1,0:T(8,128)S(1)} collective-permute-done((f32[25,1024]{1,0:T(8,128)S(1)}, f32[25,1024]{1,0:T(8,128)S(1)}, u32[]{:S(2)}, u32[]{:S(2)}) %collective-permute-start.22) | collective-permute-done | bytes 102432 | tf_op jit(solution)/shard_map/ppermute | solution.py:64
  108.0 2.0 %collective-permute-done.24 = f32[25,1024]{1,0:T(8,128)S(1)} collective-permute-done((f32[25,1024]{1,0:T(8,128)S(1)}, f32[25,1024]{1,0:T(8,128)S(1)}, u32[]{:S(2)}, u32[]{:S(2)}) %collective-permute-start.24) | collective-permute-done | bytes 102432 | tf_op jit(solution)/shard_map/ppermute | solution.py:64
  (127 shorter events, 34.5 us)
Async XLA Ops:
  1.4 6.5 %collective-permute-start = (bf16[2,1024]{1,0:T(2,128)(2,1)S(1)}, bf16[2,1024]{1,0:T(2,128)(2,1)S(1)}, u32[]{:S(2)}, u32[]{:S(2)}) collective-permute-start(bf16[2,1024]{1,0:T(2,128)(2,1)S(1)} %slice.598), channel_id=1, source_target_pairs={{0,4},{4,8},{8,12},{12,16},{16,20},{20,24},{24,28},{28,32},{32,36}... | collective-permute-start | bytes 12296 | tf_op jit(solution)/shard_map/ppermute | solution.py:17
  8.0 4.5 %collective-permute-start.1 = (f32[130]{0:T(256)S(1)}, f32[130]{0:T(256)S(1)}, u32[]{:S(2)}, u32[]{:S(2)}) collective-permute-start(f32[130]{0:T(256)S(1)} %fusion.3), channel_id=1, source_target_pairs={{1,0},{2,1},{3,2},{0,3},{5,4},{6,5},{7,6},{4,7},{9,8},{10,9},{11,1... | collective-permute-start | bytes 1568 | tf_op jit(solution)/shard_map/ppermute | solution.py:64
  10.9 5.1 %collective-permute-start.2 = (f32[130]{0:T(256)S(1)}, f32[130]{0:T(256)S(1)}, u32[]{:S(2)}, u32[]{:S(2)}) collective-permute-start(f32[130]{0:T(256)S(1)} %fusion.3), channel_id=1, source_target_pairs={{2,0},{3,1},{0,2},{1,3},{6,4},{7,5},{4,6},{5,7},{10,8},{11,9},{8,1... | collective-permute-start | bytes 1568 | tf_op jit(solution)/shard_map/ppermute | solution.py:64
  11.7 4.8 %collective-permute-start.3 = (f32[130]{0:T(256)S(1)}, f32[130]{0:T(256)S(1)}, u32[]{:S(2)}, u32[]{:S(2)}) collective-permute-start(f32[130]{0:T(256)S(1)} %fusion.3), channel_id=1, source_target_pairs={{3,0},{0,1},{1,2},{2,3},{7,4},{4,5},{5,6},{6,7},{11,8},{8,9},{9,10... | collective-permute-start | bytes 1568 | tf_op jit(solution)/shard_map/ppermute | solution.py:64
  21.2 4.0 %collective-permute-start.4 = (f32[2,16,1024]{2,1,0:T(8,128)S(1)}, f32[2,16,1024]{2,1,0:T(8,128)S(1)}, u32[]{:S(2)}, u32[]{:S(2)}) collective-permute-start(f32[2,16,1024]{2,1,0:T(8,128)S(1)} %pad_maximum_fusion.3), channel_id=1, source_target_pairs={{4,0},{8,4},{12,8},{0,12},{20,16},{24,20},{28,24},{16,28},{36,32},... | collective-permute-start | bytes 393224 | tf_op jit(solution)/shard_map/ppermute | solution.py:64
  21.3 8.7 %collective-permute-start.5 = (f32[2,16,1024]{2,1,0:T(8,128)S(1)}, f32[2,16,1024]{2,1,0:T(8,128)S(1)}, u32[]{:S(2)}, u32[]{:S(2)}) collective-permute-start(f32[2,16,1024]{2,1,0:T(8,128)S(1)} %pad_maximum_fusion.3), channel_id=1, source_target_pairs={{8,0},{12,4},{0,8},{4,12},{24,16},{28,20},{16,24},{20,28},{40,32},... | collective-permute-start | bytes 393224 | tf_op jit(solution)/shard_map/ppermute | solution.py:64
  23.3 6.8 %collective-permute-start.6 = (f32[2,16,1024]{2,1,0:T(8,128)S(1)}, f32[2,16,1024]{2,1,0:T(8,128)S(1)}, u32[]{:S(2)}, u32[]{:S(2)}) collective-permute-start(f32[2,16,1024]{2,1,0:T(8,128)S(1)} %pad_maximum_fusion.3), channel_id=1, source_target_pairs={{12,0},{0,4},{4,8},{8,12},{28,16},{16,20},{20,24},{24,28},{44,32},... | collective-permute-start | bytes 393224 | tf_op jit(solution)/shard_map/ppermute | solution.py:64
  30.3 11.9 %collective-permute-start.7 = (f32[2,16,1024]{2,1,0:T(8,128)S(1)}, f32[2,16,1024]{2,1,0:T(8,128)S(1)}, u32[]{:S(2)}, u32[]{:S(2)}) collective-permute-start(f32[2,16,1024]{2,1,0:T(8,128)S(1)} %pad_maximum_fusion.4), channel_id=1, source_target_pairs={{16,0},{20,4},{24,8},{28,12},{32,16},{36,20},{40,24},{44,28},{48,3... | collective-permute-start | bytes 393224 | tf_op jit(solution)/shard_map/ppermute | solution.py:64
  35.2 12.6 %collective-permute-start.8 = (f32[2,16,1024]{2,1,0:T(8,128)S(1)}, f32[2,16,1024]{2,1,0:T(8,128)S(1)}, u32[]{:S(2)}, u32[]{:S(2)}) collective-permute-start(f32[2,16,1024]{2,1,0:T(8,128)S(1)} %pad_maximum_fusion.4), channel_id=1, source_target_pairs={{40,0},{44,4},{32,8},{36,12},{56,16},{60,20},{48,24},{52,28},{8,32... | collective-permute-start | bytes 393224 | tf_op jit(solution)/shard_map/ppermute | solution.py:64
  36.4 11.9 %collective-permute-start.9 = (f32[2,16,1024]{2,1,0:T(8,128)S(1)}, f32[2,16,1024]{2,1,0:T(8,128)S(1)}, u32[]{:S(2)}, u32[]{:S(2)}) collective-permute-start(f32[2,16,1024]{2,1,0:T(8,128)S(1)} %pad_maximum_fusion.4), channel_id=1, source_target_pairs={{48,0},{52,4},{56,8},{60,12},{0,16},{4,20},{8,24},{12,28},{16,32},... | collective-permute-start | bytes 393224 | tf_op jit(solution)/shard_map/ppermute | solution.py:64
  48.4 8.9 %collective-permute-start.10 = (f32[2,16,1024]{2,1,0:T(8,128)S(1)}, f32[2,16,1024]{2,1,0:T(8,128)S(1)}, u32[]{:S(2)}, u32[]{:S(2)}) collective-permute-start(f32[2,16,1024]{2,1,0:T(8,128)S(1)} %pad_maximum_fusion.5), channel_id=1, source_target_pairs={{64,0},{68,4},{72,8},{76,12},{80,16},{84,20},{88,24},{92,28},{96,3... | collective-permute-start | bytes 393224 | tf_op jit(solution)/shard_map/ppermute | solution.py:64
  51.5 7.9 %collective-permute-start.11 = (f32[2,16,1024]{2,1,0:T(8,128)S(1)}, f32[2,16,1024]{2,1,0:T(8,128)S(1)}, u32[]{:S(2)}, u32[]{:S(2)}) collective-permute-start(f32[2,16,1024]{2,1,0:T(8,128)S(1)} %pad_maximum_fusion.5), channel_id=1, source_target_pairs={{128,0},{132,4},{136,8},{140,12},{144,16},{148,20},{152,24},{156,2... | collective-permute-start | bytes 393224 | tf_op jit(solution)/shard_map/ppermute | solution.py:64
  52.1 8.9 %collective-permute-start.12 = (f32[2,16,1024]{2,1,0:T(8,128)S(1)}, f32[2,16,1024]{2,1,0:T(8,128)S(1)}, u32[]{:S(2)}, u32[]{:S(2)}) collective-permute-start(f32[2,16,1024]{2,1,0:T(8,128)S(1)} %pad_maximum_fusion.5), channel_id=1, source_target_pairs={{192,0},{196,4},{200,8},{204,12},{208,16},{212,20},{216,24},{220,2... | collective-permute-start | bytes 393224 | tf_op jit(solution)/shard_map/ppermute | solution.py:64
  72.5 3.8 %collective-permute-start.14 = (f32[128]{0:T(128)S(1)}, f32[128]{0:T(128)S(1)}, u32[]{:S(2)}, u32[]{:S(2)}) collective-permute-start(f32[128]{0:T(128)S(1)} %get-tuple-element.59), channel_id=1, source_target_pairs={{1,0},{0,1},{3,2},{2,3},{5,4},{4,5},{7,6},{6,7},{9,8},{8,9},{11,10... | collective-permute-start | bytes 1544 | tf_op jit(solution)/shard_map/ppermute | solution.py:64
  72.6 5.8 %collective-permute-start.16 = (f32[25,1024]{1,0:T(8,128)S(1)}, f32[25,1024]{1,0:T(8,128)S(1)}, u32[]{:S(2)}, u32[]{:S(2)}) collective-permute-start(f32[25,1024]{1,0:T(8,128)S(1)} %pad_maximum_fusion.6), channel_id=1, source_target_pairs={{4,0},{8,4},{12,8},{0,12},{20,16},{24,20},{28,24},{16,28},{36,32},... | collective-permute-start | bytes 307208 | tf_op jit(solution)/shard_map/ppermute | solution.py:64
  74.6 8.3 %collective-permute-start.17 = (f32[25,1024]{1,0:T(8,128)S(1)}, f32[25,1024]{1,0:T(8,128)S(1)}, u32[]{:S(2)}, u32[]{:S(2)}) collective-permute-start(f32[25,1024]{1,0:T(8,128)S(1)} %pad_maximum_fusion.6), channel_id=1, source_target_pairs={{8,0},{12,4},{0,8},{4,12},{24,16},{28,20},{16,24},{20,28},{40,32},... | collective-permute-start | bytes 307208 | tf_op jit(solution)/shard_map/ppermute | solution.py:64
  76.3 6.7 %collective-permute-start.18 = (f32[25,1024]{1,0:T(8,128)S(1)}, f32[25,1024]{1,0:T(8,128)S(1)}, u32[]{:S(2)}, u32[]{:S(2)}) collective-permute-start(f32[25,1024]{1,0:T(8,128)S(1)} %pad_maximum_fusion.6), channel_id=1, source_target_pairs={{12,0},{0,4},{4,8},{8,12},{28,16},{16,20},{20,24},{24,28},{44,32},... | collective-permute-start | bytes 307208 | tf_op jit(solution)/shard_map/ppermute | solution.py:64
  76.3 12.5 %collective-permute-start.15 = (f32[128]{0:T(128)S(1)}, f32[128]{0:T(128)S(1)}, u32[]{:S(2)}, u32[]{:S(2)}) collective-permute-start(f32[128]{0:T(128)S(1)} %fusion.275), channel_id=1, source_target_pairs={{3,0},{2,1},{1,2},{0,3},{7,4},{6,5},{5,6},{4,7},{11,8},{10,9},{9,1... | collective-permute-start | bytes 1544 | tf_op jit(solution)/shard_map/ppermute | solution.py:64
  83.0 6.2 %collective-permute-start.19 = (f32[25,1024]{1,0:T(8,128)S(1)}, f32[25,1024]{1,0:T(8,128)S(1)}, u32[]{:S(2)}, u32[]{:S(2)}) collective-permute-start(f32[25,1024]{1,0:T(8,128)S(1)} %add_add_fusion.2), channel_id=1, source_target_pairs={{16,0},{20,4},{24,8},{28,12},{32,16},{36,20},{40,24},{44,28},{48,3... | collective-permute-start | bytes 307208 | tf_op jit(solution)/shard_map/ppermute | solution.py:64
  86.0 13.3 %collective-permute-start.20 = (f32[25,1024]{1,0:T(8,128)S(1)}, f32[25,1024]{1,0:T(8,128)S(1)}, u32[]{:S(2)}, u32[]{:S(2)}) collective-permute-start(f32[25,1024]{1,0:T(8,128)S(1)} %add_add_fusion.2), channel_id=1, source_target_pairs={{40,0},{44,4},{32,8},{36,12},{56,16},{60,20},{48,24},{52,28},{8,32... | collective-permute-start | bytes 307208 | tf_op jit(solution)/shard_map/ppermute | solution.py:64
  88.1 11.9 %collective-permute-start.21 = (f32[25,1024]{1,0:T(8,128)S(1)}, f32[25,1024]{1,0:T(8,128)S(1)}, u32[]{:S(2)}, u32[]{:S(2)}) collective-permute-start(f32[25,1024]{1,0:T(8,128)S(1)} %add_add_fusion.2), channel_id=1, source_target_pairs={{48,0},{52,4},{56,8},{60,12},{0,16},{4,20},{8,24},{12,28},{16,32},... | collective-permute-start | bytes 307208 | tf_op jit(solution)/shard_map/ppermute | solution.py:64
  100.0 6.4 %collective-permute-start.22 = (f32[25,1024]{1,0:T(8,128)S(1)}, f32[25,1024]{1,0:T(8,128)S(1)}, u32[]{:S(2)}, u32[]{:S(2)}) collective-permute-start(f32[25,1024]{1,0:T(8,128)S(1)} %add_add_fusion.1), channel_id=1, source_target_pairs={{64,0},{68,4},{72,8},{76,12},{80,16},{84,20},{88,24},{92,28},{96,3... | collective-permute-start | bytes 307208 | tf_op jit(solution)/shard_map/ppermute | solution.py:64
  100.1 7.8 %collective-permute-start.23 = (f32[25,1024]{1,0:T(8,128)S(1)}, f32[25,1024]{1,0:T(8,128)S(1)}, u32[]{:S(2)}, u32[]{:S(2)}) collective-permute-start(f32[25,1024]{1,0:T(8,128)S(1)} %add_add_fusion.1), channel_id=1, source_target_pairs={{128,0},{132,4},{136,8},{140,12},{144,16},{148,20},{152,24},{156,2... | collective-permute-start | bytes 307208 | tf_op jit(solution)/shard_map/ppermute | solution.py:64
  100.9 9.0 %collective-permute-start.24 = (f32[25,1024]{1,0:T(8,128)S(1)}, f32[25,1024]{1,0:T(8,128)S(1)}, u32[]{:S(2)}, u32[]{:S(2)}) collective-permute-start(f32[25,1024]{1,0:T(8,128)S(1)} %add_add_fusion.1), channel_id=1, source_target_pairs={{192,0},{196,4},{200,8},{204,12},{208,16},{212,20},{216,24},{220,2... | collective-permute-start | bytes 307208 | tf_op jit(solution)/shard_map/ppermute | solution.py:64
  (16 other events, 83.9 us)
